TPU v7x, 32 devices: a whole 2x2x4 slice. The times are simulated.
32 devices in a mesh: groups: 2 (over y), tiles: 4 (over z), band: 2 (over x), rep: 2 (over core).
Axes of the slice: x: 2, y: 2, z: 4, core: 2. Of those that a mesh axis runs over, the one named last changes fastest.
Arguments:
- features: bfloat16 [8, 16, 2, 16, 128], P(('groups', 'band'), 'tiles'), parts along dimension 0, may hold values from -6 to 6
- state: float32 [8, 16, 16, 16, 128], P(('groups', 'band'), 'tiles'), parts along dimension 0, may hold values from -3 to 3
- live: int32 [16], P('tiles'), may hold values from 0 to 1, as said below
- neighbours: int32 [16, 2], P('tiles'), may hold values from -1 to 15, as said below
- coarse_perm: int32 [4, 4], P('tiles'), may hold values from 0 to 3, as said below
- coarse_state: float32 [32, 16, 4, 32], P(('groups', 'tiles', 'band')), parts along dimension 0, may hold values from -3 to 3
- w_update: bfloat16 [9, 16, 18], replicated, may hold values from -0.5 to 0.5
- b_update: float32 [16], replicated, may hold values from -3 to 3
- w_reset: bfloat16 [9, 16, 18], replicated, may hold values from -0.5 to 0.5
- b_reset: float32 [16], replicated, may hold values from -3 to 3
- w_cand: bfloat16 [9, 16, 18], replicated, may hold values from -0.5 to 0.5
- b_cand: float32 [16], replicated, may hold values from -3 to 3
- u_pool: float32 [16, 16], replicated, may hold values from -1.5 to 1.5
- u_state: float32 [16, 16], replicated, may hold values from -1.5 to 1.5
- b_coarse: float32 [16], replicated, may hold values from -3 to 3
Outputs:
- new_state: float32 [8, 16, 16, 16, 128], P(('groups', 'band'), 'tiles', 'rep'), parts along dimension 0
- coarse_next: float32 [32, 16, 4, 32], P(('groups', 'tiles', 'band')), parts along dimension 0
There are 2 independent parts, one for each index of `groups`. A program takes and returns all parts, laid end to end along the dimension named above; an argument that names none is the same for every part. Nothing has to cross between parts.
Inputs may be any that keep to these rules, and one draw needn't show every extreme that they name: Every device of tiles has between 1 and 4 live slots, at any positions; in every draw some device has all 4 live. `neighbours`: the live tiles form one vertical chain that passes the devices of tiles in index order, each device's live tiles forming one run of the chain in some order; entry 0 names the tile above, entry 1 the tile below, -1 at the chain's two ends and in both entries of an empty slot. `coarse_perm`: each row is a permutation of 0 to 3.
All inputs are finite; a program needn't handle non-finite values.
Results may differ from a plain program's by a relative error of at most 0.0013.
Values may be sent and summed in bfloat16 or wider, within the bound.
No kernel may reach another device: no remote copies, remote signals or barrier semaphores. Data moves between devices by JAX's collectives and lax.ppermute only.
A program may use at most 64 MiB of HBM per device.

v0:
```python
import jax
import jax.numpy as jnp
from jax import lax
from jax.sharding import PartitionSpec as P


def padded(block, sides, width):
    for axis, dim in sides:
        count = lax.axis_size(axis)
        forward = [(i, i + 1) for i in range(count - 1)]
        backward = [(target, source) for source, target in forward]
        low = lax.ppermute(
            lax.slice_in_dim(block, block.shape[dim] - width, None, axis=dim), axis, forward
        )
        high = lax.ppermute(lax.slice_in_dim(block, 0, width, axis=dim), axis, backward)
        block = jnp.concatenate([low, block, high], axis=dim)
    return block


def apply_filter(
    padded_input, filter_weight, dilation_rate, first_row_index, row_count, column_count
):
    total = None
    for left_operand in (-1, 0, 1):
        for right_operand in (-1, 0, 1):
            window_slice = padded_input[
                :,
                :,
                :,
                first_row_index
                + left_operand * dilation_rate : first_row_index
                + left_operand * dilation_rate
                + row_count,
                2
                + right_operand * dilation_rate : 2
                + right_operand * dilation_rate
                + column_count,
            ]
            term = jnp.einsum(
                "oi,bsirw->bsorw",
                filter_weight[(left_operand + 1) * 3 + (right_operand + 1)],
                window_slice,
                preferred_element_type=jnp.float32,
            )
            total = term if total is None else total + term
    return total


def choose_rows(block, select):
    masked = jnp.where(select[None, :, None, None, None], block, jnp.zeros_like(block))
    return jnp.sum(masked, axis=1)


def shards(
    features,
    state,
    live,
    neighbours,
    coarse_perm,
    coarse_state,
    w_update,
    b_update,
    w_reset,
    b_reset,
    w_cand,
    b_cand,
    u_pool,
    u_state,
    b_coarse,
):
    slots = state.shape[1]
    chans = state.shape[2]
    row_count = state.shape[3]
    column_count = state.shape[4]
    inputs_count = features.shape[2]
    half = chans // lax.axis_size("rep")
    start = lax.axis_index("rep") * half
    base = lax.axis_index("tiles") * slots
    ups = neighbours[:, 0]
    downs = neighbours[:, 1]
    up_here = (ups >= base) & (ups < base + slots)
    down_here = (downs >= base) & (downs < base + slots)
    up_far = (ups >= 0) & jnp.logical_not(up_here)
    down_far = (downs >= 0) & jnp.logical_not(down_here)
    alive = live > 0
    first_sel = alive & jnp.logical_not(up_here)
    last_sel = alive & jnp.logical_not(down_here)

    def own_out(filter_weight):
        return lax.dynamic_slice_in_dim(filter_weight, start, half, 1)

    def own_bias(bias):
        return lax.dynamic_slice_in_dim(bias, start, half, 0)[:, None, None]

    hb = state.astype(jnp.bfloat16)
    joined = jnp.concatenate([features, hb], axis=2)
    top = choose_rows(joined[:, :, :, :3, :], first_sel)
    bottom = choose_rows(joined[:, :, :, row_count - 3 :, :], last_sel)
    cycle = padded(jnp.concatenate([top, bottom], axis=2), (("tiles", 2),), 3)
    cycle_prev = cycle[:, None, :, :3, :]
    cycle_next = cycle[:, None, :, 3 * 3 : 4 * 3, :]
    top_local = jnp.take(
        joined[:, :, :, row_count - 3 :, :], jnp.clip(ups - base, 0, slots - 1), axis=1
    )
    bottom_local = jnp.take(joined[:, :, :, :3, :], jnp.clip(downs - base, 0, slots - 1), axis=1)
    zeros_rows = jnp.zeros_like(top_local)
    top = jnp.where(
        up_here[None, :, None, None, None],
        top_local,
        jnp.where(up_far[None, :, None, None, None], cycle_prev + zeros_rows, zeros_rows),
    )
    bottom = jnp.where(
        down_here[None, :, None, None, None],
        bottom_local,
        jnp.where(down_far[None, :, None, None, None], cycle_next + zeros_rows, zeros_rows),
    )
    full = jnp.concatenate([top, joined, bottom], axis=3)
    first = jnp.pad(full, ((0, 0), (0, 0), (0, 0), (0, 0), (2, 2)))
    update = jax.nn.sigmoid(
        apply_filter(first, own_out(w_update), 1, 3, row_count, column_count) + own_bias(b_update)
    )
    hidden_wide = first[:, :, inputs_count:, 1 : row_count + 5, 2 : column_count + 2]
    reset_half = jax.nn.sigmoid(
        apply_filter(first, own_out(w_reset), 1, 1, row_count + 4, column_count) + own_bias(b_reset)
    )
    wide_half = lax.dynamic_slice_in_dim(hidden_wide, start, half, 2)
    gated = lax.all_gather(
        (reset_half * wide_half.astype(jnp.float32)).astype(jnp.bfloat16), "rep", axis=2, tiled=True
    )
    gated_pad = jnp.pad(gated, ((0, 0), (0, 0), (0, 0), (0, 0), (2, 2)))
    second = jnp.concatenate([first[:, :, :inputs_count, 1 : row_count + 5, :], gated_pad], axis=2)
    candidate = jnp.tanh(
        apply_filter(second, own_out(w_cand), 2, 2, row_count, column_count) + own_bias(b_cand)
    )
    state_half = lax.dynamic_slice_in_dim(state, start, half, 2)
    live_scale = alive.astype(jnp.float32)[None, :, None, None, None]
    new_half = ((1.0 - update) * state_half + update * candidate) * live_scale
    band_local = new_half.shape[0]
    blocks = new_half.reshape(band_local, slots, half, row_count // 4, 4, column_count // 4, 4)
    pooled = jnp.sum(jnp.sum(blocks, axis=(4, 6)), axis=0) / 16.0
    ordered = jnp.take(pooled, coarse_perm[0], axis=0)
    owned = lax.psum_scatter(ordered, "band", scatter_dimension=0, tiled=True)
    pooled_all = lax.all_gather(owned, "rep", axis=1, tiled=True)
    pre = jnp.einsum("oc,kcij->koij", u_pool, pooled_all, precision=lax.Precision.HIGHEST)
    pre = pre + jnp.einsum("oc,kcij->koij", u_state, coarse_state, precision=lax.Precision.HIGHEST)
    pre = pre + b_coarse[None, :, None, None]
    coarse_next = coarse_state + jnp.tanh(pre)
    return (new_half, coarse_next)


def solution(mesh):
    return jax.shard_map(
        shards,
        mesh=mesh,
        in_specs=(
            P(("groups", "band"), "tiles", None, None, None),
            P(("groups", "band"), "tiles", None, None, None),
            P("tiles"),
            P("tiles", None),
            P("tiles", None),
            P(("groups", "tiles", "band"), None, None, None),
            P(),
            P(),
            P(),
            P(),
            P(),
            P(),
            P(),
            P(),
            P(),
        ),
        out_specs=(
            P(("groups", "band"), "tiles", "rep", None, None),
            P(("groups", "tiles", "band"), None, None, None),
        ),
        check_vma=False,
    )
```

profile of v0, /device:TPU:0, one launch (start us, length us, event | category | flops | bytes accessed | tf_op | source)
XLA Modules:
  0.0 65.9 jit_solution(5684396351804242542)
XLA Ops:
  7.3 0.8 %not_and_fusion = (pred[4]{0:T(512)(128)(4,1)S(1)}, pred[4]{0:T(512)(128)(4,1)S(1)}) fusion(s32[4]{0:T(128)} %param.19, s32[]{:T(128)S(6)} %add.187, s32[]{:T(128)S(6)} %mul.23, s32[4,2]{0,1:T(2,128)} %param.20), kind=kLoop, calls=%fused_computation.176 | loop fusion | flops 24 | bytes 48 | tf_op jit(solution)/shard_map/and | solution.py:87
  8.0 0.8 %compare_and_fusion.1 = (pred[4]{0:T(512)(128)(4,1)S(1)}, s32[4]{0:T(128)S(1)}, pred[4]{0:T(512)(128)(4,1)S(1)}, pred[4]{0:T(512)(128)(4,1)S(1)}, s32[4]{0:T(128...) fusion(s32[]{:T(128)S(6)} %mul.23, s32[4,2]{0,1:T(2,128)} %param.20, ...), kind=kLoop, calls=%fused_computation.172 | loop fusion | flops 124 | bytes 116 | tf_op jit(solution)/shard_map/jit(_take)/and | solution.py:102
  8.8 0.7 %fusion.109 = (f32[4]{0:T(128)S(1)}, pred[4]{0:T(512)(128)(4,1)S(1)}) fusion(s32[4]{0:T(128)} %param.19, pred[4]{0:T(512)(128)(4,1)S(1)} %get-tuple-element.27), kind=kLoop, calls=%fused_computation.180 | loop fusion | flops 16 | bytes 40 | tf_op jit(solution)/shard_map/convert_element_type | solution.py:136
  9.5 1.6 %copy.83 = bf16[2,4,16,16,128]{4,2,3,1,0:T(8,128)(2,1)S(1)} copy(f32[2,4,16,16,128]{4,3,2,1,0:T(8,128)} %param.18) | data formatting | bytes 1572864 | tf_op args[1]
  11.1 0.9 %copy.36 = bf16[2,4,2,16,128]{4,2,3,1,0:T(2,128)(2,1)S(1)} copy(bf16[2,4,2,16,128]{4,3,2,1,0:T(8,128)(2,1)} %param.17) | data formatting | bytes 131072 | tf_op args[0]
  12.2 1.3 %collective-permute-start.1 = (bf16[2,18,3,128]{3,1,2,0:T(8,128)(2,1)S(1)}, bf16[2,18,3,128]{3,1,2,0:T(8,128)(2,1)S(1)}, u32[]{:S(2)}, u32[]{:S(2)}) collective-permute-start(bf16[2,18,3,128]{3,1,2,0:T(8,128)(2,1)S(1)} %get-tuple-element.21), channel_id=1, source_target_pairs={{4,0},{8,4},{12,8},{5,1},{9,5},{13,9},{6,2},{10,6},{14,10},{7,3},{... | collective-permute-start | bytes 82952 | tf_op jit(solution)/shard_map/ppermute | solution.py:15
  13.5 5.6 %collective-permute-start = (bf16[2,18,3,128]{3,1,2,0:T(8,128)(2,1)S(1)}, bf16[2,18,3,128]{3,1,2,0:T(8,128)(2,1)S(1)}, u32[]{:S(2)}, u32[]{:S(2)}) collective-permute-start(bf16[2,18,3,128]{3,1,2,0:T(8,128)(2,1)S(1)} %get-tuple-element.9), channel_id=1, source_target_pairs={{0,4},{4,8},{8,12},{1,5},{5,9},{9,13},{2,6},{6,10},{10,14},{3,7},{... | collective-permute-start | bytes 82952 | tf_op jit(solution)/shard_map/ppermute | solution.py:12
  19.1 0.3 copy.35
  19.8 0.6 gather_fusion.2
  20.4 0.8 %gather_fusion.1 = bf16[4,2,18,3,128]{4,1,3,2,0:T(2,128)(2,1)S(1)} fusion(bf16[2,4,18,3,128]{4,0,3,2,1:T(2,128)(2,1)S(1)} %copy.37, s32[1024]{0:T(1024)S(1)} %pad_clamp_fusion.2), kind=kCustom, calls=%fused_computation.clone | custom fusion | bytes 221200 | tf_op jit(solution)/shard_map/jit(_take)/gather | solution.py:102
  21.4 0.3 pad_maximum_fusion
  21.8 0.3 slice.254
  22.3 0.4 fusion.35
  22.7 0.3 convolution_add_fusion.9
  23.1 0.3 fusion.94
  23.4 0.4 convolution_add_fusion.5
  23.8 0.4 convolution_add_fusion.23
  24.2 0.4 convolution_add_fusion.4
  24.7 0.4 convolution_add_fusion.22
  25.1 0.4 convolution_add_fusion.3
  25.5 0.3 convolution_add_fusion.21
  25.8 0.3 convolution_add_fusion.7
  26.2 0.4 convolution_add_fusion.20
  26.6 0.4 convolution_add_fusion.2
  27.0 0.4 convolution_add_fusion.19
  27.4 0.4 convolution_add_fusion.1
  27.8 0.3 convolution_add_fusion.8
  28.2 0.3 convolution_add_fusion.6
  28.5 0.5 fusion.20
  29.0 2.5 %all_gather.6 = bf16[2,4,16,20,128]{4,2,3,1,0:T(8,128)(2,1)S(1)} all-gather(bf16[2,4,8,20,128]{4,2,3,1,0:T(8,128)(2,1)S(1)} %fusion.20), channel_id=1, replica_groups=mesh['groups'=2,'tiles'=4,'band'=2,'rep'=2] {'rep'}, dimensions={2}, use_global_device_ids=true | all-gather | bytes 983040 | tf_op jit(solution)/shard_map/all_gather | solution.py:127
  31.5 1.1 %fusion.1 = bf16[2,4,18,20,132]{4,2,3,1,0:T(8,128)(2,1)S(1)} fusion(bf16[2,4,16,20,128]{4,2,3,1,0:T(8,128)(2,1)S(1)} %all_gather.6, bf16[2,4,2,20,132]{4,2,3,1,0:T(2,128)(2,1)S(1)} %pad_slice_fusion.6), kind=kLoop, calls=%fused_computation.18 | loop fusion | flops 2280960 | bytes 1500160 | tf_op jit(solution)/shard_map/concatenate | solution.py:131
  32.9 0.4 convolution_add_fusion.17
  33.3 0.4 convolution_add_fusion.16
  33.7 0.2 convolution_add_fusion.15
  34.0 0.4 convolution_add_fusion.14
  34.4 0.4 convolution_add_fusion.13
  34.8 0.2 convolution_add_fusion.12
  35.1 0.4 convolution_add_fusion.11
  35.5 0.4 fusion.13
  35.9 0.4 fusion.125
  36.3 2.6 %copy.41 = f32[4,8,16,128]{1,3,2,0:T(8,128)} copy(f32[4,8,16,128]{3,1,2,0:T(8,128)S(1)} %get-tuple-element.30) | data formatting | bytes 524288 | tf_op jit(solution)/shard_map/reduce_sum | solution.py:140
  38.9 3.6 %reduce_sum.48 = f32[4,8,4,32]{1,3,2,0:T(8,128)S(1)} reduce(f32[4,8,4,4,32,4]{1,5,4,3,2,0:T(4,128)} %bitcast.250, f32[]{:T(128)} %constant.53.clone.1), dimensions={3,5}, to_apply=%region_3.5 | reduce | flops 61440 | bytes 278532 | tf_op jit(solution)/shard_map/reduce_sum | solution.py:140
  42.7 0.6 gather_fusion
  43.2 0.7 %broadcast_select_fusion = f32[4,8,4,32]{3,1,2,0:T(8,128)} fusion(f32[4,8,4,32]{3,1,2,0:T(8,128)S(1)} %gather_fusion, pred[4]{0:T(512)(128)(4,1)S(1)} %get-tuple-element.32), kind=kLoop, calls=%fused_computation.102 | loop fusion | flops 4096 | bytes 32772 | tf_op jit(solution)/shard_map/jit(_take)/select_n | solution.py:141
  44.0 0.9 %copy.45 = f32[2,4,8,16,128]{4,3,2,1,0:T(8,128)} copy(f32[2,4,8,16,128]{4,2,3,1,0:T(8,128)S(1)} %get-tuple-element.31) | data formatting | bytes 1048576
  44.9 11.1 %reduce-scatter.2.cloned.1.call-done = f32[2,8,4,32]{3,1,2,0:T(8,128)} async-done(((f32[4,8,4,32]{3,1,2,0:T(8,128)}), f32[2,8,4,32]{3,1,2,0:T(8,128)}) %reduce-scatter.2.cloned.1.call-update) | async-done | bytes 8208 | tf_op jit(solution)/shard_map/reduce_scatter | solution.py:142
  55.9 2.1 %all_gather.7 = f32[2,16,4,32]{3,1,2,0:T(8,128)S(1)} all-gather(f32[2,8,4,32]{3,1,2,0:T(8,128)} %reduce-scatter.2.cloned.1.call-done), channel_id=1, replica_groups=mesh['groups'=2,'tiles'=4,'band'=2,'rep'=2] {'rep'}, dimensions={1}, use_global_device_ids=true | all-gather | bytes 24576 | tf_op jit(solution)/shard_map/all_gather | solution.py:143
  58.4 0.7 copy.46
  (45 shorter events, 1.9 us)
Async XLA Ops:
  7.2 15.9 %copy-start = (bf16[9,16,18]{2,1,0:T(8,128)(2,1)S(1)}, bf16[9,16,18]{2,1,0:T(8,128)(2,1)}, u32[]{:S(2)}) copy-start(bf16[9,16,18]{2,1,0:T(8,128)(2,1)} %param.25) | copy-start | bytes 15556
  7.2 11.9 %copy-start.8 = (s32[1,4]{1,0:T(1,128)S(1)}, s32[1,4]{1,0:T(1,128)}, u32[]{:S(2)}) copy-start(s32[1,4]{1,0:T(1,128)} %param.21) | copy-start | bytes 52
  7.2 11.9 %copy-start.1 = (f32[2,4,16,16,128]{4,3,2,1,0:T(8,128)S(1)}, f32[2,4,16,16,128]{4,3,2,1,0:T(8,128)}, u32[]{:S(2)}) copy-start(f32[2,4,16,16,128]{4,3,2,1,0:T(8,128)} %param.18) | copy-start | bytes 3145732
  7.2 48.7 %reduce-scatter.2.cloned.1.call-start = ((), (), s32[]{:S(2)}) async-start(), calls=%async_computation.1 | async-start | bytes 98304 | tf_op jit(solution)/shard_map/reduce_scatter | solution.py:142
  11.0 8.5 %copy-start.9 = (f32[16]{0:T(128)S(1)}, f32[16]{0:T(128)}, u32[]{:S(2)}) copy-start(f32[16]{0:T(128)} %param.24) | copy-start | bytes 196
  11.1 8.6 %copy-start.10 = (f32[16]{0:T(128)S(1)}, f32[16]{0:T(128)}, u32[]{:S(2)}) copy-start(f32[16]{0:T(128)} %param.28) | copy-start | bytes 196
  11.1 8.7 %copy-start.11 = (f32[16]{0:T(128)S(1)}, f32[16]{0:T(128)}, u32[]{:S(2)}) copy-start(f32[16]{0:T(128)} %param.26) | copy-start | bytes 196
  12.2 9.0 %collective-permute-start.1 = (bf16[2,18,3,128]{3,1,2,0:T(8,128)(2,1)S(1)}, bf16[2,18,3,128]{3,1,2,0:T(8,128)(2,1)S(1)}, u32[]{:S(2)}, u32[]{:S(2)}) collective-permute-start(bf16[2,18,3,128]{3,1,2,0:T(8,128)(2,1)S(1)} %get-tuple-element.21), channel_id=1, source_target_pairs={{4,0},{8,4},{12,8},{5,1},{9,5},{13,9},{6,2},{10,6},{14,10},{7,3},{... | collective-permute-start | bytes 82952 | tf_op jit(solution)/shard_map/ppermute | solution.py:15
  13.5 7.8 %collective-permute-start = (bf16[2,18,3,128]{3,1,2,0:T(8,128)(2,1)S(1)}, bf16[2,18,3,128]{3,1,2,0:T(8,128)(2,1)S(1)}, u32[]{:S(2)}, u32[]{:S(2)}) collective-permute-start(bf16[2,18,3,128]{3,1,2,0:T(8,128)(2,1)S(1)} %get-tuple-element.9), channel_id=1, source_target_pairs={{0,4},{4,8},{8,12},{1,5},{5,9},{9,13},{2,6},{6,10},{10,14},{3,7},{... | collective-permute-start | bytes 82952 | tf_op jit(solution)/shard_map/ppermute | solution.py:12
  21.4 0.9 %copy-start.6 = (bf16[9,16,18]{2,1,0:T(8,128)(2,1)S(1)}, bf16[9,16,18]{2,1,0:T(8,128)(2,1)}, u32[]{:S(2)}) copy-start(bf16[9,16,18]{2,1,0:T(8,128)(2,1)} %param.23) | copy-start | bytes 15556
  29.0 3.6 %copy-start.3 = (bf16[9,16,18]{2,1,0:T(8,128)(2,1)S(1)}, bf16[9,16,18]{2,1,0:T(8,128)(2,1)}, u32[]{:S(2)}) copy-start(bf16[9,16,18]{2,1,0:T(8,128)(2,1)} %param.27) | copy-start | bytes 15556
  38.9 19.0 %copy-start.4 = (f32[16,16]{1,0:T(8,128)S(1)}, f32[16,16]{1,0:T(8,128)}, u32[]{:S(2)}) copy-start(f32[16,16]{1,0:T(8,128)} %param.29) | copy-start | bytes 3076
  42.5 15.7 %copy-start.2 = (f32[2,16,4,32]{3,2,1,0:T(4,128)S(1)}, f32[2,16,4,32]{3,2,1,0:T(4,128)}, u32[]{:S(2)}) copy-start(f32[2,16,4,32]{3,2,1,0:T(4,128)} %param.22) | copy-start | bytes 49156
  42.5 15.7 %copy-start.5 = (f32[16,16]{1,0:T(8,128)S(1)}, f32[16,16]{1,0:T(8,128)}, u32[]{:S(2)}) copy-start(f32[16,16]{1,0:T(8,128)} %param.30) | copy-start | bytes 3076
  42.5 15.7 %copy-start.7 = (f32[16]{0:T(128)S(1)}, f32[16]{0:T(128)}, u32[]{:S(2)}) copy-start(f32[16]{0:T(128)} %param.31) | copy-start | bytes 196
Sparse Core Ops, SparseCore 0:
  44.1 11.7 reduce-scatter.1
where the time goes:
time: 66.3 us; the launch traced here: 65.9 us
  between operations  14.4 us (22%)
  waiting for transfers between devices  11.1 us (17%)
  matrix products  10.7 us (16%)
  local copies, waits for them, and re-layouts  9.87 us (15%)
  other arithmetic  8.41 us (13%)
  starting transfers between devices  6.92 us (10%)
  blocking collectives  4.54 us (7%)
    reduce_scatter x1, waiting for transfers between devices, shards(): owned = lax.psum_scatter(ordered, 'band', scatter_dimension=0, tiled=True)  11.1 us
    dot_general x27, matrix products, apply_filter(): jnp.einsum('oi,bsirw->bsorw', filter_weight[(left_operand + 1) * 3 + (rig...  10.3 us
    ppermute x1, starting transfers between devices, padded(): lax.ppermute(lax.slice_in_dim(block, block.shape[dim] - width, None, axis...  5.59 us
    unnamed x29, local copies, waits for them, and re-layouts  4.41 us
    reduce_sum x1, other arithmetic, shards(): pooled = jnp.sum(jnp.sum(blocks, axis=(4, 6)), axis=0) / 16.0  3.57 us
    reduce_sum x2, local copies, waits for them, and re-layouts, shards(): pooled = jnp.sum(jnp.sum(blocks, axis=(4, 6)), axis=0) / 16.0  2.71 us
    all_gather x1, blocking collectives, shards(): lax.all_gather((reset_half * wide_half.astype(jnp.float32)).astype(jnp.bf...  2.49 us
    all_gather x1, blocking collectives, shards(): pooled_all = lax.all_gather(owned, 'rep', axis=1, tiled=True)  2.05 us
  transfers between devices with their start and end apart: 3, of which 1 were waited for; matrix products, arithmetic and copies ran while one was open for 5% of the time, Pallas kernels for 0%

commit v1 on v0

--- a/solution.py
+++ b/solution.py
@@ -49,6 +49,28 @@
 def choose_rows(block, select):
     masked = jnp.where(select[None, :, None, None, None], block, jnp.zeros_like(block))
     return jnp.sum(masked, axis=1)
+
+
+def exchange_sum(part, owned):
+    bands = lax.axis_size("band")
+    reps = lax.axis_size("rep")
+    band = lax.axis_index("band")
+    total = None
+    for shift in range(bands):
+        pair = None
+        for step in range(reps):
+            target = (band + shift) % bands
+            chunk = lax.dynamic_slice_in_dim(part, target * owned, owned, 0)
+            if shift or step:
+                perm = [
+                    (b * reps + r, ((b + shift) % bands) * reps + (r + step) % reps)
+                    for b in range(bands)
+                    for r in range(reps)
+                ]
+                chunk = lax.ppermute(chunk, ("band", "rep"), perm)
+            pair = chunk if pair is None else pair + chunk
+        total = pair if total is None else total + pair
+    return total
 
 
 def shards(
@@ -139,9 +161,13 @@
     blocks = new_half.reshape(band_local, slots, half, row_count // 4, 4, column_count // 4, 4)
     pooled = jnp.sum(jnp.sum(blocks, axis=(4, 6)), axis=0) / 16.0
     ordered = jnp.take(pooled, coarse_perm[0], axis=0)
-    owned = lax.psum_scatter(ordered, "band", scatter_dimension=0, tiled=True)
-    pooled_all = lax.all_gather(owned, "rep", axis=1, tiled=True)
-    pre = jnp.einsum("oc,kcij->koij", u_pool, pooled_all, precision=lax.Precision.HIGHEST)
+    part = jnp.einsum(
+        "oc,kcij->koij",
+        lax.dynamic_slice_in_dim(u_pool, start, half, 1),
+        ordered,
+        precision=lax.Precision.HIGHEST,
+    )
+    pre = exchange_sum(part, coarse_state.shape[0])
     pre = pre + jnp.einsum("oc,kcij->koij", u_state, coarse_state, precision=lax.Precision.HIGHEST)
     pre = pre + b_coarse[None, :, None, None]
     coarse_next = coarse_state + jnp.tanh(pre)

time: 66.3 us -> 44.7 us (0.67)
  between operations: 14.4 us -> 1.06 us
  waiting for transfers between devices: 11.1 us -> 3.25 us
  starting transfers between devices: 6.92 us -> 9.09 us
  blocking collectives: 4.54 us -> 2.49 us
  other arithmetic: 8.41 us -> 7.72 us
    reduce_scatter x1 -> x0, waiting for transfers between devices: 11.1 us -> none  [shards(): owned = lax.psum_scatter(ordered, 'band', scatter_dimension=0, tiled=True)]
    ppermute x0 -> x3, waiting for transfers between devices: none -> 3.24 us  [exchange_sum(): chunk = lax.ppermute(chunk, ('band', 'rep'), perm)]
    ppermute x0 -> x3, starting transfers between devices: none -> 2.21 us  [exchange_sum(): chunk = lax.ppermute(chunk, ('band', 'rep'), perm)]
    all_gather x1 -> x0, blocking collectives: 2.05 us -> none  [shards(): pooled_all = lax.all_gather(owned, 'rep', axis=1, tiled=True)]
    select_n x2 -> x1, other arithmetic: 0.71 us -> 0.01 us  [shards(): ordered = jnp.take(pooled, coarse_perm[0], axis=0)]
  transfers between devices with their start and end apart: 3 -> 5, of which waited for: 1 -> 2; matrix products, arithmetic and copies ran while one was open for 5% -> 7% of each run, Pallas kernels for 0% -> 0%
where the time goes in v1:
time: 44.7 us; the launch traced here: 44.3 us
  matrix products  10.8 us (24%)
  local copies, waits for them, and re-layouts  9.9 us (22%)
  starting transfers between devices  9.09 us (20%)
  other arithmetic  7.72 us (17%)
  waiting for transfers between devices  3.25 us (7%)
  blocking collectives  2.49 us (6%)
  between operations  1.06 us (2%)
    dot_general x27, matrix products, apply_filter(): jnp.einsum('oi,bsirw->bsorw', filter_weight[(left_operand + 1) * 3 + (rig...  10.3 us
    ppermute x1, starting transfers between devices, padded(): lax.ppermute(lax.slice_in_dim(block, block.shape[dim] - width, None, axis...  5.59 us
    unnamed x29, local copies, waits for them, and re-layouts  4.41 us
    reduce_sum x1, other arithmetic, shards(): pooled = jnp.sum(jnp.sum(blocks, axis=(4, 6)), axis=0) / 16.0  3.57 us
    ppermute x3, waiting for transfers between devices, exchange_sum(): chunk = lax.ppermute(chunk, ('band', 'rep'), perm)  3.24 us
    reduce_sum x2, local copies, waits for them, and re-layouts, shards(): pooled = jnp.sum(jnp.sum(blocks, axis=(4, 6)), axis=0) / 16.0  2.73 us
    all_gather x1, blocking collectives, shards(): lax.all_gather((reset_half * wide_half.astype(jnp.float32)).astype(jnp.bf...  2.49 us
    ppermute x3, starting transfers between devices, exchange_sum(): chunk = lax.ppermute(chunk, ('band', 'rep'), perm)  2.21 us
  transfers between devices with their start and end apart: 5, of which 2 were waited for; matrix products, arithmetic and copies ran while one was open for 7% of the time, Pallas kernels for 0%

profile of v1, /device:TPU:0, one launch (start us, length us, event | category | flops | bytes accessed | tf_op | source)
XLA Modules:
  0.0 44.3 jit_solution(15582070527180395934)
XLA Ops:
  0.7 0.8 %not_and_fusion = (pred[4]{0:T(512)(128)(4,1)S(1)}, pred[4]{0:T(512)(128)(4,1)S(1)}) fusion(s32[4]{0:T(128)} %param.19, s32[]{:T(128)S(6)} %add.214, s32[]{:T(128)S(6)} %mul.31, s32[4,2]{0,1:T(2,128)} %param.20), kind=kLoop, calls=%fused_computation.179 | loop fusion | flops 24 | bytes 48 | tf_op jit(solution)/shard_map/and | solution.py:109
  1.5 0.8 %compare_and_fusion.1 = (pred[4]{0:T(512)(128)(4,1)S(1)}, s32[4]{0:T(128)S(1)}, pred[4]{0:T(512)(128)(4,1)S(1)}, pred[4]{0:T(512)(128)(4,1)S(1)}, s32[4]{0:T(128...) fusion(s32[]{:T(128)S(6)} %mul.31, s32[4,2]{0,1:T(2,128)} %param.20, ...), kind=kLoop, calls=%fused_computation.175 | loop fusion | flops 124 | bytes 116 | tf_op jit(solution)/shard_map/jit(_take)/and | solution.py:124
  2.2 0.7 %fusion.112 = (f32[4]{0:T(128)S(1)}, pred[4]{0:T(512)(128)(4,1)S(1)}) fusion(s32[4]{0:T(128)} %param.19, pred[4]{0:T(512)(128)(4,1)S(1)} %get-tuple-element.29), kind=kLoop, calls=%fused_computation.183 | loop fusion | flops 16 | bytes 40 | tf_op jit(solution)/shard_map/convert_element_type | solution.py:158
  2.9 1.6 %copy.90 = bf16[2,4,16,16,128]{4,2,3,1,0:T(8,128)(2,1)S(1)} copy(f32[2,4,16,16,128]{4,3,2,1,0:T(8,128)} %param.18) | data formatting | bytes 1572864 | tf_op args[1]
  4.5 0.9 %copy.38 = bf16[2,4,2,16,128]{4,2,3,1,0:T(2,128)(2,1)S(1)} copy(bf16[2,4,2,16,128]{4,3,2,1,0:T(8,128)(2,1)} %param.17) | data formatting | bytes 131072 | tf_op args[0]
  5.6 1.3 %collective-permute-start.1 = (bf16[2,18,3,128]{3,1,2,0:T(8,128)(2,1)S(1)}, bf16[2,18,3,128]{3,1,2,0:T(8,128)(2,1)S(1)}, u32[]{:S(2)}, u32[]{:S(2)}) collective-permute-start(bf16[2,18,3,128]{3,1,2,0:T(8,128)(2,1)S(1)} %get-tuple-element.21), channel_id=1, source_target_pairs={{4,0},{8,4},{12,8},{5,1},{9,5},{13,9},{6,2},{10,6},{14,10},{7,3},{... | collective-permute-start | bytes 82952 | tf_op jit(solution)/shard_map/ppermute | solution.py:15
  6.9 5.6 %collective-permute-start = (bf16[2,18,3,128]{3,1,2,0:T(8,128)(2,1)S(1)}, bf16[2,18,3,128]{3,1,2,0:T(8,128)(2,1)S(1)}, u32[]{:S(2)}, u32[]{:S(2)}) collective-permute-start(bf16[2,18,3,128]{3,1,2,0:T(8,128)(2,1)S(1)} %get-tuple-element.9), channel_id=1, source_target_pairs={{0,4},{4,8},{8,12},{1,5},{5,9},{9,13},{2,6},{6,10},{10,14},{3,7},{... | collective-permute-start | bytes 82952 | tf_op jit(solution)/shard_map/ppermute | solution.py:12
  12.6 0.3 copy.37
  13.3 0.6 %gather_fusion.2 = bf16[4,2,18,3,128]{4,2,3,1,0:T(8,128)(2,1)S(1)} fusion(bf16[2,4,18,3,128]{4,2,3,1,0:T(8,128)(2,1)S(1)} %get-tuple-element.22, s32[1024]{0:T(1024)S(1)} %pad_clamp_fusion.1), kind=kCustom, calls=%fused_computation.1.clone | custom fusion | bytes 221200 | tf_op jit(solution)/shard_map/jit(_take)/gather | solution.py:127
  13.8 0.8 %gather_fusion.1 = bf16[4,2,18,3,128]{4,1,3,2,0:T(2,128)(2,1)S(1)} fusion(bf16[2,4,18,3,128]{4,0,3,2,1:T(2,128)(2,1)S(1)} %copy.39, s32[1024]{0:T(1024)S(1)} %pad_clamp_fusion.2), kind=kCustom, calls=%fused_computation.clone | custom fusion | bytes 221200 | tf_op jit(solution)/shard_map/jit(_take)/gather | solution.py:124
  14.9 0.3 pad_maximum_fusion
  15.3 0.3 slice.254
  15.8 0.4 fusion.31
  16.2 0.3 convolution_add_fusion.9
  16.5 0.3 fusion.97
  16.9 0.4 convolution_add_fusion.5
  17.3 0.4 convolution_add_fusion.23
  17.7 0.4 convolution_add_fusion.4
  18.1 0.4 convolution_add_fusion.22
  18.5 0.4 convolution_add_fusion.3
  19.0 0.3 convolution_add_fusion.21
  19.3 0.3 convolution_add_fusion.7
  19.6 0.4 convolution_add_fusion.20
  20.0 0.4 convolution_add_fusion.2
  20.5 0.4 convolution_add_fusion.19
  20.9 0.4 convolution_add_fusion.1
  21.3 0.3 convolution_add_fusion.8
  21.6 0.3 convolution_add_fusion.6
  22.0 0.5 %fusion.20 = bf16[2,4,8,20,128]{4,2,3,1,0:T(8,128)(2,1)S(1)} fusion(f32[2,4,20,128,8]{3,4,2,1,0:T(8,128)S(1)} %convolution_add_fusion.6, bf16[2,4,18,22,128]{4,2,3,1,0:T(8,128)(2,1)S(1)} %pad_maximum_fusion, f32[8]{0:T(128)S(1)} %dynamic_slice.39, bf16[2,4,16,20,128]{4,2,3,1,0:T(8,128)(2,1)S(1)} %slice.254, s32[]{:T(128)S(6)} %select_n.85, ...), kind=kOutput, calls=%fused_computation.61 | convolution fusion | flops 7208960 | bytes 2396160 | tf_op jit(solution)/shard_map/oi,bsirw->bsorw/dot_general | solution.py:39
  22.5 2.5 %all_gather.3 = bf16[2,4,16,20,128]{4,2,3,1,0:T(8,128)(2,1)S(1)} all-gather(bf16[2,4,8,20,128]{4,2,3,1,0:T(8,128)(2,1)S(1)} %fusion.20), channel_id=1, replica_groups=mesh['groups'=2,'tiles'=4,'band'=2,'rep'=2] {'rep'}, dimensions={2}, use_global_device_ids=true | all-gather | bytes 983040 | tf_op jit(solution)/shard_map/all_gather | solution.py:149
  25.0 1.1 %fusion.1 = bf16[2,4,18,20,132]{4,2,3,1,0:T(8,128)(2,1)S(1)} fusion(bf16[2,4,16,20,128]{4,2,3,1,0:T(8,128)(2,1)S(1)} %all_gather.3, bf16[2,4,2,20,132]{4,2,3,1,0:T(2,128)(2,1)S(1)} %pad_slice_fusion.6), kind=kLoop, calls=%fused_computation.18 | loop fusion | flops 2280960 | bytes 1500160 | tf_op jit(solution)/shard_map/concatenate | solution.py:153
  26.4 0.4 convolution_add_fusion.17
  26.8 0.4 convolution_add_fusion.16
  27.2 0.2 convolution_add_fusion.15
  27.5 0.4 convolution_add_fusion.14
  27.9 0.4 convolution_add_fusion.13
  28.5 0.4 convolution_add_fusion.11
  28.9 0.4 fusion.13
  29.4 0.4 fusion.129
  29.8 2.6 %copy.43 = f32[4,8,16,128]{1,3,2,0:T(8,128)} copy(f32[4,8,16,128]{3,1,2,0:T(8,128)S(1)} %get-tuple-element.32) | data formatting | bytes 524288 | tf_op jit(solution)/shard_map/reduce_sum | solution.py:162
  32.4 3.6 %reduce_sum.48 = f32[4,8,4,32]{1,3,2,0:T(8,128)S(1)} reduce(f32[4,8,4,4,32,4]{1,5,4,3,2,0:T(4,128)} %bitcast.254, f32[]{:T(128)} %constant.74.clone.1), dimensions={3,5}, to_apply=%region_3.5 | reduce | flops 61440 | bytes 278532 | tf_op jit(solution)/shard_map/reduce_sum | solution.py:162
  36.2 0.6 %gather_fusion = f32[4,8,4,32]{3,1,2,0:T(8,128)S(1)} fusion(f32[4,8,4,32]{3,1,2,0:T(8,128)S(1)} %broadcast_multiply_fusion, s32[1024]{0:T(1024)S(1)} %pad_clamp_fusion), kind=kCustom, calls=%fused_computation.2 | custom fusion | bytes 32784 | tf_op jit(solution)/shard_map/jit(_take)/gather | solution.py:163
  36.7 0.3 fusion.45
  37.1 2.0 %collective-permute-start.3 = (f32[2,16,4,32]{3,1,2,0:T(8,128)S(1)}, f32[2,16,4,32]{3,1,2,0:T(8,128)S(1)}, u32[]{:S(2)}, u32[]{:S(2)}) collective-permute-start(f32[2,16,4,32]{3,1,2,0:T(8,128)S(1)} %get-tuple-element.24), channel_id=1, source_target_pairs={{0,2},{1,3},{2,0},{3,1},{4,6},{5,7},{6,4},{7,5},{8,10},{9,11},{10,... | collective-permute-start | bytes 49160 | tf_op jit(solution)/shard_map/ppermute | solution.py:70
  39.3 0.9 %copy.48 = f32[2,4,8,16,128]{4,3,2,1,0:T(8,128)} copy(f32[2,4,8,16,128]{4,2,3,1,0:T(8,128)S(1)} %get-tuple-element.33) | data formatting | bytes 1048576
  40.2 1.3 %collective-permute-done.3 = f32[2,16,4,32]{3,1,2,0:T(8,128)S(1)} collective-permute-done((f32[2,16,4,32]{3,1,2,0:T(8,128)S(1)}, f32[2,16,4,32]{3,1,2,0:T(8,128)S(1)}, u32[]{:S(2)}, u32[]{:S(2)}) %collective-permute-start.3) | collective-permute-done | bytes 16416 | tf_op jit(solution)/shard_map/ppermute | solution.py:70
  41.5 1.9 %collective-permute-done.4 = f32[2,16,4,32]{3,1,2,0:T(8,128)S(1)} collective-permute-done((f32[2,16,4,32]{3,1,2,0:T(8,128)S(1)}, f32[2,16,4,32]{3,1,2,0:T(8,128)S(1)}, u32[]{:S(2)}, u32[]{:S(2)}) %collective-permute-start.4) | collective-permute-done | bytes 16416 | tf_op jit(solution)/shard_map/ppermute | solution.py:70
  43.7 0.7 %copy.49 = f32[2,16,4,32]{3,2,1,0:T(4,128)} copy(f32[2,16,4,32]{3,1,2,0:T(8,128)S(1)} %tanh_add_fusion) | data formatting | bytes 32768
  (47 shorter events, 2.1 us)
Async XLA Ops:
  0.6 15.9 %copy-start = (bf16[9,16,18]{2,1,0:T(8,128)(2,1)S(1)}, bf16[9,16,18]{2,1,0:T(8,128)(2,1)}, u32[]{:S(2)}) copy-start(bf16[9,16,18]{2,1,0:T(8,128)(2,1)} %param.25) | copy-start | bytes 15556
  0.6 11.8 %copy-start.8 = (s32[1,4]{1,0:T(1,128)S(1)}, s32[1,4]{1,0:T(1,128)}, u32[]{:S(2)}) copy-start(s32[1,4]{1,0:T(1,128)} %param.21) | copy-start | bytes 52
  0.7 11.9 %copy-start.1 = (f32[2,4,16,16,128]{4,3,2,1,0:T(8,128)S(1)}, f32[2,4,16,16,128]{4,3,2,1,0:T(8,128)}, u32[]{:S(2)}) copy-start(f32[2,4,16,16,128]{4,3,2,1,0:T(8,128)} %param.18) | copy-start | bytes 3145732
  4.5 8.5 %copy-start.9 = (f32[16]{0:T(128)S(1)}, f32[16]{0:T(128)}, u32[]{:S(2)}) copy-start(f32[16]{0:T(128)} %param.24) | copy-start | bytes 196
  4.5 8.6 %copy-start.10 = (f32[16]{0:T(128)S(1)}, f32[16]{0:T(128)}, u32[]{:S(2)}) copy-start(f32[16]{0:T(128)} %param.28) | copy-start | bytes 196
  4.5 8.7 %copy-start.11 = (f32[16]{0:T(128)S(1)}, f32[16]{0:T(128)}, u32[]{:S(2)}) copy-start(f32[16]{0:T(128)} %param.26) | copy-start | bytes 196
  5.6 9.0 %collective-permute-start.1 = (bf16[2,18,3,128]{3,1,2,0:T(8,128)(2,1)S(1)}, bf16[2,18,3,128]{3,1,2,0:T(8,128)(2,1)S(1)}, u32[]{:S(2)}, u32[]{:S(2)}) collective-permute-start(bf16[2,18,3,128]{3,1,2,0:T(8,128)(2,1)S(1)} %get-tuple-element.21), channel_id=1, source_target_pairs={{4,0},{8,4},{12,8},{5,1},{9,5},{13,9},{6,2},{10,6},{14,10},{7,3},{... | collective-permute-start | bytes 82952 | tf_op jit(solution)/shard_map/ppermute | solution.py:15
  6.9 7.9 %collective-permute-start = (bf16[2,18,3,128]{3,1,2,0:T(8,128)(2,1)S(1)}, bf16[2,18,3,128]{3,1,2,0:T(8,128)(2,1)S(1)}, u32[]{:S(2)}, u32[]{:S(2)}) collective-permute-start(bf16[2,18,3,128]{3,1,2,0:T(8,128)(2,1)S(1)} %get-tuple-element.9), channel_id=1, source_target_pairs={{0,4},{4,8},{8,12},{1,5},{5,9},{9,13},{2,6},{6,10},{10,14},{3,7},{... | collective-permute-start | bytes 82952 | tf_op jit(solution)/shard_map/ppermute | solution.py:12
  14.9 0.9 %copy-start.6 = (bf16[9,16,18]{2,1,0:T(8,128)(2,1)S(1)}, bf16[9,16,18]{2,1,0:T(8,128)(2,1)}, u32[]{:S(2)}) copy-start(bf16[9,16,18]{2,1,0:T(8,128)(2,1)} %param.23) | copy-start | bytes 15556
  22.5 3.6 %copy-start.3 = (bf16[9,16,18]{2,1,0:T(8,128)(2,1)S(1)}, bf16[9,16,18]{2,1,0:T(8,128)(2,1)}, u32[]{:S(2)}) copy-start(bf16[9,16,18]{2,1,0:T(8,128)(2,1)} %param.27) | copy-start | bytes 15556
  32.4 4.3 %copy-start.4 = (f32[16,16]{1,0:T(8,128)S(1)}, f32[16,16]{1,0:T(8,128)}, u32[]{:S(2)}) copy-start(f32[16,16]{1,0:T(8,128)} %param.29) | copy-start | bytes 3076
  36.0 7.4 %copy-start.2 = (f32[2,16,4,32]{3,2,1,0:T(4,128)S(1)}, f32[2,16,4,32]{3,2,1,0:T(4,128)}, u32[]{:S(2)}) copy-start(f32[2,16,4,32]{3,2,1,0:T(4,128)} %param.22) | copy-start | bytes 49156
  36.0 7.4 %copy-start.5 = (f32[16,16]{1,0:T(8,128)S(1)}, f32[16,16]{1,0:T(8,128)}, u32[]{:S(2)}) copy-start(f32[16,16]{1,0:T(8,128)} %param.30) | copy-start | bytes 3076
  36.0 7.4 %copy-start.7 = (f32[16]{0:T(128)S(1)}, f32[16]{0:T(128)}, u32[]{:S(2)}) copy-start(f32[16]{0:T(128)} %param.31) | copy-start | bytes 196
  37.1 4.4 %collective-permute-start.3 = (f32[2,16,4,32]{3,1,2,0:T(8,128)S(1)}, f32[2,16,4,32]{3,1,2,0:T(8,128)S(1)}, u32[]{:S(2)}, u32[]{:S(2)}) collective-permute-start(f32[2,16,4,32]{3,1,2,0:T(8,128)S(1)} %get-tuple-element.24), channel_id=1, source_target_pairs={{0,2},{1,3},{2,0},{3,1},{4,6},{5,7},{6,4},{7,5},{8,10},{9,11},{10,... | collective-permute-start | bytes 49160 | tf_op jit(solution)/shard_map/ppermute | solution.py:70
  39.1 4.3 %collective-permute-start.4 = (f32[2,16,4,32]{3,1,2,0:T(8,128)S(1)}, f32[2,16,4,32]{3,1,2,0:T(8,128)S(1)}, u32[]{:S(2)}, u32[]{:S(2)}) collective-permute-start(f32[2,16,4,32]{3,1,2,0:T(8,128)S(1)} %get-tuple-element.24), channel_id=1, source_target_pairs={{0,3},{1,2},{2,1},{3,0},{4,7},{5,6},{6,5},{7,4},{8,11},{9,10},{10,... | collective-permute-start | bytes 49160 | tf_op jit(solution)/shard_map/ppermute | solution.py:70
  39.1 4.3 %collective-permute-start.2 = (f32[2,16,4,32]{3,1,2,0:T(8,128)S(1)}, f32[2,16,4,32]{3,1,2,0:T(8,128)S(1)}, u32[]{:S(2)}, u32[]{:S(2)}) collective-permute-start(f32[2,16,4,32]{3,1,2,0:T(8,128)S(1)} %get-tuple-element.23), channel_id=1, source_target_pairs={{0,1},{1,0},{2,3},{3,2},{4,5},{5,4},{6,7},{7,6},{8,9},{9,8},{10,11... | collective-permute-start | bytes 49160 | tf_op jit(solution)/shard_map/ppermute | solution.py:70

commit v2 on v1

--- a/solution.py
+++ b/solution.py
@@ -157,9 +157,16 @@
     state_half = lax.dynamic_slice_in_dim(state, start, half, 2)
     live_scale = alive.astype(jnp.float32)[None, :, None, None, None]
     new_half = ((1.0 - update) * state_half + update * candidate) * live_scale
-    band_local = new_half.shape[0]
-    blocks = new_half.reshape(band_local, slots, half, row_count // 4, 4, column_count // 4, 4)
-    pooled = jnp.sum(jnp.sum(blocks, axis=(4, 6)), axis=0) / 16.0
+    summed = jnp.sum(new_half, axis=0)
+    column_pool = (
+        jnp.arange(column_count)[:, None] // 4 == jnp.arange(column_count // 4)[None, :]
+    ).astype(jnp.float32)
+    cols = jnp.einsum(
+        "schw,wj->schj", summed, column_pool, precision=lax.Precision.HIGHEST
+    )
+    pooled = jnp.sum(
+        cols.reshape(slots, half, row_count // 4, 4, column_count // 4), axis=3
+    ) / 16.0
     ordered = jnp.take(pooled, coarse_perm[0], axis=0)
     part = jnp.einsum(
         "oc,kcij->koij",

time: 44.7 us -> 38.9 us (0.87)
  other arithmetic: 7.72 us -> 4.15 us
  local copies, waits for them, and re-layouts: 9.9 us -> 7.18 us
  matrix products: 10.8 us -> 11.4 us
    reduce_sum x1 -> x0, other arithmetic: 3.57 us -> none  [shards(): pooled = jnp.sum(jnp.sum(blocks, axis=(4, 6)), axis=0) / 16.0]
    reduce_sum x2 -> x0, local copies, waits for them, and re-layouts: 2.73 us -> none  [shards(): pooled = jnp.sum(jnp.sum(blocks, axis=(4, 6)), axis=0) / 16.0]
    dot_general x0 -> x1, matrix products: none -> 0.53 us  [shards(): jnp.einsum('schw,wj->schj', summed, column_pool, precision=lax.Precision....]
  transfers between devices with their start and end apart: 5 -> 5, of which waited for: 2 -> 2; matrix products, arithmetic and copies ran while one was open for 7% -> 8% of each run, Pallas kernels for 0% -> 0%
where the time goes in v2:
time: 38.9 us; the launch traced here: 38.6 us
  matrix products  11.4 us (29%)
  starting transfers between devices  9.09 us (23%)
  local copies, waits for them, and re-layouts  7.18 us (18%)
  other arithmetic  4.15 us (11%)
  waiting for transfers between devices  3.26 us (8%)
  blocking collectives  2.49 us (6%)
  between operations  1.07 us (3%)
    dot_general x27, matrix products, apply_filter(): jnp.einsum('oi,bsirw->bsorw', filter_weight[(left_operand + 1) * 3 + (rig...  10.3 us
    ppermute x1, starting transfers between devices, padded(): lax.ppermute(lax.slice_in_dim(block, block.shape[dim] - width, None, axis...  5.59 us
    unnamed x29, local copies, waits for them, and re-layouts  4.41 us
    ppermute x3, waiting for transfers between devices, exchange_sum(): chunk = lax.ppermute(chunk, ('band', 'rep'), perm)  3.25 us
    all_gather x1, blocking collectives, shards(): lax.all_gather((reset_half * wide_half.astype(jnp.float32)).astype(jnp.bf...  2.49 us
    ppermute x3, starting transfers between devices, exchange_sum(): chunk = lax.ppermute(chunk, ('band', 'rep'), perm)  2.21 us
    ppermute x1, starting transfers between devices, padded(): lax.ppermute(lax.slice_in_dim(block, 0, width, axis=dim), axis, backward)  1.29 us
    concatenate x1, other arithmetic, shards(): jnp.concatenate([first[:, :, :inputs_count, 1:row_count + 5, :], gated_pa...  1.14 us
  transfers between devices with their start and end apart: 5, of which 2 were waited for; matrix products, arithmetic and copies ran while one was open for 8% of the time, Pallas kernels for 0%

profile of v2, /device:TPU:0, one launch (start us, length us, event | category | flops | bytes accessed | tf_op | source)
XLA Modules:
  0.0 38.6 jit_solution(2907730600854043749)
XLA Ops:
  0.7 0.8 %not_and_fusion = (pred[4]{0:T(512)(128)(4,1)S(1)}, pred[4]{0:T(512)(128)(4,1)S(1)}) fusion(s32[4]{0:T(128)} %param.19, s32[]{:T(128)S(6)} %add.220, s32[]{:T(128)S(6)} %mul.31, s32[4,2]{0,1:T(2,128)} %param.20), kind=kLoop, calls=%fused_computation.185 | loop fusion | flops 24 | bytes 48 | tf_op jit(solution)/shard_map/and | solution.py:109
  1.5 0.8 %compare_and_fusion.1 = (pred[4]{0:T(512)(128)(4,1)S(1)}, s32[4]{0:T(128)S(1)}, pred[4]{0:T(512)(128)(4,1)S(1)}, pred[4]{0:T(512)(128)(4,1)S(1)}, s32[4]{0:T(128...) fusion(s32[]{:T(128)S(6)} %mul.31, s32[4,2]{0,1:T(2,128)} %param.20, ...), kind=kLoop, calls=%fused_computation.180 | loop fusion | flops 124 | bytes 116 | tf_op jit(solution)/shard_map/jit(_take)/and | solution.py:124
  2.2 0.7 %fusion.116 = (f32[4]{0:T(128)S(1)}, pred[4]{0:T(512)(128)(4,1)S(1)}) fusion(s32[4]{0:T(128)} %param.19, pred[4]{0:T(512)(128)(4,1)S(1)} %get-tuple-element.31), kind=kLoop, calls=%fused_computation.192 | loop fusion | flops 16 | bytes 40 | tf_op jit(solution)/shard_map/convert_element_type | solution.py:158
  2.9 1.6 %copy.106 = bf16[2,4,16,16,128]{4,2,3,1,0:T(8,128)(2,1)S(1)} copy(f32[2,4,16,16,128]{4,3,2,1,0:T(8,128)} %param.18) | data formatting | bytes 1572864 | tf_op args[1]
  4.5 0.9 %copy.50 = bf16[2,4,2,16,128]{4,2,3,1,0:T(2,128)(2,1)S(1)} copy(bf16[2,4,2,16,128]{4,3,2,1,0:T(8,128)(2,1)} %param.17) | data formatting | bytes 131072 | tf_op args[0]
  5.6 1.3 %collective-permute-start.1 = (bf16[2,18,3,128]{3,1,2,0:T(8,128)(2,1)S(1)}, bf16[2,18,3,128]{3,1,2,0:T(8,128)(2,1)S(1)}, u32[]{:S(2)}, u32[]{:S(2)}) collective-permute-start(bf16[2,18,3,128]{3,1,2,0:T(8,128)(2,1)S(1)} %get-tuple-element.23), channel_id=1, source_target_pairs={{4,0},{8,4},{12,8},{5,1},{9,5},{13,9},{6,2},{10,6},{14,10},{7,3},{... | collective-permute-start | bytes 82952 | tf_op jit(solution)/shard_map/ppermute | solution.py:15
  6.9 5.6 %collective-permute-start = (bf16[2,18,3,128]{3,1,2,0:T(8,128)(2,1)S(1)}, bf16[2,18,3,128]{3,1,2,0:T(8,128)(2,1)S(1)}, u32[]{:S(2)}, u32[]{:S(2)}) collective-permute-start(bf16[2,18,3,128]{3,1,2,0:T(8,128)(2,1)S(1)} %get-tuple-element.11), channel_id=1, source_target_pairs={{0,4},{4,8},{8,12},{1,5},{5,9},{9,13},{2,6},{6,10},{10,14},{3,7},{... | collective-permute-start | bytes 82952 | tf_op jit(solution)/shard_map/ppermute | solution.py:12
  12.6 0.3 copy.49
  13.3 0.6 %gather_fusion.2 = bf16[4,2,18,3,128]{4,2,3,1,0:T(8,128)(2,1)S(1)} fusion(bf16[2,4,18,3,128]{4,2,3,1,0:T(8,128)(2,1)S(1)} %get-tuple-element.24, s32[1024]{0:T(1024)S(1)} %pad_clamp_fusion.1), kind=kCustom, calls=%fused_computation.1.clone | custom fusion | bytes 221200 | tf_op jit(solution)/shard_map/jit(_take)/gather | solution.py:127
  13.8 0.8 %gather_fusion.1 = bf16[4,2,18,3,128]{4,1,3,2,0:T(2,128)(2,1)S(1)} fusion(bf16[2,4,18,3,128]{4,0,3,2,1:T(2,128)(2,1)S(1)} %copy.51, s32[1024]{0:T(1024)S(1)} %pad_clamp_fusion.2), kind=kCustom, calls=%fused_computation.clone | custom fusion | bytes 221200 | tf_op jit(solution)/shard_map/jit(_take)/gather | solution.py:124
  14.9 0.3 pad_maximum_fusion
  15.3 0.3 slice.254
  15.8 0.4 %fusion.31 = f32[2,4,16,128,8]{3,4,2,1,0:T(8,128)S(1)} fusion(bf16[2,4,18,22,128]{4,2,3,1,0:T(8,128)(2,1)S(1)} %pad_maximum_fusion, bf16[9,16,18]{2,1,0:T(8,128)(2,1)S(1)} %copy-done.6, s32[]{:T(128)S(6)} %select_n.95), kind=kOutput, calls=%fused_computation.75 | convolution fusion | flops 4718592 | bytes 1607684 | tf_op jit(solution)/shard_map/oi,bsirw->bsorw/dot_general | solution.py:39
  16.2 0.3 convolution_add_fusion.9
  16.5 0.3 fusion.101
  16.9 0.4 %convolution_add_fusion.5 = f32[2,4,20,128,8]{3,4,2,1,0:T(8,128)S(1)} fusion(f32[2,4,20,128,8]{3,4,2,1,0:T(8,128)S(1)} %fusion.101, bf16[2,4,18,22,128]{4,2,3,1,0:T(8,128)(2,1)S(1)} %pad_maximum_fusion, bf16[9,16,18]{2,1,0:T(8,128)(2,1)S(1)} %copy-done, s32[]{:T(128)S(6)} %select_n.95), kind=kOutput, calls=%fused_computation.24 | convolution fusion | flops 6062080 | bytes 2394116 | tf_op jit(solution)/shard_map/oi,bsirw->bsorw/dot_general | solution.py:39
  17.3 0.4 %convolution_add_fusion.23 = f32[2,4,16,128,8]{3,4,2,1,0:T(8,128)S(1)} fusion(f32[2,4,16,128,8]{3,4,2,1,0:T(8,128)S(1)} %convolution_add_fusion.9, bf16[2,4,18,22,128]{4,2,3,1,0:T(8,128)(2,1)S(1)} %pad_maximum_fusion, bf16[9,16,18]{2,1,0:T(8,128)(2,1)S(1)} %copy-done.6, s32[]{:T(128)S(6)} %add.303, s32[]{:T(128)S(6)} %select_n.95), kind=kOutput, calls=%fused_computation.49 | convolution fusion | flops 4849664 | bytes 2131976 | tf_op jit(solution)/shard_map/oi,bsirw->bsorw/dot_general | solution.py:39
  17.7 0.4 %convolution_add_fusion.4 = f32[2,4,20,128,8]{3,4,2,1,0:T(8,128)S(1)} fusion(f32[2,4,20,128,8]{3,4,2,1,0:T(8,128)S(1)} %convolution_add_fusion.5, bf16[2,4,18,22,128]{4,2,3,1,0:T(8,128)(2,1)S(1)} %pad_maximum_fusion, bf16[9,16,18]{2,1,0:T(8,128)(2,1)S(1)} %copy-done, s32[]{:T(128)S(6)} %add.303, s32[]{:T(128)S(6)} %select_n.95), kind=kOutput, calls=%fused_computation.23 | convolution fusion | flops 6062080 | bytes 2394120 | tf_op jit(solution)/shard_map/oi,bsirw->bsorw/dot_general | solution.py:39
  18.2 0.4 %convolution_add_fusion.22 = f32[2,4,16,128,8]{3,4,2,1,0:T(8,128)S(1)} fusion(f32[2,4,16,128,8]{3,4,2,1,0:T(8,128)S(1)} %convolution_add_fusion.23, bf16[2,4,18,22,128]{4,2,3,1,0:T(8,128)(2,1)S(1)} %pad_maximum_fusion, bf16[9,16,18]{2,1,0:T(8,128)(2,1)S(1)} %copy-done.6, s32[]{:T(128)S(6)} %add.304, s32[]{:T(128)S(6)} %select_n.95), kind=kOutput, calls=%fused_computation.48 | convolution fusion | flops 4849664 | bytes 2131976 | tf_op jit(solution)/shard_map/oi,bsirw->bsorw/dot_general | solution.py:39
  18.5 0.4 %convolution_add_fusion.3 = f32[2,4,20,128,8]{3,4,2,1,0:T(8,128)S(1)} fusion(f32[2,4,20,128,8]{3,4,2,1,0:T(8,128)S(1)} %convolution_add_fusion.4, bf16[2,4,18,22,128]{4,2,3,1,0:T(8,128)(2,1)S(1)} %pad_maximum_fusion, bf16[9,16,18]{2,1,0:T(8,128)(2,1)S(1)} %copy-done, s32[]{:T(128)S(6)} %add.304, s32[]{:T(128)S(6)} %select_n.95), kind=kOutput, calls=%fused_computation.22 | convolution fusion | flops 6062080 | bytes 2394120 | tf_op jit(solution)/shard_map/oi,bsirw->bsorw/dot_general | solution.py:39
  19.0 0.3 convolution_add_fusion.21
  19.3 0.3 convolution_add_fusion.7
  19.7 0.4 %convolution_add_fusion.20 = f32[2,4,16,128,8]{3,4,2,1,0:T(8,128)S(1)} fusion(f32[2,4,16,128,8]{3,4,2,1,0:T(8,128)S(1)} %convolution_add_fusion.21, bf16[2,4,18,22,128]{4,2,3,1,0:T(8,128)(2,1)S(1)} %pad_maximum_fusion, bf16[9,16,18]{2,1,0:T(8,128)(2,1)S(1)} %copy-done.6, s32[]{:T(128)S(6)} %add.306, s32[]{:T(128)S(6)} %select_n.95), kind=kOutput, calls=%fused_computation.46 | convolution fusion | flops 4849664 | bytes 2131976 | tf_op jit(solution)/shard_map/oi,bsirw->bsorw/dot_general | solution.py:39
  20.1 0.4 %convolution_add_fusion.2 = f32[2,4,20,128,8]{3,4,2,1,0:T(8,128)S(1)} fusion(f32[2,4,20,128,8]{3,4,2,1,0:T(8,128)S(1)} %convolution_add_fusion.7, bf16[2,4,18,22,128]{4,2,3,1,0:T(8,128)(2,1)S(1)} %pad_maximum_fusion, bf16[9,16,18]{2,1,0:T(8,128)(2,1)S(1)} %copy-done, s32[]{:T(128)S(6)} %add.306, s32[]{:T(128)S(6)} %select_n.95), kind=kOutput, calls=%fused_computation.21 | convolution fusion | flops 6062080 | bytes 2394120 | tf_op jit(solution)/shard_map/oi,bsirw->bsorw/dot_general | solution.py:39
  20.5 0.4 %convolution_add_fusion.19 = f32[2,4,16,128,8]{3,4,2,1,0:T(8,128)S(1)} fusion(f32[2,4,16,128,8]{3,4,2,1,0:T(8,128)S(1)} %convolution_add_fusion.20, bf16[2,4,18,22,128]{4,2,3,1,0:T(8,128)(2,1)S(1)} %pad_maximum_fusion, bf16[9,16,18]{2,1,0:T(8,128)(2,1)S(1)} %copy-done.6, s32[]{:T(128)S(6)} %add.307, s32[]{:T(128)S(6)} %select_n.95), kind=kOutput, calls=%fused_computation.45 | convolution fusion | flops 4849664 | bytes 2131976 | tf_op jit(solution)/shard_map/oi,bsirw->bsorw/dot_general | solution.py:39
  20.9 0.4 %convolution_add_fusion.1 = f32[2,4,20,128,8]{3,4,2,1,0:T(8,128)S(1)} fusion(f32[2,4,20,128,8]{3,4,2,1,0:T(8,128)S(1)} %convolution_add_fusion.2, bf16[2,4,18,22,128]{4,2,3,1,0:T(8,128)(2,1)S(1)} %pad_maximum_fusion, bf16[9,16,18]{2,1,0:T(8,128)(2,1)S(1)} %copy-done, s32[]{:T(128)S(6)} %add.307, s32[]{:T(128)S(6)} %select_n.95), kind=kOutput, calls=%fused_computation.20 | convolution fusion | flops 6062080 | bytes 2394120 | tf_op jit(solution)/shard_map/oi,bsirw->bsorw/dot_general | solution.py:39
  21.3 0.3 convolution_add_fusion.8
  21.6 0.3 convolution_add_fusion.6
  22.0 0.5 %fusion.20 = bf16[2,4,8,20,128]{4,2,3,1,0:T(8,128)(2,1)S(1)} fusion(f32[2,4,20,128,8]{3,4,2,1,0:T(8,128)S(1)} %convolution_add_fusion.6, bf16[2,4,18,22,128]{4,2,3,1,0:T(8,128)(2,1)S(1)} %pad_maximum_fusion, f32[8]{0:T(128)S(1)} %dynamic_slice.39, bf16[2,4,16,20,128]{4,2,3,1,0:T(8,128)(2,1)S(1)} %slice.254, s32[]{:T(128)S(6)} %select_n.95, ...), kind=kOutput, calls=%fused_computation.61 | convolution fusion | flops 7208960 | bytes 2396160 | tf_op jit(solution)/shard_map/oi,bsirw->bsorw/dot_general | solution.py:39
  22.5 2.5 %all_gather.3 = bf16[2,4,16,20,128]{4,2,3,1,0:T(8,128)(2,1)S(1)} all-gather(bf16[2,4,8,20,128]{4,2,3,1,0:T(8,128)(2,1)S(1)} %fusion.20), channel_id=1, replica_groups=mesh['groups'=2,'tiles'=4,'band'=2,'rep'=2] {'rep'}, dimensions={2}, use_global_device_ids=true | all-gather | bytes 983040 | tf_op jit(solution)/shard_map/all_gather | solution.py:149
  25.0 1.1 %fusion.1 = bf16[2,4,18,20,132]{4,2,3,1,0:T(8,128)(2,1)S(1)} fusion(bf16[2,4,16,20,128]{4,2,3,1,0:T(8,128)(2,1)S(1)} %all_gather.3, bf16[2,4,2,20,132]{4,2,3,1,0:T(2,128)(2,1)S(1)} %pad_slice_fusion.6), kind=kLoop, calls=%fused_computation.18 | loop fusion | flops 2280960 | bytes 1500160 | tf_op jit(solution)/shard_map/concatenate | solution.py:153
  26.4 0.4 %convolution_add_fusion.17 = f32[2,4,16,128,8]{3,4,2,1,0:T(8,128)S(1)} fusion(f32[2,4,16,128,8]{3,4,2,1,0:T(8,128)S(1)} %fusion.40, bf16[2,4,18,20,132]{4,2,3,1,0:T(8,128)(2,1)S(1)} %fusion.1, bf16[9,16,18]{2,1,0:T(8,128)(2,1)S(1)} %copy-done.3, s32[]{:T(128)S(6)} %add.302, s32[]{:T(128)S(6)} %select_n.95), kind=kOutput, calls=%fused_computation.43 | convolution fusion | flops 4849664 | bytes 1837064 | tf_op jit(solution)/shard_map/oi,bsirw->bsorw/dot_general | solution.py:39
  26.8 0.4 %convolution_add_fusion.16 = f32[2,4,16,128,8]{3,4,2,1,0:T(8,128)S(1)} fusion(f32[2,4,16,128,8]{3,4,2,1,0:T(8,128)S(1)} %convolution_add_fusion.17, bf16[2,4,18,20,132]{4,2,3,1,0:T(8,128)(2,1)S(1)} %fusion.1, bf16[9,16,18]{2,1,0:T(8,128)(2,1)S(1)} %copy-done.3, s32[]{:T(128)S(6)} %add.303, s32[]{:T(128)S(6)} %select_n.95), kind=kOutput, calls=%fused_computation.42 | convolution fusion | flops 4849664 | bytes 1837064 | tf_op jit(solution)/shard_map/oi,bsirw->bsorw/dot_general | solution.py:39
  27.2 0.2 convolution_add_fusion.15
  27.5 0.4 %convolution_add_fusion.14 = f32[2,4,16,128,8]{3,4,2,1,0:T(8,128)S(1)} fusion(f32[2,4,16,128,8]{3,4,2,1,0:T(8,128)S(1)} %convolution_add_fusion.15, bf16[2,4,18,20,132]{4,2,3,1,0:T(8,128)(2,1)S(1)} %fusion.1, bf16[9,16,18]{2,1,0:T(8,128)(2,1)S(1)} %copy-done.3, s32[]{:T(128)S(6)} %add.305, s32[]{:T(128)S(6)} %select_n.95), kind=kOutput, calls=%fused_computation.40 | convolution fusion | flops 4849664 | bytes 1837064 | tf_op jit(solution)/shard_map/oi,bsirw->bsorw/dot_general | solution.py:39
  27.9 0.4 %convolution_add_fusion.13 = f32[2,4,16,128,8]{3,4,2,1,0:T(8,128)S(1)} fusion(f32[2,4,16,128,8]{3,4,2,1,0:T(8,128)S(1)} %convolution_add_fusion.14, bf16[2,4,18,20,132]{4,2,3,1,0:T(8,128)(2,1)S(1)} %fusion.1, bf16[9,16,18]{2,1,0:T(8,128)(2,1)S(1)} %copy-done.3, s32[]{:T(128)S(6)} %add.306, s32[]{:T(128)S(6)} %select_n.95), kind=kOutput, calls=%fused_computation.39 | convolution fusion | flops 4849664 | bytes 1837064 | tf_op jit(solution)/shard_map/oi,bsirw->bsorw/dot_general | solution.py:39
  28.3 0.2 convolution_add_fusion.12
  28.6 0.4 %convolution_add_fusion.11 = f32[2,4,16,128,8]{3,4,2,1,0:T(8,128)S(1)} fusion(f32[2,4,16,128,8]{3,4,2,1,0:T(8,128)S(1)} %convolution_add_fusion.12, bf16[2,4,18,20,132]{4,2,3,1,0:T(8,128)(2,1)S(1)} %fusion.1, bf16[9,16,18]{2,1,0:T(8,128)(2,1)S(1)} %copy-done.3, s32[]{:T(128)S(6)} %add.308, s32[]{:T(128)S(6)} %select_n.95), kind=kOutput, calls=%fused_computation.37 | convolution fusion | flops 4849664 | bytes 1837064 | tf_op jit(solution)/shard_map/oi,bsirw->bsorw/dot_general | solution.py:39
  29.0 0.4 %fusion.13 = f32[2,4,16,128,8]{3,4,2,1,0:T(8,128)S(1)} fusion(f32[2,4,16,128,8]{3,4,2,1,0:T(8,128)S(1)} %convolution_add_fusion.8, bf16[2,4,18,22,128]{4,2,3,1,0:T(8,128)(2,1)S(1)} %pad_maximum_fusion, f32[8]{0:T(128)S(1)} %dynamic_slice.36, bf16[9,16,18]{2,1,0:T(8,128)(2,1)S(1)} %copy-done.6, s32[]{:T(128)S(6)} %add.309, s32[]{:T(128)S(6)} %select_n.95), kind=kOutput, calls=%fused_computation.54 | convolution fusion | flops 5373952 | bytes 2132488 | tf_op jit(solution)/shard_map/oi,bsirw->bsorw/dot_general | solution.py:39
  29.4 0.5 %fusion.133 = (f32[4,8,16,128]{3,1,2,0:T(8,128)S(1)}, f32[2,4,8,16,128]{4,2,3,1,0:T(8,128)S(1)}) fusion(f32[4]{0:T(128)S(1)} %get-tuple-element.32, f32[2,4,16,128,8]{3,4,2,1,0:T(8,128)S(1)} %fusion.13, f32[8]{0:T(128)S(1)} %dynamic_slice.42, f32[2,4,16,128,8]{3,4,2,1,0:T(8,128)S(1)} %convolution_add_fusion.11, bf16[9,16,18]{2,1,0:T(8,128)(2,1)S(1)} %copy-done.3, ...), kind=kOutput, calls=%fused_computation.210 | convolution fusion | flops 5701632 | bytes 3150336 | tf_op jit(solution)/shard_map/oi,bsirw->bsorw/dot_general | solution.py:39
  29.9 0.5 %convolution_reduce_fusion = f32[4,8,4,32]{3,2,1,0:T(4,128)S(1)} fusion(f32[4,8,4,4,128]{4,1,3,2,0:T(8,128)S(1)} %bitcast.259, s32[128]{0:T(128)S(1)} %and_select_fusion), kind=kOutput, calls=%fused_computation.62 | convolution fusion | flops 25182208 | bytes 279040 | tf_op jit(solution)/shard_map/schw,wj->schj/dot_general | solution.py:164
  30.4 0.6 %gather_fusion = f32[4,8,4,32]{3,1,2,0:T(8,128)S(1)} fusion(f32[4,8,4,32]{3,1,2,0:T(8,128)S(1)} %copy_multiply_fusion, s32[1024]{0:T(1024)S(1)} %pad_clamp_fusion), kind=kCustom, calls=%fused_computation.2 | custom fusion | bytes 32784 | tf_op jit(solution)/shard_map/jit(_take)/gather | solution.py:170
  31.0 0.3 fusion.46
  31.4 2.0 %collective-permute-start.3 = (f32[2,16,4,32]{3,1,2,0:T(8,128)S(1)}, f32[2,16,4,32]{3,1,2,0:T(8,128)S(1)}, u32[]{:S(2)}, u32[]{:S(2)}) collective-permute-start(f32[2,16,4,32]{3,1,2,0:T(8,128)S(1)} %get-tuple-element.26), channel_id=1, source_target_pairs={{0,2},{1,3},{2,0},{3,1},{4,6},{5,7},{6,4},{7,5},{8,10},{9,11},{10,... | collective-permute-start | bytes 49160 | tf_op jit(solution)/shard_map/ppermute | solution.py:70
  33.6 0.9 %copy.60 = f32[2,4,8,16,128]{4,3,2,1,0:T(8,128)} copy(f32[2,4,8,16,128]{4,2,3,1,0:T(8,128)S(1)} %get-tuple-element.35) | data formatting | bytes 1048576
  34.5 1.3 %collective-permute-done.3 = f32[2,16,4,32]{3,1,2,0:T(8,128)S(1)} collective-permute-done((f32[2,16,4,32]{3,1,2,0:T(8,128)S(1)}, f32[2,16,4,32]{3,1,2,0:T(8,128)S(1)}, u32[]{:S(2)}, u32[]{:S(2)}) %collective-permute-start.3) | collective-permute-done | bytes 16416 | tf_op jit(solution)/shard_map/ppermute | solution.py:70
  35.7 2.0 %collective-permute-done.4 = f32[2,16,4,32]{3,1,2,0:T(8,128)S(1)} collective-permute-done((f32[2,16,4,32]{3,1,2,0:T(8,128)S(1)}, f32[2,16,4,32]{3,1,2,0:T(8,128)S(1)}, u32[]{:S(2)}, u32[]{:S(2)}) %collective-permute-start.4) | collective-permute-done | bytes 16416 | tf_op jit(solution)/shard_map/ppermute | solution.py:70
  37.9 0.7 %copy.61 = f32[2,16,4,32]{3,2,1,0:T(4,128)} copy(f32[2,16,4,32]{3,1,2,0:T(8,128)S(1)} %tanh_add_fusion) | data formatting | bytes 32768
  (46 shorter events, 1.7 us)
Async XLA Ops:
  0.6 15.9 %copy-start = (bf16[9,16,18]{2,1,0:T(8,128)(2,1)S(1)}, bf16[9,16,18]{2,1,0:T(8,128)(2,1)}, u32[]{:S(2)}) copy-start(bf16[9,16,18]{2,1,0:T(8,128)(2,1)} %param.25) | copy-start | bytes 15556
  0.6 11.8 %copy-start.8 = (s32[1,4]{1,0:T(1,128)S(1)}, s32[1,4]{1,0:T(1,128)}, u32[]{:S(2)}) copy-start(s32[1,4]{1,0:T(1,128)} %param.21) | copy-start | bytes 52
  0.7 11.9 %copy-start.1 = (f32[2,4,16,16,128]{4,3,2,1,0:T(8,128)S(1)}, f32[2,4,16,16,128]{4,3,2,1,0:T(8,128)}, u32[]{:S(2)}) copy-start(f32[2,4,16,16,128]{4,3,2,1,0:T(8,128)} %param.18) | copy-start | bytes 3145732
  4.5 8.6 %copy-start.9 = (f32[16]{0:T(128)S(1)}, f32[16]{0:T(128)}, u32[]{:S(2)}) copy-start(f32[16]{0:T(128)} %param.24) | copy-start | bytes 196
  4.5 8.6 %copy-start.10 = (f32[16]{0:T(128)S(1)}, f32[16]{0:T(128)}, u32[]{:S(2)}) copy-start(f32[16]{0:T(128)} %param.28) | copy-start | bytes 196
  4.5 8.7 %copy-start.11 = (f32[16]{0:T(128)S(1)}, f32[16]{0:T(128)}, u32[]{:S(2)}) copy-start(f32[16]{0:T(128)} %param.26) | copy-start | bytes 196
  5.6 9.0 %collective-permute-start.1 = (bf16[2,18,3,128]{3,1,2,0:T(8,128)(2,1)S(1)}, bf16[2,18,3,128]{3,1,2,0:T(8,128)(2,1)S(1)}, u32[]{:S(2)}, u32[]{:S(2)}) collective-permute-start(bf16[2,18,3,128]{3,1,2,0:T(8,128)(2,1)S(1)} %get-tuple-element.23), channel_id=1, source_target_pairs={{4,0},{8,4},{12,8},{5,1},{9,5},{13,9},{6,2},{10,6},{14,10},{7,3},{... | collective-permute-start | bytes 82952 | tf_op jit(solution)/shard_map/ppermute | solution.py:15
  6.9 7.9 %collective-permute-start = (bf16[2,18,3,128]{3,1,2,0:T(8,128)(2,1)S(1)}, bf16[2,18,3,128]{3,1,2,0:T(8,128)(2,1)S(1)}, u32[]{:S(2)}, u32[]{:S(2)}) collective-permute-start(bf16[2,18,3,128]{3,1,2,0:T(8,128)(2,1)S(1)} %get-tuple-element.11), channel_id=1, source_target_pairs={{0,4},{4,8},{8,12},{1,5},{5,9},{9,13},{2,6},{6,10},{10,14},{3,7},{... | collective-permute-start | bytes 82952 | tf_op jit(solution)/shard_map/ppermute | solution.py:12
  14.9 0.9 %copy-start.6 = (bf16[9,16,18]{2,1,0:T(8,128)(2,1)S(1)}, bf16[9,16,18]{2,1,0:T(8,128)(2,1)}, u32[]{:S(2)}) copy-start(bf16[9,16,18]{2,1,0:T(8,128)(2,1)} %param.23) | copy-start | bytes 15556
  22.5 3.6 %copy-start.3 = (bf16[9,16,18]{2,1,0:T(8,128)(2,1)S(1)}, bf16[9,16,18]{2,1,0:T(8,128)(2,1)}, u32[]{:S(2)}) copy-start(bf16[9,16,18]{2,1,0:T(8,128)(2,1)} %param.27) | copy-start | bytes 15556
  29.4 1.6 %copy-start.4 = (f32[16,16]{1,0:T(8,128)S(1)}, f32[16,16]{1,0:T(8,128)}, u32[]{:S(2)}) copy-start(f32[16,16]{1,0:T(8,128)} %param.29) | copy-start | bytes 3076
  29.4 8.3 %copy-start.2 = (f32[2,16,4,32]{3,2,1,0:T(4,128)S(1)}, f32[2,16,4,32]{3,2,1,0:T(4,128)}, u32[]{:S(2)}) copy-start(f32[2,16,4,32]{3,2,1,0:T(4,128)} %param.22) | copy-start | bytes 49156
  29.4 8.3 %copy-start.5 = (f32[16,16]{1,0:T(8,128)S(1)}, f32[16,16]{1,0:T(8,128)}, u32[]{:S(2)}) copy-start(f32[16,16]{1,0:T(8,128)} %param.30) | copy-start | bytes 3076
  29.4 8.3 %copy-start.7 = (f32[16]{0:T(128)S(1)}, f32[16]{0:T(128)}, u32[]{:S(2)}) copy-start(f32[16]{0:T(128)} %param.31) | copy-start | bytes 196
  31.4 4.4 %collective-permute-start.3 = (f32[2,16,4,32]{3,1,2,0:T(8,128)S(1)}, f32[2,16,4,32]{3,1,2,0:T(8,128)S(1)}, u32[]{:S(2)}, u32[]{:S(2)}) collective-permute-start(f32[2,16,4,32]{3,1,2,0:T(8,128)S(1)} %get-tuple-element.26), channel_id=1, source_target_pairs={{0,2},{1,3},{2,0},{3,1},{4,6},{5,7},{6,4},{7,5},{8,10},{9,11},{10,... | collective-permute-start | bytes 49160 | tf_op jit(solution)/shard_map/ppermute | solution.py:70
  33.4 4.4 %collective-permute-start.4 = (f32[2,16,4,32]{3,1,2,0:T(8,128)S(1)}, f32[2,16,4,32]{3,1,2,0:T(8,128)S(1)}, u32[]{:S(2)}, u32[]{:S(2)}) collective-permute-start(f32[2,16,4,32]{3,1,2,0:T(8,128)S(1)} %get-tuple-element.26), channel_id=1, source_target_pairs={{0,3},{1,2},{2,1},{3,0},{4,7},{5,6},{6,5},{7,4},{8,11},{9,10},{10,... | collective-permute-start | bytes 49160 | tf_op jit(solution)/shard_map/ppermute | solution.py:70
  33.4 4.4 %collective-permute-start.2 = (f32[2,16,4,32]{3,1,2,0:T(8,128)S(1)}, f32[2,16,4,32]{3,1,2,0:T(8,128)S(1)}, u32[]{:S(2)}, u32[]{:S(2)}) collective-permute-start(f32[2,16,4,32]{3,1,2,0:T(8,128)S(1)} %get-tuple-element.25), channel_id=1, source_target_pairs={{0,1},{1,0},{2,3},{3,2},{4,5},{5,4},{6,7},{7,6},{8,9},{9,8},{10,11... | collective-permute-start | bytes 49160 | tf_op jit(solution)/shard_map/ppermute | solution.py:70

commit v3 on v2

--- a/solution.py
+++ b/solution.py
@@ -146,8 +146,22 @@
         apply_filter(first, own_out(w_reset), 1, 1, row_count + 4, column_count) + own_bias(b_reset)
     )
     wide_half = lax.dynamic_slice_in_dim(hidden_wide, start, half, 2)
-    gated = lax.all_gather(
-        (reset_half * wide_half.astype(jnp.float32)).astype(jnp.bfloat16), "rep", axis=2, tiled=True
+    gated_half = (reset_half * wide_half.astype(jnp.float32)).astype(jnp.bfloat16)
+    reps = lax.axis_size("rep")
+    pieces = [gated_half]
+    for step in range(1, reps):
+        perm = [(r, (r + step) % reps) for r in range(reps)]
+        pieces.append(lax.ppermute(gated_half, "rep", perm))
+    rep = lax.axis_index("rep")
+    gated = jnp.concatenate(
+        [
+            sum(
+                jnp.where((rep - step) % reps == owner, piece, jnp.zeros_like(piece))
+                for step, piece in enumerate(pieces)
+            )
+            for owner in range(reps)
+        ],
+        axis=2,
     )
     gated_pad = jnp.pad(gated, ((0, 0), (0, 0), (0, 0), (0, 0), (2, 2)))
     second = jnp.concatenate([first[:, :, :inputs_count, 1 : row_count + 5, :], gated_pad], axis=2)

time: 38.9 us -> 39.1 us (level)
  matrix products: 11.4 us -> 13.9 us
  blocking collectives: 2.49 us -> 0 us
  waiting for transfers between devices: 3.26 us -> 4.22 us
  other arithmetic: 4.15 us -> 3.59 us
  local copies, waits for them, and re-layouts: 7.18 us -> 6.71 us
    all_gather x1 -> x0, blocking collectives: 2.49 us -> none  [shards(): lax.all_gather((reset_half * wide_half.astype(jnp.float32)).astype(jnp.bf...]
    dot_general x27, matrix products: 10.3 us -> 12.8 us  [apply_filter(): jnp.einsum('oi,bsirw->bsorw', filter_weight[(left_operand + 1) * 3 + (rig...]
    ppermute x0 -> x1, waiting for transfers between devices: none -> 0.95 us  [shards(): pieces.append(lax.ppermute(gated_half, 'rep', perm))]
    concatenate x1, other arithmetic: 1.14 us -> 0.56 us  [shards(): jnp.concatenate([sum((jnp.where((rep - step) % reps == owner, piece, jnp....]
    unnamed x29 -> x31, local copies, waits for them, and re-layouts: 4.41 us -> 3.94 us
  transfers between devices with their start and end apart: 5 -> 6, of which waited for: 2 -> 3; matrix products, arithmetic and copies ran while one was open for 8% -> 9% of each run, Pallas kernels for 0% -> 0%
where the time goes in v3:
time: 39.1 us; the launch traced here: 38.7 us
  matrix products  13.9 us (36%)
  starting transfers between devices  9.29 us (24%)
  local copies, waits for them, and re-layouts  6.71 us (17%)
  waiting for transfers between devices  4.22 us (11%)
  other arithmetic  3.59 us (9%)
  between operations  1.09 us (3%)
    dot_general x27, matrix products, apply_filter(): jnp.einsum('oi,bsirw->bsorw', filter_weight[(left_operand + 1) * 3 + (rig...  12.8 us
    ppermute x1, starting transfers between devices, padded(): lax.ppermute(lax.slice_in_dim(block, block.shape[dim] - width, None, axis...  5.59 us
    unnamed x31, local copies, waits for them, and re-layouts  3.94 us
    ppermute x3, waiting for transfers between devices, exchange_sum(): chunk = lax.ppermute(chunk, ('band', 'rep'), perm)  3.26 us
    ppermute x3, starting transfers between devices, exchange_sum(): chunk = lax.ppermute(chunk, ('band', 'rep'), perm)  2.21 us
    ppermute x1, starting transfers between devices, padded(): lax.ppermute(lax.slice_in_dim(block, 0, width, axis=dim), axis, backward)  1.42 us
    ppermute x1, waiting for transfers between devices, shards(): pieces.append(lax.ppermute(gated_half, 'rep', perm))  0.95 us
  transfers between devices with their start and end apart: 6, of which 3 were waited for; matrix products, arithmetic and copies ran while one was open for 9% of the time, Pallas kernels for 0%

profile of v3, /device:TPU:0, one launch (start us, length us, event | category | flops | bytes accessed | tf_op | source)
XLA Modules:
  0.0 38.7 jit_solution(15439153176629613178)
XLA Ops:
  0.7 0.7 %not_and_fusion = (pred[4]{0:T(512)(128)(4,1)S(1)}, pred[4]{0:T(512)(128)(4,1)S(1)}) fusion(s32[4]{0:T(128)} %param.19, s32[]{:T(128)S(6)} %add.235, s32[]{:T(128)S(6)} %mul.31, s32[4,2]{0,1:T(2,128)} %param.20), kind=kLoop, calls=%fused_computation.207 | loop fusion | flops 24 | bytes 48 | tf_op jit(solution)/shard_map/and | solution.py:109
  1.4 0.8 %compare_and_fusion.1 = (pred[4]{0:T(512)(128)(4,1)S(1)}, s32[4]{0:T(128)S(1)}, pred[4]{0:T(512)(128)(4,1)S(1)}, pred[4]{0:T(512)(128)(4,1)S(1)}, s32[4]{0:T(128...) fusion(s32[]{:T(128)S(6)} %mul.31, s32[4,2]{0,1:T(2,128)} %param.20, ...), kind=kLoop, calls=%fused_computation.202 | loop fusion | flops 124 | bytes 116 | tf_op jit(solution)/shard_map/jit(_take)/and | solution.py:124
  2.2 0.7 %fusion.126 = (f32[4]{0:T(128)S(1)}, pred[4]{0:T(512)(128)(4,1)S(1)}) fusion(s32[4]{0:T(128)} %param.19, pred[4]{0:T(512)(128)(4,1)S(1)} %get-tuple-element.33), kind=kLoop, calls=%fused_computation.214 | loop fusion | flops 16 | bytes 40 | tf_op jit(solution)/shard_map/convert_element_type | solution.py:172
  2.8 1.7 %copy.106 = bf16[2,4,16,16,128]{4,2,3,1,0:T(8,128)(2,1)S(1)} copy(f32[2,4,16,16,128]{4,3,2,1,0:T(8,128)} %param.18) | data formatting | bytes 1572864 | tf_op args[1]
  4.8 1.4 %collective-permute-start.1 = (bf16[2,18,3,128]{3,1,2,0:T(8,128)(2,1)S(1)}, bf16[2,18,3,128]{3,1,2,0:T(8,128)(2,1)S(1)}, u32[]{:S(2)}, u32[]{:S(2)}) collective-permute-start(bf16[2,18,3,128]{3,1,2,0:T(8,128)(2,1)S(1)} %get-tuple-element.25), channel_id=1, source_target_pairs={{4,0},{8,4},{12,8},{5,1},{9,5},{13,9},{6,2},{10,6},{14,10},{7,3},{... | collective-permute-start | bytes 82952 | tf_op jit(solution)/shard_map/ppermute | solution.py:15
  6.2 5.6 %collective-permute-start = (bf16[2,18,3,128]{3,1,2,0:T(8,128)(2,1)S(1)}, bf16[2,18,3,128]{3,1,2,0:T(8,128)(2,1)S(1)}, u32[]{:S(2)}, u32[]{:S(2)}) collective-permute-start(bf16[2,18,3,128]{3,1,2,0:T(8,128)(2,1)S(1)} %get-tuple-element.11), channel_id=1, source_target_pairs={{0,4},{4,8},{8,12},{1,5},{5,9},{9,13},{2,6},{6,10},{10,14},{3,7},{... | collective-permute-start | bytes 82952 | tf_op jit(solution)/shard_map/ppermute | solution.py:12
  11.9 0.3 copy.49
  12.6 0.6 %gather_fusion.2 = bf16[4,2,18,3,128]{4,2,3,1,0:T(8,128)(2,1)S(1)} fusion(bf16[2,4,18,3,128]{4,2,3,1,0:T(8,128)(2,1)S(1)} %get-tuple-element.26, s32[1024]{0:T(1024)S(1)} %pad_clamp_fusion.1), kind=kCustom, calls=%fused_computation.1.clone | custom fusion | bytes 221200 | tf_op jit(solution)/shard_map/jit(_take)/gather | solution.py:127
  13.2 0.8 %gather_fusion.1 = bf16[4,2,18,3,128]{4,1,3,2,0:T(2,128)(2,1)S(1)} fusion(bf16[2,4,18,3,128]{4,0,3,2,1:T(2,128)(2,1)S(1)} %copy.51, s32[1024]{0:T(1024)S(1)} %pad_clamp_fusion.2), kind=kCustom, calls=%fused_computation.clone | custom fusion | bytes 221200 | tf_op jit(solution)/shard_map/jit(_take)/gather | solution.py:124
  14.3 0.3 pad_maximum_fusion
  14.6 0.3 slice.254
  15.0 0.4 fusion.48
  15.4 0.3 convolution_add_fusion.9
  15.7 0.3 fusion.97
  16.1 0.4 %convolution_add_fusion.5 = f32[2,4,20,128,8]{3,4,2,1,0:T(8,128)S(1)} fusion(f32[2,4,20,128,8]{3,4,2,1,0:T(8,128)S(1)} %fusion.97, bf16[2,4,18,22,128]{4,2,3,1,0:T(8,128)(2,1)S(1)} %pad_maximum_fusion, bf16[9,16,18]{2,1,0:T(8,128)(2,1)S(1)} %copy-done, s32[]{:T(128)S(6)} %select_n.133), kind=kOutput, calls=%fused_computation.43 | convolution fusion | flops 6062080 | bytes 2394116 | tf_op jit(solution)/shard_map/oi,bsirw->bsorw/dot_general | solution.py:39
  16.5 0.4 %convolution_add_fusion.23 = f32[2,4,16,128,8]{3,4,2,1,0:T(8,128)S(1)} fusion(f32[2,4,16,128,8]{3,4,2,1,0:T(8,128)S(1)} %convolution_add_fusion.9, bf16[2,4,18,22,128]{4,2,3,1,0:T(8,128)(2,1)S(1)} %pad_maximum_fusion, bf16[9,16,18]{2,1,0:T(8,128)(2,1)S(1)} %copy-done.7, s32[]{:T(128)S(6)} %add.314, s32[]{:T(128)S(6)} %select_n.133), kind=kOutput, calls=%fused_computation.68 | convolution fusion | flops 4849664 | bytes 2131976 | tf_op jit(solution)/shard_map/oi,bsirw->bsorw/dot_general | solution.py:39
  16.9 0.4 %convolution_add_fusion.4 = f32[2,4,20,128,8]{3,4,2,1,0:T(8,128)S(1)} fusion(f32[2,4,20,128,8]{3,4,2,1,0:T(8,128)S(1)} %convolution_add_fusion.5, bf16[2,4,18,22,128]{4,2,3,1,0:T(8,128)(2,1)S(1)} %pad_maximum_fusion, bf16[9,16,18]{2,1,0:T(8,128)(2,1)S(1)} %copy-done, s32[]{:T(128)S(6)} %add.314, s32[]{:T(128)S(6)} %select_n.133), kind=kOutput, calls=%fused_computation.42 | convolution fusion | flops 6062080 | bytes 2394120 | tf_op jit(solution)/shard_map/oi,bsirw->bsorw/dot_general | solution.py:39
  17.4 0.4 %convolution_add_fusion.22 = f32[2,4,16,128,8]{3,4,2,1,0:T(8,128)S(1)} fusion(f32[2,4,16,128,8]{3,4,2,1,0:T(8,128)S(1)} %convolution_add_fusion.23, bf16[2,4,18,22,128]{4,2,3,1,0:T(8,128)(2,1)S(1)} %pad_maximum_fusion, bf16[9,16,18]{2,1,0:T(8,128)(2,1)S(1)} %copy-done.7, s32[]{:T(128)S(6)} %add.315, s32[]{:T(128)S(6)} %select_n.133), kind=kOutput, calls=%fused_computation.67 | convolution fusion | flops 4849664 | bytes 2131976 | tf_op jit(solution)/shard_map/oi,bsirw->bsorw/dot_general | solution.py:39
  17.7 0.4 %convolution_add_fusion.3 = f32[2,4,20,128,8]{3,4,2,1,0:T(8,128)S(1)} fusion(f32[2,4,20,128,8]{3,4,2,1,0:T(8,128)S(1)} %convolution_add_fusion.4, bf16[2,4,18,22,128]{4,2,3,1,0:T(8,128)(2,1)S(1)} %pad_maximum_fusion, bf16[9,16,18]{2,1,0:T(8,128)(2,1)S(1)} %copy-done, s32[]{:T(128)S(6)} %add.315, s32[]{:T(128)S(6)} %select_n.133), kind=kOutput, calls=%fused_computation.41 | convolution fusion | flops 6062080 | bytes 2394120 | tf_op jit(solution)/shard_map/oi,bsirw->bsorw/dot_general | solution.py:39
  18.2 0.3 convolution_add_fusion.21
  18.5 0.3 convolution_add_fusion.7
  18.9 0.4 %convolution_add_fusion.20 = f32[2,4,16,128,8]{3,4,2,1,0:T(8,128)S(1)} fusion(f32[2,4,16,128,8]{3,4,2,1,0:T(8,128)S(1)} %convolution_add_fusion.21, bf16[2,4,18,22,128]{4,2,3,1,0:T(8,128)(2,1)S(1)} %pad_maximum_fusion, bf16[9,16,18]{2,1,0:T(8,128)(2,1)S(1)} %copy-done.7, s32[]{:T(128)S(6)} %add.317, s32[]{:T(128)S(6)} %select_n.133), kind=kOutput, calls=%fused_computation.65 | convolution fusion | flops 4849664 | bytes 2131976 | tf_op jit(solution)/shard_map/oi,bsirw->bsorw/dot_general | solution.py:39
  19.3 0.4 %convolution_add_fusion.2 = f32[2,4,20,128,8]{3,4,2,1,0:T(8,128)S(1)} fusion(f32[2,4,20,128,8]{3,4,2,1,0:T(8,128)S(1)} %convolution_add_fusion.7, bf16[2,4,18,22,128]{4,2,3,1,0:T(8,128)(2,1)S(1)} %pad_maximum_fusion, bf16[9,16,18]{2,1,0:T(8,128)(2,1)S(1)} %copy-done, s32[]{:T(128)S(6)} %add.317, s32[]{:T(128)S(6)} %select_n.133), kind=kOutput, calls=%fused_computation.40 | convolution fusion | flops 6062080 | bytes 2394120 | tf_op jit(solution)/shard_map/oi,bsirw->bsorw/dot_general | solution.py:39
  19.7 0.4 %convolution_add_fusion.19 = f32[2,4,16,128,8]{3,4,2,1,0:T(8,128)S(1)} fusion(f32[2,4,16,128,8]{3,4,2,1,0:T(8,128)S(1)} %convolution_add_fusion.20, bf16[2,4,18,22,128]{4,2,3,1,0:T(8,128)(2,1)S(1)} %pad_maximum_fusion, bf16[9,16,18]{2,1,0:T(8,128)(2,1)S(1)} %copy-done.7, s32[]{:T(128)S(6)} %add.318, s32[]{:T(128)S(6)} %select_n.133), kind=kOutput, calls=%fused_computation.64 | convolution fusion | flops 4849664 | bytes 2131976 | tf_op jit(solution)/shard_map/oi,bsirw->bsorw/dot_general | solution.py:39
  20.1 0.4 %convolution_add_fusion.1 = f32[2,4,20,128,8]{3,4,2,1,0:T(8,128)S(1)} fusion(f32[2,4,20,128,8]{3,4,2,1,0:T(8,128)S(1)} %convolution_add_fusion.2, bf16[2,4,18,22,128]{4,2,3,1,0:T(8,128)(2,1)S(1)} %pad_maximum_fusion, bf16[9,16,18]{2,1,0:T(8,128)(2,1)S(1)} %copy-done, s32[]{:T(128)S(6)} %add.318, s32[]{:T(128)S(6)} %select_n.133), kind=kOutput, calls=%fused_computation.39 | convolution fusion | flops 6062080 | bytes 2394120 | tf_op jit(solution)/shard_map/oi,bsirw->bsorw/dot_general | solution.py:39
  20.5 0.3 convolution_add_fusion.8
  20.8 0.3 convolution_add_fusion.6
  21.2 0.5 %fusion.22 = bf16[2,4,8,20,128]{4,2,3,1,0:T(8,128)(2,1)S(1)} fusion(f32[2,4,20,128,8]{3,4,2,1,0:T(8,128)S(1)} %convolution_add_fusion.6, bf16[2,4,18,22,128]{4,2,3,1,0:T(8,128)(2,1)S(1)} %pad_maximum_fusion, f32[8]{0:T(128)S(1)} %dynamic_slice.39, bf16[2,4,16,20,128]{4,2,3,1,0:T(8,128)(2,1)S(1)} %slice.254, s32[]{:T(128)S(6)} %select_n.133, ...), kind=kOutput, calls=%fused_computation.80 | convolution fusion | flops 7208960 | bytes 2396160 | tf_op jit(solution)/shard_map/oi,bsirw->bsorw/dot_general | solution.py:39
  22.0 0.4 %fusion.15 = f32[2,4,16,128,8]{3,4,2,1,0:T(8,128)S(1)} fusion(f32[2,4,16,128,8]{3,4,2,1,0:T(8,128)S(1)} %convolution_add_fusion.8, bf16[2,4,18,22,128]{4,2,3,1,0:T(8,128)(2,1)S(1)} %pad_maximum_fusion, f32[8]{0:T(128)S(1)} %dynamic_slice.36, bf16[9,16,18]{2,1,0:T(8,128)(2,1)S(1)} %copy-done.7, s32[]{:T(128)S(6)} %add.320, s32[]{:T(128)S(6)} %select_n.133), kind=kOutput, calls=%fused_computation.73 | convolution fusion | flops 5373952 | bytes 2132488 | tf_op jit(solution)/shard_map/oi,bsirw->bsorw/dot_general | solution.py:39
  22.4 1.0 %collective-permute-done.2 = bf16[2,4,8,20,128]{4,2,3,1,0:T(8,128)(2,1)S(1)} collective-permute-done((bf16[2,4,8,20,128]{4,2,3,1,0:T(8,128)(2,1)S(1)}, bf16[2,4,8,20,128]{4,2,3,1,0:T(8,128)(2,1)S(1)}, u32[]{:S(2)}, u32[]{:S(2)}) %collective-permute-start.2) | collective-permute-done | bytes 327712 | tf_op jit(solution)/shard_map/ppermute | solution.py:154
  23.5 0.6 %fusion.3 = bf16[2,4,16,20,132]{4,2,3,1,0:T(8,128)(2,1)S(1)} fusion(bf16[2,4,8,20,128]{4,2,3,1,0:T(8,128)(2,1)S(1)} %get-tuple-element.24, bf16[2,4,8,20,128]{4,2,3,1,0:T(8,128)(2,1)S(1)} %get-tuple-element.23), kind=kLoop, calls=%fused_computation.37 | loop fusion | flops 3041280 | bytes 1331200 | tf_op jit(solution)/shard_map/concatenate | solution.py:156
  24.2 0.3 fusion.53
  24.6 0.8 %convolution_add_fusion.17 = f32[2,4,16,128,8]{3,4,2,1,0:T(8,128)S(1)} fusion(f32[2,4,16,128,8]{3,4,2,1,0:T(8,128)S(1)} %fusion.53, bf16[2,4,16,20,132]{4,2,3,1,0:T(8,128)(2,1)S(1)} %fusion.3, bf16[2,4,2,20,132]{4,2,3,1,0:T(2,128)(2,1)S(1)} %pad_slice_fusion.14, bf16[9,16,18]{2,1,0:T(8,128)(2,1)S(1)} %copy-done.6, s32[]{:T(128)S(6)} %add.313, s32[]{:T(128)S(6)} %select_n.133), kind=kOutput, calls=%fused_computation.62 | convolution fusion | flops 6029312 | bytes 2525192 | tf_op jit(solution)/shard_map/oi,bsirw->bsorw/dot_general | solution.py:39
  25.3 0.8 %convolution_add_fusion.16 = f32[2,4,16,128,8]{3,4,2,1,0:T(8,128)S(1)} fusion(f32[2,4,16,128,8]{3,4,2,1,0:T(8,128)S(1)} %convolution_add_fusion.17, bf16[2,4,16,20,132]{4,2,3,1,0:T(8,128)(2,1)S(1)} %fusion.3, bf16[2,4,2,20,132]{4,2,3,1,0:T(2,128)(2,1)S(1)} %pad_slice_fusion.14, bf16[9,16,18]{2,1,0:T(8,128)(2,1)S(1)} %copy-done.6, s32[]{:T(128)S(6)} %add.314, ...), kind=kOutput, calls=%fused_computation.61 | convolution fusion | flops 6029312 | bytes 2525192 | tf_op jit(solution)/shard_map/oi,bsirw->bsorw/dot_general | solution.py:39
  26.1 0.3 convolution_add_fusion.15
  26.4 0.9 %convolution_add_fusion.14 = f32[2,4,16,128,8]{3,4,2,1,0:T(8,128)S(1)} fusion(f32[2,4,16,128,8]{3,4,2,1,0:T(8,128)S(1)} %convolution_add_fusion.15, bf16[2,4,16,20,132]{4,2,3,1,0:T(8,128)(2,1)S(1)} %fusion.3, bf16[2,4,2,20,132]{4,2,3,1,0:T(2,128)(2,1)S(1)} %pad_slice_fusion.14, bf16[9,16,18]{2,1,0:T(8,128)(2,1)S(1)} %copy-done.6, s32[]{:T(128)S(6)} %add.316, ...), kind=kOutput, calls=%fused_computation.59 | convolution fusion | flops 6029312 | bytes 2525192 | tf_op jit(solution)/shard_map/oi,bsirw->bsorw/dot_general | solution.py:39
  27.3 0.8 %convolution_add_fusion.13 = f32[2,4,16,128,8]{3,4,2,1,0:T(8,128)S(1)} fusion(f32[2,4,16,128,8]{3,4,2,1,0:T(8,128)S(1)} %convolution_add_fusion.14, bf16[2,4,16,20,132]{4,2,3,1,0:T(8,128)(2,1)S(1)} %fusion.3, bf16[2,4,2,20,132]{4,2,3,1,0:T(2,128)(2,1)S(1)} %pad_slice_fusion.14, bf16[9,16,18]{2,1,0:T(8,128)(2,1)S(1)} %copy-done.6, s32[]{:T(128)S(6)} %add.317, ...), kind=kOutput, calls=%fused_computation.58 | convolution fusion | flops 6029312 | bytes 2525192 | tf_op jit(solution)/shard_map/oi,bsirw->bsorw/dot_general | solution.py:39
  28.1 0.3 convolution_add_fusion.12
  28.4 0.8 %convolution_add_fusion.11 = f32[2,4,16,128,8]{3,4,2,1,0:T(8,128)S(1)} fusion(f32[2,4,16,128,8]{3,4,2,1,0:T(8,128)S(1)} %convolution_add_fusion.12, bf16[2,4,16,20,132]{4,2,3,1,0:T(8,128)(2,1)S(1)} %fusion.3, bf16[2,4,2,20,132]{4,2,3,1,0:T(2,128)(2,1)S(1)} %pad_slice_fusion.14, bf16[9,16,18]{2,1,0:T(8,128)(2,1)S(1)} %copy-done.6, s32[]{:T(128)S(6)} %add.319, ...), kind=kOutput, calls=%fused_computation.56 | convolution fusion | flops 6029312 | bytes 2525192 | tf_op jit(solution)/shard_map/oi,bsirw->bsorw/dot_general | solution.py:39
  29.2 0.8 %fusion.152 = (f32[4,8,16,128]{3,1,2,0:T(8,128)S(1)}, f32[2,4,8,16,128]{4,2,3,1,0:T(8,128)S(1)}) fusion(f32[4]{0:T(128)S(1)} %get-tuple-element.34, f32[2,4,16,128,8]{3,4,2,1,0:T(8,128)S(1)} %fusion.15, f32[8]{0:T(128)S(1)} %dynamic_slice.42, f32[2,4,16,128,8]{3,4,2,1,0:T(8,128)S(1)} %convolution_add_fusion.11, bf16[9,16,18]{2,1,0:T(8,128)(2,1)S(1)} %copy-done.6, ...), kind=kOutput, calls=%fused_computation.241 | convolution fusion | flops 6881280 | bytes 3838464 | tf_op jit(solution)/shard_map/oi,bsirw->bsorw/dot_general | solution.py:39
  30.0 0.5 %convolution_reduce_fusion = f32[4,8,4,32]{3,2,1,0:T(4,128)S(1)} fusion(f32[4,8,4,4,128]{4,1,3,2,0:T(8,128)S(1)} %bitcast.259, s32[128]{0:T(128)S(1)} %and_select_fusion), kind=kOutput, calls=%fused_computation.81 | convolution fusion | flops 25182208 | bytes 279040 | tf_op jit(solution)/shard_map/schw,wj->schj/dot_general | solution.py:178
  30.6 0.6 %gather_fusion = f32[4,8,4,32]{3,1,2,0:T(8,128)S(1)} fusion(f32[4,8,4,32]{3,1,2,0:T(8,128)S(1)} %copy_multiply_fusion, s32[1024]{0:T(1024)S(1)} %pad_clamp_fusion), kind=kCustom, calls=%fused_computation.2 | custom fusion | bytes 32784 | tf_op jit(solution)/shard_map/jit(_take)/gather | solution.py:184
  31.1 0.3 fusion.56
  31.5 2.0 %collective-permute-start.4 = (f32[2,16,4,32]{3,1,2,0:T(8,128)S(1)}, f32[2,16,4,32]{3,1,2,0:T(8,128)S(1)}, u32[]{:S(2)}, u32[]{:S(2)}) collective-permute-start(f32[2,16,4,32]{3,1,2,0:T(8,128)S(1)} %get-tuple-element.28), channel_id=1, source_target_pairs={{0,2},{1,3},{2,0},{3,1},{4,6},{5,7},{6,4},{7,5},{8,10},{9,11},{10,... | collective-permute-start | bytes 49160 | tf_op jit(solution)/shard_map/ppermute | solution.py:70
  33.7 0.9 %copy.60 = f32[2,4,8,16,128]{4,3,2,1,0:T(8,128)} copy(f32[2,4,8,16,128]{4,2,3,1,0:T(8,128)S(1)} %get-tuple-element.37) | data formatting | bytes 1048576
  34.6 1.3 %collective-permute-done.4 = f32[2,16,4,32]{3,1,2,0:T(8,128)S(1)} collective-permute-done((f32[2,16,4,32]{3,1,2,0:T(8,128)S(1)}, f32[2,16,4,32]{3,1,2,0:T(8,128)S(1)}, u32[]{:S(2)}, u32[]{:S(2)}) %collective-permute-start.4) | collective-permute-done | bytes 16416 | tf_op jit(solution)/shard_map/ppermute | solution.py:70
  35.9 2.0 %collective-permute-done.5 = f32[2,16,4,32]{3,1,2,0:T(8,128)S(1)} collective-permute-done((f32[2,16,4,32]{3,1,2,0:T(8,128)S(1)}, f32[2,16,4,32]{3,1,2,0:T(8,128)S(1)}, u32[]{:S(2)}, u32[]{:S(2)}) %collective-permute-start.5) | collective-permute-done | bytes 16416 | tf_op jit(solution)/shard_map/ppermute | solution.py:70
  38.1 0.7 %copy.61 = f32[2,16,4,32]{3,2,1,0:T(4,128)} copy(f32[2,16,4,32]{3,1,2,0:T(8,128)S(1)} %tanh_add_fusion) | data formatting | bytes 32768
  (50 shorter events, 2.0 us)
Async XLA Ops:
  0.6 15.1 %copy-start = (bf16[9,16,18]{2,1,0:T(8,128)(2,1)S(1)}, bf16[9,16,18]{2,1,0:T(8,128)(2,1)}, u32[]{:S(2)}) copy-start(bf16[9,16,18]{2,1,0:T(8,128)(2,1)} %param.25) | copy-start | bytes 15556
  0.6 3.9 %copy-start.3 = (bf16[2,4,2,16,128]{4,3,2,1,0:T(8,128)(2,1)S(1)}, bf16[2,4,2,16,128]{4,3,2,1,0:T(8,128)(2,1)}, u32[]{:S(2)}) copy-start(bf16[2,4,2,16,128]{4,3,2,1,0:T(8,128)(2,1)} %param.17) | copy-start | bytes 196612
  2.8 9.0 %copy-start.9 = (s32[1,4]{1,0:T(1,128)S(1)}, s32[1,4]{1,0:T(1,128)}, u32[]{:S(2)}) copy-start(s32[1,4]{1,0:T(1,128)} %param.21) | copy-start | bytes 52
  2.8 9.1 %copy-start.1 = (f32[2,4,16,16,128]{4,3,2,1,0:T(8,128)S(1)}, f32[2,4,16,16,128]{4,3,2,1,0:T(8,128)}, u32[]{:S(2)}) copy-start(f32[2,4,16,16,128]{4,3,2,1,0:T(8,128)} %param.18) | copy-start | bytes 3145732
  4.7 7.6 %copy-start.10 = (f32[16]{0:T(128)S(1)}, f32[16]{0:T(128)}, u32[]{:S(2)}) copy-start(f32[16]{0:T(128)} %param.24) | copy-start | bytes 196
  4.8 7.7 %copy-start.11 = (f32[16]{0:T(128)S(1)}, f32[16]{0:T(128)}, u32[]{:S(2)}) copy-start(f32[16]{0:T(128)} %param.28) | copy-start | bytes 196
  4.8 7.8 %copy-start.12 = (f32[16]{0:T(128)S(1)}, f32[16]{0:T(128)}, u32[]{:S(2)}) copy-start(f32[16]{0:T(128)} %param.26) | copy-start | bytes 196
  4.8 9.2 %collective-permute-start.1 = (bf16[2,18,3,128]{3,1,2,0:T(8,128)(2,1)S(1)}, bf16[2,18,3,128]{3,1,2,0:T(8,128)(2,1)S(1)}, u32[]{:S(2)}, u32[]{:S(2)}) collective-permute-start(bf16[2,18,3,128]{3,1,2,0:T(8,128)(2,1)S(1)} %get-tuple-element.25), channel_id=1, source_target_pairs={{4,0},{8,4},{12,8},{5,1},{9,5},{13,9},{6,2},{10,6},{14,10},{7,3},{... | collective-permute-start | bytes 82952 | tf_op jit(solution)/shard_map/ppermute | solution.py:15
  6.2 7.9 %collective-permute-start = (bf16[2,18,3,128]{3,1,2,0:T(8,128)(2,1)S(1)}, bf16[2,18,3,128]{3,1,2,0:T(8,128)(2,1)S(1)}, u32[]{:S(2)}, u32[]{:S(2)}) collective-permute-start(bf16[2,18,3,128]{3,1,2,0:T(8,128)(2,1)S(1)} %get-tuple-element.11), channel_id=1, source_target_pairs={{0,4},{4,8},{8,12},{1,5},{5,9},{9,13},{2,6},{6,10},{10,14},{3,7},{... | collective-permute-start | bytes 82952 | tf_op jit(solution)/shard_map/ppermute | solution.py:12
  14.3 0.8 %copy-start.7 = (bf16[9,16,18]{2,1,0:T(8,128)(2,1)S(1)}, bf16[9,16,18]{2,1,0:T(8,128)(2,1)}, u32[]{:S(2)}) copy-start(bf16[9,16,18]{2,1,0:T(8,128)(2,1)} %param.23) | copy-start | bytes 15556
  21.7 1.7 %collective-permute-start.2 = (bf16[2,4,8,20,128]{4,2,3,1,0:T(8,128)(2,1)S(1)}, bf16[2,4,8,20,128]{4,2,3,1,0:T(8,128)(2,1)S(1)}, u32[]{:S(2)}, u32[]{:S(2)}) collective-permute-start(bf16[2,4,8,20,128]{4,2,3,1,0:T(8,128)(2,1)S(1)} %fusion.22), channel_id=1, source_target_pairs={{0,1},{1,0},{2,3},{3,2},{4,5},{5,4},{6,7},{7,6},{8,9},{9,8},{10,11... | collective-permute-start | bytes 983048 | tf_op jit(solution)/shard_map/ppermute | solution.py:154
  23.5 0.8 %copy-start.6 = (bf16[9,16,18]{2,1,0:T(8,128)(2,1)S(1)}, bf16[9,16,18]{2,1,0:T(8,128)(2,1)}, u32[]{:S(2)}) copy-start(bf16[9,16,18]{2,1,0:T(8,128)(2,1)} %param.27) | copy-start | bytes 15556
  29.2 2.0 %copy-start.4 = (f32[16,16]{1,0:T(8,128)S(1)}, f32[16,16]{1,0:T(8,128)}, u32[]{:S(2)}) copy-start(f32[16,16]{1,0:T(8,128)} %param.29) | copy-start | bytes 3076
  30.0 7.9 %copy-start.2 = (f32[2,16,4,32]{3,2,1,0:T(4,128)S(1)}, f32[2,16,4,32]{3,2,1,0:T(4,128)}, u32[]{:S(2)}) copy-start(f32[2,16,4,32]{3,2,1,0:T(4,128)} %param.22) | copy-start | bytes 49156
  30.0 7.9 %copy-start.5 = (f32[16,16]{1,0:T(8,128)S(1)}, f32[16,16]{1,0:T(8,128)}, u32[]{:S(2)}) copy-start(f32[16,16]{1,0:T(8,128)} %param.30) | copy-start | bytes 3076
  30.0 7.9 %copy-start.8 = (f32[16]{0:T(128)S(1)}, f32[16]{0:T(128)}, u32[]{:S(2)}) copy-start(f32[16]{0:T(128)} %param.31) | copy-start | bytes 196
  31.5 4.4 %collective-permute-start.4 = (f32[2,16,4,32]{3,1,2,0:T(8,128)S(1)}, f32[2,16,4,32]{3,1,2,0:T(8,128)S(1)}, u32[]{:S(2)}, u32[]{:S(2)}) collective-permute-start(f32[2,16,4,32]{3,1,2,0:T(8,128)S(1)} %get-tuple-element.28), channel_id=1, source_target_pairs={{0,2},{1,3},{2,0},{3,1},{4,6},{5,7},{6,4},{7,5},{8,10},{9,11},{10,... | collective-permute-start | bytes 49160 | tf_op jit(solution)/shard_map/ppermute | solution.py:70
  33.5 4.4 %collective-permute-start.5 = (f32[2,16,4,32]{3,1,2,0:T(8,128)S(1)}, f32[2,16,4,32]{3,1,2,0:T(8,128)S(1)}, u32[]{:S(2)}, u32[]{:S(2)}) collective-permute-start(f32[2,16,4,32]{3,1,2,0:T(8,128)S(1)} %get-tuple-element.28), channel_id=1, source_target_pairs={{0,3},{1,2},{2,1},{3,0},{4,7},{5,6},{6,5},{7,4},{8,11},{9,10},{10,... | collective-permute-start | bytes 49160 | tf_op jit(solution)/shard_map/ppermute | solution.py:70
  33.5 4.4 %collective-permute-start.3 = (f32[2,16,4,32]{3,1,2,0:T(8,128)S(1)}, f32[2,16,4,32]{3,1,2,0:T(8,128)S(1)}, u32[]{:S(2)}, u32[]{:S(2)}) collective-permute-start(f32[2,16,4,32]{3,1,2,0:T(8,128)S(1)} %get-tuple-element.27), channel_id=1, source_target_pairs={{0,1},{1,0},{2,3},{3,2},{4,5},{5,4},{6,7},{7,6},{8,9},{9,8},{10,11... | collective-permute-start | bytes 49160 | tf_op jit(solution)/shard_map/ppermute | solution.py:70

commit v4 on v2

--- a/solution.py
+++ b/solution.py
@@ -118,9 +118,13 @@
     joined = jnp.concatenate([features, hb], axis=2)
     top = choose_rows(joined[:, :, :, :3, :], first_sel)
     bottom = choose_rows(joined[:, :, :, row_count - 3 :, :], last_sel)
-    cycle = padded(jnp.concatenate([top, bottom], axis=2), (("tiles", 2),), 3)
-    cycle_prev = cycle[:, None, :, :3, :]
-    cycle_next = cycle[:, None, :, 3 * 3 : 4 * 3, :]
+    tiles_count = lax.axis_size("tiles")
+    tile = lax.axis_index("tiles")
+    edges = lax.all_gather(jnp.concatenate([top, bottom], axis=2), "tiles")
+    cycle_prev = lax.dynamic_index_in_dim(edges, (tile + tiles_count - 1) % tiles_count, 0, False)
+    cycle_next = lax.dynamic_index_in_dim(edges, (tile + 1) % tiles_count, 0, False)
+    cycle_prev = cycle_prev[:, None, :, 3:6, :]
+    cycle_next = cycle_next[:, None, :, :3, :]
     top_local = jnp.take(
         joined[:, :, :, row_count - 3 :, :], jnp.clip(ups - base, 0, slots - 1), axis=1
     )

time: 38.9 us -> 50.2 us (1.29)
  blocking collectives: 2.49 us -> 18.2 us
  starting transfers between devices: 9.09 us -> 2.21 us
  matrix products: 11.4 us -> 13.3 us
  local copies, waits for them, and re-layouts: 7.18 us -> 8.23 us
    all_gather x0 -> x1, blocking collectives: none -> 15.7 us  [shards(): edges = lax.all_gather(jnp.concatenate([top, bottom], axis=2), 'tiles')]
    ppermute x2 -> x0, starting transfers between devices: 6.88 us -> none  [the longest x1 5.59 us: padded(): lax.ppermute(lax.slice_in_dim(block, block.shape[dim] - width, None, axis...]
    dot_general x27, matrix products: 10.3 us -> 12.2 us  [apply_filter(): jnp.einsum('oi,bsirw->bsorw', filter_weight[(left_operand + 1) * 3 + (rig...]
    slice x1, local copies, waits for them, and re-layouts: 0.24 us -> 0.91 us  [shards(): first[:, :, :inputs_count, 1:row_count + 5, :]]
    and x0 -> x1, other arithmetic: none -> 0.67 us  [shards(): first_sel = alive & jnp.logical_not(up_here)]
    convert_element_type x1 -> x0, other arithmetic: 0.67 us -> none  [shards(): live_scale = alive.astype(jnp.float32)[None, :, None, None, None]]
    unnamed x29 -> x39, local copies, waits for them, and re-layouts: 4.41 us -> 4.72 us
  transfers between devices with their start and end apart: 5 -> 3, of which waited for: 2 -> 2; matrix products, arithmetic and copies ran while one was open for 8% -> 2% of each run, Pallas kernels for 0% -> 0%
where the time goes in v4:
time: 50.2 us; the launch traced here: 49.9 us
  blocking collectives  18.2 us (36%)
  matrix products  13.3 us (26%)
  local copies, waits for them, and re-layouts  8.23 us (16%)
  other arithmetic  4.08 us (8%)
  waiting for transfers between devices  2.81 us (6%)
  starting transfers between devices  2.21 us (4%)
  between operations  1.11 us (2%)
    all_gather x1, blocking collectives, shards(): edges = lax.all_gather(jnp.concatenate([top, bottom], axis=2), 'tiles')  15.7 us
    dot_general x27, matrix products, apply_filter(): jnp.einsum('oi,bsirw->bsorw', filter_weight[(left_operand + 1) * 3 + (rig...  12.2 us
    unnamed x39, local copies, waits for them, and re-layouts  4.72 us
    ppermute x3, waiting for transfers between devices, exchange_sum(): chunk = lax.ppermute(chunk, ('band', 'rep'), perm)  2.81 us
    all_gather x1, blocking collectives, shards(): lax.all_gather((reset_half * wide_half.astype(jnp.float32)).astype(jnp.bf...  2.49 us
    ppermute x3, starting transfers between devices, exchange_sum(): chunk = lax.ppermute(chunk, ('band', 'rep'), perm)  2.21 us
    concatenate x1, other arithmetic, shards(): jnp.concatenate([first[:, :, :inputs_count, 1:row_count + 5, :], gated_pa...  1.14 us
  transfers between devices with their start and end apart: 3, of which 2 were waited for; matrix products, arithmetic and copies ran while one was open for 2% of the time, Pallas kernels for 0%

profile of v4, /device:TPU:0, one launch (start us, length us, event | category | flops | bytes accessed | tf_op | source)
XLA Modules:
  0.0 49.9 jit_solution(195071952042089168)
XLA Ops:
  0.7 1.6 %copy.113 = bf16[2,4,16,16,128]{4,2,3,1,0:T(8,128)(2,1)S(1)} copy(f32[2,4,16,16,128]{4,3,2,1,0:T(8,128)} %param.18) | data formatting | bytes 1572864 | tf_op args[1]
  2.2 0.9 %copy.52 = bf16[2,4,2,16,128]{4,2,3,1,0:T(2,128)(2,1)S(1)} copy(bf16[2,4,2,16,128]{4,3,2,1,0:T(8,128)(2,1)} %param.17) | data formatting | bytes 131072 | tf_op args[0]
  3.1 0.7 %not_and_fusion = (pred[4]{0:T(512)(128)(4,1)S(1)}, pred[4]{0:T(512)(128)(4,1)S(1)}, f32[4]{0:T(128)S(1)}) fusion(s32[4]{0:T(128)} %param.19, s32[]{:T(128)S(6)} %add.240, s32[]{:T(128)S(6)} %mul.31, s32[4,2]{0,1:T(2,128)} %param.20), kind=kLoop, calls=%fused_computation.189 | loop fusion | flops 28 | bytes 64 | tf_op jit(solution)/shard_map/and | solution.py:109
  3.9 0.8 %compare_and_fusion.1 = (pred[4]{0:T(512)(128)(4,1)S(1)}, s32[4]{0:T(128)S(1)}, pred[4]{0:T(512)(128)(4,1)S(1)}, pred[4]{0:T(512)(128)(4,1)S(1)}, s32[4]{0:T(128...) fusion(s32[]{:T(128)S(6)} %mul.31, s32[4,2]{0,1:T(2,128)} %param.20, ...), kind=kLoop, calls=%fused_computation.184 | loop fusion | flops 124 | bytes 116 | tf_op jit(solution)/shard_map/jit(_take)/and | solution.py:128
  4.6 0.7 %not_and_fusion.1 = pred[4]{0:T(512)(128)(4,1)S(1)} fusion(pred[4]{0:T(512)(128)(4,1)S(1)} %get-tuple-element.33, s32[4]{0:T(128)} %param.19), kind=kLoop, calls=%fused_computation.190 | loop fusion | flops 12 | bytes 24 | tf_op jit(solution)/shard_map/and | solution.py:108
  5.5 15.7 %all-gather = bf16[8,18,6,128]{3,2,1,0:T(8,128)(2,1)S(1)} all-gather(bf16[2,18,6,128]{3,2,1,0:T(8,128)(2,1)S(1)} %copy.55), channel_id=2, replica_groups=mesh['groups'=2,'tiles'=4,'band'=2,'rep'=2] {'tiles'}, dimensions={0}, use_global_device_ids=true | all-gather | bytes 276480 | tf_op jit(solution)/shard_map/all_gather | solution.py:123
  21.4 0.6 %gather_fusion.2 = bf16[4,2,18,3,128]{4,2,3,1,0:T(8,128)(2,1)S(1)} fusion(bf16[2,4,18,3,128]{4,2,3,1,0:T(8,128)(2,1)S(1)} %get-tuple-element.24, s32[1024]{0:T(1024)S(1)} %pad_clamp_fusion.1), kind=kCustom, calls=%fused_computation.1.clone | custom fusion | bytes 221200 | tf_op jit(solution)/shard_map/jit(_take)/gather | solution.py:131
  22.0 0.8 %gather_fusion.1 = bf16[4,2,18,3,128]{4,1,3,2,0:T(2,128)(2,1)S(1)} fusion(bf16[2,4,18,3,128]{4,0,3,2,1:T(2,128)(2,1)S(1)} %copy.53, s32[1024]{0:T(1024)S(1)} %pad_clamp_fusion.2), kind=kCustom, calls=%fused_computation.clone | custom fusion | bytes 221200 | tf_op jit(solution)/shard_map/jit(_take)/gather | solution.py:128
  23.0 0.3 pad_maximum_fusion
  23.4 0.3 slice.264
  23.7 0.9 %pad_slice_fusion.6 = bf16[2,4,2,20,132]{4,2,3,1,0:T(2,128)(2,1)} fusion(bf16[2,4,18,22,128]{4,2,3,1,0:T(8,128)(2,1)S(1)} %pad_maximum_fusion), kind=kLoop, calls=%fused_computation.9 | loop fusion | bytes 895488 | tf_op jit(solution)/shard_map/slice | solution.py:157
  24.6 0.3 copy.51
  25.0 1.2 %fusion.31 = f32[2,4,16,128,8]{3,4,2,1,0:T(8,128)} fusion(bf16[2,4,18,22,128]{4,2,3,1,0:T(8,128)(2,1)S(1)} %pad_maximum_fusion, bf16[9,16,18]{2,1,0:T(8,128)(2,1)S(1)} %copy-done.11, s32[]{:T(128)S(6)} %select_n.114), kind=kOutput, calls=%fused_computation.75 | convolution fusion | flops 4718592 | bytes 1607684 | tf_op jit(solution)/shard_map/oi,bsirw->bsorw/dot_general | solution.py:39
  26.4 1.5 %convolution_add_fusion.9 = f32[2,4,16,128,8]{3,4,2,1,0:T(8,128)S(1)} fusion(f32[2,4,16,128,8]{3,4,2,1,0:T(8,128)} %fusion.31, bf16[2,4,16,16,128]{4,2,3,1,0:T(8,128)(2,1)S(1)} %copy.113, bf16[2,4,2,16,128]{4,2,3,1,0:T(2,128)(2,1)S(1)} %copy.52, bf16[2,4,18,3,128]{4,2,3,1,0:T(8,128)(2,1)} %copy-done.5, bf16[9,16,18]{2,1,0:T(8,128)(2,1)S(1)} %copy-done.11, ...), kind=kOutput, calls=%fused_computation.35 | convolution fusion | flops 6950912 | bytes 1751048 | tf_op jit(solution)/shard_map/oi,bsirw->bsorw/dot_general | solution.py:39
  27.9 0.3 fusion.100
  28.2 0.4 convolution_add_fusion.5
  28.6 0.4 convolution_add_fusion.23
  29.0 0.4 convolution_add_fusion.4
  29.5 0.4 convolution_add_fusion.22
  29.9 0.4 convolution_add_fusion.3
  30.3 0.3 convolution_add_fusion.21
  30.6 0.3 convolution_add_fusion.7
  31.0 0.4 convolution_add_fusion.20
  31.4 0.4 convolution_add_fusion.2
  31.8 0.4 convolution_add_fusion.19
  32.2 0.4 convolution_add_fusion.1
  32.6 0.3 convolution_add_fusion.8
  33.0 0.3 convolution_add_fusion.6
  33.3 0.3 copy-done.16
  33.7 0.5 %fusion.20 = bf16[2,4,8,20,128]{4,2,3,1,0:T(8,128)(2,1)S(1)} fusion(f32[2,4,20,128,8]{3,4,2,1,0:T(8,128)S(1)} %convolution_add_fusion.6, bf16[2,4,18,22,128]{4,2,3,1,0:T(8,128)(2,1)S(1)} %pad_maximum_fusion, f32[8]{0:T(128)S(1)} %dynamic_slice.48, bf16[2,4,16,20,128]{4,2,3,1,0:T(8,128)(2,1)S(1)} %slice.264, s32[]{:T(128)S(6)} %select_n.114, ...), kind=kOutput, calls=%fused_computation.61 | convolution fusion | flops 7208960 | bytes 2396160 | tf_op jit(solution)/shard_map/oi,bsirw->bsorw/dot_general | solution.py:39
  34.2 2.5 %all_gather.11 = bf16[2,4,16,20,128]{4,2,3,1,0:T(8,128)(2,1)S(1)} all-gather(bf16[2,4,8,20,128]{4,2,3,1,0:T(8,128)(2,1)S(1)} %fusion.20), channel_id=1, replica_groups=mesh['groups'=2,'tiles'=4,'band'=2,'rep'=2] {'rep'}, dimensions={2}, use_global_device_ids=true | all-gather | bytes 983040 | tf_op jit(solution)/shard_map/all_gather | solution.py:153
  36.7 1.1 %fusion.1 = bf16[2,4,18,20,132]{4,2,3,1,0:T(8,128)(2,1)S(1)} fusion(bf16[2,4,16,20,128]{4,2,3,1,0:T(8,128)(2,1)S(1)} %all_gather.11, bf16[2,4,2,20,132]{4,2,3,1,0:T(2,128)(2,1)S(1)} %copy-done.2), kind=kLoop, calls=%fused_computation.18 | loop fusion | flops 2280960 | bytes 1500160 | tf_op jit(solution)/shard_map/concatenate | solution.py:157
  38.1 0.4 convolution_add_fusion.17
  38.5 0.4 convolution_add_fusion.16
  39.2 0.4 convolution_add_fusion.14
  39.6 0.4 convolution_add_fusion.13
  40.3 0.4 convolution_add_fusion.11
  40.7 0.4 fusion.13
  41.1 0.4 fusion.132
  41.6 0.5 %convolution_reduce_fusion = f32[4,8,4,32]{3,2,1,0:T(4,128)S(1)} fusion(f32[4,8,4,4,128]{4,1,3,2,0:T(8,128)S(1)} %bitcast.266, s32[128]{0:T(128)S(1)} %and_select_fusion), kind=kOutput, calls=%fused_computation.62 | convolution fusion | flops 25182208 | bytes 279040 | tf_op jit(solution)/shard_map/schw,wj->schj/dot_general | solution.py:168
  42.1 0.6 %gather_fusion = f32[4,8,4,32]{3,1,2,0:T(8,128)S(1)} fusion(f32[4,8,4,32]{3,1,2,0:T(8,128)S(1)} %copy_multiply_fusion, s32[1024]{0:T(1024)S(1)} %pad_clamp_fusion), kind=kCustom, calls=%fused_computation.2 | custom fusion | bytes 32784 | tf_op jit(solution)/shard_map/jit(_take)/gather | solution.py:174
  42.7 0.3 fusion.46
  43.1 1.6 %collective-permute-start.1 = (f32[2,16,4,32]{3,1,2,0:T(8,128)S(1)}, f32[2,16,4,32]{3,1,2,0:T(8,128)S(1)}, u32[]{:S(2)}, u32[]{:S(2)}) collective-permute-start(f32[2,16,4,32]{3,1,2,0:T(8,128)S(1)} %get-tuple-element.28), channel_id=1, source_target_pairs={{0,2},{1,3},{2,0},{3,1},{4,6},{5,7},{6,4},{7,5},{8,10},{9,11},{10,... | collective-permute-start | bytes 49160 | tf_op jit(solution)/shard_map/ppermute | solution.py:70
  44.6 0.6 %collective-permute-start = (f32[2,16,4,32]{3,1,2,0:T(8,128)S(1)}, f32[2,16,4,32]{3,1,2,0:T(8,128)S(1)}, u32[]{:S(2)}, u32[]{:S(2)}) collective-permute-start(f32[2,16,4,32]{3,1,2,0:T(8,128)S(1)} %get-tuple-element.27), channel_id=1, source_target_pairs={{0,1},{1,0},{2,3},{3,2},{4,5},{5,4},{6,7},{7,6},{8,9},{9,8},{10,11... | collective-permute-start | bytes 49160 | tf_op jit(solution)/shard_map/ppermute | solution.py:70
  45.3 0.9 %copy.65 = f32[2,4,8,16,128]{4,3,2,1,0:T(8,128)} copy(f32[2,4,8,16,128]{4,2,3,1,0:T(8,128)S(1)} %get-tuple-element.36) | data formatting | bytes 1048576
  46.2 1.2 %collective-permute-done.1 = f32[2,16,4,32]{3,1,2,0:T(8,128)S(1)} collective-permute-done((f32[2,16,4,32]{3,1,2,0:T(8,128)S(1)}, f32[2,16,4,32]{3,1,2,0:T(8,128)S(1)}, u32[]{:S(2)}, u32[]{:S(2)}) %collective-permute-start.1) | collective-permute-done | bytes 16416 | tf_op jit(solution)/shard_map/ppermute | solution.py:70
  47.4 1.6 %collective-permute-done.2 = f32[2,16,4,32]{3,1,2,0:T(8,128)S(1)} collective-permute-done((f32[2,16,4,32]{3,1,2,0:T(8,128)S(1)}, f32[2,16,4,32]{3,1,2,0:T(8,128)S(1)}, u32[]{:S(2)}, u32[]{:S(2)}) %collective-permute-start.2) | collective-permute-done | bytes 16416 | tf_op jit(solution)/shard_map/ppermute | solution.py:70
  49.2 0.7 %copy.66 = f32[2,16,4,32]{3,2,1,0:T(4,128)} copy(f32[2,16,4,32]{3,1,2,0:T(8,128)S(1)} %tanh_add_fusion) | data formatting | bytes 32768
  (60 shorter events, 1.9 us)
Async XLA Ops:
  0.6 27.2 %copy-start = (bf16[9,16,18]{2,1,0:T(8,128)(2,1)S(1)}, bf16[9,16,18]{2,1,0:T(8,128)(2,1)}, u32[]{:S(2)}) copy-start(bf16[9,16,18]{2,1,0:T(8,128)(2,1)} %param.25) | copy-start | bytes 15556
  22.9 0.8 %copy-start.3 = (bf16[2,4,18,3,128]{4,2,3,1,0:T(8,128)(2,1)}, bf16[2,4,18,3,128]{4,2,3,1,0:T(8,128)(2,1)S(1)}, u32[]{:S(2)}) copy-start(bf16[2,4,18,3,128]{4,2,3,1,0:T(8,128)(2,1)S(1)} %copy_select_fusion) | copy-start | bytes 331780
  23.0 1.6 %copy-start.5 = (bf16[2,4,18,3,128]{4,2,3,1,0:T(8,128)(2,1)}, bf16[2,4,18,3,128]{4,2,3,1,0:T(8,128)(2,1)S(1)}, u32[]{:S(2)}) copy-start(bf16[2,4,18,3,128]{4,2,3,1,0:T(8,128)(2,1)S(1)} %bitcast_select_fusion) | copy-start | bytes 331780
  23.0 1.6 %copy-start.1 = (f32[2,4,16,16,128]{4,3,2,1,0:T(8,128)S(1)}, f32[2,4,16,16,128]{4,3,2,1,0:T(8,128)}, u32[]{:S(2)}) copy-start(f32[2,4,16,16,128]{4,3,2,1,0:T(8,128)} %param.18) | copy-start | bytes 3145732
  23.7 1.3 %copy-start.13 = (s32[1,4]{1,0:T(1,128)S(1)}, s32[1,4]{1,0:T(1,128)}, u32[]{:S(2)}) copy-start(s32[1,4]{1,0:T(1,128)} %param.21) | copy-start | bytes 52
  23.7 1.3 %copy-start.11 = (bf16[9,16,18]{2,1,0:T(8,128)(2,1)S(1)}, bf16[9,16,18]{2,1,0:T(8,128)(2,1)}, u32[]{:S(2)}) copy-start(bf16[9,16,18]{2,1,0:T(8,128)(2,1)} %param.23) | copy-start | bytes 15556
  24.6 1.6 %copy-start.14 = (f32[16]{0:T(128)S(1)}, f32[16]{0:T(128)}, u32[]{:S(2)}) copy-start(f32[16]{0:T(128)} %param.24) | copy-start | bytes 196
  24.6 1.7 %copy-start.15 = (f32[16]{0:T(128)S(1)}, f32[16]{0:T(128)}, u32[]{:S(2)}) copy-start(f32[16]{0:T(128)} %param.28) | copy-start | bytes 196
  26.3 1.5 %copy-start.4 = (bf16[2,4,18,3,128]{4,2,3,1,0:T(8,128)(2,1)S(1)}, bf16[2,4,18,3,128]{4,2,3,1,0:T(8,128)(2,1)}, u32[]{:S(2)}) copy-start(bf16[2,4,18,3,128]{4,2,3,1,0:T(8,128)(2,1)} %copy-done.3) | copy-start | bytes 331780
  26.3 1.5 %copy-start.6 = (bf16[2,4,18,3,128]{4,2,3,1,0:T(8,128)(2,1)S(1)}, bf16[2,4,18,3,128]{4,2,3,1,0:T(8,128)(2,1)}, u32[]{:S(2)}) copy-start(bf16[2,4,18,3,128]{4,2,3,1,0:T(8,128)(2,1)} %copy-done.5) | copy-start | bytes 331780
  33.0 0.7 %copy-start.16 = (f32[16]{0:T(128)S(1)}, f32[16]{0:T(128)}, u32[]{:S(2)}) copy-start(f32[16]{0:T(128)} %param.26) | copy-start | bytes 196
  33.7 3.0 %copy-start.2 = (bf16[2,4,2,20,132]{4,2,3,1,0:T(2,128)(2,1)S(1)}, bf16[2,4,2,20,132]{4,2,3,1,0:T(2,128)(2,1)}, u32[]{:S(2)}) copy-start(bf16[2,4,2,20,132]{4,2,3,1,0:T(2,128)(2,1)} %pad_slice_fusion.6) | copy-start | bytes 253444
  34.2 3.7 %copy-start.8 = (bf16[9,16,18]{2,1,0:T(8,128)(2,1)S(1)}, bf16[9,16,18]{2,1,0:T(8,128)(2,1)}, u32[]{:S(2)}) copy-start(bf16[9,16,18]{2,1,0:T(8,128)(2,1)} %param.27) | copy-start | bytes 15556
  41.1 1.6 %copy-start.9 = (f32[16,16]{1,0:T(8,128)S(1)}, f32[16,16]{1,0:T(8,128)}, u32[]{:S(2)}) copy-start(f32[16,16]{1,0:T(8,128)} %param.29) | copy-start | bytes 3076
  41.1 7.9 %copy-start.7 = (f32[2,16,4,32]{3,2,1,0:T(4,128)S(1)}, f32[2,16,4,32]{3,2,1,0:T(4,128)}, u32[]{:S(2)}) copy-start(f32[2,16,4,32]{3,2,1,0:T(4,128)} %param.22) | copy-start | bytes 49156
  41.1 7.9 %copy-start.10 = (f32[16,16]{1,0:T(8,128)S(1)}, f32[16,16]{1,0:T(8,128)}, u32[]{:S(2)}) copy-start(f32[16,16]{1,0:T(8,128)} %param.30) | copy-start | bytes 3076
  41.1 7.9 %copy-start.12 = (f32[16]{0:T(128)S(1)}, f32[16]{0:T(128)}, u32[]{:S(2)}) copy-start(f32[16]{0:T(128)} %param.31) | copy-start | bytes 196
  43.1 4.3 %collective-permute-start.1 = (f32[2,16,4,32]{3,1,2,0:T(8,128)S(1)}, f32[2,16,4,32]{3,1,2,0:T(8,128)S(1)}, u32[]{:S(2)}, u32[]{:S(2)}) collective-permute-start(f32[2,16,4,32]{3,1,2,0:T(8,128)S(1)} %get-tuple-element.28), channel_id=1, source_target_pairs={{0,2},{1,3},{2,0},{3,1},{4,6},{5,7},{6,4},{7,5},{8,10},{9,11},{10,... | collective-permute-start | bytes 49160 | tf_op jit(solution)/shard_map/ppermute | solution.py:70
  44.6 4.3 %collective-permute-start.2 = (f32[2,16,4,32]{3,1,2,0:T(8,128)S(1)}, f32[2,16,4,32]{3,1,2,0:T(8,128)S(1)}, u32[]{:S(2)}, u32[]{:S(2)}) collective-permute-start(f32[2,16,4,32]{3,1,2,0:T(8,128)S(1)} %get-tuple-element.28), channel_id=1, source_target_pairs={{0,3},{1,2},{2,1},{3,0},{4,7},{5,6},{6,5},{7,4},{8,11},{9,10},{10,... | collective-permute-start | bytes 49160 | tf_op jit(solution)/shard_map/ppermute | solution.py:70
  44.6 4.3 %collective-permute-start = (f32[2,16,4,32]{3,1,2,0:T(8,128)S(1)}, f32[2,16,4,32]{3,1,2,0:T(8,128)S(1)}, u32[]{:S(2)}, u32[]{:S(2)}) collective-permute-start(f32[2,16,4,32]{3,1,2,0:T(8,128)S(1)} %get-tuple-element.27), channel_id=1, source_target_pairs={{0,1},{1,0},{2,3},{3,2},{4,5},{5,4},{6,7},{7,6},{8,9},{9,8},{10,11... | collective-permute-start | bytes 49160 | tf_op jit(solution)/shard_map/ppermute | solution.py:70

commit v5 on v2

--- a/solution.py
+++ b/solution.py
@@ -44,6 +44,20 @@
             )
             total = term if total is None else total + term
     return total
+
+
+def conv(images, filter_weight, dilation_rate):
+    taps, outs, ins = filter_weight.shape
+    kernel = filter_weight.reshape(3, 3, outs, ins).transpose(2, 3, 0, 1)
+    return lax.conv_general_dilated(
+        images,
+        kernel,
+        window_strides=(1, 1),
+        padding="VALID",
+        rhs_dilation=(dilation_rate, dilation_rate),
+        dimension_numbers=("NCHW", "OIHW", "NCHW"),
+        preferred_element_type=jnp.float32,
+    )
 
 
 def choose_rows(block, select):
@@ -138,22 +152,24 @@
     )
     full = jnp.concatenate([top, joined, bottom], axis=3)
     first = jnp.pad(full, ((0, 0), (0, 0), (0, 0), (0, 0), (2, 2)))
-    update = jax.nn.sigmoid(
-        apply_filter(first, own_out(w_update), 1, 3, row_count, column_count) + own_bias(b_update)
-    )
-    hidden_wide = first[:, :, inputs_count:, 1 : row_count + 5, 2 : column_count + 2]
-    reset_half = jax.nn.sigmoid(
-        apply_filter(first, own_out(w_reset), 1, 1, row_count + 4, column_count) + own_bias(b_reset)
-    )
-    wide_half = lax.dynamic_slice_in_dim(hidden_wide, start, half, 2)
-    gated = lax.all_gather(
-        (reset_half * wide_half.astype(jnp.float32)).astype(jnp.bfloat16), "rep", axis=2, tiled=True
-    )
-    gated_pad = jnp.pad(gated, ((0, 0), (0, 0), (0, 0), (0, 0), (2, 2)))
-    second = jnp.concatenate([first[:, :, :inputs_count, 1 : row_count + 5, :], gated_pad], axis=2)
-    candidate = jnp.tanh(
-        apply_filter(second, own_out(w_cand), 2, 2, row_count, column_count) + own_bias(b_cand)
-    )
+    band_local = first.shape[0]
+    images = band_local * slots
+    flat = first.reshape((images,) + first.shape[2:])
+    gates = conv(
+        flat[:, :, :, 1 : column_count + 3],
+        jnp.concatenate([own_out(w_update), w_reset], axis=1),
+        1,
+    )
+    gate_bias = jnp.concatenate([own_bias(b_update), b_reset[:, None, None]], axis=0)
+    gates = jax.nn.sigmoid(gates + gate_bias)
+    update = gates[:, :half, 2 : row_count + 2].reshape((band_local, slots, half, row_count, column_count))
+    reset = gates[:, half:]
+    hidden_wide = flat[:, inputs_count:, 1 : row_count + 5, 2 : column_count + 2]
+    gated = (reset * hidden_wide.astype(jnp.float32)).astype(jnp.bfloat16)
+    gated_pad = jnp.pad(gated, ((0, 0), (0, 0), (0, 0), (2, 2)))
+    second = jnp.concatenate([flat[:, :inputs_count, 1 : row_count + 5, :], gated_pad], axis=1)
+    candidate = jnp.tanh(conv(second, own_out(w_cand), 2) + own_bias(b_cand))
+    candidate = candidate.reshape((band_local, slots, half, row_count, column_count))
     state_half = lax.dynamic_slice_in_dim(state, start, half, 2)
     live_scale = alive.astype(jnp.float32)[None, :, None, None, None]
     new_half = ((1.0 - update) * state_half + update * candidate) * live_scale

time: 38.9 us -> 102 us (2.62)
  local copies, waits for them, and re-layouts: 7.18 us -> 37.3 us
  other arithmetic: 4.15 us -> 27.8 us
  matrix products: 11.4 us -> 22.7 us
  blocking collectives: 2.49 us -> 0 us
    conv_general_dilated x0 -> x2, matrix products: none -> 21.7 us  [conv(): lax.conv_general_dilated(images, kernel, window_strides=(1, 1), padding='...]
    convert_element_type x1, other arithmetic: 0.67 us -> 11.9 us  [shards(): gated = (reset * hidden_wide.astype(jnp.float32)).astype(jnp.bfloat16)]
    dot_general x27 -> x0, matrix products: 10.3 us -> none  [apply_filter(): jnp.einsum('oi,bsirw->bsorw', filter_weight[(left_operand + 1) * 3 + (rig...]
    unnamed x29 -> x20, local copies, waits for them, and re-layouts: 4.41 us -> 14.1 us
    sub x0 -> x1, other arithmetic: none -> 8.56 us  [shards(): new_half = ((1.0 - update) * state_half + update * candidate) * live_scale]
    pad x0 -> x1, local copies, waits for them, and re-layouts: none -> 5.64 us  [shards(): first = jnp.pad(full, ((0, 0), (0, 0), (0, 0), (0, 0), (2, 2)))]
    mul x0 -> x1, local copies, waits for them, and re-layouts: none -> 5.21 us  [shards(): new_half = ((1.0 - update) * state_half + update * candidate) * live_scale]
    sub x0 -> x1, local copies, waits for them, and re-layouts: none -> 5.16 us  [shards(): new_half = ((1.0 - update) * state_half + update * candidate) * live_scale]
  transfers between devices with their start and end apart: 5 -> 5, of which waited for: 2 -> 2; matrix products, arithmetic and copies ran while one was open for 8% -> 6% of each run, Pallas kernels for 0% -> 0%
where the time goes in v5:
time: 102 us; the launch traced here: 101 us
  local copies, waits for them, and re-layouts  37.3 us (37%)
  other arithmetic  27.8 us (27%)
  matrix products  22.7 us (22%)
  starting transfers between devices  9.08 us (9%)
  waiting for transfers between devices  3.53 us (3%)
    conv_general_dilated x2, matrix products, conv(): lax.conv_general_dilated(images, kernel, window_strides=(1, 1), padding='...  21.7 us
    unnamed x20, local copies, waits for them, and re-layouts  14.1 us
    convert_element_type x1, other arithmetic, shards(): gated = (reset * hidden_wide.astype(jnp.float32)).astype(jnp.bfloat16)  11.9 us
    sub x1, other arithmetic, shards(): new_half = ((1.0 - update) * state_half + update * candidate) * live_scale  8.56 us
    pad x1, local copies, waits for them, and re-layouts, shards(): first = jnp.pad(full, ((0, 0), (0, 0), (0, 0), (0, 0), (2, 2)))  5.64 us
    ppermute x1, starting transfers between devices, padded(): lax.ppermute(lax.slice_in_dim(block, block.shape[dim] - width, None, axis...  5.59 us
    mul x1, local copies, waits for them, and re-layouts, shards(): new_half = ((1.0 - update) * state_half + update * candidate) * live_scale  5.21 us
    sub x1, local copies, waits for them, and re-layouts, shards(): new_half = ((1.0 - update) * state_half + update * candidate) * live_scale  5.16 us
  transfers between devices with their start and end apart: 5, of which 2 were waited for; matrix products, arithmetic and copies ran while one was open for 6% of the time, Pallas kernels for 0%

profile of v5, /device:TPU:0, one launch (start us, length us, event | category | flops | bytes accessed | tf_op | source)
XLA Modules:
  0.0 101.3 jit_solution(9380419292937625421)
XLA Ops:
  0.6 0.0 copy-start
  0.7 0.7 not_and_fusion
  1.4 0.8 compare_and_fusion.1
  2.1 0.7 not_and_fusion.1
  2.8 2.0 %copy.81 = bf16[2,4,16,16,128]{4,0,3,2,1:T(2,128)(2,1)S(1)} copy(f32[2,4,16,16,128]{4,3,2,1,0:T(8,128)} %param.18) | data formatting | bytes 1572864 | tf_op args[1]
  4.8 0.9 copy.60
  5.7 0.4 fusion.11
  6.2 1.3 %collective-permute-start.1 = (bf16[2,18,3,128]{3,0,2,1:T(2,128)(2,1)S(1)}, bf16[2,18,3,128]{3,0,2,1:T(2,128)(2,1)S(1)}, u32[]{:S(2)}, u32[]{:S(2)}) collective-permute-start(bf16[2,18,3,128]{3,0,2,1:T(2,128)(2,1)S(1)} %get-tuple-element.27), channel_id=1, source_target_pairs={{4,0},{8,4},{12,8},{5,1},{9,5},{13,9},{6,2},{10,6},{14,10},{7,3},{... | collective-permute-start | bytes 82952 | tf_op jit(solution)/shard_map/ppermute | solution.py:15
  7.5 5.6 %collective-permute-start = (bf16[2,18,3,128]{3,0,2,1:T(2,128)(2,1)S(1)}, bf16[2,18,3,128]{3,0,2,1:T(2,128)(2,1)S(1)}, u32[]{:S(2)}, u32[]{:S(2)}) collective-permute-start(bf16[2,18,3,128]{3,0,2,1:T(2,128)(2,1)S(1)} %get-tuple-element.15), channel_id=1, source_target_pairs={{0,4},{4,8},{8,12},{1,5},{5,9},{9,13},{2,6},{6,10},{10,14},{3,7},{... | collective-permute-start | bytes 82952 | tf_op jit(solution)/shard_map/ppermute | solution.py:12
  13.1 0.7 fusion.27
  13.7 0.7 dynamic-slice_bitcast_fusion.2
  14.5 0.7 constant_dynamic-slice_fusion
  15.2 0.8 pad_maximum_fusion.3
  16.0 0.7 maximum_bitcast_fusion
  16.7 0.7 dynamic_slice.30
  17.5 0.8 gather_fusion.2
  18.2 0.8 gather_fusion.1
  19.0 0.0 collective-permute-done.1
  19.0 0.2 broadcast_select_fusion
  19.2 0.0 collective-permute-done
  19.3 0.2 broadcast_select_fusion.1
  19.4 1.3 %pad_maximum_fusion = bf16[2,4,18,22,128]{4,0,3,2,1:T(2,128)(2,1)S(1)} fusion(bf16[2,4,18,3,128]{4,0,3,2,1:T(2,128)(2,1)S(1)} %broadcast_select_fusion, bf16[2,4,16,16,128]{4,0,3,2,1:T(2,128)(2,1)S(1)} %copy.81, bf16[2,4,2,16,128]{4,0,3,2,1:T(2,128)(2,1)S(1)} %copy.60, bf16[2,4,18,3,128]{4,0,3,2,1:T(2,128)(2,1)S(1)} %broadcast_select_fusion.1), kind=kLoop, calls=%fused_computation.19 | loop fusion | flops 1216512 | bytes 1622016 | tf_op jit(solution)/shard_map/concatenate | solution.py:153
  20.8 6.9 %copy.73 = bf16[2,4,18,22,128]{2,1,0,4,3:T(4,128)(2,1)} copy(bf16[2,4,18,22,128]{4,0,3,2,1:T(2,128)(2,1)S(1)} %pad_maximum_fusion) | data formatting | bytes 1622016
  27.7 5.6 %pad.8.clone = bf16[2,4,18,22,132]{2,1,0,4,3:T(4,128)(2,1)S(1)} pad(bf16[2,4,18,22,128]{2,1,0,4,3:T(4,128)(2,1)} %copy.73, bf16[]{:T(256)} %constant.82.clone.1), padding=0_0x0_0x0_0x0_0x2_2 | pad | bytes 1647362 | tf_op jit(solution)/shard_map/jit(_pad)/pad | solution.py:154
  33.3 2.9 %slice.42 = bf16[8,2,20,132]{1,0,3,2:T(8,128)(2,1)} slice(bf16[8,18,22,132]{1,0,3,2:T(8,128)(2,1)S(1)} %bitcast.65), slice={[0:8], [0:2], [1:21], [0:132]} | slice | bytes 168960 | tf_op jit(solution)/shard_map/slice | solution.py:170
  36.2 1.2 %copy-done.1 = bf16[2,4,18,22,132]{2,1,0,4,3:T(4,128)(2,1)} copy-done((bf16[2,4,18,22,132]{2,1,0,4,3:T(4,128)(2,1)}, bf16[2,4,18,22,132]{2,1,0,4,3:T(4,128)(2,1)S(1)}, u32[]{:S(2)}) %copy-start.1) | copy-done | bytes 836376
  37.4 9.5 %add_divide_fusion = f32[8,24,20,128]{1,0,3,2:T(8,128)} fusion(f32[24]{0:T(128)S(1)} %maximum_bitcast_fusion, bf16[8,18,22,132]{1,0,3,2:T(8,128)(2,1)S(1)} %bitcast.66, bf16[3,3,24,18]{3,2,1,0:T(8,128)(2,1)S(1)} %bitcast.71), kind=kOutput, calls=%fused_computation.7 | convolution fusion | flops 161218560 | bytes 2810304 | tf_op jit(solution)/shard_map/conv_general_dilated | solution.py:52
  46.9 11.9 %fusion.1 = bf16[8,16,20,128]{1,0,3,2:T(8,128)(2,1)} fusion(f32[8,24,20,128]{1,0,3,2:T(8,128)} %add_divide_fusion, bf16[8,18,22,132]{1,0,3,2:T(8,128)(2,1)} %bitcast.67), kind=kLoop, calls=%fused_computation.6 | loop fusion | flops 983040 | bytes 2621440 | tf_op jit(solution)/shard_map/convert_element_type | solution.py:168
  58.8 8.6 %slice_subtract_fusion = f32[8,8,16,128]{1,0,3,2:T(8,128)} fusion(f32[8,24,20,128]{1,0,3,2:T(8,128)} %add_divide_fusion), kind=kLoop, calls=%fused_computation.9 | loop fusion | flops 131072 | bytes 1048576 | tf_op jit(solution)/shard_map/sub | solution.py:175
  67.3 0.4 copy-done.2
  67.7 2.0 %copy-done.3 = bf16[8,2,20,132]{1,0,3,2:T(8,128)(2,1)S(1)} copy-done((bf16[8,2,20,132]{1,0,3,2:T(8,128)(2,1)S(1)}, bf16[8,2,20,132]{1,0,3,2:T(8,128)(2,1)}, u32[]{:S(2)}) %copy-start.3) | copy-done | bytes 84504
  69.7 12.2 %tanh_multiply_fusion = f32[8,8,16,128]{1,0,3,2:T(8,128)} fusion(f32[8,24,20,128]{1,0,3,2:T(8,128)S(1)} %copy-done.2, f32[8]{0:T(128)S(1)} %dynamic_slice.30, bf16[3,3,8,18]{3,2,1,0:T(8,128)(2,1)S(1)} %bitcast.72, bf16[8,16,20,128]{1,0,3,2:T(8,128)(2,1)} %fusion.1, bf16[8,2,20,132]{1,0,3,2:T(8,128)(2,1)S(1)} %copy-done.3), kind=kOutput, calls=%fused_computation.8 | convolution fusion | flops 45010432 | bytes 1791040 | tf_op jit(solution)/shard_map/conv_general_dilated | solution.py:52
  81.9 5.2 %copy.63 = f32[2,4,8,16,128]{4,3,2,1,0:T(8,128)S(1)} copy(f32[2,4,8,16,128]{2,1,0,4,3:T(4,128)} %bitcast.69) | data formatting | bytes 1048576 | tf_op jit(solution)/shard_map/mul | solution.py:175
  87.1 0.0 copy-start.6
  87.1 0.0 copy-start.7
  87.1 5.2 %copy.62 = f32[2,4,8,16,128]{4,3,2,1,0:T(8,128)S(1)} copy(f32[2,4,8,16,128]{2,1,0,4,3:T(4,128)} %bitcast.68) | data formatting | bytes 1048576 | tf_op jit(solution)/shard_map/sub | solution.py:175
  92.3 1.0 fusion.33
  93.3 0.5 convolution_reduce_fusion
  93.8 0.6 gather_fusion
  94.3 0.3 fusion.13
  94.7 2.0 %collective-permute-start.3 = (f32[2,16,4,32]{3,1,2,0:T(8,128)S(1)}, f32[2,16,4,32]{3,1,2,0:T(8,128)S(1)}, u32[]{:S(2)}, u32[]{:S(2)}) collective-permute-start(f32[2,16,4,32]{3,1,2,0:T(8,128)S(1)} %get-tuple-element.30), channel_id=1, source_target_pairs={{0,2},{1,3},{2,0},{3,1},{4,6},{5,7},{6,4},{7,5},{8,10},{9,11},{10,... | collective-permute-start | bytes 49160 | tf_op jit(solution)/shard_map/ppermute | solution.py:84
  96.7 0.0 collective-permute-start.4
  96.7 0.2 collective-permute-start.2
  96.9 2.1 %collective-permute-done.3 = f32[2,16,4,32]{3,1,2,0:T(8,128)S(1)} collective-permute-done((f32[2,16,4,32]{3,1,2,0:T(8,128)S(1)}, f32[2,16,4,32]{3,1,2,0:T(8,128)S(1)}, u32[]{:S(2)}, u32[]{:S(2)}) %collective-permute-start.3) | collective-permute-done | bytes 16416 | tf_op jit(solution)/shard_map/ppermute | solution.py:84
  99.0 1.4 %collective-permute-done.4 = f32[2,16,4,32]{3,1,2,0:T(8,128)S(1)} collective-permute-done((f32[2,16,4,32]{3,1,2,0:T(8,128)S(1)}, f32[2,16,4,32]{3,1,2,0:T(8,128)S(1)}, u32[]{:S(2)}, u32[]{:S(2)}) %collective-permute-start.4) | collective-permute-done | bytes 16416 | tf_op jit(solution)/shard_map/ppermute | solution.py:84
  100.4 0.0 collective-permute-done.2
  100.4 0.2 tanh_add_fusion
  100.7 0.7 copy.68
  (16 shorter events, 0.1 us)
Async XLA Ops:
  0.6 93.7 %copy-start = (f32[16,16]{1,0:T(8,128)S(1)}, f32[16,16]{1,0:T(8,128)}, u32[]{:S(2)}) copy-start(f32[16,16]{1,0:T(8,128)} %param.29) | copy-start | bytes 3076
  6.2 12.9 %collective-permute-start.1 = (bf16[2,18,3,128]{3,0,2,1:T(2,128)(2,1)S(1)}, bf16[2,18,3,128]{3,0,2,1:T(2,128)(2,1)S(1)}, u32[]{:S(2)}, u32[]{:S(2)}) collective-permute-start(bf16[2,18,3,128]{3,0,2,1:T(2,128)(2,1)S(1)} %get-tuple-element.27), channel_id=1, source_target_pairs={{4,0},{8,4},{12,8},{5,1},{9,5},{13,9},{6,2},{10,6},{14,10},{7,3},{... | collective-permute-start | bytes 82952 | tf_op jit(solution)/shard_map/ppermute | solution.py:15
  7.5 11.8 %collective-permute-start = (bf16[2,18,3,128]{3,0,2,1:T(2,128)(2,1)S(1)}, bf16[2,18,3,128]{3,0,2,1:T(2,128)(2,1)S(1)}, u32[]{:S(2)}, u32[]{:S(2)}) collective-permute-start(bf16[2,18,3,128]{3,0,2,1:T(2,128)(2,1)S(1)} %get-tuple-element.15), channel_id=1, source_target_pairs={{0,4},{4,8},{8,12},{1,5},{5,9},{9,13},{2,6},{6,10},{10,14},{3,7},{... | collective-permute-start | bytes 82952 | tf_op jit(solution)/shard_map/ppermute | solution.py:12
  33.3 4.1 %copy-start.1 = (bf16[2,4,18,22,132]{2,1,0,4,3:T(4,128)(2,1)}, bf16[2,4,18,22,132]{2,1,0,4,3:T(4,128)(2,1)S(1)}, u32[]{:S(2)}) copy-start(bf16[2,4,18,22,132]{2,1,0,4,3:T(4,128)(2,1)S(1)} %pad.8.clone) | copy-start | bytes 2509060
  58.8 9.0 %copy-start.2 = (f32[8,24,20,128]{1,0,3,2:T(8,128)S(1)}, f32[8,24,20,128]{1,0,3,2:T(8,128)}, u32[]{:S(2)}) copy-start(f32[8,24,20,128]{1,0,3,2:T(8,128)} %add_divide_fusion) | copy-start | bytes 5898244
  58.8 10.9 %copy-start.3 = (bf16[8,2,20,132]{1,0,3,2:T(8,128)(2,1)S(1)}, bf16[8,2,20,132]{1,0,3,2:T(8,128)(2,1)}, u32[]{:S(2)}) copy-start(bf16[8,2,20,132]{1,0,3,2:T(8,128)(2,1)} %slice.42) | copy-start | bytes 253444
  81.9 10.4 %copy-start.4 = (f32[2,4,16,16,128]{4,3,2,1,0:T(8,128)S(1)}, f32[2,4,16,16,128]{4,3,2,1,0:T(8,128)}, u32[]{:S(2)}) copy-start(f32[2,4,16,16,128]{4,3,2,1,0:T(8,128)} %param.18) | copy-start | bytes 3145732
  87.1 13.3 %copy-start.5 = (f32[2,16,4,32]{3,2,1,0:T(4,128)S(1)}, f32[2,16,4,32]{3,2,1,0:T(4,128)}, u32[]{:S(2)}) copy-start(f32[2,16,4,32]{3,2,1,0:T(4,128)} %param.22) | copy-start | bytes 49156
  87.1 13.3 %copy-start.6 = (f32[16,16]{1,0:T(8,128)S(1)}, f32[16,16]{1,0:T(8,128)}, u32[]{:S(2)}) copy-start(f32[16,16]{1,0:T(8,128)} %param.30) | copy-start | bytes 3076
  87.1 13.3 %copy-start.7 = (f32[16]{0:T(128)S(1)}, f32[16]{0:T(128)}, u32[]{:S(2)}) copy-start(f32[16]{0:T(128)} %param.31) | copy-start | bytes 196
  94.7 4.3 %collective-permute-start.3 = (f32[2,16,4,32]{3,1,2,0:T(8,128)S(1)}, f32[2,16,4,32]{3,1,2,0:T(8,128)S(1)}, u32[]{:S(2)}, u32[]{:S(2)}) collective-permute-start(f32[2,16,4,32]{3,1,2,0:T(8,128)S(1)} %get-tuple-element.30), channel_id=1, source_target_pairs={{0,2},{1,3},{2,0},{3,1},{4,6},{5,7},{6,4},{7,5},{8,10},{9,11},{10,... | collective-permute-start | bytes 49160 | tf_op jit(solution)/shard_map/ppermute | solution.py:84
  96.7 3.7 %collective-permute-start.4 = (f32[2,16,4,32]{3,1,2,0:T(8,128)S(1)}, f32[2,16,4,32]{3,1,2,0:T(8,128)S(1)}, u32[]{:S(2)}, u32[]{:S(2)}) collective-permute-start(f32[2,16,4,32]{3,1,2,0:T(8,128)S(1)} %get-tuple-element.30), channel_id=1, source_target_pairs={{0,3},{1,2},{2,1},{3,0},{4,7},{5,6},{6,5},{7,4},{8,11},{9,10},{10,... | collective-permute-start | bytes 49160 | tf_op jit(solution)/shard_map/ppermute | solution.py:84
  96.7 3.7 %collective-permute-start.2 = (f32[2,16,4,32]{3,1,2,0:T(8,128)S(1)}, f32[2,16,4,32]{3,1,2,0:T(8,128)S(1)}, u32[]{:S(2)}, u32[]{:S(2)}) collective-permute-start(f32[2,16,4,32]{3,1,2,0:T(8,128)S(1)} %get-tuple-element.29), channel_id=1, source_target_pairs={{0,1},{1,0},{2,3},{3,2},{4,5},{5,4},{6,7},{7,6},{8,9},{9,8},{10,11... | collective-permute-start | bytes 49160 | tf_op jit(solution)/shard_map/ppermute | solution.py:84

commit v6 on v2

--- a/solution.py
+++ b/solution.py
@@ -142,13 +142,10 @@
         apply_filter(first, own_out(w_update), 1, 3, row_count, column_count) + own_bias(b_update)
     )
     hidden_wide = first[:, :, inputs_count:, 1 : row_count + 5, 2 : column_count + 2]
-    reset_half = jax.nn.sigmoid(
-        apply_filter(first, own_out(w_reset), 1, 1, row_count + 4, column_count) + own_bias(b_reset)
-    )
-    wide_half = lax.dynamic_slice_in_dim(hidden_wide, start, half, 2)
-    gated = lax.all_gather(
-        (reset_half * wide_half.astype(jnp.float32)).astype(jnp.bfloat16), "rep", axis=2, tiled=True
-    )
+    reset = jax.nn.sigmoid(
+        apply_filter(first, w_reset, 1, 1, row_count + 4, column_count) + b_reset[:, None, None]
+    )
+    gated = (reset * hidden_wide.astype(jnp.float32)).astype(jnp.bfloat16)
     gated_pad = jnp.pad(gated, ((0, 0), (0, 0), (0, 0), (0, 0), (2, 2)))
     second = jnp.concatenate([first[:, :, :inputs_count, 1 : row_count + 5, :], gated_pad], axis=2)
     candidate = jnp.tanh(

time: 38.9 us -> 37.3 us (0.959)
  blocking collectives: 2.49 us -> 0 us
  waiting for transfers between devices: 3.26 us -> 5.25 us
  starting transfers between devices: 9.09 us -> 8.17 us
  local copies, waits for them, and re-layouts: 7.18 us -> 6.48 us
  matrix products: 11.4 us -> 11.9 us
    all_gather x1 -> x0, blocking collectives: 2.49 us -> none  [shards(): lax.all_gather((reset_half * wide_half.astype(jnp.float32)).astype(jnp.bf...]
    ppermute x1, waiting for transfers between devices: 0.01 us -> 2.36 us  [padded(): lax.ppermute(lax.slice_in_dim(block, 0, width, axis=dim), axis, backward)]
    ppermute x1, starting transfers between devices: 5.59 us -> 4.96 us  [padded(): lax.ppermute(lax.slice_in_dim(block, block.shape[dim] - width, None, axis...]
    dot_general x27, matrix products: 10.3 us -> 10.8 us  [apply_filter(): jnp.einsum('oi,bsirw->bsorw', filter_weight[(left_operand + 1) * 3 + (rig...]
    unnamed x29 -> x31, local copies, waits for them, and re-layouts: 4.41 us -> 4.09 us
  transfers between devices with their start and end apart: 5 -> 5, of which waited for: 2 -> 3; matrix products, arithmetic and copies ran while one was open for 8% -> 8% of each run, Pallas kernels for 0% -> 0%
where the time goes in v6:
time: 37.3 us; the launch traced here: 36.9 us
  matrix products  11.9 us (32%)
  starting transfers between devices  8.17 us (22%)
  local copies, waits for them, and re-layouts  6.48 us (17%)
  waiting for transfers between devices  5.25 us (14%)
  other arithmetic  4.09 us (11%)
  between operations  1.09 us (3%)
    dot_general x27, matrix products, apply_filter(): jnp.einsum('oi,bsirw->bsorw', filter_weight[(left_operand + 1) * 3 + (rig...  10.8 us
    ppermute x1, starting transfers between devices, padded(): lax.ppermute(lax.slice_in_dim(block, block.shape[dim] - width, None, axis...  4.96 us
    unnamed x31, local copies, waits for them, and re-layouts  4.09 us
    ppermute x3, waiting for transfers between devices, exchange_sum(): chunk = lax.ppermute(chunk, ('band', 'rep'), perm)  2.89 us
    ppermute x1, waiting for transfers between devices, padded(): lax.ppermute(lax.slice_in_dim(block, 0, width, axis=dim), axis, backward)  2.36 us
    ppermute x3, starting transfers between devices, exchange_sum(): chunk = lax.ppermute(chunk, ('band', 'rep'), perm)  1.92 us
    ppermute x1, starting transfers between devices, padded(): lax.ppermute(lax.slice_in_dim(block, 0, width, axis=dim), axis, backward)  1.29 us
    concatenate x1, other arithmetic, shards(): jnp.concatenate([first[:, :, :inputs_count, 1:row_count + 5, :], gated_pa...  1.14 us
  transfers between devices with their start and end apart: 5, of which 3 were waited for; matrix products, arithmetic and copies ran while one was open for 8% of the time, Pallas kernels for 0%

profile of v6, /device:TPU:0, one launch (start us, length us, event | category | flops | bytes accessed | tf_op | source)
XLA Modules:
  0.0 36.9 jit_solution(14747710783227797482)
XLA Ops:
  0.7 0.7 %not_and_fusion = (pred[4]{0:T(512)(128)(4,1)S(1)}, pred[4]{0:T(512)(128)(4,1)S(1)}) fusion(s32[4]{0:T(128)} %param.19, s32[]{:T(128)S(6)} %add.217, s32[]{:T(128)S(6)} %mul.31, s32[4,2]{0,1:T(2,128)} %param.20), kind=kLoop, calls=%fused_computation.187 | loop fusion | flops 24 | bytes 48 | tf_op jit(solution)/shard_map/and | solution.py:109
  1.4 0.8 %compare_and_fusion.1 = (pred[4]{0:T(512)(128)(4,1)S(1)}, s32[4]{0:T(128)S(1)}, pred[4]{0:T(512)(128)(4,1)S(1)}, pred[4]{0:T(512)(128)(4,1)S(1)}, s32[4]{0:T(128...) fusion(s32[]{:T(128)S(6)} %mul.31, s32[4,2]{0,1:T(2,128)} %param.20, ...), kind=kLoop, calls=%fused_computation.182 | loop fusion | flops 124 | bytes 116 | tf_op jit(solution)/shard_map/jit(_take)/and | solution.py:124
  2.2 0.7 %fusion.120 = (f32[4]{0:T(128)S(1)}, pred[4]{0:T(512)(128)(4,1)S(1)}) fusion(s32[4]{0:T(128)} %param.19, pred[4]{0:T(512)(128)(4,1)S(1)} %get-tuple-element.31), kind=kLoop, calls=%fused_computation.194 | loop fusion | flops 16 | bytes 40 | tf_op jit(solution)/shard_map/convert_element_type | solution.py:155
  2.8 1.7 %copy.106 = bf16[2,4,16,16,128]{4,2,3,1,0:T(8,128)(2,1)S(1)} copy(f32[2,4,16,16,128]{4,3,2,1,0:T(8,128)} %param.18) | data formatting | bytes 1572864 | tf_op args[1]
  4.8 5.0 %collective-permute-start = (bf16[2,18,3,128]{3,1,2,0:T(8,128)(2,1)S(1)}, bf16[2,18,3,128]{3,1,2,0:T(8,128)(2,1)S(1)}, u32[]{:S(2)}, u32[]{:S(2)}) collective-permute-start(bf16[2,18,3,128]{3,1,2,0:T(8,128)(2,1)S(1)} %get-tuple-element.11), channel_id=1, source_target_pairs={{0,4},{4,8},{8,12},{1,5},{5,9},{9,13},{2,6},{6,10},{10,14},{3,7},{... | collective-permute-start | bytes 82952 | tf_op jit(solution)/shard_map/ppermute | solution.py:12
  9.7 1.3 %collective-permute-start.1 = (bf16[2,18,3,128]{3,1,2,0:T(8,128)(2,1)S(1)}, bf16[2,18,3,128]{3,1,2,0:T(8,128)(2,1)S(1)}, u32[]{:S(2)}, u32[]{:S(2)}) collective-permute-start(bf16[2,18,3,128]{3,1,2,0:T(8,128)(2,1)S(1)} %get-tuple-element.23), channel_id=1, source_target_pairs={{4,0},{8,4},{12,8},{5,1},{9,5},{13,9},{6,2},{10,6},{14,10},{7,3},{... | collective-permute-start | bytes 82952 | tf_op jit(solution)/shard_map/ppermute | solution.py:15
  11.1 0.3 copy.49
  11.7 0.8 %gather_fusion.1 = bf16[4,2,18,3,128]{4,1,3,2,0:T(2,128)(2,1)S(1)} fusion(bf16[2,4,18,3,128]{4,0,3,2,1:T(2,128)(2,1)S(1)} %copy.51, s32[1024]{0:T(1024)S(1)} %pad_clamp_fusion.2), kind=kCustom, calls=%fused_computation.clone | custom fusion | bytes 221200 | tf_op jit(solution)/shard_map/jit(_take)/gather | solution.py:124
  12.5 0.6 %gather_fusion.2 = bf16[4,2,18,3,128]{4,2,3,1,0:T(8,128)(2,1)S(1)} fusion(bf16[2,4,18,3,128]{4,2,3,1,0:T(8,128)(2,1)S(1)} %get-tuple-element.24, s32[1024]{0:T(1024)S(1)} %pad_clamp_fusion.1), kind=kCustom, calls=%fused_computation.1.clone | custom fusion | bytes 221200 | tf_op jit(solution)/shard_map/jit(_take)/gather | solution.py:127
  13.2 2.4 %collective-permute-done.1 = bf16[2,18,3,128]{3,1,2,0:T(8,128)(2,1)S(1)} collective-permute-done((bf16[2,18,3,128]{3,1,2,0:T(8,128)(2,1)S(1)}, bf16[2,18,3,128]{3,1,2,0:T(8,128)(2,1)S(1)}, u32[]{:S(2)}, u32[]{:S(2)}) %collective-permute-start.1) | collective-permute-done | bytes 27680 | tf_op jit(solution)/shard_map/ppermute | solution.py:15
  15.7 0.3 pad_maximum_fusion
  16.1 0.4 fusion.71
  16.5 0.3 fusion.67
  16.8 0.3 fusion.63
  17.4 0.5 %convolution_add_fusion.5 = f32[2,4,20,128,16]{3,4,2,1,0:T(8,128)S(1)} fusion(f32[2,4,20,128,16]{3,4,2,1,0:T(8,128)S(1)} %fusion.71, bf16[2,4,18,22,128]{4,2,3,1,0:T(8,128)(2,1)S(1)} %pad_maximum_fusion, bf16[9,16,18]{2,1,0:T(8,128)(2,1)S(1)} %copy-done.4), kind=kOutput, calls=%fused_computation.32 | convolution fusion | flops 12124160 | bytes 3706880 | tf_op jit(solution)/shard_map/oi,bsirw->bsorw/dot_general | solution.py:39
  17.9 0.5 %convolution_add_fusion.4 = f32[2,4,20,128,16]{3,4,2,1,0:T(8,128)S(1)} fusion(f32[2,4,20,128,16]{3,4,2,1,0:T(8,128)S(1)} %convolution_add_fusion.5, bf16[2,4,18,22,128]{4,2,3,1,0:T(8,128)(2,1)S(1)} %pad_maximum_fusion, bf16[9,16,18]{2,1,0:T(8,128)(2,1)S(1)} %copy-done.4), kind=kOutput, calls=%fused_computation.31 | convolution fusion | flops 12124160 | bytes 3706880 | tf_op jit(solution)/shard_map/oi,bsirw->bsorw/dot_general | solution.py:39
  18.3 0.5 %fusion.9 = f32[2,4,20,128,16]{3,4,2,1,0:T(8,128)S(1)} fusion(f32[2,4,20,128,16]{3,4,2,1,0:T(8,128)S(1)} %fusion.67, f32[2,4,20,128,16]{3,4,2,1,0:T(8,128)S(1)} %convolution_add_fusion.4, bf16[2,4,18,22,128]{4,2,3,1,0:T(8,128)(2,1)S(1)} %pad_maximum_fusion, bf16[9,16,18]{2,1,0:T(8,128)(2,1)S(1)} %copy-done.4), kind=kOutput, calls=%fused_computation.30 | convolution fusion | flops 12451840 | bytes 5017600 | tf_op jit(solution)/shard_map/oi,bsirw->bsorw/dot_general | solution.py:39
  18.9 0.5 %convolution_add_fusion.2 = f32[2,4,20,128,16]{3,4,2,1,0:T(8,128)S(1)} fusion(f32[2,4,20,128,16]{3,4,2,1,0:T(8,128)S(1)} %fusion.9, bf16[2,4,18,22,128]{4,2,3,1,0:T(8,128)(2,1)S(1)} %pad_maximum_fusion, bf16[9,16,18]{2,1,0:T(8,128)(2,1)S(1)} %copy-done.4), kind=kOutput, calls=%fused_computation.28 | convolution fusion | flops 12124160 | bytes 3706880 | tf_op jit(solution)/shard_map/oi,bsirw->bsorw/dot_general | solution.py:39
  19.3 0.3 copy-done.7
  19.6 0.4 %fusion.33 = f32[2,4,16,128,8]{3,4,2,1,0:T(8,128)S(1)} fusion(bf16[2,4,18,22,128]{4,2,3,1,0:T(8,128)(2,1)S(1)} %pad_maximum_fusion, bf16[9,16,18]{2,1,0:T(8,128)(2,1)S(1)} %copy-done.7, s32[]{:T(128)S(6)} %select_n.92), kind=kOutput, calls=%fused_computation.75 | convolution fusion | flops 4718592 | bytes 1607684 | tf_op jit(solution)/shard_map/oi,bsirw->bsorw/dot_general | solution.py:39
  20.0 0.5 %fusion.8 = f32[2,4,20,128,16]{3,4,2,1,0:T(8,128)S(1)} fusion(f32[2,4,20,128,16]{3,4,2,1,0:T(8,128)S(1)} %fusion.63, f32[2,4,20,128,16]{3,4,2,1,0:T(8,128)S(1)} %convolution_add_fusion.2, bf16[2,4,18,22,128]{4,2,3,1,0:T(8,128)(2,1)S(1)} %pad_maximum_fusion, bf16[9,16,18]{2,1,0:T(8,128)(2,1)S(1)} %copy-done.4), kind=kOutput, calls=%fused_computation.27 | convolution fusion | flops 12451840 | bytes 5017600 | tf_op jit(solution)/shard_map/oi,bsirw->bsorw/dot_general | solution.py:39
  20.7 0.8 %fusion.11 = bf16[2,4,16,20,128]{4,2,3,1,0:T(8,128)(2,1)S(1)} fusion(f32[2,4,20,128,16]{3,4,2,1,0:T(8,128)S(1)} %fusion.8, bf16[2,4,18,22,128]{4,2,3,1,0:T(8,128)(2,1)S(1)} %pad_maximum_fusion, f32[16]{0:T(128)S(1)} %copy-done.12, bf16[9,16,18]{2,1,0:T(8,128)(2,1)S(1)} %copy-done.4), kind=kOutput, calls=%fused_computation.34 | convolution fusion | flops 14417920 | bytes 3707392 | tf_op jit(solution)/shard_map/oi,bsirw->bsorw/dot_general | solution.py:39
  21.5 1.1 %fusion.1 = bf16[2,4,18,20,132]{4,2,3,1,0:T(8,128)(2,1)S(1)} fusion(bf16[2,4,16,20,128]{4,2,3,1,0:T(8,128)(2,1)S(1)} %fusion.11, bf16[2,4,2,20,132]{4,2,3,1,0:T(2,128)(2,1)S(1)} %pad_slice_fusion.6), kind=kLoop, calls=%fused_computation.18 | loop fusion | flops 2280960 | bytes 1500160 | tf_op jit(solution)/shard_map/concatenate | solution.py:150
  22.6 0.2 fusion.42
  22.9 0.4 %convolution_add_fusion.15 = f32[2,4,16,128,8]{3,4,2,1,0:T(8,128)S(1)} fusion(f32[2,4,16,128,8]{3,4,2,1,0:T(8,128)S(1)} %fusion.42, bf16[2,4,18,20,132]{4,2,3,1,0:T(8,128)(2,1)S(1)} %fusion.1, bf16[9,16,18]{2,1,0:T(8,128)(2,1)S(1)} %copy-done, s32[]{:T(128)S(6)} %add.291, s32[]{:T(128)S(6)} %select_n.92), kind=kOutput, calls=%fused_computation.44 | convolution fusion | flops 4849664 | bytes 1837064 | tf_op jit(solution)/shard_map/oi,bsirw->bsorw/dot_general | solution.py:39
  23.3 0.3 convolution_add_fusion.7
  23.6 0.4 %convolution_add_fusion.14 = f32[2,4,16,128,8]{3,4,2,1,0:T(8,128)S(1)} fusion(f32[2,4,16,128,8]{3,4,2,1,0:T(8,128)S(1)} %convolution_add_fusion.15, bf16[2,4,18,20,132]{4,2,3,1,0:T(8,128)(2,1)S(1)} %fusion.1, bf16[9,16,18]{2,1,0:T(8,128)(2,1)S(1)} %copy-done, s32[]{:T(128)S(6)} %add.292, s32[]{:T(128)S(6)} %select_n.92), kind=kOutput, calls=%fused_computation.43 | convolution fusion | flops 4849664 | bytes 1837064 | tf_op jit(solution)/shard_map/oi,bsirw->bsorw/dot_general | solution.py:39
  24.0 0.4 %convolution_add_fusion.21 = f32[2,4,16,128,8]{3,4,2,1,0:T(8,128)S(1)} fusion(f32[2,4,16,128,8]{3,4,2,1,0:T(8,128)S(1)} %convolution_add_fusion.7, bf16[2,4,18,22,128]{4,2,3,1,0:T(8,128)(2,1)S(1)} %pad_maximum_fusion, bf16[9,16,18]{2,1,0:T(8,128)(2,1)S(1)} %copy-done.7, s32[]{:T(128)S(6)} %add.292, s32[]{:T(128)S(6)} %select_n.92), kind=kOutput, calls=%fused_computation.50 | convolution fusion | flops 4849664 | bytes 2131976 | tf_op jit(solution)/shard_map/oi,bsirw->bsorw/dot_general | solution.py:39
  24.4 0.2 convolution_add_fusion.13
  24.7 0.4 %convolution_add_fusion.20 = f32[2,4,16,128,8]{3,4,2,1,0:T(8,128)S(1)} fusion(f32[2,4,16,128,8]{3,4,2,1,0:T(8,128)S(1)} %convolution_add_fusion.21, bf16[2,4,18,22,128]{4,2,3,1,0:T(8,128)(2,1)S(1)} %pad_maximum_fusion, bf16[9,16,18]{2,1,0:T(8,128)(2,1)S(1)} %copy-done.7, s32[]{:T(128)S(6)} %add.293, s32[]{:T(128)S(6)} %select_n.92), kind=kOutput, calls=%fused_computation.49 | convolution fusion | flops 4849664 | bytes 2131976 | tf_op jit(solution)/shard_map/oi,bsirw->bsorw/dot_general | solution.py:39
  25.1 0.4 %convolution_add_fusion.12 = f32[2,4,16,128,8]{3,4,2,1,0:T(8,128)S(1)} fusion(f32[2,4,16,128,8]{3,4,2,1,0:T(8,128)S(1)} %convolution_add_fusion.13, bf16[2,4,18,20,132]{4,2,3,1,0:T(8,128)(2,1)S(1)} %fusion.1, bf16[9,16,18]{2,1,0:T(8,128)(2,1)S(1)} %copy-done, s32[]{:T(128)S(6)} %add.294, s32[]{:T(128)S(6)} %select_n.92), kind=kOutput, calls=%fused_computation.41 | convolution fusion | flops 4849664 | bytes 1837064 | tf_op jit(solution)/shard_map/oi,bsirw->bsorw/dot_general | solution.py:39
  25.5 0.3 convolution_add_fusion.19
  25.8 0.4 %convolution_add_fusion.11 = f32[2,4,16,128,8]{3,4,2,1,0:T(8,128)S(1)} fusion(f32[2,4,16,128,8]{3,4,2,1,0:T(8,128)S(1)} %convolution_add_fusion.12, bf16[2,4,18,20,132]{4,2,3,1,0:T(8,128)(2,1)S(1)} %fusion.1, bf16[9,16,18]{2,1,0:T(8,128)(2,1)S(1)} %copy-done, s32[]{:T(128)S(6)} %add.295, s32[]{:T(128)S(6)} %select_n.92), kind=kOutput, calls=%fused_computation.40 | convolution fusion | flops 4849664 | bytes 1837064 | tf_op jit(solution)/shard_map/oi,bsirw->bsorw/dot_general | solution.py:39
  26.2 0.4 %convolution_add_fusion.18 = f32[2,4,16,128,8]{3,4,2,1,0:T(8,128)S(1)} fusion(f32[2,4,16,128,8]{3,4,2,1,0:T(8,128)S(1)} %convolution_add_fusion.19, bf16[2,4,18,22,128]{4,2,3,1,0:T(8,128)(2,1)S(1)} %pad_maximum_fusion, bf16[9,16,18]{2,1,0:T(8,128)(2,1)S(1)} %copy-done.7, s32[]{:T(128)S(6)} %add.295, s32[]{:T(128)S(6)} %select_n.92), kind=kOutput, calls=%fused_computation.47 | convolution fusion | flops 4849664 | bytes 2131976 | tf_op jit(solution)/shard_map/oi,bsirw->bsorw/dot_general | solution.py:39
  26.8 0.4 %convolution_add_fusion.17 = f32[2,4,16,128,8]{3,4,2,1,0:T(8,128)S(1)} fusion(f32[2,4,16,128,8]{3,4,2,1,0:T(8,128)S(1)} %convolution_add_fusion.18, bf16[2,4,18,22,128]{4,2,3,1,0:T(8,128)(2,1)S(1)} %pad_maximum_fusion, bf16[9,16,18]{2,1,0:T(8,128)(2,1)S(1)} %copy-done.7, s32[]{:T(128)S(6)} %add.296, s32[]{:T(128)S(6)} %select_n.92), kind=kOutput, calls=%fused_computation.46 | convolution fusion | flops 4849664 | bytes 2131976 | tf_op jit(solution)/shard_map/oi,bsirw->bsorw/dot_general | solution.py:39
  27.2 0.4 %convolution_add_fusion.9 = f32[2,4,16,128,8]{3,4,2,1,0:T(8,128)S(1)} fusion(f32[2,4,16,128,8]{3,4,2,1,0:T(8,128)S(1)} %convolution_add_fusion.10, bf16[2,4,18,20,132]{4,2,3,1,0:T(8,128)(2,1)S(1)} %fusion.1, bf16[9,16,18]{2,1,0:T(8,128)(2,1)S(1)} %copy-done, s32[]{:T(128)S(6)} %add.297, s32[]{:T(128)S(6)} %select_n.92), kind=kOutput, calls=%fused_computation.38 | convolution fusion | flops 4849664 | bytes 1837064 | tf_op jit(solution)/shard_map/oi,bsirw->bsorw/dot_general | solution.py:39
  27.6 0.3 convolution_add_fusion.6
  28.0 0.4 %fusion.16 = f32[2,4,16,128,8]{3,4,2,1,0:T(8,128)S(1)} fusion(f32[2,4,16,128,8]{3,4,2,1,0:T(8,128)S(1)} %convolution_add_fusion.6, bf16[2,4,18,22,128]{4,2,3,1,0:T(8,128)(2,1)S(1)} %pad_maximum_fusion, f32[8]{0:T(128)S(1)} %dynamic_slice.27, bf16[9,16,18]{2,1,0:T(8,128)(2,1)S(1)} %copy-done.7, s32[]{:T(128)S(6)} %add.298, s32[]{:T(128)S(6)} %select_n.92), kind=kOutput, calls=%fused_computation.55 | convolution fusion | flops 5373952 | bytes 2132488 | tf_op jit(solution)/shard_map/oi,bsirw->bsorw/dot_general | solution.py:39
  28.4 0.5 %fusion.137 = (f32[4,8,16,128]{3,1,2,0:T(8,128)S(1)}, f32[2,4,8,16,128]{4,2,3,1,0:T(8,128)S(1)}) fusion(f32[4]{0:T(128)S(1)} %get-tuple-element.32, f32[2,4,16,128,8]{3,4,2,1,0:T(8,128)S(1)} %fusion.16, f32[8]{0:T(128)S(1)} %dynamic_slice.30, f32[2,4,16,128,8]{3,4,2,1,0:T(8,128)S(1)} %convolution_add_fusion.9, bf16[9,16,18]{2,1,0:T(8,128)(2,1)S(1)} %copy-done, ...), kind=kOutput, calls=%fused_computation.212 | convolution fusion | flops 5701632 | bytes 3150336 | tf_op jit(solution)/shard_map/oi,bsirw->bsorw/dot_general | solution.py:39
  28.9 0.5 %convolution_reduce_fusion = f32[4,8,4,32]{3,2,1,0:T(4,128)S(1)} fusion(f32[4,8,4,4,128]{4,1,3,2,0:T(8,128)S(1)} %bitcast.259, s32[128]{0:T(128)S(1)} %and_select_fusion), kind=kOutput, calls=%fused_computation.62 | convolution fusion | flops 25182208 | bytes 279040 | tf_op jit(solution)/shard_map/schw,wj->schj/dot_general | solution.py:161
  29.4 0.6 %gather_fusion = f32[4,8,4,32]{3,1,2,0:T(8,128)S(1)} fusion(f32[4,8,4,32]{3,1,2,0:T(8,128)S(1)} %copy_multiply_fusion, s32[1024]{0:T(1024)S(1)} %pad_clamp_fusion), kind=kCustom, calls=%fused_computation.2 | custom fusion | bytes 32784 | tf_op jit(solution)/shard_map/jit(_take)/gather | solution.py:167
  30.0 0.3 fusion.48
  30.4 1.6 %collective-permute-start.3 = (f32[2,16,4,32]{3,1,2,0:T(8,128)S(1)}, f32[2,16,4,32]{3,1,2,0:T(8,128)S(1)}, u32[]{:S(2)}, u32[]{:S(2)}) collective-permute-start(f32[2,16,4,32]{3,1,2,0:T(8,128)S(1)} %get-tuple-element.26), channel_id=1, source_target_pairs={{0,2},{1,3},{2,0},{3,1},{4,6},{5,7},{6,4},{7,5},{8,10},{9,11},{10,... | collective-permute-start | bytes 49160 | tf_op jit(solution)/shard_map/ppermute | solution.py:70
  32.0 0.3 collective-permute-start.4
  32.3 0.9 %copy.60 = f32[2,4,8,16,128]{4,3,2,1,0:T(8,128)} copy(f32[2,4,8,16,128]{4,2,3,1,0:T(8,128)S(1)} %get-tuple-element.35) | data formatting | bytes 1048576
  33.2 1.8 %collective-permute-done.3 = f32[2,16,4,32]{3,1,2,0:T(8,128)S(1)} collective-permute-done((f32[2,16,4,32]{3,1,2,0:T(8,128)S(1)}, f32[2,16,4,32]{3,1,2,0:T(8,128)S(1)}, u32[]{:S(2)}, u32[]{:S(2)}) %collective-permute-start.3) | collective-permute-done | bytes 16416 | tf_op jit(solution)/shard_map/ppermute | solution.py:70
  34.9 1.1 %collective-permute-done.4 = f32[2,16,4,32]{3,1,2,0:T(8,128)S(1)} collective-permute-done((f32[2,16,4,32]{3,1,2,0:T(8,128)S(1)}, f32[2,16,4,32]{3,1,2,0:T(8,128)S(1)}, u32[]{:S(2)}, u32[]{:S(2)}) %collective-permute-start.4) | collective-permute-done | bytes 16416 | tf_op jit(solution)/shard_map/ppermute | solution.py:70
  36.3 0.7 %copy.61 = f32[2,16,4,32]{3,2,1,0:T(4,128)} copy(f32[2,16,4,32]{3,1,2,0:T(8,128)S(1)} %tanh_add_fusion) | data formatting | bytes 32768
  (45 shorter events, 1.7 us)
Async XLA Ops:
  0.6 22.0 %copy-start = (bf16[9,16,18]{2,1,0:T(8,128)(2,1)S(1)}, bf16[9,16,18]{2,1,0:T(8,128)(2,1)}, u32[]{:S(2)}) copy-start(bf16[9,16,18]{2,1,0:T(8,128)(2,1)} %param.27) | copy-start | bytes 15556
  0.6 3.9 %copy-start.3 = (bf16[2,4,2,16,128]{4,3,2,1,0:T(8,128)(2,1)S(1)}, bf16[2,4,2,16,128]{4,3,2,1,0:T(8,128)(2,1)}, u32[]{:S(2)}) copy-start(bf16[2,4,2,16,128]{4,3,2,1,0:T(8,128)(2,1)} %param.17) | copy-start | bytes 196612
  2.8 8.2 %copy-start.9 = (s32[1,4]{1,0:T(1,128)S(1)}, s32[1,4]{1,0:T(1,128)}, u32[]{:S(2)}) copy-start(s32[1,4]{1,0:T(1,128)} %param.21) | copy-start | bytes 52
  2.8 8.3 %copy-start.1 = (f32[2,4,16,16,128]{4,3,2,1,0:T(8,128)S(1)}, f32[2,4,16,16,128]{4,3,2,1,0:T(8,128)}, u32[]{:S(2)}) copy-start(f32[2,4,16,16,128]{4,3,2,1,0:T(8,128)} %param.18) | copy-start | bytes 3145732
  4.7 6.8 %copy-start.10 = (f32[16]{0:T(128)S(1)}, f32[16]{0:T(128)}, u32[]{:S(2)}) copy-start(f32[16]{0:T(128)} %param.24) | copy-start | bytes 196
  4.8 6.9 %copy-start.11 = (f32[16]{0:T(128)S(1)}, f32[16]{0:T(128)}, u32[]{:S(2)}) copy-start(f32[16]{0:T(128)} %param.28) | copy-start | bytes 196
  4.8 8.4 %collective-permute-start = (bf16[2,18,3,128]{3,1,2,0:T(8,128)(2,1)S(1)}, bf16[2,18,3,128]{3,1,2,0:T(8,128)(2,1)S(1)}, u32[]{:S(2)}, u32[]{:S(2)}) collective-permute-start(bf16[2,18,3,128]{3,1,2,0:T(8,128)(2,1)S(1)} %get-tuple-element.11), channel_id=1, source_target_pairs={{0,4},{4,8},{8,12},{1,5},{5,9},{9,13},{2,6},{6,10},{10,14},{3,7},{... | collective-permute-start | bytes 82952 | tf_op jit(solution)/shard_map/ppermute | solution.py:12
  9.7 5.9 %collective-permute-start.1 = (bf16[2,18,3,128]{3,1,2,0:T(8,128)(2,1)S(1)}, bf16[2,18,3,128]{3,1,2,0:T(8,128)(2,1)S(1)}, u32[]{:S(2)}, u32[]{:S(2)}) collective-permute-start(bf16[2,18,3,128]{3,1,2,0:T(8,128)(2,1)S(1)} %get-tuple-element.23), channel_id=1, source_target_pairs={{4,0},{8,4},{12,8},{5,1},{9,5},{13,9},{6,2},{10,6},{14,10},{7,3},{... | collective-permute-start | bytes 82952 | tf_op jit(solution)/shard_map/ppermute | solution.py:15
  13.1 3.0 %copy-start.4 = (bf16[9,16,18]{2,1,0:T(8,128)(2,1)S(1)}, bf16[9,16,18]{2,1,0:T(8,128)(2,1)}, u32[]{:S(2)}) copy-start(bf16[9,16,18]{2,1,0:T(8,128)(2,1)} %param.25) | copy-start | bytes 15556
  18.9 0.8 %copy-start.7 = (bf16[9,16,18]{2,1,0:T(8,128)(2,1)S(1)}, bf16[9,16,18]{2,1,0:T(8,128)(2,1)}, u32[]{:S(2)}) copy-start(bf16[9,16,18]{2,1,0:T(8,128)(2,1)} %param.23) | copy-start | bytes 15556
  20.0 0.7 %copy-start.12 = (f32[16]{0:T(128)S(1)}, f32[16]{0:T(128)}, u32[]{:S(2)}) copy-start(f32[16]{0:T(128)} %param.26) | copy-start | bytes 196
  28.4 1.6 %copy-start.5 = (f32[16,16]{1,0:T(8,128)S(1)}, f32[16,16]{1,0:T(8,128)}, u32[]{:S(2)}) copy-start(f32[16,16]{1,0:T(8,128)} %param.29) | copy-start | bytes 3076
  28.9 7.2 %copy-start.2 = (f32[2,16,4,32]{3,2,1,0:T(4,128)S(1)}, f32[2,16,4,32]{3,2,1,0:T(4,128)}, u32[]{:S(2)}) copy-start(f32[2,16,4,32]{3,2,1,0:T(4,128)} %param.22) | copy-start | bytes 49156
  28.9 7.2 %copy-start.6 = (f32[16,16]{1,0:T(8,128)S(1)}, f32[16,16]{1,0:T(8,128)}, u32[]{:S(2)}) copy-start(f32[16,16]{1,0:T(8,128)} %param.30) | copy-start | bytes 3076
  28.9 7.2 %copy-start.8 = (f32[16]{0:T(128)S(1)}, f32[16]{0:T(128)}, u32[]{:S(2)}) copy-start(f32[16]{0:T(128)} %param.31) | copy-start | bytes 196
  30.4 2.8 %collective-permute-start.2 = (f32[2,16,4,32]{3,1,2,0:T(8,128)S(1)}, f32[2,16,4,32]{3,1,2,0:T(8,128)S(1)}, u32[]{:S(2)}, u32[]{:S(2)}) collective-permute-start(f32[2,16,4,32]{3,1,2,0:T(8,128)S(1)} %get-tuple-element.25), channel_id=1, source_target_pairs={{0,1},{1,0},{2,3},{3,2},{4,5},{5,4},{6,7},{7,6},{8,9},{9,8},{10,11... | collective-permute-start | bytes 49160 | tf_op jit(solution)/shard_map/ppermute | solution.py:70
  30.4 4.5 %collective-permute-start.3 = (f32[2,16,4,32]{3,1,2,0:T(8,128)S(1)}, f32[2,16,4,32]{3,1,2,0:T(8,128)S(1)}, u32[]{:S(2)}, u32[]{:S(2)}) collective-permute-start(f32[2,16,4,32]{3,1,2,0:T(8,128)S(1)} %get-tuple-element.26), channel_id=1, source_target_pairs={{0,2},{1,3},{2,0},{3,1},{4,6},{5,7},{6,4},{7,5},{8,10},{9,11},{10,... | collective-permute-start | bytes 49160 | tf_op jit(solution)/shard_map/ppermute | solution.py:70
  32.0 4.1 %collective-permute-start.4 = (f32[2,16,4,32]{3,1,2,0:T(8,128)S(1)}, f32[2,16,4,32]{3,1,2,0:T(8,128)S(1)}, u32[]{:S(2)}, u32[]{:S(2)}) collective-permute-start(f32[2,16,4,32]{3,1,2,0:T(8,128)S(1)} %get-tuple-element.26), channel_id=1, source_target_pairs={{0,3},{1,2},{2,1},{3,0},{4,7},{5,6},{6,5},{7,4},{8,11},{9,10},{10,... | collective-permute-start | bytes 49160 | tf_op jit(solution)/shard_map/ppermute | solution.py:70

commit v7 on v6

--- a/solution.py
+++ b/solution.py
@@ -53,23 +53,15 @@
 
 def exchange_sum(part, owned):
     bands = lax.axis_size("band")
-    reps = lax.axis_size("rep")
     band = lax.axis_index("band")
     total = None
     for shift in range(bands):
-        pair = None
-        for step in range(reps):
-            target = (band + shift) % bands
-            chunk = lax.dynamic_slice_in_dim(part, target * owned, owned, 0)
-            if shift or step:
-                perm = [
-                    (b * reps + r, ((b + shift) % bands) * reps + (r + step) % reps)
-                    for b in range(bands)
-                    for r in range(reps)
-                ]
-                chunk = lax.ppermute(chunk, ("band", "rep"), perm)
-            pair = chunk if pair is None else pair + chunk
-        total = pair if total is None else total + pair
+        target = (band + shift) % bands
+        chunk = lax.dynamic_slice_in_dim(part, target * owned, owned, 0)
+        if shift:
+            perm = [(b, (b + shift) % bands) for b in range(bands)]
+            chunk = lax.ppermute(chunk, "band", perm)
+        total = chunk if total is None else total + chunk
     return total
 
 
@@ -139,7 +131,7 @@
     full = jnp.concatenate([top, joined, bottom], axis=3)
     first = jnp.pad(full, ((0, 0), (0, 0), (0, 0), (0, 0), (2, 2)))
     update = jax.nn.sigmoid(
-        apply_filter(first, own_out(w_update), 1, 3, row_count, column_count) + own_bias(b_update)
+        apply_filter(first, w_update, 1, 3, row_count, column_count) + b_update[:, None, None]
     )
     hidden_wide = first[:, :, inputs_count:, 1 : row_count + 5, 2 : column_count + 2]
     reset = jax.nn.sigmoid(
@@ -149,12 +141,12 @@
     gated_pad = jnp.pad(gated, ((0, 0), (0, 0), (0, 0), (0, 0), (2, 2)))
     second = jnp.concatenate([first[:, :, :inputs_count, 1 : row_count + 5, :], gated_pad], axis=2)
     candidate = jnp.tanh(
-        apply_filter(second, own_out(w_cand), 2, 2, row_count, column_count) + own_bias(b_cand)
+        apply_filter(second, w_cand, 2, 2, row_count, column_count) + b_cand[:, None, None]
     )
-    state_half = lax.dynamic_slice_in_dim(state, start, half, 2)
     live_scale = alive.astype(jnp.float32)[None, :, None, None, None]
-    new_half = ((1.0 - update) * state_half + update * candidate) * live_scale
-    summed = jnp.sum(new_half, axis=0)
+    new_state = ((1.0 - update) * state + update * candidate) * live_scale
+    new_half = lax.dynamic_slice_in_dim(new_state, start, half, 2)
+    summed = jnp.sum(new_state, axis=0)
     column_pool = (
         jnp.arange(column_count)[:, None] // 4 == jnp.arange(column_count // 4)[None, :]
     ).astype(jnp.float32)
@@ -162,15 +154,10 @@
         "schw,wj->schj", summed, column_pool, precision=lax.Precision.HIGHEST
     )
     pooled = jnp.sum(
-        cols.reshape(slots, half, row_count // 4, 4, column_count // 4), axis=3
+        cols.reshape(slots, chans, row_count // 4, 4, column_count // 4), axis=3
     ) / 16.0
     ordered = jnp.take(pooled, coarse_perm[0], axis=0)
-    part = jnp.einsum(
-        "oc,kcij->koij",
-        lax.dynamic_slice_in_dim(u_pool, start, half, 1),
-        ordered,
-        precision=lax.Precision.HIGHEST,
-    )
+    part = jnp.einsum("oc,kcij->koij", u_pool, ordered, precision=lax.Precision.HIGHEST)
     pre = exchange_sum(part, coarse_state.shape[0])
     pre = pre + jnp.einsum("oc,kcij->koij", u_state, coarse_state, precision=lax.Precision.HIGHEST)
     pre = pre + b_coarse[None, :, None, None]

time: 37.3 us -> 35.4 us (0.949)
  waiting for transfers between devices: 5.25 us -> 1.42 us
  matrix products: 11.9 us -> 12.8 us
  starting transfers between devices: 8.17 us -> 8.87 us
    ppermute x1, waiting for transfers between devices: 2.36 us -> 0.01 us  [padded(): lax.ppermute(lax.slice_in_dim(block, 0, width, axis=dim), axis, backward)]
    ppermute x3 -> x1, waiting for transfers between devices: 2.89 us -> 1.41 us  [exchange_sum(): chunk = lax.ppermute(chunk, 'band', perm)]
    dot_general x27, matrix products: 10.8 us -> 11.9 us  [apply_filter(): jnp.einsum('oi,bsirw->bsorw', filter_weight[(left_operand + 1) * 3 + (rig...]
    ppermute x1, starting transfers between devices: 4.96 us -> 5.59 us  [padded(): lax.ppermute(lax.slice_in_dim(block, block.shape[dim] - width, None, axis...]
    unnamed x31 -> x30, local copies, waits for them, and re-layouts: 4.09 us -> 4.47 us
    ppermute x3 -> x1, starting transfers between devices: 1.92 us -> 1.99 us  [exchange_sum(): chunk = lax.ppermute(chunk, 'band', perm)]
  transfers between devices with their start and end apart: 5 -> 3, of which waited for: 3 -> 1; matrix products, arithmetic and copies ran while one was open for 8% -> 8% of each run, Pallas kernels for 0% -> 0%
where the time goes in v7:
time: 35.4 us; the launch traced here: 35.1 us
  matrix products  12.8 us (36%)
  starting transfers between devices  8.87 us (25%)
  local copies, waits for them, and re-layouts  6.74 us (19%)
  other arithmetic  4.09 us (12%)
  waiting for transfers between devices  1.42 us (4%)
  between operations  1.16 us (3%)
    dot_general x27, matrix products, apply_filter(): jnp.einsum('oi,bsirw->bsorw', filter_weight[(left_operand + 1) * 3 + (rig...  11.9 us
    ppermute x1, starting transfers between devices, padded(): lax.ppermute(lax.slice_in_dim(block, block.shape[dim] - width, None, axis...  5.59 us
    unnamed x30, local copies, waits for them, and re-layouts  4.47 us
    ppermute x1, starting transfers between devices, exchange_sum(): chunk = lax.ppermute(chunk, 'band', perm)  1.99 us
    ppermute x1, waiting for transfers between devices, exchange_sum(): chunk = lax.ppermute(chunk, 'band', perm)  1.41 us
    ppermute x1, starting transfers between devices, padded(): lax.ppermute(lax.slice_in_dim(block, 0, width, axis=dim), axis, backward)  1.29 us
    concatenate x1, other arithmetic, shards(): jnp.concatenate([first[:, :, :inputs_count, 1:row_count + 5, :], gated_pa...  1.14 us
    gather x1, local copies, waits for them, and re-layouts, shards(): jnp.take(joined[:, :, :, row_count - 3:, :], jnp.clip(ups - base, 0, slot...  0.77 us
  transfers between devices with their start and end apart: 3, of which 1 were waited for; matrix products, arithmetic and copies ran while one was open for 8% of the time, Pallas kernels for 0%

profile of v7, /device:TPU:0, one launch (start us, length us, event | category | flops | bytes accessed | tf_op | source)
XLA Modules:
  0.0 35.1 jit_solution(5509316472702588818)
XLA Ops:
  0.7 0.7 %not_and_fusion = (pred[4]{0:T(512)(128)(4,1)S(1)}, pred[4]{0:T(512)(128)(4,1)S(1)}) fusion(s32[4]{0:T(128)} %param.19, s32[]{:T(128)S(6)} %add.201, s32[]{:T(128)S(6)} %mul.29, s32[4,2]{0,1:T(2,128)} %param.20), kind=kLoop, calls=%fused_computation.194 | loop fusion | flops 24 | bytes 48 | tf_op jit(solution)/shard_map/and | solution.py:101
  1.4 0.8 %compare_and_fusion.1 = (pred[4]{0:T(512)(128)(4,1)S(1)}, s32[4]{0:T(128)S(1)}, pred[4]{0:T(512)(128)(4,1)S(1)}, pred[4]{0:T(512)(128)(4,1)S(1)}, s32[4]{0:T(128...) fusion(s32[]{:T(128)S(6)} %mul.29, s32[4,2]{0,1:T(2,128)} %param.20, ...), kind=kLoop, calls=%fused_computation.189 | loop fusion | flops 124 | bytes 116 | tf_op jit(solution)/shard_map/jit(_take)/and | solution.py:116
  2.2 0.7 %fusion.133 = (f32[4]{0:T(128)S(1)}, pred[4]{0:T(512)(128)(4,1)S(1)}) fusion(s32[4]{0:T(128)} %param.19, pred[4]{0:T(512)(128)(4,1)S(1)} %get-tuple-element.27), kind=kLoop, calls=%fused_computation.202 | loop fusion | flops 16 | bytes 40 | tf_op jit(solution)/shard_map/convert_element_type | solution.py:146
  2.8 1.6 %copy.86 = bf16[2,4,16,16,128]{4,2,3,1,0:T(8,128)(2,1)S(1)} copy(f32[2,4,16,16,128]{4,3,2,1,0:T(8,128)} %param.18) | data formatting | bytes 1572864 | tf_op args[1]
  4.7 1.3 %collective-permute-start.1 = (bf16[2,18,3,128]{3,1,2,0:T(8,128)(2,1)S(1)}, bf16[2,18,3,128]{3,1,2,0:T(8,128)(2,1)S(1)}, u32[]{:S(2)}, u32[]{:S(2)}) collective-permute-start(bf16[2,18,3,128]{3,1,2,0:T(8,128)(2,1)S(1)} %get-tuple-element.21), channel_id=1, source_target_pairs={{4,0},{8,4},{12,8},{5,1},{9,5},{13,9},{6,2},{10,6},{14,10},{7,3},{... | collective-permute-start | bytes 82952 | tf_op jit(solution)/shard_map/ppermute | solution.py:15
  6.0 5.6 %collective-permute-start = (bf16[2,18,3,128]{3,1,2,0:T(8,128)(2,1)S(1)}, bf16[2,18,3,128]{3,1,2,0:T(8,128)(2,1)S(1)}, u32[]{:S(2)}, u32[]{:S(2)}) collective-permute-start(bf16[2,18,3,128]{3,1,2,0:T(8,128)(2,1)S(1)} %get-tuple-element.9), channel_id=1, source_target_pairs={{0,4},{4,8},{8,12},{1,5},{5,9},{9,13},{2,6},{6,10},{10,14},{3,7},{... | collective-permute-start | bytes 82952 | tf_op jit(solution)/shard_map/ppermute | solution.py:12
  11.6 0.3 fusion.55
  12.1 0.6 %gather_fusion.2 = bf16[4,2,18,3,128]{4,2,3,1,0:T(8,128)(2,1)S(1)} fusion(bf16[2,4,18,3,128]{4,2,3,1,0:T(8,128)(2,1)S(1)} %get-tuple-element.22, s32[1024]{0:T(1024)S(1)} %pad_clamp_fusion.1), kind=kCustom, calls=%fused_computation.1.clone | custom fusion | bytes 221200 | tf_op jit(solution)/shard_map/jit(_take)/gather | solution.py:119
  12.7 0.8 %gather_fusion.1 = bf16[4,2,18,3,128]{4,1,3,2,0:T(2,128)(2,1)S(1)} fusion(bf16[2,4,18,3,128]{4,0,3,2,1:T(2,128)(2,1)S(1)} %copy.37, s32[1024]{0:T(1024)S(1)} %pad_clamp_fusion.2), kind=kCustom, calls=%fused_computation.clone | custom fusion | bytes 221200 | tf_op jit(solution)/shard_map/jit(_take)/gather | solution.py:116
  13.8 0.3 pad_maximum_fusion
  14.1 0.4 %fusion.44 = f32[2,4,16,128,16]{3,4,2,1,0:T(8,128)S(1)} fusion(bf16[2,4,18,22,128]{4,2,3,1,0:T(8,128)(2,1)S(1)} %pad_maximum_fusion, bf16[9,16,18]{2,1,0:T(8,128)(2,1)S(1)} %copy-done.5), kind=kOutput, calls=%fused_computation.82 | convolution fusion | flops 9437184 | bytes 2134016 | tf_op jit(solution)/shard_map/oi,bsirw->bsorw/dot_general | solution.py:39
  14.5 0.4 %fusion.43 = f32[2,4,16,128,16]{3,4,2,1,0:T(8,128)S(1)} fusion(bf16[2,4,18,22,128]{4,2,3,1,0:T(8,128)(2,1)S(1)} %pad_maximum_fusion, bf16[9,16,18]{2,1,0:T(8,128)(2,1)S(1)} %copy-done.5), kind=kOutput, calls=%fused_computation.81 | convolution fusion | flops 9437184 | bytes 2134016 | tf_op jit(solution)/shard_map/oi,bsirw->bsorw/dot_general | solution.py:39
  14.9 0.4 %fusion.42 = f32[2,4,16,128,16]{3,4,2,1,0:T(8,128)S(1)} fusion(bf16[2,4,18,22,128]{4,2,3,1,0:T(8,128)(2,1)S(1)} %pad_maximum_fusion, bf16[9,16,18]{2,1,0:T(8,128)(2,1)S(1)} %copy-done.5), kind=kOutput, calls=%fused_computation.80 | convolution fusion | flops 9437184 | bytes 2134016 | tf_op jit(solution)/shard_map/oi,bsirw->bsorw/dot_general | solution.py:39
  15.3 0.4 %fusion.41 = f32[2,4,16,128,16]{3,4,2,1,0:T(8,128)S(1)} fusion(bf16[2,4,18,22,128]{4,2,3,1,0:T(8,128)(2,1)S(1)} %pad_maximum_fusion, bf16[9,16,18]{2,1,0:T(8,128)(2,1)S(1)} %copy-done.5), kind=kOutput, calls=%fused_computation.79 | convolution fusion | flops 9437184 | bytes 2134016 | tf_op jit(solution)/shard_map/oi,bsirw->bsorw/dot_general | solution.py:39
  15.7 0.4 %fusion.40 = f32[2,4,16,128,16]{3,4,2,1,0:T(8,128)S(1)} fusion(bf16[2,4,18,22,128]{4,2,3,1,0:T(8,128)(2,1)S(1)} %pad_maximum_fusion, bf16[9,16,18]{2,1,0:T(8,128)(2,1)S(1)} %copy-done.5), kind=kOutput, calls=%fused_computation.78 | convolution fusion | flops 9437184 | bytes 2134016 | tf_op jit(solution)/shard_map/oi,bsirw->bsorw/dot_general | solution.py:39
  16.1 0.4 %fusion.39 = f32[2,4,16,128,16]{3,4,2,1,0:T(8,128)S(1)} fusion(bf16[2,4,18,22,128]{4,2,3,1,0:T(8,128)(2,1)S(1)} %pad_maximum_fusion, bf16[9,16,18]{2,1,0:T(8,128)(2,1)S(1)} %copy-done.5), kind=kOutput, calls=%fused_computation.77 | convolution fusion | flops 9437184 | bytes 2134016 | tf_op jit(solution)/shard_map/oi,bsirw->bsorw/dot_general | solution.py:39
  16.5 0.4 %copy-done.6 = bf16[9,16,18]{2,1,0:T(8,128)(2,1)S(1)} copy-done((bf16[9,16,18]{2,1,0:T(8,128)(2,1)S(1)}, bf16[9,16,18]{2,1,0:T(8,128)(2,1)}, u32[]{:S(2)}) %copy-start.6) | copy-done | bytes 5208
  16.9 0.3 fusion.85
  17.2 0.3 fusion.89
  17.6 0.3 fusion.93
  17.9 0.2 pad_slice_fusion.6
  18.2 0.5 %convolution_add_fusion.5 = f32[2,4,20,128,16]{3,4,2,1,0:T(8,128)S(1)} fusion(f32[2,4,20,128,16]{3,4,2,1,0:T(8,128)S(1)} %fusion.93, bf16[2,4,18,22,128]{4,2,3,1,0:T(8,128)(2,1)S(1)} %pad_maximum_fusion, bf16[9,16,18]{2,1,0:T(8,128)(2,1)S(1)} %copy-done.6), kind=kOutput, calls=%fused_computation.32 | convolution fusion | flops 12124160 | bytes 3706880 | tf_op jit(solution)/shard_map/oi,bsirw->bsorw/dot_general | solution.py:39
  18.6 0.5 %convolution_add_fusion.4 = f32[2,4,20,128,16]{3,4,2,1,0:T(8,128)S(1)} fusion(f32[2,4,20,128,16]{3,4,2,1,0:T(8,128)S(1)} %convolution_add_fusion.5, bf16[2,4,18,22,128]{4,2,3,1,0:T(8,128)(2,1)S(1)} %pad_maximum_fusion, bf16[9,16,18]{2,1,0:T(8,128)(2,1)S(1)} %copy-done.6), kind=kOutput, calls=%fused_computation.31 | convolution fusion | flops 12124160 | bytes 3706880 | tf_op jit(solution)/shard_map/oi,bsirw->bsorw/dot_general | solution.py:39
  19.1 0.5 %fusion.9 = f32[2,4,20,128,16]{3,4,2,1,0:T(8,128)S(1)} fusion(f32[2,4,20,128,16]{3,4,2,1,0:T(8,128)S(1)} %fusion.89, f32[2,4,20,128,16]{3,4,2,1,0:T(8,128)S(1)} %convolution_add_fusion.4, bf16[2,4,18,22,128]{4,2,3,1,0:T(8,128)(2,1)S(1)} %pad_maximum_fusion, bf16[9,16,18]{2,1,0:T(8,128)(2,1)S(1)} %copy-done.6), kind=kOutput, calls=%fused_computation.30 | convolution fusion | flops 12451840 | bytes 5017600 | tf_op jit(solution)/shard_map/oi,bsirw->bsorw/dot_general | solution.py:39
  19.6 0.5 %convolution_add_fusion.2 = f32[2,4,20,128,16]{3,4,2,1,0:T(8,128)S(1)} fusion(f32[2,4,20,128,16]{3,4,2,1,0:T(8,128)S(1)} %fusion.9, bf16[2,4,18,22,128]{4,2,3,1,0:T(8,128)(2,1)S(1)} %pad_maximum_fusion, bf16[9,16,18]{2,1,0:T(8,128)(2,1)S(1)} %copy-done.6), kind=kOutput, calls=%fused_computation.28 | convolution fusion | flops 12124160 | bytes 3706880 | tf_op jit(solution)/shard_map/oi,bsirw->bsorw/dot_general | solution.py:39
  20.1 0.5 %fusion.8 = f32[2,4,20,128,16]{3,4,2,1,0:T(8,128)S(1)} fusion(f32[2,4,20,128,16]{3,4,2,1,0:T(8,128)S(1)} %fusion.85, f32[2,4,20,128,16]{3,4,2,1,0:T(8,128)S(1)} %convolution_add_fusion.2, bf16[2,4,18,22,128]{4,2,3,1,0:T(8,128)(2,1)S(1)} %pad_maximum_fusion, bf16[9,16,18]{2,1,0:T(8,128)(2,1)S(1)} %copy-done.6), kind=kOutput, calls=%fused_computation.27 | convolution fusion | flops 12451840 | bytes 5017600 | tf_op jit(solution)/shard_map/oi,bsirw->bsorw/dot_general | solution.py:39
  20.7 0.8 %fusion.28 = bf16[2,4,16,20,128]{4,2,3,1,0:T(8,128)(2,1)S(1)} fusion(f32[2,4,20,128,16]{3,4,2,1,0:T(8,128)S(1)} %fusion.8, bf16[2,4,18,22,128]{4,2,3,1,0:T(8,128)(2,1)S(1)} %pad_maximum_fusion, f32[16]{0:T(128)S(1)} %copy-done.11, bf16[9,16,18]{2,1,0:T(8,128)(2,1)S(1)} %copy-done.6), kind=kOutput, calls=%fused_computation.61 | convolution fusion | flops 14417920 | bytes 3707392 | tf_op jit(solution)/shard_map/oi,bsirw->bsorw/dot_general | solution.py:39
  21.6 1.1 %fusion.1 = bf16[2,4,18,20,132]{4,2,3,1,0:T(8,128)(2,1)S(1)} fusion(bf16[2,4,16,20,128]{4,2,3,1,0:T(8,128)(2,1)S(1)} %fusion.28, bf16[2,4,2,20,132]{4,2,3,1,0:T(2,128)(2,1)S(1)} %pad_slice_fusion.6), kind=kLoop, calls=%fused_computation.18 | loop fusion | flops 2280960 | bytes 1500160 | tf_op jit(solution)/shard_map/concatenate | solution.py:142
  22.7 0.3 fusion.53
  23.0 0.4 %convolution_add_fusion.15 = f32[2,4,16,128,16]{3,4,2,1,0:T(8,128)S(1)} fusion(f32[2,4,16,128,16]{3,4,2,1,0:T(8,128)S(1)} %fusion.53, bf16[2,4,18,20,132]{4,2,3,1,0:T(8,128)(2,1)S(1)} %fusion.1, bf16[9,16,18]{2,1,0:T(8,128)(2,1)S(1)} %copy-done.4), kind=kOutput, calls=%fused_computation.60 | convolution fusion | flops 9699328 | bytes 2887680 | tf_op jit(solution)/shard_map/oi,bsirw->bsorw/dot_general | solution.py:39
  23.4 0.4 %convolution_add_fusion.14 = f32[2,4,16,128,16]{3,4,2,1,0:T(8,128)S(1)} fusion(f32[2,4,16,128,16]{3,4,2,1,0:T(8,128)S(1)} %convolution_add_fusion.15, bf16[2,4,18,20,132]{4,2,3,1,0:T(8,128)(2,1)S(1)} %fusion.1, bf16[9,16,18]{2,1,0:T(8,128)(2,1)S(1)} %copy-done.4), kind=kOutput, calls=%fused_computation.59 | convolution fusion | flops 9699328 | bytes 2887680 | tf_op jit(solution)/shard_map/oi,bsirw->bsorw/dot_general | solution.py:39
  23.9 0.3 convolution_add_fusion.13
  24.2 0.4 %convolution_add_fusion.12 = f32[2,4,16,128,16]{3,4,2,1,0:T(8,128)S(1)} fusion(f32[2,4,16,128,16]{3,4,2,1,0:T(8,128)S(1)} %convolution_add_fusion.13, bf16[2,4,18,20,132]{4,2,3,1,0:T(8,128)(2,1)S(1)} %fusion.1, bf16[9,16,18]{2,1,0:T(8,128)(2,1)S(1)} %copy-done.4), kind=kOutput, calls=%fused_computation.57 | convolution fusion | flops 9699328 | bytes 2887680 | tf_op jit(solution)/shard_map/oi,bsirw->bsorw/dot_general | solution.py:39
  24.6 0.4 %convolution_add_fusion.11 = f32[2,4,16,128,16]{3,4,2,1,0:T(8,128)S(1)} fusion(f32[2,4,16,128,16]{3,4,2,1,0:T(8,128)S(1)} %convolution_add_fusion.12, bf16[2,4,18,20,132]{4,2,3,1,0:T(8,128)(2,1)S(1)} %fusion.1, bf16[9,16,18]{2,1,0:T(8,128)(2,1)S(1)} %copy-done.4), kind=kOutput, calls=%fused_computation.56 | convolution fusion | flops 9699328 | bytes 2887680 | tf_op jit(solution)/shard_map/oi,bsirw->bsorw/dot_general | solution.py:39
  25.0 0.3 convolution_add_fusion.10
  25.3 0.4 %convolution_add_fusion.9 = f32[2,4,16,128,16]{3,4,2,1,0:T(8,128)S(1)} fusion(f32[2,4,16,128,16]{3,4,2,1,0:T(8,128)S(1)} %convolution_add_fusion.10, bf16[2,4,18,20,132]{4,2,3,1,0:T(8,128)(2,1)S(1)} %fusion.1, bf16[9,16,18]{2,1,0:T(8,128)(2,1)S(1)} %copy-done.4), kind=kOutput, calls=%fused_computation.54 | convolution fusion | flops 9699328 | bytes 2887680 | tf_op jit(solution)/shard_map/oi,bsirw->bsorw/dot_general | solution.py:39
  25.7 0.7 %fusion.21 = f32[2,4,16,128,16]{3,4,2,1,0:T(8,128)S(1)} fusion(f32[2,4,16,128,16]{3,4,2,1,0:T(8,128)S(1)} %fusion.43, f32[2,4,16,128,16]{3,4,2,1,0:T(8,128)S(1)} %fusion.42, f32[2,4,16,128,16]{3,4,2,1,0:T(8,128)S(1)} %fusion.55, f32[2,4,16,128,16]{3,4,2,1,0:T(8,128)S(1)} %fusion.41, f32[2,4,16,128,16]{3,4,2,1,0:T(8,128)S(1)} %fusion.40, ...), kind=kOutput, calls=%fused_computation.46 | convolution fusion | flops 13111296 | bytes 8081408 | tf_op jit(solution)/shard_map/oi,bsirw->bsorw/dot_general | solution.py:39
  26.5 0.5 %fusion.16 = f32[2,4,16,128,16]{3,4,2,1,0:T(8,128)S(1)} fusion(f32[2,4,16,128,16]{3,4,2,1,0:T(8,128)S(1)} %fusion.44, f32[2,4,16,128,16]{3,4,2,1,0:T(8,128)S(1)} %fusion.21, bf16[2,4,18,3,128]{4,2,3,1,0:T(8,128)(2,1)S(1)} %copy_select_fusion, bf16[2,4,16,16,128]{4,2,3,1,0:T(8,128)(2,1)S(1)} %copy.86, bf16[2,4,2,16,128]{4,2,3,1,0:T(2,128)(2,1)S(1)} %copy.36, ...), kind=kOutput, calls=%fused_computation.40 | convolution fusion | flops 13111296 | bytes 3887616 | tf_op jit(solution)/shard_map/oi,bsirw->bsorw/dot_general | solution.py:39
  27.0 0.7 %copy-done.1 = f32[2,4,16,16,128]{4,3,2,1,0:T(8,128)S(1)} copy-done((f32[2,4,16,16,128]{4,3,2,1,0:T(8,128)S(1)}, f32[2,4,16,16,128]{4,3,2,1,0:T(8,128)}, u32[]{:S(2)}) %copy-start.1) | copy-done | bytes 1048600
  27.7 0.8 %fusion.150 = (f32[4,16,16,128]{3,1,2,0:T(8,128)S(1)}, f32[2,4,16,16,128]{4,2,3,1,0:T(8,128)S(1)}) fusion(f32[4]{0:T(128)S(1)} %get-tuple-element.28, f32[2,4,16,128,16]{3,4,2,1,0:T(8,128)S(1)} %fusion.16, f32[16]{0:T(128)S(1)} %copy-done.10, f32[2,4,16,128,16]{3,4,2,1,0:T(8,128)S(1)} %convolution_add_fusion.9, bf16[9,16,18]{2,1,0:T(8,128)(2,1)S(1)} %copy-done.4, ...), kind=kOutput, calls=%fused_computation.219 | convolution fusion | flops 11403264 | bytes 5510144 | tf_op jit(solution)/shard_map/oi,bsirw->bsorw/dot_general | solution.py:39
  28.5 0.4 %convolution_reduce_fusion = f32[4,16,4,32]{3,1,2,0:T(8,128)S(1)} fusion(f32[4,16,4,4,128]{4,1,3,2,0:T(8,128)S(1)} %bitcast.267, s32[128]{0:T(128)S(1)} %and_select_fusion), kind=kOutput, calls=%fused_computation.62 | convolution fusion | flops 50360320 | bytes 557568 | tf_op jit(solution)/shard_map/schw,wj->schj/dot_general | solution.py:153
  28.9 0.6 %gather_fusion = f32[4,16,4,32]{3,1,2,0:T(8,128)S(1)} fusion(f32[4,16,4,32]{3,1,2,0:T(8,128)S(1)} %broadcast_multiply_fusion, s32[1024]{0:T(1024)S(1)} %pad_clamp_fusion), kind=kCustom, calls=%fused_computation.2 | custom fusion | bytes 65552 | tf_op jit(solution)/shard_map/jit(_take)/gather | solution.py:159
  29.5 0.3 fusion.59
  29.9 2.0 %collective-permute-start.2 = (f32[2,16,4,32]{3,1,2,0:T(8,128)S(1)}, f32[2,16,4,32]{3,1,2,0:T(8,128)S(1)}, u32[]{:S(2)}, u32[]{:S(2)}) collective-permute-start(f32[2,16,4,32]{3,1,2,0:T(8,128)S(1)} %dynamic-slice_bitcast_fusion), channel_id=1, source_target_pairs={{0,2},{2,0},{1,3},{3,1},{4,6},{6,4},{5,7},{7,5},{8,10},{10,8},{9,1... | collective-permute-start | bytes 49160 | tf_op jit(solution)/shard_map/ppermute | solution.py:63
  31.9 0.9 %copy.43 = f32[2,4,8,16,128]{4,3,2,1,0:T(8,128)} copy(f32[2,4,8,16,128]{4,2,3,1,0:T(8,128)S(1)} %constant_dynamic-slice_fusion) | data formatting | bytes 1048576
  32.8 1.4 %collective-permute-done.2 = f32[2,16,4,32]{3,1,2,0:T(8,128)S(1)} collective-permute-done((f32[2,16,4,32]{3,1,2,0:T(8,128)S(1)}, f32[2,16,4,32]{3,1,2,0:T(8,128)S(1)}, u32[]{:S(2)}, u32[]{:S(2)}) %collective-permute-start.2) | collective-permute-done | bytes 16416 | tf_op jit(solution)/shard_map/ppermute | solution.py:63
  34.2 0.2 fusion.64
  34.4 0.7 %copy.44 = f32[2,16,4,32]{3,2,1,0:T(4,128)} copy(f32[2,16,4,32]{3,1,2,0:T(8,128)S(1)} %fusion.64) | data formatting | bytes 32768
  (39 shorter events, 0.8 us)
Async XLA Ops:
  0.6 28.9 %copy-start = (f32[16,16]{1,0:T(8,128)S(1)}, f32[16,16]{1,0:T(8,128)}, u32[]{:S(2)}) copy-start(f32[16,16]{1,0:T(8,128)} %param.29) | copy-start | bytes 3076
  0.6 3.8 %copy-start.2 = (bf16[2,4,2,16,128]{4,3,2,1,0:T(8,128)(2,1)S(1)}, bf16[2,4,2,16,128]{4,3,2,1,0:T(8,128)(2,1)}, u32[]{:S(2)}) copy-start(bf16[2,4,2,16,128]{4,3,2,1,0:T(8,128)(2,1)} %param.17) | copy-start | bytes 196612
  2.8 8.7 %copy-start.9 = (s32[1,4]{1,0:T(1,128)S(1)}, s32[1,4]{1,0:T(1,128)}, u32[]{:S(2)}) copy-start(s32[1,4]{1,0:T(1,128)} %param.21) | copy-start | bytes 52
  2.8 8.8 %copy-start.5 = (bf16[9,16,18]{2,1,0:T(8,128)(2,1)S(1)}, bf16[9,16,18]{2,1,0:T(8,128)(2,1)}, u32[]{:S(2)}) copy-start(bf16[9,16,18]{2,1,0:T(8,128)(2,1)} %param.23) | copy-start | bytes 15556
  4.7 8.8 %collective-permute-start.1 = (bf16[2,18,3,128]{3,1,2,0:T(8,128)(2,1)S(1)}, bf16[2,18,3,128]{3,1,2,0:T(8,128)(2,1)S(1)}, u32[]{:S(2)}, u32[]{:S(2)}) collective-permute-start(bf16[2,18,3,128]{3,1,2,0:T(8,128)(2,1)S(1)} %get-tuple-element.21), channel_id=1, source_target_pairs={{4,0},{8,4},{12,8},{5,1},{9,5},{13,9},{6,2},{10,6},{14,10},{7,3},{... | collective-permute-start | bytes 82952 | tf_op jit(solution)/shard_map/ppermute | solution.py:15
  6.0 7.7 %collective-permute-start = (bf16[2,18,3,128]{3,1,2,0:T(8,128)(2,1)S(1)}, bf16[2,18,3,128]{3,1,2,0:T(8,128)(2,1)S(1)}, u32[]{:S(2)}, u32[]{:S(2)}) collective-permute-start(bf16[2,18,3,128]{3,1,2,0:T(8,128)(2,1)S(1)} %get-tuple-element.9), channel_id=1, source_target_pairs={{0,4},{4,8},{8,12},{1,5},{5,9},{9,13},{2,6},{6,10},{10,14},{3,7},{... | collective-permute-start | bytes 82952 | tf_op jit(solution)/shard_map/ppermute | solution.py:12
  16.1 0.8 %copy-start.6 = (bf16[9,16,18]{2,1,0:T(8,128)(2,1)S(1)}, bf16[9,16,18]{2,1,0:T(8,128)(2,1)}, u32[]{:S(2)}) copy-start(bf16[9,16,18]{2,1,0:T(8,128)(2,1)} %param.25) | copy-start | bytes 15556
  20.1 0.7 %copy-start.11 = (f32[16]{0:T(128)S(1)}, f32[16]{0:T(128)}, u32[]{:S(2)}) copy-start(f32[16]{0:T(128)} %param.26) | copy-start | bytes 196
  21.6 1.2 %copy-start.4 = (bf16[9,16,18]{2,1,0:T(8,128)(2,1)S(1)}, bf16[9,16,18]{2,1,0:T(8,128)(2,1)}, u32[]{:S(2)}) copy-start(bf16[9,16,18]{2,1,0:T(8,128)(2,1)} %param.27) | copy-start | bytes 15556
  25.7 0.7 %copy-start.12 = (f32[16]{0:T(128)S(1)}, f32[16]{0:T(128)}, u32[]{:S(2)}) copy-start(f32[16]{0:T(128)} %param.24) | copy-start | bytes 196
  26.5 1.2 %copy-start.1 = (f32[2,4,16,16,128]{4,3,2,1,0:T(8,128)S(1)}, f32[2,4,16,16,128]{4,3,2,1,0:T(8,128)}, u32[]{:S(2)}) copy-start(f32[2,4,16,16,128]{4,3,2,1,0:T(8,128)} %param.18) | copy-start | bytes 3145732
  26.5 1.2 %copy-start.10 = (f32[16]{0:T(128)S(1)}, f32[16]{0:T(128)}, u32[]{:S(2)}) copy-start(f32[16]{0:T(128)} %param.28) | copy-start | bytes 196
  29.5 4.7 %copy-start.3 = (f32[2,16,4,32]{3,2,1,0:T(4,128)S(1)}, f32[2,16,4,32]{3,2,1,0:T(4,128)}, u32[]{:S(2)}) copy-start(f32[2,16,4,32]{3,2,1,0:T(4,128)} %param.22) | copy-start | bytes 49156
  29.5 4.7 %copy-start.7 = (f32[16,16]{1,0:T(8,128)S(1)}, f32[16,16]{1,0:T(8,128)}, u32[]{:S(2)}) copy-start(f32[16,16]{1,0:T(8,128)} %param.30) | copy-start | bytes 3076
  29.5 4.7 %copy-start.8 = (f32[16]{0:T(128)S(1)}, f32[16]{0:T(128)}, u32[]{:S(2)}) copy-start(f32[16]{0:T(128)} %param.31) | copy-start | bytes 196
  29.9 4.3 %collective-permute-start.2 = (f32[2,16,4,32]{3,1,2,0:T(8,128)S(1)}, f32[2,16,4,32]{3,1,2,0:T(8,128)S(1)}, u32[]{:S(2)}, u32[]{:S(2)}) collective-permute-start(f32[2,16,4,32]{3,1,2,0:T(8,128)S(1)} %dynamic-slice_bitcast_fusion), channel_id=1, source_target_pairs={{0,2},{2,0},{1,3},{3,1},{4,6},{6,4},{5,7},{7,5},{8,10},{10,8},{9,1... | collective-permute-start | bytes 49160 | tf_op jit(solution)/shard_map/ppermute | solution.py:63

commit v8 on v7

--- a/solution.py
+++ b/solution.py
@@ -20,29 +20,37 @@
 def apply_filter(
     padded_input, filter_weight, dilation_rate, first_row_index, row_count, column_count
 ):
+    offsets = (-1, 0, 1)
+    stacked = jnp.concatenate(
+        [
+            padded_input[
+                :,
+                :,
+                :,
+                first_row_index
+                + row_offset * dilation_rate : first_row_index
+                + row_offset * dilation_rate
+                + row_count,
+                :,
+            ]
+            for row_offset in offsets
+        ],
+        axis=2,
+    )
     total = None
-    for left_operand in (-1, 0, 1):
-        for right_operand in (-1, 0, 1):
-            window_slice = padded_input[
-                :,
-                :,
-                :,
-                first_row_index
-                + left_operand * dilation_rate : first_row_index
-                + left_operand * dilation_rate
-                + row_count,
-                2
-                + right_operand * dilation_rate : 2
-                + right_operand * dilation_rate
-                + column_count,
-            ]
-            term = jnp.einsum(
-                "oi,bsirw->bsorw",
-                filter_weight[(left_operand + 1) * 3 + (right_operand + 1)],
-                window_slice,
-                preferred_element_type=jnp.float32,
-            )
-            total = term if total is None else total + term
+    for column_offset in offsets:
+        weight = jnp.concatenate(
+            [filter_weight[(row_offset + 1) * 3 + (column_offset + 1)] for row_offset in offsets],
+            axis=1,
+        )
+        window_slice = stacked[
+            ...,
+            2 + column_offset * dilation_rate : 2 + column_offset * dilation_rate + column_count,
+        ]
+        term = jnp.einsum(
+            "oi,bsirw->bsorw", weight, window_slice, preferred_element_type=jnp.float32
+        )
+        total = term if total is None else total + term
     return total
 
 
@@ -130,13 +138,20 @@
     )
     full = jnp.concatenate([top, joined, bottom], axis=3)
     first = jnp.pad(full, ((0, 0), (0, 0), (0, 0), (0, 0), (2, 2)))
-    update = jax.nn.sigmoid(
-        apply_filter(first, w_update, 1, 3, row_count, column_count) + b_update[:, None, None]
-    )
+    gates = jax.nn.sigmoid(
+        apply_filter(
+            first,
+            jnp.concatenate([w_update, w_reset], axis=1),
+            1,
+            1,
+            row_count + 4,
+            column_count,
+        )
+        + jnp.concatenate([b_update, b_reset])[:, None, None]
+    )
+    update = gates[:, :, :chans, 2 : row_count + 2]
+    reset = gates[:, :, chans:]
     hidden_wide = first[:, :, inputs_count:, 1 : row_count + 5, 2 : column_count + 2]
-    reset = jax.nn.sigmoid(
-        apply_filter(first, w_reset, 1, 1, row_count + 4, column_count) + b_reset[:, None, None]
-    )
     gated = (reset * hidden_wide.astype(jnp.float32)).astype(jnp.bfloat16)
     gated_pad = jnp.pad(gated, ((0, 0), (0, 0), (0, 0), (0, 0), (2, 2)))
     second = jnp.concatenate([first[:, :, :inputs_count, 1 : row_count + 5, :], gated_pad], axis=2)

time: 35.4 us -> 35.9 us (1.014)
  matrix products: 12.8 us -> 6.55 us
  other arithmetic: 4.09 us -> 9.01 us
  local copies, waits for them, and re-layouts: 6.74 us -> 8.68 us
    dot_general x27 -> x6, matrix products: 11.9 us -> 5.67 us  [apply_filter(): jnp.einsum('oi,bsirw->bsorw', weight, window_slice, preferred_element_typ...]
    concatenate x0 -> x3, other arithmetic: none -> 4.67 us  [the longest x2 4.6 us: apply_filter(): jnp.concatenate([padded_input[:, :, :, first_row_index + row_offset * dil...]
    slice x1 -> x2, local copies, waits for them, and re-layouts: 0.09 us -> 2.57 us  [apply_filter(): padded_input[:, :, :, first_row_index + row_offset * dilation_rate:first_...]
    unnamed x30 -> x29, local copies, waits for them, and re-layouts: 4.47 us -> 4.08 us
  transfers between devices with their start and end apart: 3 -> 3, of which waited for: 1 -> 1; matrix products, arithmetic and copies ran while one was open for 8% -> 7% of each run, Pallas kernels for 0% -> 0%
where the time goes in v8:
time: 35.9 us; the launch traced here: 35.6 us
  other arithmetic  9.01 us (25%)
  starting transfers between devices  8.87 us (25%)
  local copies, waits for them, and re-layouts  8.68 us (24%)
  matrix products  6.55 us (18%)
  waiting for transfers between devices  1.44 us (4%)
  between operations  1.05 us (3%)
    dot_general x6, matrix products, apply_filter(): jnp.einsum('oi,bsirw->bsorw', weight, window_slice, preferred_element_typ...  5.67 us
    ppermute x1, starting transfers between devices, padded(): lax.ppermute(lax.slice_in_dim(block, block.shape[dim] - width, None, axis...  5.59 us
    concatenate x2, other arithmetic, apply_filter(): jnp.concatenate([padded_input[:, :, :, first_row_index + row_offset * dil...  4.6 us
    unnamed x29, local copies, waits for them, and re-layouts  4.08 us
    slice x2, local copies, waits for them, and re-layouts, apply_filter(): padded_input[:, :, :, first_row_index + row_offset * dilation_rate:first_...  2.57 us
    ppermute x1, starting transfers between devices, exchange_sum(): chunk = lax.ppermute(chunk, 'band', perm)  1.99 us
    ppermute x1, waiting for transfers between devices, exchange_sum(): chunk = lax.ppermute(chunk, 'band', perm)  1.41 us
    ppermute x1, starting transfers between devices, padded(): lax.ppermute(lax.slice_in_dim(block, 0, width, axis=dim), axis, backward)  1.29 us
  transfers between devices with their start and end apart: 3, of which 1 were waited for; matrix products, arithmetic and copies ran while one was open for 7% of the time, Pallas kernels for 0%

profile of v8, /device:TPU:0, one launch (start us, length us, event | category | flops | bytes accessed | tf_op | source)
XLA Modules:
  0.0 35.6 jit_solution(102928039470988007)
XLA Ops:
  0.6 0.0 copy-start
  0.6 0.0 copy-start.9
  0.7 0.0 copy-start.3
  0.7 0.0 copy-start.4
  0.7 0.0 copy-start.5
  0.7 0.0 copy-start.10
  0.7 0.7 %not_and_fusion = (pred[4]{0:T(512)(128)(4,1)S(1)}, pred[4]{0:T(512)(128)(4,1)S(1)}) fusion(s32[4]{0:T(128)} %param.19, s32[]{:T(128)S(6)} %add.118, s32[]{:T(128)S(6)} %mul.29, s32[4,2]{0,1:T(2,128)} %param.20), kind=kLoop, calls=%fused_computation.128 | loop fusion | flops 24 | bytes 48 | tf_op jit(solution)/shard_map/and | solution.py:109
  1.5 0.8 %compare_and_fusion.1 = (pred[4]{0:T(512)(128)(4,1)S(1)}, s32[4]{0:T(128)S(1)}, pred[4]{0:T(512)(128)(4,1)S(1)}, pred[4]{0:T(512)(128)(4,1)S(1)}, s32[4]{0:T(128...) fusion(s32[]{:T(128)S(6)} %mul.29, s32[4,2]{0,1:T(2,128)} %param.20, ...), kind=kLoop, calls=%fused_computation.123 | loop fusion | flops 124 | bytes 116 | tf_op jit(solution)/shard_map/jit(_take)/and | solution.py:124
  2.2 0.7 %fusion.82 = (f32[4]{0:T(128)S(1)}, pred[4]{0:T(512)(128)(4,1)S(1)}) fusion(s32[4]{0:T(128)} %param.19, pred[4]{0:T(512)(128)(4,1)S(1)} %get-tuple-element.51), kind=kLoop, calls=%fused_computation.137 | loop fusion | flops 16 | bytes 40 | tf_op jit(solution)/shard_map/convert_element_type | solution.py:161
  2.9 1.6 %copy.68 = bf16[2,4,16,16,128]{4,2,3,1,0:T(8,128)(2,1)S(1)} copy(f32[2,4,16,16,128]{4,3,2,1,0:T(8,128)} %param.18) | data formatting | bytes 1572864 | tf_op args[1]
  4.5 0.9 %copy.38 = bf16[2,4,2,16,128]{4,2,3,1,0:T(2,128)(2,1)S(1)} copy(bf16[2,4,2,16,128]{4,3,2,1,0:T(8,128)(2,1)} %param.17) | data formatting | bytes 131072 | tf_op args[0]
  5.4 0.2 select_reduce_fusion.1
  5.5 1.3 %collective-permute-start.1 = (bf16[2,18,3,128]{3,1,2,0:T(8,128)(2,1)S(1)}, bf16[2,18,3,128]{3,1,2,0:T(8,128)(2,1)S(1)}, u32[]{:S(2)}, u32[]{:S(2)}) collective-permute-start(bf16[2,18,3,128]{3,1,2,0:T(8,128)(2,1)S(1)} %get-tuple-element.27), channel_id=1, source_target_pairs={{4,0},{8,4},{12,8},{5,1},{9,5},{13,9},{6,2},{10,6},{14,10},{7,3},{... | collective-permute-start | bytes 82952 | tf_op jit(solution)/shard_map/ppermute | solution.py:15
  6.8 5.6 %collective-permute-start = (bf16[2,18,3,128]{3,1,2,0:T(8,128)(2,1)S(1)}, bf16[2,18,3,128]{3,1,2,0:T(8,128)(2,1)S(1)}, u32[]{:S(2)}, u32[]{:S(2)}) collective-permute-start(bf16[2,18,3,128]{3,1,2,0:T(8,128)(2,1)S(1)} %get-tuple-element.9), channel_id=1, source_target_pairs={{0,4},{4,8},{8,12},{1,5},{5,9},{9,13},{2,6},{6,10},{10,14},{3,7},{... | collective-permute-start | bytes 82952 | tf_op jit(solution)/shard_map/ppermute | solution.py:12
  12.6 0.1 pad_maximum_fusion.5
  12.7 0.6 %gather_fusion.2 = bf16[4,2,18,3,128]{4,2,3,1,0:T(8,128)(2,1)S(1)} fusion(bf16[2,4,18,3,128]{4,2,3,1,0:T(8,128)(2,1)S(1)} %get-tuple-element.28, s32[1024]{0:T(1024)S(1)} %pad_clamp_fusion.1), kind=kCustom, calls=%fused_computation.1.clone | custom fusion | bytes 221200 | tf_op jit(solution)/shard_map/jit(_take)/gather | solution.py:127
  13.3 0.6 %gather_fusion.1 = bf16[4,2,18,3,128]{4,2,3,1,0:T(8,128)(2,1)S(1)} fusion(bf16[2,4,18,3,128]{4,2,3,1,0:T(8,128)(2,1)S(1)} %get-tuple-element.10, s32[1024]{0:T(1024)S(1)} %pad_clamp_fusion.2), kind=kCustom, calls=%fused_computation.clone | custom fusion | bytes 221200 | tf_op jit(solution)/shard_map/jit(_take)/gather | solution.py:124
  13.9 0.0 collective-permute-done.1
  13.9 0.1 copy_select_fusion
  14.0 0.0 collective-permute-done
  14.0 0.4 %pad_maximum_fusion.2 = bf16[2,4,18,22,128]{4,2,3,1,0:T(8,128)(2,1)S(1)} fusion(bf16[2,4,18,3,128]{4,2,3,1,0:T(8,128)(2,1)S(1)} %copy_select_fusion, bf16[2,4,16,16,128]{4,2,3,1,0:T(8,128)(2,1)S(1)} %copy.68, bf16[2,4,2,16,128]{4,2,3,1,0:T(2,128)(2,1)S(1)} %copy.38, bf16[4,2,18,3,128]{4,2,3,1,0:T(8,128)(2,1)S(1)} %gather_fusion.1, ...), kind=kLoop, calls=%fused_computation.37 | loop fusion | flops 3409920 | bytes 1649676 | tf_op jit(solution)/shard_map/concatenate | solution.py:139
  14.4 2.2 %pad_slice_fusion.3 = (bf16[2,4,18,20,132]{4,2,3,1,0:T(8,128)(2,1)S(1)}, bf16[2,4,18,20,132]{4,2,3,1,0:T(8,128)(2,1)S(1)}, bf16[2,4,18,20,132]{4,2,3,1,0:T(8,128)(2,1)S(1)}) fusion(bf16[2,4,18,22,128]{4,2,3,1,0:T(8,128)(2,1)S(1)} %pad_maximum_fusion.2), kind=kLoop, calls=%fused_computation.10 | loop fusion | bytes 3091968 | tf_op jit(solution)/shard_map/slice | solution.py:26
  16.6 0.2 pad_slice_fusion
  16.9 2.7 %pad_maximum_fusion = bf16[2,4,54,20,132]{4,2,3,1,0:T(8,128)(2,1)S(1)} fusion(bf16[2,4,18,20,132]{4,2,3,1,0:T(8,128)(2,1)S(1)} %get-tuple-element.26, bf16[2,4,18,20,132]{4,2,3,1,0:T(8,128)(2,1)S(1)} %get-tuple-element.25, bf16[2,4,18,20,132]{4,2,3,1,0:T(8,128)(2,1)S(1)} %get-tuple-element.24), kind=kLoop, calls=%fused_computation.3 | loop fusion | flops 6842880 | bytes 4561920 | tf_op jit(solution)/shard_map/concatenate | solution.py:24
  19.5 0.9 %fusion.1 = f32[2,4,20,128,32]{3,4,2,1,0:T(8,128)S(1)} fusion(bf16[2,4,54,20,132]{4,2,3,1,0:T(8,128)(2,1)S(1)} %pad_maximum_fusion, bf16[32,18]{1,0:T(8,128)(2,1)S(1)} %get-tuple-element.30, bf16[32,18]{1,0:T(8,128)(2,1)S(1)} %get-tuple-element.31, bf16[32,18]{1,0:T(8,128)(2,1)S(1)} %get-tuple-element.32), kind=kOutput, calls=%fused_computation.12 | convolution fusion | flops 70789248 | bytes 4939776 | tf_op jit(solution)/shard_map/oi,bsirw->bsorw/dot_general | solution.py:50
  20.5 0.9 %fusion.3 = f32[2,4,20,128,32]{3,4,2,1,0:T(8,128)S(1)} fusion(bf16[2,4,54,20,132]{4,2,3,1,0:T(8,128)(2,1)S(1)} %pad_maximum_fusion, bf16[32,18]{1,0:T(8,128)(2,1)S(1)} %get-tuple-element.33, bf16[32,18]{1,0:T(8,128)(2,1)S(1)} %get-tuple-element.34, bf16[32,18]{1,0:T(8,128)(2,1)S(1)} %get-tuple-element.35), kind=kOutput, calls=%fused_computation.14 | convolution fusion | flops 70789248 | bytes 4939776 | tf_op jit(solution)/shard_map/oi,bsirw->bsorw/dot_general | solution.py:50
  21.4 1.4 %divide_bitcast_fusion = f32[2,4,32,20,128]{4,2,3,1,0:T(8,128)S(1)} fusion(f32[2,4,20,128,32]{3,4,2,1,0:T(8,128)S(1)} %fusion.1, f32[2,4,20,128,32]{3,4,2,1,0:T(8,128)S(1)} %fusion.3, bf16[2,4,54,20,132]{4,2,3,1,0:T(8,128)(2,1)S(1)} %pad_maximum_fusion, f32[32]{0:T(128)S(1)} %pad_maximum_fusion.5, bf16[32,18]{1,0:T(8,128)(2,1)S(1)} %get-tuple-element.36, ...), kind=kOutput, calls=%fused_computation.11 | convolution fusion | flops 74721408 | bytes 10183168 | tf_op jit(solution)/shard_map/oi,bsirw->bsorw/dot_general | solution.py:50
  22.8 0.3 fusion.40
  23.1 1.1 %fusion.7 = bf16[2,4,18,20,132]{4,2,3,1,0:T(8,128)(2,1)S(1)} fusion(bf16[2,4,16,20,128]{4,2,3,1,0:T(8,128)(2,1)S(1)} %fusion.40, bf16[2,4,2,20,132]{4,2,3,1,0:T(2,128)(2,1)S(1)} %pad_slice_fusion), kind=kLoop, calls=%fused_computation.18 | loop fusion | flops 2280960 | bytes 1500160 | tf_op jit(solution)/shard_map/concatenate | solution.py:157
  24.2 0.4 %fusion.90 = (bf16[2,4,18,16,132]{4,2,3,1,0:T(8,128)(2,1)S(1)}, bf16[2,4,18,16,132]{4,2,3,1,0:T(8,128)(2,1)S(1)}, bf16[2,4,18,16,132]{4,2,3,1,0:T(8,128)(2,1)S(1)}) fusion(bf16[2,4,18,20,132]{4,2,3,1,0:T(8,128)(2,1)S(1)} %fusion.7), kind=kLoop, calls=%fused_computation.145 | loop fusion | bytes 3649536 | tf_op jit(solution)/shard_map/slice | solution.py:26
  24.7 1.9 %pad_maximum_fusion.1 = bf16[2,4,54,16,132]{4,2,3,1,0:T(8,128)(2,1)S(1)} fusion(bf16[2,4,18,16,132]{4,2,3,1,0:T(8,128)(2,1)S(1)} %get-tuple-element.22, bf16[2,4,18,16,132]{4,2,3,1,0:T(8,128)(2,1)S(1)} %get-tuple-element.23, bf16[2,4,18,16,132]{4,2,3,1,0:T(8,128)(2,1)S(1)} %get-tuple-element.21), kind=kLoop, calls=%fused_computation.6 | loop fusion | flops 5474304 | bytes 3649536 | tf_op jit(solution)/shard_map/concatenate | solution.py:24
  26.6 0.0 copy-start.1
  26.6 0.0 copy-start.7
  26.6 0.8 %fusion.8 = f32[2,4,16,128,16]{3,4,2,1,0:T(8,128)S(1)} fusion(bf16[2,4,54,16,132]{4,2,3,1,0:T(8,128)(2,1)S(1)} %pad_maximum_fusion.1, bf16[16,18]{1,0:T(8,128)(2,1)S(1)} %get-tuple-element.45, bf16[16,18]{1,0:T(8,128)(2,1)S(1)} %get-tuple-element.46, bf16[16,18]{1,0:T(8,128)(2,1)S(1)} %get-tuple-element.39), kind=kOutput, calls=%fused_computation.19 | convolution fusion | flops 28316736 | bytes 2895872 | tf_op jit(solution)/shard_map/oi,bsirw->bsorw/dot_general | solution.py:50
  27.4 0.8 %fusion.10 = f32[2,4,16,128,16]{3,4,2,1,0:T(8,128)S(1)} fusion(bf16[2,4,54,16,132]{4,2,3,1,0:T(8,128)(2,1)S(1)} %pad_maximum_fusion.1, bf16[16,18]{1,0:T(8,128)(2,1)S(1)} %get-tuple-element.40, bf16[16,18]{1,0:T(8,128)(2,1)S(1)} %get-tuple-element.41, bf16[16,18]{1,0:T(8,128)(2,1)S(1)} %get-tuple-element.42), kind=kOutput, calls=%fused_computation.21 | convolution fusion | flops 28316736 | bytes 2895872 | tf_op jit(solution)/shard_map/oi,bsirw->bsorw/dot_general | solution.py:50
  28.1 0.9 %fusion.91 = (f32[4,16,16,128]{3,1,2,0:T(8,128)S(1)}, f32[2,4,16,16,128]{4,2,3,1,0:T(8,128)S(1)}) fusion(f32[4]{0:T(128)S(1)} %get-tuple-element.52, f32[16]{0:T(128)S(1)} %copy-done.7, f32[2,4,16,128,16]{3,4,2,1,0:T(8,128)S(1)} %fusion.8, f32[2,4,16,128,16]{3,4,2,1,0:T(8,128)S(1)} %fusion.10, bf16[16,18]{1,0:T(8,128)(2,1)S(1)} %get-tuple-element.43, ...), kind=kOutput, calls=%fused_computation.146 | convolution fusion | flops 30544960 | bytes 7615488 | tf_op jit(solution)/shard_map/oi,bsirw->bsorw/dot_general | solution.py:50
  29.0 0.0 copy-start.2
  29.1 0.0 copy-start.6
  29.1 0.0 copy-start.8
  29.1 0.4 %convolution_reduce_fusion = f32[4,16,4,32]{3,1,2,0:T(8,128)S(1)} fusion(f32[4,16,4,4,128]{4,1,3,2,0:T(8,128)S(1)} %bitcast.140, s32[128]{0:T(128)S(1)} %and_select_fusion), kind=kOutput, calls=%fused_computation.35 | convolution fusion | flops 50360320 | bytes 557568 | tf_op jit(solution)/shard_map/schw,wj->schj/dot_general | solution.py:168
  29.5 0.6 %gather_fusion = f32[4,16,4,32]{3,1,2,0:T(8,128)S(1)} fusion(f32[4,16,4,32]{3,1,2,0:T(8,128)S(1)} %broadcast_multiply_fusion, s32[1024]{0:T(1024)S(1)} %pad_clamp_fusion), kind=kCustom, calls=%fused_computation.2 | custom fusion | bytes 65552 | tf_op jit(solution)/shard_map/jit(_take)/gather | solution.py:174
  30.0 0.3 fusion.41
  30.4 2.0 %collective-permute-start.2 = (f32[2,16,4,32]{3,1,2,0:T(8,128)S(1)}, f32[2,16,4,32]{3,1,2,0:T(8,128)S(1)}, u32[]{:S(2)}, u32[]{:S(2)}) collective-permute-start(f32[2,16,4,32]{3,1,2,0:T(8,128)S(1)} %dynamic-slice_bitcast_fusion), channel_id=1, source_target_pairs={{0,2},{2,0},{1,3},{3,1},{4,6},{6,4},{5,7},{7,5},{8,10},{10,8},{9,1... | collective-permute-start | bytes 49160 | tf_op jit(solution)/shard_map/ppermute | solution.py:71
  32.4 0.9 %copy.45 = f32[2,4,8,16,128]{4,3,2,1,0:T(8,128)} copy(f32[2,4,8,16,128]{4,2,3,1,0:T(8,128)S(1)} %constant_dynamic-slice_fusion) | data formatting | bytes 1048576
  33.3 1.4 %collective-permute-done.2 = f32[2,16,4,32]{3,1,2,0:T(8,128)S(1)} collective-permute-done((f32[2,16,4,32]{3,1,2,0:T(8,128)S(1)}, f32[2,16,4,32]{3,1,2,0:T(8,128)S(1)}, u32[]{:S(2)}, u32[]{:S(2)}) %collective-permute-start.2) | collective-permute-done | bytes 16416 | tf_op jit(solution)/shard_map/ppermute | solution.py:71
  34.7 0.0 copy-done.2
  34.7 0.2 fusion.46
  34.9 0.7 %copy.46 = f32[2,16,4,32]{3,2,1,0:T(4,128)} copy(f32[2,16,4,32]{3,1,2,0:T(8,128)S(1)} %fusion.46) | data formatting | bytes 32768
  (24 shorter events, 0.1 us)
Async XLA Ops:
  0.6 29.4 %copy-start = (f32[16,16]{1,0:T(8,128)S(1)}, f32[16,16]{1,0:T(8,128)}, u32[]{:S(2)}) copy-start(f32[16,16]{1,0:T(8,128)} %param.29) | copy-start | bytes 3076
  0.6 11.8 %copy-start.9 = (s32[1,4]{1,0:T(1,128)S(1)}, s32[1,4]{1,0:T(1,128)}, u32[]{:S(2)}) copy-start(s32[1,4]{1,0:T(1,128)} %param.21) | copy-start | bytes 52
  0.7 11.8 %copy-start.3 = (bf16[9,16,18]{2,1,0:T(8,128)(2,1)S(1)}, bf16[9,16,18]{2,1,0:T(8,128)(2,1)}, u32[]{:S(2)}) copy-start(bf16[9,16,18]{2,1,0:T(8,128)(2,1)} %param.23) | copy-start | bytes 15556
  0.7 11.8 %copy-start.4 = (bf16[9,16,18]{2,1,0:T(8,128)(2,1)S(1)}, bf16[9,16,18]{2,1,0:T(8,128)(2,1)}, u32[]{:S(2)}) copy-start(bf16[9,16,18]{2,1,0:T(8,128)(2,1)} %param.25) | copy-start | bytes 15556
  0.7 11.9 %copy-start.5 = (bf16[9,16,18]{2,1,0:T(8,128)(2,1)S(1)}, bf16[9,16,18]{2,1,0:T(8,128)(2,1)}, u32[]{:S(2)}) copy-start(bf16[9,16,18]{2,1,0:T(8,128)(2,1)} %param.27) | copy-start | bytes 15556
  0.7 11.9 %copy-start.10 = (f32[16]{0:T(128)S(1)}, f32[16]{0:T(128)}, u32[]{:S(2)}) copy-start(f32[16]{0:T(128)} %param.26) | copy-start | bytes 196
  0.7 11.9 %copy-start.11 = (f32[16]{0:T(128)S(1)}, f32[16]{0:T(128)}, u32[]{:S(2)}) copy-start(f32[16]{0:T(128)} %param.24) | copy-start | bytes 196
  5.5 8.3 %collective-permute-start.1 = (bf16[2,18,3,128]{3,1,2,0:T(8,128)(2,1)S(1)}, bf16[2,18,3,128]{3,1,2,0:T(8,128)(2,1)S(1)}, u32[]{:S(2)}, u32[]{:S(2)}) collective-permute-start(bf16[2,18,3,128]{3,1,2,0:T(8,128)(2,1)S(1)} %get-tuple-element.27), channel_id=1, source_target_pairs={{4,0},{8,4},{12,8},{5,1},{9,5},{13,9},{6,2},{10,6},{14,10},{7,3},{... | collective-permute-start | bytes 82952 | tf_op jit(solution)/shard_map/ppermute | solution.py:15
  6.8 7.2 %collective-permute-start = (bf16[2,18,3,128]{3,1,2,0:T(8,128)(2,1)S(1)}, bf16[2,18,3,128]{3,1,2,0:T(8,128)(2,1)S(1)}, u32[]{:S(2)}, u32[]{:S(2)}) collective-permute-start(bf16[2,18,3,128]{3,1,2,0:T(8,128)(2,1)S(1)} %get-tuple-element.9), channel_id=1, source_target_pairs={{0,4},{4,8},{8,12},{1,5},{5,9},{9,13},{2,6},{6,10},{10,14},{3,7},{... | collective-permute-start | bytes 82952 | tf_op jit(solution)/shard_map/ppermute | solution.py:12
  26.6 1.5 %copy-start.1 = (f32[2,4,16,16,128]{4,3,2,1,0:T(8,128)S(1)}, f32[2,4,16,16,128]{4,3,2,1,0:T(8,128)}, u32[]{:S(2)}) copy-start(f32[2,4,16,16,128]{4,3,2,1,0:T(8,128)} %param.18) | copy-start | bytes 3145732
  26.6 1.5 %copy-start.7 = (f32[16]{0:T(128)S(1)}, f32[16]{0:T(128)}, u32[]{:S(2)}) copy-start(f32[16]{0:T(128)} %param.28) | copy-start | bytes 196
  29.0 5.7 %copy-start.2 = (f32[2,16,4,32]{3,2,1,0:T(4,128)S(1)}, f32[2,16,4,32]{3,2,1,0:T(4,128)}, u32[]{:S(2)}) copy-start(f32[2,16,4,32]{3,2,1,0:T(4,128)} %param.22) | copy-start | bytes 49156
  29.1 5.7 %copy-start.6 = (f32[16,16]{1,0:T(8,128)S(1)}, f32[16,16]{1,0:T(8,128)}, u32[]{:S(2)}) copy-start(f32[16,16]{1,0:T(8,128)} %param.30) | copy-start | bytes 3076
  29.1 5.7 %copy-start.8 = (f32[16]{0:T(128)S(1)}, f32[16]{0:T(128)}, u32[]{:S(2)}) copy-start(f32[16]{0:T(128)} %param.31) | copy-start | bytes 196
  30.4 4.3 %collective-permute-start.2 = (f32[2,16,4,32]{3,1,2,0:T(8,128)S(1)}, f32[2,16,4,32]{3,1,2,0:T(8,128)S(1)}, u32[]{:S(2)}, u32[]{:S(2)}) collective-permute-start(f32[2,16,4,32]{3,1,2,0:T(8,128)S(1)} %dynamic-slice_bitcast_fusion), channel_id=1, source_target_pairs={{0,2},{2,0},{1,3},{3,1},{4,6},{6,4},{5,7},{7,5},{8,10},{10,8},{9,1... | collective-permute-start | bytes 49160 | tf_op jit(solution)/shard_map/ppermute | solution.py:71

commit v9 on v7

--- a/solution.py
+++ b/solution.py
@@ -2,6 +2,7 @@
 import jax.numpy as jnp
 from jax import lax
 from jax.sharding import PartitionSpec as P
+from jax.experimental import pallas as pl
 
 
 def padded(block, sides, width):
@@ -44,6 +45,45 @@
             )
             total = term if total is None else total + term
     return total
+
+
+PADW = 132
+WIDE = 2688
+OUT = 2176
+MARGIN = 128
+
+
+def gru_kernel(x_ref, wg_ref, bg_ref, wcf_ref, wcg_ref, bc_ref, upd_ref, cand_ref):
+    width = PADW
+    x = x_ref[0]
+    acc = None
+    for a in (-1, 0, 1):
+        for b in (-1, 0, 1):
+            off = (1 + a) * width + 2 + b
+            term = jnp.dot(
+                wg_ref[(a + 1) * 3 + (b + 1)], x[:, off : off + WIDE],
+                preferred_element_type=jnp.float32,
+            )
+            acc = term if acc is None else acc + term
+    gates = jax.nn.sigmoid(acc + bg_ref[...])
+    chans = gates.shape[0] // 2
+    hidden = x[:chans, width + 2 : width + 2 + WIDE].astype(jnp.float32)
+    col = lax.broadcasted_iota(jnp.int32, (chans, WIDE), 1) % width
+    gated = jnp.where(col < width - 4, gates[chans:] * hidden, 0.0).astype(jnp.bfloat16)
+    edge = jnp.zeros((chans, MARGIN), jnp.bfloat16)
+    gm = jnp.concatenate([edge, gated, edge], axis=1)
+    cacc = None
+    for a in (-1, 0, 1):
+        for b in (-1, 0, 1):
+            tap = (a + 1) * 3 + (b + 1)
+            xo = (3 + 2 * a) * width + 2 + 2 * b
+            go = MARGIN + (2 + 2 * a) * width + 2 * b
+            term = jnp.dot(
+                wcf_ref[tap], x[:, xo : xo + OUT], preferred_element_type=jnp.float32
+            ) + jnp.dot(wcg_ref[tap], gm[:, go : go + OUT], preferred_element_type=jnp.float32)
+            cacc = term if cacc is None else cacc + term
+    cand_ref[0] = jnp.tanh(cacc + bc_ref[...])
+    upd_ref[0] = gates[:chans, 2 * width : 2 * width + OUT]
 
 
 def choose_rows(block, select):
@@ -130,19 +170,59 @@
     )
     full = jnp.concatenate([top, joined, bottom], axis=3)
     first = jnp.pad(full, ((0, 0), (0, 0), (0, 0), (0, 0), (2, 2)))
-    update = jax.nn.sigmoid(
-        apply_filter(first, w_update, 1, 3, row_count, column_count) + b_update[:, None, None]
-    )
-    hidden_wide = first[:, :, inputs_count:, 1 : row_count + 5, 2 : column_count + 2]
-    reset = jax.nn.sigmoid(
-        apply_filter(first, w_reset, 1, 1, row_count + 4, column_count) + b_reset[:, None, None]
-    )
-    gated = (reset * hidden_wide.astype(jnp.float32)).astype(jnp.bfloat16)
-    gated_pad = jnp.pad(gated, ((0, 0), (0, 0), (0, 0), (0, 0), (2, 2)))
-    second = jnp.concatenate([first[:, :, :inputs_count, 1 : row_count + 5, :], gated_pad], axis=2)
-    candidate = jnp.tanh(
-        apply_filter(second, w_cand, 2, 2, row_count, column_count) + b_cand[:, None, None]
-    )
+    band_local = first.shape[0]
+    images = band_local * slots
+    width = column_count + 4
+    rows_first = row_count + 6
+    cpad = 2 * chans
+    reordered = jnp.concatenate(
+        [first[:, :, inputs_count:], first[:, :, :inputs_count]], axis=2
+    ).reshape(images, chans + inputs_count, rows_first * width)
+    length = 128 * ((rows_first * width + 2 * width + 128) // 128)
+    xin = jnp.pad(
+        reordered,
+        ((0, 0), (0, cpad - chans - inputs_count), (0, length - rows_first * width)),
+    )
+
+    def in_order(weight):
+        moved = jnp.concatenate([weight[:, :, inputs_count:], weight[:, :, :inputs_count]], axis=2)
+        return jnp.pad(moved, ((0, 0), (0, 0), (0, cpad - chans - inputs_count)))
+
+    wg = jnp.concatenate([in_order(w_update), in_order(w_reset)], axis=1)
+    bg = jnp.concatenate([b_update, b_reset])[:, None]
+    wcf = jnp.pad(
+        w_cand[:, :, :inputs_count], ((0, 0), (0, 0), (chans, cpad - chans - inputs_count))
+    )
+    wcg = w_cand[:, :, inputs_count:]
+    bc = b_cand[:, None]
+    full_spec = lambda shape: pl.BlockSpec(shape, lambda n: (0,) * len(shape))
+    upd, cand = pl.pallas_call(
+        gru_kernel,
+        grid=(images,),
+        in_specs=[
+            pl.BlockSpec((1, cpad, length), lambda n: (n, 0, 0)),
+            full_spec(wg.shape),
+            full_spec(bg.shape),
+            full_spec(wcf.shape),
+            full_spec(wcg.shape),
+            full_spec(bc.shape),
+        ],
+        out_specs=[
+            pl.BlockSpec((1, chans, OUT), lambda n: (n, 0, 0)),
+            pl.BlockSpec((1, chans, OUT), lambda n: (n, 0, 0)),
+        ],
+        out_shape=[
+            jax.ShapeDtypeStruct((images, chans, OUT), jnp.float32),
+            jax.ShapeDtypeStruct((images, chans, OUT), jnp.float32),
+        ],
+    )(xin, wg, bg, wcf, wcg, bc)
+
+    def unflat(v):
+        v = v[:, :, : row_count * width].reshape(images, chans, row_count, width)
+        return v[..., :column_count].reshape(band_local, slots, chans, row_count, column_count)
+
+    update = unflat(upd)
+    candidate = unflat(cand)
     live_scale = alive.astype(jnp.float32)[None, :, None, None, None]
     new_state = ((1.0 - update) * state + update * candidate) * live_scale
     new_half = lax.dynamic_slice_in_dim(new_state, start, half, 2)

time: 35.4 us -> 58.9 us (1.66)
  local copies, waits for them, and re-layouts: 6.74 us -> 21.9 us
  matrix products: 12.8 us -> 1.01 us
  Pallas kernels: 0 us -> 11.6 us
  other arithmetic: 4.09 us -> 12.7 us
    dot_general x27 -> x0, matrix products: 11.9 us -> none  [apply_filter(): jnp.einsum('oi,bsirw->bsorw', filter_weight[(left_operand + 1) * 3 + (rig...]
    pallas_call x0 -> x1, Pallas kernels: none -> 11.6 us  [shards(): pl.pallas_call(gru_kernel, grid=(images,), in_specs=[pl.BlockSpec((1, cpa...]
    reshape x0 -> x4, local copies, waits for them, and re-layouts: none -> 10.8 us  [the longest x2 8.64 us: unflat(): v = v[:, :, :row_count * width].reshape(images, chans, row_count, width)]
    concatenate x1, other arithmetic: 0.35 us -> 4.7 us  [shards(): full = jnp.concatenate([top, joined, bottom], axis=3)]
    pad x0 -> x2, local copies, waits for them, and re-layouts: none -> 1.99 us  [the longest x1 1.29 us: shards(): jnp.pad(reordered, ((0, 0), (0, cpad - chans - inputs_count), (0, length...]
    concatenate x1 -> x3, other arithmetic: 1.14 us -> 3.05 us  [the longest x1 2.3 us: shards(): jnp.concatenate([first[:, :, inputs_count:], first[:, :, :inputs_count]],...]
    slice x2 -> x5, local copies, waits for them, and re-layouts: 0.33 us -> 1.98 us  [the longest x1 0.99 us: shards(): first[:, :, inputs_count:]]
    unnamed x30 -> x29, local copies, waits for them, and re-layouts: 4.47 us -> 2.84 us
  transfers between devices with their start and end apart: 3 -> 3, of which waited for: 1 -> 1; matrix products, arithmetic and copies ran while one was open for 8% -> 11% of each run, Pallas kernels for 0% -> 0%
where the time goes in v9:
time: 58.9 us; the launch traced here: 58.6 us
  local copies, waits for them, and re-layouts  21.9 us (37%)
  other arithmetic  12.7 us (22%)
  Pallas kernels  11.6 us (20%)
  starting transfers between devices  8.85 us (15%)
  waiting for transfers between devices  1.52 us (3%)
  matrix products  1.01 us (2%)
  between operations  1 us (2%)
    pallas_call x1, Pallas kernels, shards(): pl.pallas_call(gru_kernel, grid=(images,), in_specs=[pl.BlockSpec((1, cpa...  11.6 us
    reshape x2, local copies, waits for them, and re-layouts, unflat(): v = v[:, :, :row_count * width].reshape(images, chans, row_count, width)  8.64 us
    ppermute x1, starting transfers between devices, padded(): lax.ppermute(lax.slice_in_dim(block, block.shape[dim] - width, None, axis...  5.59 us
    concatenate x1, other arithmetic, shards(): full = jnp.concatenate([top, joined, bottom], axis=3)  4.7 us
    unnamed x29, local copies, waits for them, and re-layouts  2.84 us
    concatenate x1, other arithmetic, shards(): jnp.concatenate([first[:, :, inputs_count:], first[:, :, :inputs_count]],...  2.3 us
    reshape x2, local copies, waits for them, and re-layouts, shards(): reordered = jnp.concatenate([first[:, :, inputs_count:], first[:, :, :inp...  2.11 us
    ppermute x1, starting transfers between devices, exchange_sum(): chunk = lax.ppermute(chunk, 'band', perm)  1.97 us
  transfers between devices with their start and end apart: 3, of which 1 were waited for; matrix products, arithmetic and copies ran while one was open for 11% of the time, Pallas kernels for 0%

profile of v9, /device:TPU:0, one launch (start us, length us, event | category | flops | bytes accessed | tf_op | source)
XLA Modules:
  0.0 58.6 jit_solution(17579558477209089946)
XLA Ops:
  0.6 0.0 copy-start
  0.6 0.0 copy-start.9
  0.7 0.7 %not_and_fusion = (pred[4]{0:T(512)(128)(4,1)S(1)}, pred[4]{0:T(512)(128)(4,1)S(1)}) fusion(s32[4]{0:T(128)} %param.19, s32[]{:T(128)S(6)} %add.87, s32[]{:T(128)S(6)} %mul.29, s32[4,2]{0,1:T(2,128)} %param.20), kind=kLoop, calls=%fused_computation.69 | loop fusion | flops 24 | bytes 48 | tf_op jit(solution)/shard_map/and | solution.py:141
  1.5 0.8 %compare_and_fusion.2 = (pred[4]{0:T(512)(128)(4,1)S(1)}, s32[4]{0:T(128)S(1)}, pred[4]{0:T(512)(128)(4,1)S(1)}, pred[4]{0:T(512)(128)(4,1)S(1)}, s32[4]{0:T(128...) fusion(s32[]{:T(128)S(6)} %mul.29, s32[4,2]{0,1:T(2,128)} %param.20, ...), kind=kLoop, calls=%fused_computation.64 | loop fusion | flops 124 | bytes 116 | tf_op jit(solution)/shard_map/jit(_take)/and | solution.py:156
  2.2 0.7 %not_and_fusion.1 = (pred[4]{0:T(512)(128)(4,1)S(1)}, f32[4]{0:T(128)S(1)}) fusion(pred[4]{0:T(512)(128)(4,1)S(1)} %get-tuple-element.37, s32[4]{0:T(128)} %param.19), kind=kLoop, calls=%fused_computation.70 | loop fusion | flops 16 | bytes 40 | tf_op jit(solution)/shard_map/and | solution.py:140
  2.9 2.0 %copy.64 = bf16[2,4,16,16,128]{4,0,3,2,1:T(2,128)(2,1)S(1)} copy(f32[2,4,16,16,128]{4,3,2,1,0:T(8,128)} %param.18) | data formatting | bytes 1572864 | tf_op args[1]
  5.0 0.1 copy.42
  5.0 0.4 fusion.6
  5.5 1.3 %collective-permute-start.1 = (bf16[2,18,3,128]{3,0,2,1:T(2,128)(2,1)S(1)}, bf16[2,18,3,128]{3,0,2,1:T(2,128)(2,1)S(1)}, u32[]{:S(2)}, u32[]{:S(2)}) collective-permute-start(bf16[2,18,3,128]{3,0,2,1:T(2,128)(2,1)S(1)} %get-tuple-element.31), channel_id=1, source_target_pairs={{4,0},{8,4},{12,8},{5,1},{9,5},{13,9},{6,2},{10,6},{14,10},{7,3},{... | collective-permute-start | bytes 82952 | tf_op jit(solution)/shard_map/ppermute | solution.py:16
  6.8 5.6 %collective-permute-start = (bf16[2,18,3,128]{3,0,2,1:T(2,128)(2,1)S(1)}, bf16[2,18,3,128]{3,0,2,1:T(2,128)(2,1)S(1)}, u32[]{:S(2)}, u32[]{:S(2)}) collective-permute-start(bf16[2,18,3,128]{3,0,2,1:T(2,128)(2,1)S(1)} %get-tuple-element.17), channel_id=1, source_target_pairs={{0,4},{4,8},{8,12},{1,5},{5,9},{9,13},{2,6},{6,10},{10,14},{3,7},{... | collective-permute-start | bytes 82952 | tf_op jit(solution)/shard_map/ppermute | solution.py:13
  12.4 0.1 slice.56
  12.5 0.1 slice.58
  12.6 0.1 fusion.21
  12.7 0.7 %pad_maximum_fusion.3.wg_ref = bf16[9,32,32]{2,1,0:T(8,128)(2,1)} fusion(bf16[9,16,32]{2,1,0:T(8,128)(2,1)S(1)} %get-tuple-element.42, bf16[9,16,32]{2,1,0:T(8,128)(2,1)S(1)} %get-tuple-element.41), kind=kLoop, calls=%fused_computation.36 | loop fusion | flops 36864 | bytes 36864 | tf_op jit(solution)/shard_map/concatenate | solution.py:191
  13.4 0.1 maximum_bitcast_fusion
  13.4 0.7 %copy.45.bg_ref = f32[32,1]{1,0:T(8,128)} copy(f32[32,1]{0,1:T(1,128)S(1)} %maximum_bitcast_fusion) | data formatting | bytes 256 | tf_op jit(solution)/shard_map/broadcast_in_dim | solution.py:192
  14.1 0.7 %slice.61.wcg_ref = bf16[9,16,16]{2,1,0:T(8,128)(2,1)} slice(bf16[9,16,18]{2,1,0:T(8,128)(2,1)S(1)} %copy-done.4), slice={[0:9], [0:16], [2:18]} | slice | bytes 9216 | tf_op jit(solution)/shard_map/slice | solution.py:196
  14.8 0.7 %copy.46.bc_ref = f32[16,1]{1,0:T(8,128)} copy(f32[16,1]{0,1:T(1,128)S(1)} %bitcast.76) | data formatting | bytes 128 | tf_op jit(solution)/shard_map/broadcast_in_dim | solution.py:197
  15.5 0.8 %gather_fusion.2 = bf16[4,2,18,3,128]{4,1,3,2,0:T(2,128)(2,1)S(1)} fusion(bf16[2,4,18,3,128]{4,0,3,2,1:T(2,128)(2,1)S(1)} %get-tuple-element.32, s32[1024]{0:T(1024)S(1)} %pad_clamp_fusion.1), kind=kCustom, calls=%fused_computation.1.clone | custom fusion | bytes 221200 | tf_op jit(solution)/shard_map/jit(_take)/gather | solution.py:159
  16.3 0.8 %gather_fusion.1 = bf16[4,2,18,3,128]{4,1,3,2,0:T(2,128)(2,1)S(1)} fusion(bf16[2,4,18,3,128]{4,0,3,2,1:T(2,128)(2,1)S(1)} %get-tuple-element.18, s32[1024]{0:T(1024)S(1)} %pad_clamp_fusion.2), kind=kCustom, calls=%fused_computation.clone | custom fusion | bytes 221200 | tf_op jit(solution)/shard_map/jit(_take)/gather | solution.py:156
  17.0 0.7 %pad.23.wcf_ref = bf16[9,16,32]{2,1,0:T(8,128)(2,1)} pad(bf16[9,16,2]{2,1,0:T(8,128)(2,1)S(1)} %bitcast.75, bf16[]{:T(256)} %constant.77.clone.1), padding=0_0x0_0x16_14 | pad | bytes 9794 | tf_op jit(solution)/shard_map/jit(_pad)/pad | solution.py:193
  17.7 0.0 collective-permute-done.1
  17.8 0.2 broadcast_select_fusion
  17.9 0.0 collective-permute-done
  18.0 0.2 broadcast_select_fusion.1
  18.2 4.7 %select_maximum_fusion = bf16[2,4,18,22,132]{4,0,3,2,1:T(2,128)(2,1)S(1)} fusion(bf16[2,4,18,3,128]{4,0,3,2,1:T(2,128)(2,1)S(1)} %broadcast_select_fusion, bf16[2,4,18,3,128]{4,0,3,2,1:T(2,128)(2,1)S(1)} %broadcast_select_fusion.1, bf16[2,4,16,16,128]{4,0,3,2,1:T(2,128)(2,1)S(1)} %copy.64, bf16[2,4,2,16,128]{4,0,3,2,1:T(2,128)(2,1)S(1)} %copy.42), kind=kLoop, calls=%fused_computation.4 | loop fusion | flops 6272640 | bytes 1647360 | tf_op jit(solution)/shard_map/concatenate | solution.py:171
  22.9 0.1 slice.73
  23.0 1.0 %slice.72 = bf16[2,4,16,22,132]{4,0,3,2,1:T(2,128)(2,1)S(1)} slice(bf16[2,4,18,22,132]{4,0,3,2,1:T(2,128)(2,1)S(1)} %select_maximum_fusion), slice={[0:2], [0:4], [2:18], [0:22], [0:132]} | slice | bytes 1486848 | tf_op jit(solution)/shard_map/slice | solution.py:179
  24.0 2.3 %pad_maximum_fusion = bf16[2,4,18,22,132]{4,0,3,2,1:T(2,128)(2,1)S(1)} fusion(bf16[2,4,2,22,132]{4,0,3,2,1:T(2,128)(2,1)S(1)} %slice.73, bf16[2,4,16,22,132]{4,0,3,2,1:T(2,128)(2,1)S(1)} %slice.72), kind=kLoop, calls=%fused_computation.9 | loop fusion | flops 418176 | bytes 1672704 | tf_op jit(solution)/shard_map/concatenate | solution.py:178
  26.3 0.3 copy.54
  26.6 1.9 %reshape.204 = bf16[8,18,2904]{2,1,0:T(8,128)(2,1)S(1)} reshape(bf16[2,4,18,22,132]{4,3,2,1,0:T(8,128)(2,1)S(1)} %copy.54) | data formatting | bytes 1672704 | tf_op jit(solution)/shard_map/reshape | solution.py:180
  28.4 1.3 %pad.20.x_ref = bf16[8,32,3200]{2,1,0:T(8,128)(2,1)} pad(bf16[8,18,2904]{2,1,0:T(8,128)(2,1)S(1)} %reshape.204, bf16[]{:T(256)} %constant.77.clone.1), padding=0_0x0_14x0_296 | pad | bytes 2474754 | tf_op jit(solution)/shard_map/jit(_pad)/pad | solution.py:182
  29.7 11.6 %shard_map.158 = (f32[8,16,2176]{2,1,0:T(8,128)}, f32[8,16,2176]{2,1,0:T(8,128)}) custom-call(bf16[8,32,3200]{2,1,0:T(8,128)(2,1)} %pad.20.x_ref, bf16[9,32,32]{2,1,0:T(8,128)(2,1)} %pad_maximum_fusion.3.wg_ref, f32[32,1]{1,0:T(8,128)} %copy.45.bg_ref, bf16[9,16,32]{2,1,0:T(8,128)(2,1)} %pad.23.wcf_ref, bf16[9,16,16]{2,1,0:T(8,128)(2,1)} %slice.61.wcg_ref, ...), custom_call_target="tpu_custom_call" | custom-call | tf_op jit(solution)/shard_map/pallas_call | solution.py:199
  41.3 3.9 %reshape.169 = f32[8,16,16,132]{3,2,1,0:T(8,128)S(1)} reshape(f32[8,16,2112]{2,1,0:T(8,128)} %bitcast.72) | data formatting | bytes 2162688 | tf_op jit(solution)/shard_map/reshape | solution.py:221
  45.2 4.8 %reshape.170 = f32[8,16,16,132]{3,2,1,0:T(8,128)} reshape(f32[8,16,2112]{2,1,0:T(8,128)} %bitcast.71) | data formatting | bytes 2162688 | tf_op jit(solution)/shard_map/reshape | solution.py:221
  50.0 1.5 %slice_subtract_fusion = (f32[8,16,16,128]{3,2,1,0:T(8,128)S(1)}, f32[8,16,16,128]{3,2,1,0:T(8,128)S(1)}) fusion(f32[8,16,16,132]{3,2,1,0:T(8,128)S(1)} %reshape.169, f32[8,16,16,132]{3,2,1,0:T(8,128)} %reshape.170), kind=kLoop, calls=%fused_computation.15 | loop fusion | flops 524288 | bytes 4194304 | tf_op jit(solution)/shard_map/sub | solution.py:227
  51.5 0.3 fusion.31
  51.9 0.0 copy-start.6
  51.9 0.0 copy-start.7
  51.9 0.0 copy-start.8
  51.9 0.5 convolution_reduce_fusion
  52.5 0.6 gather_fusion
  53.0 0.3 fusion.4
  53.4 2.0 %collective-permute-start.2 = (f32[2,16,4,32]{3,1,2,0:T(8,128)S(1)}, f32[2,16,4,32]{3,1,2,0:T(8,128)S(1)}, u32[]{:S(2)}, u32[]{:S(2)}) collective-permute-start(f32[2,16,4,32]{3,1,2,0:T(8,128)S(1)} %dynamic-slice_bitcast_fusion), channel_id=1, source_target_pairs={{0,2},{2,0},{1,3},{3,1},{4,6},{6,4},{5,7},{7,5},{8,10},{10,8},{9,1... | collective-permute-start | bytes 49160 | tf_op jit(solution)/shard_map/ppermute | solution.py:103
  55.3 0.8 %constant_dynamic-slice_fusion = f32[2,4,8,16,128]{4,3,2,1,0:T(8,128)} fusion(f32[2,4,16,16,128]{4,3,2,1,0:T(8,128)S(1)} %get-tuple-element.16, s32[]{:T(128)S(6)} %select_n.81), kind=kLoop, calls=%fused_computation.74 | loop fusion | bytes 1048580 | tf_op jit(solution)/shard_map/dynamic_slice | solution.py:228
  56.2 1.5 %collective-permute-done.2 = f32[2,16,4,32]{3,1,2,0:T(8,128)S(1)} collective-permute-done((f32[2,16,4,32]{3,1,2,0:T(8,128)S(1)}, f32[2,16,4,32]{3,1,2,0:T(8,128)S(1)}, u32[]{:S(2)}, u32[]{:S(2)}) %collective-permute-start.2) | collective-permute-done | bytes 16416 | tf_op jit(solution)/shard_map/ppermute | solution.py:103
  57.7 0.2 fusion.15
  57.9 0.7 %copy.50 = f32[2,16,4,32]{3,2,1,0:T(4,128)} copy(f32[2,16,4,32]{3,1,2,0:T(8,128)S(1)} %fusion.15) | data formatting | bytes 32768
  (28 shorter events, 0.1 us)
Async XLA Ops:
  0.6 52.4 %copy-start = (f32[16,16]{1,0:T(8,128)S(1)}, f32[16,16]{1,0:T(8,128)}, u32[]{:S(2)}) copy-start(f32[16,16]{1,0:T(8,128)} %param.29) | copy-start | bytes 3076
  0.6 11.7 %copy-start.9 = (s32[1,4]{1,0:T(1,128)S(1)}, s32[1,4]{1,0:T(1,128)}, u32[]{:S(2)}) copy-start(s32[1,4]{1,0:T(1,128)} %param.21) | copy-start | bytes 52
  0.7 4.3 %copy-start.5 = (bf16[2,4,2,16,128]{4,3,2,1,0:T(8,128)(2,1)S(1)}, bf16[2,4,2,16,128]{4,3,2,1,0:T(8,128)(2,1)}, u32[]{:S(2)}) copy-start(bf16[2,4,2,16,128]{4,3,2,1,0:T(8,128)(2,1)} %param.17) | copy-start | bytes 196612
  0.7 11.7 %copy-start.2 = (bf16[9,16,18]{2,1,0:T(8,128)(2,1)S(1)}, bf16[9,16,18]{2,1,0:T(8,128)(2,1)}, u32[]{:S(2)}) copy-start(bf16[9,16,18]{2,1,0:T(8,128)(2,1)} %param.23) | copy-start | bytes 15556
  0.7 11.8 %copy-start.3 = (bf16[9,16,18]{2,1,0:T(8,128)(2,1)S(1)}, bf16[9,16,18]{2,1,0:T(8,128)(2,1)}, u32[]{:S(2)}) copy-start(bf16[9,16,18]{2,1,0:T(8,128)(2,1)} %param.25) | copy-start | bytes 15556
  0.7 12.7 %copy-start.11 = (f32[16]{0:T(128)S(1)}, f32[16]{0:T(128)}, u32[]{:S(2)}) copy-start(f32[16]{0:T(128)} %param.26) | copy-start | bytes 196
  0.7 12.7 %copy-start.12 = (f32[16]{0:T(128)S(1)}, f32[16]{0:T(128)}, u32[]{:S(2)}) copy-start(f32[16]{0:T(128)} %param.24) | copy-start | bytes 196
  0.7 13.4 %copy-start.4 = (bf16[9,16,18]{2,1,0:T(8,128)(2,1)S(1)}, bf16[9,16,18]{2,1,0:T(8,128)(2,1)}, u32[]{:S(2)}) copy-start(bf16[9,16,18]{2,1,0:T(8,128)(2,1)} %param.27) | copy-start | bytes 15556
  2.9 11.9 %copy-start.10 = (f32[16]{0:T(128)S(1)}, f32[16]{0:T(128)}, u32[]{:S(2)}) copy-start(f32[16]{0:T(128)} %param.28) | copy-start | bytes 196
  5.5 12.3 %collective-permute-start.1 = (bf16[2,18,3,128]{3,0,2,1:T(2,128)(2,1)S(1)}, bf16[2,18,3,128]{3,0,2,1:T(2,128)(2,1)S(1)}, u32[]{:S(2)}, u32[]{:S(2)}) collective-permute-start(bf16[2,18,3,128]{3,0,2,1:T(2,128)(2,1)S(1)} %get-tuple-element.31), channel_id=1, source_target_pairs={{4,0},{8,4},{12,8},{5,1},{9,5},{13,9},{6,2},{10,6},{14,10},{7,3},{... | collective-permute-start | bytes 82952 | tf_op jit(solution)/shard_map/ppermute | solution.py:16
  6.8 11.2 %collective-permute-start = (bf16[2,18,3,128]{3,0,2,1:T(2,128)(2,1)S(1)}, bf16[2,18,3,128]{3,0,2,1:T(2,128)(2,1)S(1)}, u32[]{:S(2)}, u32[]{:S(2)}) collective-permute-start(bf16[2,18,3,128]{3,0,2,1:T(2,128)(2,1)S(1)} %get-tuple-element.17), channel_id=1, source_target_pairs={{0,4},{4,8},{8,12},{1,5},{5,9},{9,13},{2,6},{6,10},{10,14},{3,7},{... | collective-permute-start | bytes 82952 | tf_op jit(solution)/shard_map/ppermute | solution.py:13
  50.0 1.6 %copy-start.1 = (f32[2,4,16,16,128]{4,3,2,1,0:T(8,128)S(1)}, f32[2,4,16,16,128]{4,3,2,1,0:T(8,128)}, u32[]{:S(2)}) copy-start(f32[2,4,16,16,128]{4,3,2,1,0:T(8,128)} %param.18) | copy-start | bytes 3145732
  51.9 5.8 %copy-start.6 = (f32[2,16,4,32]{3,2,1,0:T(4,128)S(1)}, f32[2,16,4,32]{3,2,1,0:T(4,128)}, u32[]{:S(2)}) copy-start(f32[2,16,4,32]{3,2,1,0:T(4,128)} %param.22) | copy-start | bytes 49156
  51.9 5.8 %copy-start.7 = (f32[16,16]{1,0:T(8,128)S(1)}, f32[16,16]{1,0:T(8,128)}, u32[]{:S(2)}) copy-start(f32[16,16]{1,0:T(8,128)} %param.30) | copy-start | bytes 3076
  51.9 5.8 %copy-start.8 = (f32[16]{0:T(128)S(1)}, f32[16]{0:T(128)}, u32[]{:S(2)}) copy-start(f32[16]{0:T(128)} %param.31) | copy-start | bytes 196
  53.4 4.3 %collective-permute-start.2 = (f32[2,16,4,32]{3,1,2,0:T(8,128)S(1)}, f32[2,16,4,32]{3,1,2,0:T(8,128)S(1)}, u32[]{:S(2)}, u32[]{:S(2)}) collective-permute-start(f32[2,16,4,32]{3,1,2,0:T(8,128)S(1)} %dynamic-slice_bitcast_fusion), channel_id=1, source_target_pairs={{0,2},{2,0},{1,3},{3,1},{4,6},{6,4},{5,7},{7,5},{8,10},{10,8},{9,1... | collective-permute-start | bytes 49160 | tf_op jit(solution)/shard_map/ppermute | solution.py:103

commit v10 on v7

--- a/solution.py
+++ b/solution.py
@@ -49,6 +49,13 @@
 def choose_rows(block, select):
     masked = jnp.where(select[None, :, None, None, None], block, jnp.zeros_like(block))
     return jnp.sum(masked, axis=1)
+
+
+def pick_rows(rows, index):
+    slots = rows.shape[1]
+    hits = index[:, None] == jnp.arange(slots)[None, :]
+    chosen = jnp.where(hits[None, :, :, None, None, None], rows[:, None], jnp.zeros_like(rows[:, None]))
+    return jnp.sum(chosen, axis=2)
 
 
 def exchange_sum(part, owned):
@@ -113,10 +120,8 @@
     cycle = padded(jnp.concatenate([top, bottom], axis=2), (("tiles", 2),), 3)
     cycle_prev = cycle[:, None, :, :3, :]
     cycle_next = cycle[:, None, :, 3 * 3 : 4 * 3, :]
-    top_local = jnp.take(
-        joined[:, :, :, row_count - 3 :, :], jnp.clip(ups - base, 0, slots - 1), axis=1
-    )
-    bottom_local = jnp.take(joined[:, :, :, :3, :], jnp.clip(downs - base, 0, slots - 1), axis=1)
+    top_local = pick_rows(joined[:, :, :, row_count - 3 :, :], ups - base)
+    bottom_local = pick_rows(joined[:, :, :, :3, :], downs - base)
     zeros_rows = jnp.zeros_like(top_local)
     top = jnp.where(
         up_here[None, :, None, None, None],

time: 35.4 us -> 35.6 us (level)
  other arithmetic: 4.09 us -> 5.49 us
  local copies, waits for them, and re-layouts: 6.74 us -> 5.53 us
    gather x2 -> x0, local copies, waits for them, and re-layouts: 1.35 us -> none  [the longest x1 0.77 us: shards(): jnp.take(joined[:, :, :, row_count - 3:, :], jnp.clip(ups - base, 0, slot...]
    reduce_sum x0 -> x2, other arithmetic: none -> 1.3 us  [pick_rows(): return jnp.sum(chosen, axis=2)]
    unnamed x30 -> x32, local copies, waits for them, and re-layouts: 4.47 us -> 4.59 us
where the time goes in v10:
time: 35.6 us; the launch traced here: 35.2 us
  matrix products  12.8 us (36%)
  starting transfers between devices  8.87 us (25%)
  local copies, waits for them, and re-layouts  5.53 us (16%)
  other arithmetic  5.49 us (15%)
  waiting for transfers between devices  1.42 us (4%)
  between operations  1.13 us (3%)
    dot_general x27, matrix products, apply_filter(): jnp.einsum('oi,bsirw->bsorw', filter_weight[(left_operand + 1) * 3 + (rig...  11.9 us
    ppermute x1, starting transfers between devices, padded(): lax.ppermute(lax.slice_in_dim(block, block.shape[dim] - width, None, axis...  5.59 us
    unnamed x32, local copies, waits for them, and re-layouts  4.59 us
    ppermute x1, starting transfers between devices, exchange_sum(): chunk = lax.ppermute(chunk, 'band', perm)  1.99 us
    ppermute x1, waiting for transfers between devices, exchange_sum(): chunk = lax.ppermute(chunk, 'band', perm)  1.41 us
    reduce_sum x2, other arithmetic, pick_rows(): return jnp.sum(chosen, axis=2)  1.3 us
    ppermute x1, starting transfers between devices, padded(): lax.ppermute(lax.slice_in_dim(block, 0, width, axis=dim), axis, backward)  1.29 us
    concatenate x1, other arithmetic, shards(): jnp.concatenate([first[:, :, :inputs_count, 1:row_count + 5, :], gated_pa...  1.14 us
  transfers between devices with their start and end apart: 3, of which 1 were waited for; matrix products, arithmetic and copies ran while one was open for 8% of the time, Pallas kernels for 0%

profile of v10, /device:TPU:0, one launch (start us, length us, event | category | flops | bytes accessed | tf_op | source)
XLA Modules:
  0.0 35.2 jit_solution(17036133893682085891)
XLA Ops:
  0.7 0.7 %not_and_fusion = (pred[4]{0:T(512)(128)(4,1)S(1)}, pred[4]{0:T(512)(128)(4,1)S(1)}) fusion(s32[4]{0:T(128)} %param.17, s32[]{:T(128)S(6)} %add.198, s32[]{:T(128)S(6)} %mul.29, s32[4,2]{0,1:T(2,128)} %param.18), kind=kLoop, calls=%fused_computation.188 | loop fusion | flops 24 | bytes 48 | tf_op jit(solution)/shard_map/and | solution.py:108
  1.4 0.8 %bitcast_and_fusion.1 = (pred[4]{0:T(512)(128)(4,1)S(1)}, pred[4]{0:T(512)(128)(4,1)S(1)}, pred[4]{0:T(512)(128)(4,1)S(1)}, pred[4]{0:T(512)(128)(4,1)S(1)}) fusion(s32[4,2]{0,1:T(2,128)} %param.18, s32[]{:T(128)S(6)} %add.198, s32[]{:T(128)S(6)} %mul.29, pred[4]{0:T(512)(128)(4,1)S(1)} %get-tuple-element.13, s32[1,4]{1,0:T(1,128)} %param.19), kind=kLoop, calls=%fused_computation.183 | loop fusion | flops 60 | bytes 76 | tf_op jit(solution)/shard_map/and | solution.py:104
  2.2 0.7 %fusion.133 = (f32[4]{0:T(128)S(1)}, pred[4]{0:T(512)(128)(4,1)S(1)}) fusion(s32[4]{0:T(128)} %param.17, pred[4]{0:T(512)(128)(4,1)S(1)} %get-tuple-element.15), kind=kLoop, calls=%fused_computation.198 | loop fusion | flops 16 | bytes 40 | tf_op jit(solution)/shard_map/convert_element_type | solution.py:151
  2.8 1.6 %copy.94 = bf16[2,4,16,16,128]{4,2,3,1,0:T(8,128)(2,1)S(1)} copy(f32[2,4,16,16,128]{4,3,2,1,0:T(8,128)} %param.16) | data formatting | bytes 1572864 | tf_op args[1]
  4.7 1.3 %collective-permute-start.1 = (bf16[2,18,3,128]{3,1,2,0:T(8,128)(2,1)S(1)}, bf16[2,18,3,128]{3,1,2,0:T(8,128)(2,1)S(1)}, u32[]{:S(2)}, u32[]{:S(2)}) collective-permute-start(bf16[2,18,3,128]{3,1,2,0:T(8,128)(2,1)S(1)} %get-tuple-element.18), channel_id=1, source_target_pairs={{4,0},{8,4},{12,8},{5,1},{9,5},{13,9},{6,2},{10,6},{14,10},{7,3},{... | collective-permute-start | bytes 82952 | tf_op jit(solution)/shard_map/ppermute | solution.py:15
  6.0 5.6 %collective-permute-start = (bf16[2,18,3,128]{3,1,2,0:T(8,128)(2,1)S(1)}, bf16[2,18,3,128]{3,1,2,0:T(8,128)(2,1)S(1)}, u32[]{:S(2)}, u32[]{:S(2)}) collective-permute-start(bf16[2,18,3,128]{3,1,2,0:T(8,128)(2,1)S(1)} %get-tuple-element.10), channel_id=1, source_target_pairs={{0,4},{4,8},{8,12},{1,5},{5,9},{9,13},{2,6},{6,10},{10,14},{3,7},{... | collective-permute-start | bytes 82952 | tf_op jit(solution)/shard_map/ppermute | solution.py:12
  11.9 0.3 fusion.55
  12.2 0.7 %select_reduce_fusion = bf16[2,4,18,3,128]{4,3,2,1,0:T(4,128)(2,1)S(1)} fusion(pred[4,4]{1,0:T(4,128)(4,1)S(1)} %iota_compare_fusion.2, bf16[2,4,18,3,128]{4,1,3,2,0:T(4,128)(2,1)S(1)} %copy.48), kind=kLoop, calls=%fused_computation.95 | loop fusion | flops 387072 | bytes 221200 | tf_op jit(solution)/shard_map/reduce_sum | solution.py:58
  12.9 0.7 %select_reduce_fusion.1 = bf16[2,4,18,3,128]{4,3,2,1,0:T(4,128)(2,1)S(1)} fusion(pred[4,4]{1,0:T(4,128)(4,1)S(1)} %iota_compare_fusion.3, bf16[2,4,18,3,128]{4,1,3,2,0:T(4,128)(2,1)S(1)} %copy.46), kind=kLoop, calls=%fused_computation.96 | loop fusion | flops 387072 | bytes 221200 | tf_op jit(solution)/shard_map/reduce_sum | solution.py:58
  13.8 0.3 pad_maximum_fusion
  14.2 0.4 %fusion.44 = f32[2,4,16,128,16]{3,4,2,1,0:T(8,128)S(1)} fusion(bf16[2,4,18,22,128]{4,2,3,1,0:T(8,128)(2,1)S(1)} %pad_maximum_fusion, bf16[9,16,18]{2,1,0:T(8,128)(2,1)S(1)} %copy-done.5), kind=kOutput, calls=%fused_computation.80 | convolution fusion | flops 9437184 | bytes 2134016 | tf_op jit(solution)/shard_map/oi,bsirw->bsorw/dot_general | solution.py:39
  14.6 0.4 %fusion.43 = f32[2,4,16,128,16]{3,4,2,1,0:T(8,128)S(1)} fusion(bf16[2,4,18,22,128]{4,2,3,1,0:T(8,128)(2,1)S(1)} %pad_maximum_fusion, bf16[9,16,18]{2,1,0:T(8,128)(2,1)S(1)} %copy-done.5), kind=kOutput, calls=%fused_computation.79 | convolution fusion | flops 9437184 | bytes 2134016 | tf_op jit(solution)/shard_map/oi,bsirw->bsorw/dot_general | solution.py:39
  15.0 0.4 %fusion.42 = f32[2,4,16,128,16]{3,4,2,1,0:T(8,128)S(1)} fusion(bf16[2,4,18,22,128]{4,2,3,1,0:T(8,128)(2,1)S(1)} %pad_maximum_fusion, bf16[9,16,18]{2,1,0:T(8,128)(2,1)S(1)} %copy-done.5), kind=kOutput, calls=%fused_computation.78 | convolution fusion | flops 9437184 | bytes 2134016 | tf_op jit(solution)/shard_map/oi,bsirw->bsorw/dot_general | solution.py:39
  15.4 0.4 %fusion.41 = f32[2,4,16,128,16]{3,4,2,1,0:T(8,128)S(1)} fusion(bf16[2,4,18,22,128]{4,2,3,1,0:T(8,128)(2,1)S(1)} %pad_maximum_fusion, bf16[9,16,18]{2,1,0:T(8,128)(2,1)S(1)} %copy-done.5), kind=kOutput, calls=%fused_computation.77 | convolution fusion | flops 9437184 | bytes 2134016 | tf_op jit(solution)/shard_map/oi,bsirw->bsorw/dot_general | solution.py:39
  15.8 0.4 %fusion.40 = f32[2,4,16,128,16]{3,4,2,1,0:T(8,128)S(1)} fusion(bf16[2,4,18,22,128]{4,2,3,1,0:T(8,128)(2,1)S(1)} %pad_maximum_fusion, bf16[9,16,18]{2,1,0:T(8,128)(2,1)S(1)} %copy-done.5), kind=kOutput, calls=%fused_computation.76 | convolution fusion | flops 9437184 | bytes 2134016 | tf_op jit(solution)/shard_map/oi,bsirw->bsorw/dot_general | solution.py:39
  16.2 0.4 %fusion.39 = f32[2,4,16,128,16]{3,4,2,1,0:T(8,128)S(1)} fusion(bf16[2,4,18,22,128]{4,2,3,1,0:T(8,128)(2,1)S(1)} %pad_maximum_fusion, bf16[9,16,18]{2,1,0:T(8,128)(2,1)S(1)} %copy-done.5), kind=kOutput, calls=%fused_computation.75 | convolution fusion | flops 9437184 | bytes 2134016 | tf_op jit(solution)/shard_map/oi,bsirw->bsorw/dot_general | solution.py:39
  16.6 0.4 %copy-done.6 = bf16[9,16,18]{2,1,0:T(8,128)(2,1)S(1)} copy-done((bf16[9,16,18]{2,1,0:T(8,128)(2,1)S(1)}, bf16[9,16,18]{2,1,0:T(8,128)(2,1)}, u32[]{:S(2)}) %copy-start.6) | copy-done | bytes 5208
  16.9 0.3 fusion.85
  17.3 0.3 fusion.89
  17.6 0.3 fusion.93
  18.0 0.2 pad_slice_fusion.6
  18.2 0.5 %convolution_add_fusion.5 = f32[2,4,20,128,16]{3,4,2,1,0:T(8,128)S(1)} fusion(f32[2,4,20,128,16]{3,4,2,1,0:T(8,128)S(1)} %fusion.93, bf16[2,4,18,22,128]{4,2,3,1,0:T(8,128)(2,1)S(1)} %pad_maximum_fusion, bf16[9,16,18]{2,1,0:T(8,128)(2,1)S(1)} %copy-done.6), kind=kOutput, calls=%fused_computation.30 | convolution fusion | flops 12124160 | bytes 3706880 | tf_op jit(solution)/shard_map/oi,bsirw->bsorw/dot_general | solution.py:39
  18.7 0.5 %convolution_add_fusion.4 = f32[2,4,20,128,16]{3,4,2,1,0:T(8,128)S(1)} fusion(f32[2,4,20,128,16]{3,4,2,1,0:T(8,128)S(1)} %convolution_add_fusion.5, bf16[2,4,18,22,128]{4,2,3,1,0:T(8,128)(2,1)S(1)} %pad_maximum_fusion, bf16[9,16,18]{2,1,0:T(8,128)(2,1)S(1)} %copy-done.6), kind=kOutput, calls=%fused_computation.29 | convolution fusion | flops 12124160 | bytes 3706880 | tf_op jit(solution)/shard_map/oi,bsirw->bsorw/dot_general | solution.py:39
  19.2 0.5 %fusion.9 = f32[2,4,20,128,16]{3,4,2,1,0:T(8,128)S(1)} fusion(f32[2,4,20,128,16]{3,4,2,1,0:T(8,128)S(1)} %fusion.89, f32[2,4,20,128,16]{3,4,2,1,0:T(8,128)S(1)} %convolution_add_fusion.4, bf16[2,4,18,22,128]{4,2,3,1,0:T(8,128)(2,1)S(1)} %pad_maximum_fusion, bf16[9,16,18]{2,1,0:T(8,128)(2,1)S(1)} %copy-done.6), kind=kOutput, calls=%fused_computation.28 | convolution fusion | flops 12451840 | bytes 5017600 | tf_op jit(solution)/shard_map/oi,bsirw->bsorw/dot_general | solution.py:39
  19.7 0.5 %convolution_add_fusion.2 = f32[2,4,20,128,16]{3,4,2,1,0:T(8,128)S(1)} fusion(f32[2,4,20,128,16]{3,4,2,1,0:T(8,128)S(1)} %fusion.9, bf16[2,4,18,22,128]{4,2,3,1,0:T(8,128)(2,1)S(1)} %pad_maximum_fusion, bf16[9,16,18]{2,1,0:T(8,128)(2,1)S(1)} %copy-done.6), kind=kOutput, calls=%fused_computation.26 | convolution fusion | flops 12124160 | bytes 3706880 | tf_op jit(solution)/shard_map/oi,bsirw->bsorw/dot_general | solution.py:39
  20.1 0.5 %fusion.8 = f32[2,4,20,128,16]{3,4,2,1,0:T(8,128)S(1)} fusion(f32[2,4,20,128,16]{3,4,2,1,0:T(8,128)S(1)} %fusion.85, f32[2,4,20,128,16]{3,4,2,1,0:T(8,128)S(1)} %convolution_add_fusion.2, bf16[2,4,18,22,128]{4,2,3,1,0:T(8,128)(2,1)S(1)} %pad_maximum_fusion, bf16[9,16,18]{2,1,0:T(8,128)(2,1)S(1)} %copy-done.6), kind=kOutput, calls=%fused_computation.25 | convolution fusion | flops 12451840 | bytes 5017600 | tf_op jit(solution)/shard_map/oi,bsirw->bsorw/dot_general | solution.py:39
  20.8 0.8 %fusion.28 = bf16[2,4,16,20,128]{4,2,3,1,0:T(8,128)(2,1)S(1)} fusion(f32[2,4,20,128,16]{3,4,2,1,0:T(8,128)S(1)} %fusion.8, bf16[2,4,18,22,128]{4,2,3,1,0:T(8,128)(2,1)S(1)} %pad_maximum_fusion, f32[16]{0:T(128)S(1)} %copy-done.12, bf16[9,16,18]{2,1,0:T(8,128)(2,1)S(1)} %copy-done.6), kind=kOutput, calls=%fused_computation.59 | convolution fusion | flops 14417920 | bytes 3707392 | tf_op jit(solution)/shard_map/oi,bsirw->bsorw/dot_general | solution.py:39
  21.6 1.1 %fusion.1 = bf16[2,4,18,20,132]{4,2,3,1,0:T(8,128)(2,1)S(1)} fusion(bf16[2,4,16,20,128]{4,2,3,1,0:T(8,128)(2,1)S(1)} %fusion.28, bf16[2,4,2,20,132]{4,2,3,1,0:T(2,128)(2,1)S(1)} %pad_slice_fusion.6), kind=kLoop, calls=%fused_computation.16 | loop fusion | flops 2280960 | bytes 1500160 | tf_op jit(solution)/shard_map/concatenate | solution.py:147
  22.8 0.3 fusion.53
  23.1 0.4 %convolution_add_fusion.15 = f32[2,4,16,128,16]{3,4,2,1,0:T(8,128)S(1)} fusion(f32[2,4,16,128,16]{3,4,2,1,0:T(8,128)S(1)} %fusion.53, bf16[2,4,18,20,132]{4,2,3,1,0:T(8,128)(2,1)S(1)} %fusion.1, bf16[9,16,18]{2,1,0:T(8,128)(2,1)S(1)} %copy-done.4), kind=kOutput, calls=%fused_computation.58 | convolution fusion | flops 9699328 | bytes 2887680 | tf_op jit(solution)/shard_map/oi,bsirw->bsorw/dot_general | solution.py:39
  23.5 0.4 %convolution_add_fusion.14 = f32[2,4,16,128,16]{3,4,2,1,0:T(8,128)S(1)} fusion(f32[2,4,16,128,16]{3,4,2,1,0:T(8,128)S(1)} %convolution_add_fusion.15, bf16[2,4,18,20,132]{4,2,3,1,0:T(8,128)(2,1)S(1)} %fusion.1, bf16[9,16,18]{2,1,0:T(8,128)(2,1)S(1)} %copy-done.4), kind=kOutput, calls=%fused_computation.57 | convolution fusion | flops 9699328 | bytes 2887680 | tf_op jit(solution)/shard_map/oi,bsirw->bsorw/dot_general | solution.py:39
  23.9 0.3 convolution_add_fusion.13
  24.2 0.4 %convolution_add_fusion.12 = f32[2,4,16,128,16]{3,4,2,1,0:T(8,128)S(1)} fusion(f32[2,4,16,128,16]{3,4,2,1,0:T(8,128)S(1)} %convolution_add_fusion.13, bf16[2,4,18,20,132]{4,2,3,1,0:T(8,128)(2,1)S(1)} %fusion.1, bf16[9,16,18]{2,1,0:T(8,128)(2,1)S(1)} %copy-done.4), kind=kOutput, calls=%fused_computation.55 | convolution fusion | flops 9699328 | bytes 2887680 | tf_op jit(solution)/shard_map/oi,bsirw->bsorw/dot_general | solution.py:39
  24.6 0.6 %convolution_add_fusion.11 = f32[2,4,16,128,16]{3,4,2,1,0:T(8,128)S(1)} fusion(f32[2,4,16,128,16]{3,4,2,1,0:T(8,128)S(1)} %convolution_add_fusion.12, bf16[2,4,18,20,132]{4,2,3,1,0:T(8,128)(2,1)S(1)} %fusion.1, bf16[9,16,18]{2,1,0:T(8,128)(2,1)S(1)} %copy-done.4), kind=kOutput, calls=%fused_computation.54 | convolution fusion | flops 9699328 | bytes 2887680 | tf_op jit(solution)/shard_map/oi,bsirw->bsorw/dot_general | solution.py:39
  25.2 0.3 convolution_add_fusion.10
  25.5 0.4 %convolution_add_fusion.9 = f32[2,4,16,128,16]{3,4,2,1,0:T(8,128)S(1)} fusion(f32[2,4,16,128,16]{3,4,2,1,0:T(8,128)S(1)} %convolution_add_fusion.10, bf16[2,4,18,20,132]{4,2,3,1,0:T(8,128)(2,1)S(1)} %fusion.1, bf16[9,16,18]{2,1,0:T(8,128)(2,1)S(1)} %copy-done.4), kind=kOutput, calls=%fused_computation.52 | convolution fusion | flops 9699328 | bytes 2887680 | tf_op jit(solution)/shard_map/oi,bsirw->bsorw/dot_general | solution.py:39
  26.0 0.5 %fusion.21 = f32[2,4,16,128,16]{3,4,2,1,0:T(8,128)S(1)} fusion(f32[2,4,16,128,16]{3,4,2,1,0:T(8,128)S(1)} %fusion.43, f32[2,4,16,128,16]{3,4,2,1,0:T(8,128)S(1)} %fusion.42, f32[2,4,16,128,16]{3,4,2,1,0:T(8,128)S(1)} %fusion.55, f32[2,4,16,128,16]{3,4,2,1,0:T(8,128)S(1)} %fusion.41, f32[2,4,16,128,16]{3,4,2,1,0:T(8,128)S(1)} %fusion.40, ...), kind=kOutput, calls=%fused_computation.44 | convolution fusion | flops 13111296 | bytes 8081408 | tf_op jit(solution)/shard_map/oi,bsirw->bsorw/dot_general | solution.py:39
  26.6 0.5 %fusion.16 = f32[2,4,16,128,16]{3,4,2,1,0:T(8,128)S(1)} fusion(f32[2,4,16,128,16]{3,4,2,1,0:T(8,128)S(1)} %fusion.44, f32[2,4,16,128,16]{3,4,2,1,0:T(8,128)S(1)} %fusion.21, bf16[2,4,18,3,128]{4,2,3,1,0:T(8,128)(2,1)S(1)} %copy_select_fusion, bf16[2,4,16,16,128]{4,2,3,1,0:T(8,128)(2,1)S(1)} %copy.94, bf16[2,4,2,16,128]{4,2,3,1,0:T(2,128)(2,1)S(1)} %copy.45, ...), kind=kOutput, calls=%fused_computation.38 | convolution fusion | flops 13111296 | bytes 3887616 | tf_op jit(solution)/shard_map/oi,bsirw->bsorw/dot_general | solution.py:39
  27.1 0.7 %copy-done.1 = f32[2,4,16,16,128]{4,3,2,1,0:T(8,128)S(1)} copy-done((f32[2,4,16,16,128]{4,3,2,1,0:T(8,128)S(1)}, f32[2,4,16,16,128]{4,3,2,1,0:T(8,128)}, u32[]{:S(2)}) %copy-start.1) | copy-done | bytes 1048600
  27.8 0.8 %fusion.150 = (f32[4,16,16,128]{3,1,2,0:T(8,128)S(1)}, f32[2,4,16,16,128]{4,2,3,1,0:T(8,128)S(1)}) fusion(f32[4]{0:T(128)S(1)} %get-tuple-element.23, f32[2,4,16,128,16]{3,4,2,1,0:T(8,128)S(1)} %fusion.16, f32[16]{0:T(128)S(1)} %copy-done.11, f32[2,4,16,128,16]{3,4,2,1,0:T(8,128)S(1)} %convolution_add_fusion.9, bf16[9,16,18]{2,1,0:T(8,128)(2,1)S(1)} %copy-done.4, ...), kind=kOutput, calls=%fused_computation.215 | convolution fusion | flops 11403264 | bytes 5510144 | tf_op jit(solution)/shard_map/oi,bsirw->bsorw/dot_general | solution.py:39
  28.7 0.4 %convolution_reduce_fusion = f32[4,16,4,32]{3,1,2,0:T(8,128)S(1)} fusion(f32[4,16,4,4,128]{4,1,3,2,0:T(8,128)S(1)} %bitcast.260, s32[128]{0:T(128)S(1)} %and_select_fusion), kind=kOutput, calls=%fused_computation.60 | convolution fusion | flops 50360320 | bytes 557568 | tf_op jit(solution)/shard_map/schw,wj->schj/dot_general | solution.py:158
  29.1 0.6 %gather_fusion = f32[4,16,4,32]{3,1,2,0:T(8,128)S(1)} fusion(f32[4,16,4,32]{3,1,2,0:T(8,128)S(1)} %broadcast_multiply_fusion, s32[1024]{0:T(1024)S(1)} %pad_clamp_fusion), kind=kCustom, calls=%fused_computation | custom fusion | bytes 65552 | tf_op jit(solution)/shard_map/jit(_take)/gather | solution.py:164
  29.7 0.3 fusion.59
  30.0 2.0 %collective-permute-start.2 = (f32[2,16,4,32]{3,1,2,0:T(8,128)S(1)}, f32[2,16,4,32]{3,1,2,0:T(8,128)S(1)}, u32[]{:S(2)}, u32[]{:S(2)}) collective-permute-start(f32[2,16,4,32]{3,1,2,0:T(8,128)S(1)} %dynamic-slice_bitcast_fusion), channel_id=1, source_target_pairs={{0,2},{2,0},{1,3},{3,1},{4,6},{6,4},{5,7},{7,5},{8,10},{10,8},{9,1... | collective-permute-start | bytes 49160 | tf_op jit(solution)/shard_map/ppermute | solution.py:70
  32.0 0.9 %copy.53 = f32[2,4,8,16,128]{4,3,2,1,0:T(8,128)} copy(f32[2,4,8,16,128]{4,2,3,1,0:T(8,128)S(1)} %constant_dynamic-slice_fusion) | data formatting | bytes 1048576
  32.9 1.4 %collective-permute-done.2 = f32[2,16,4,32]{3,1,2,0:T(8,128)S(1)} collective-permute-done((f32[2,16,4,32]{3,1,2,0:T(8,128)S(1)}, f32[2,16,4,32]{3,1,2,0:T(8,128)S(1)}, u32[]{:S(2)}, u32[]{:S(2)}) %collective-permute-start.2) | collective-permute-done | bytes 16416 | tf_op jit(solution)/shard_map/ppermute | solution.py:70
  34.4 0.2 fusion.64
  34.6 0.7 %copy.54 = f32[2,16,4,32]{3,2,1,0:T(4,128)} copy(f32[2,16,4,32]{3,1,2,0:T(8,128)S(1)} %fusion.64) | data formatting | bytes 32768
  (43 shorter events, 1.0 us)
Async XLA Ops:
  0.6 29.0 %copy-start = (f32[16,16]{1,0:T(8,128)S(1)}, f32[16,16]{1,0:T(8,128)}, u32[]{:S(2)}) copy-start(f32[16,16]{1,0:T(8,128)} %param.27) | copy-start | bytes 3076
  0.6 3.8 %copy-start.2 = (bf16[2,4,2,16,128]{4,3,2,1,0:T(8,128)(2,1)S(1)}, bf16[2,4,2,16,128]{4,3,2,1,0:T(8,128)(2,1)}, u32[]{:S(2)}) copy-start(bf16[2,4,2,16,128]{4,3,2,1,0:T(8,128)(2,1)} %param.15) | copy-start | bytes 196612
  2.8 8.8 %copy-start.8 = (s32[4,2]{0,1:T(2,128)S(1)}, s32[4,2]{0,1:T(2,128)}, u32[]{:S(2)}) copy-start(s32[4,2]{0,1:T(2,128)} %param.18) | copy-start | bytes 100
  2.8 8.8 %copy-start.10 = (s32[1,4]{1,0:T(1,128)S(1)}, s32[1,4]{1,0:T(1,128)}, u32[]{:S(2)}) copy-start(s32[1,4]{1,0:T(1,128)} %param.19) | copy-start | bytes 52
  2.8 9.0 %copy-start.5 = (bf16[9,16,18]{2,1,0:T(8,128)(2,1)S(1)}, bf16[9,16,18]{2,1,0:T(8,128)(2,1)}, u32[]{:S(2)}) copy-start(bf16[9,16,18]{2,1,0:T(8,128)(2,1)} %param.21) | copy-start | bytes 15556
  4.7 8.9 %collective-permute-start.1 = (bf16[2,18,3,128]{3,1,2,0:T(8,128)(2,1)S(1)}, bf16[2,18,3,128]{3,1,2,0:T(8,128)(2,1)S(1)}, u32[]{:S(2)}, u32[]{:S(2)}) collective-permute-start(bf16[2,18,3,128]{3,1,2,0:T(8,128)(2,1)S(1)} %get-tuple-element.18), channel_id=1, source_target_pairs={{4,0},{8,4},{12,8},{5,1},{9,5},{13,9},{6,2},{10,6},{14,10},{7,3},{... | collective-permute-start | bytes 82952 | tf_op jit(solution)/shard_map/ppermute | solution.py:15
  6.0 7.7 %collective-permute-start = (bf16[2,18,3,128]{3,1,2,0:T(8,128)(2,1)S(1)}, bf16[2,18,3,128]{3,1,2,0:T(8,128)(2,1)S(1)}, u32[]{:S(2)}, u32[]{:S(2)}) collective-permute-start(bf16[2,18,3,128]{3,1,2,0:T(8,128)(2,1)S(1)} %get-tuple-element.10), channel_id=1, source_target_pairs={{0,4},{4,8},{8,12},{1,5},{5,9},{9,13},{2,6},{6,10},{10,14},{3,7},{... | collective-permute-start | bytes 82952 | tf_op jit(solution)/shard_map/ppermute | solution.py:12
  16.2 0.8 %copy-start.6 = (bf16[9,16,18]{2,1,0:T(8,128)(2,1)S(1)}, bf16[9,16,18]{2,1,0:T(8,128)(2,1)}, u32[]{:S(2)}) copy-start(bf16[9,16,18]{2,1,0:T(8,128)(2,1)} %param.23) | copy-start | bytes 15556
  20.1 0.7 %copy-start.12 = (f32[16]{0:T(128)S(1)}, f32[16]{0:T(128)}, u32[]{:S(2)}) copy-start(f32[16]{0:T(128)} %param.24) | copy-start | bytes 196
  21.6 1.2 %copy-start.4 = (bf16[9,16,18]{2,1,0:T(8,128)(2,1)S(1)}, bf16[9,16,18]{2,1,0:T(8,128)(2,1)}, u32[]{:S(2)}) copy-start(bf16[9,16,18]{2,1,0:T(8,128)(2,1)} %param.25) | copy-start | bytes 15556
  25.9 0.7 %copy-start.13 = (f32[16]{0:T(128)S(1)}, f32[16]{0:T(128)}, u32[]{:S(2)}) copy-start(f32[16]{0:T(128)} %param.22) | copy-start | bytes 196
  26.6 1.2 %copy-start.1 = (f32[2,4,16,16,128]{4,3,2,1,0:T(8,128)S(1)}, f32[2,4,16,16,128]{4,3,2,1,0:T(8,128)}, u32[]{:S(2)}) copy-start(f32[2,4,16,16,128]{4,3,2,1,0:T(8,128)} %param.16) | copy-start | bytes 3145732
  26.6 1.2 %copy-start.11 = (f32[16]{0:T(128)S(1)}, f32[16]{0:T(128)}, u32[]{:S(2)}) copy-start(f32[16]{0:T(128)} %param.26) | copy-start | bytes 196
  29.6 4.7 %copy-start.3 = (f32[2,16,4,32]{3,2,1,0:T(4,128)S(1)}, f32[2,16,4,32]{3,2,1,0:T(4,128)}, u32[]{:S(2)}) copy-start(f32[2,16,4,32]{3,2,1,0:T(4,128)} %param.20) | copy-start | bytes 49156
  29.6 4.7 %copy-start.7 = (f32[16,16]{1,0:T(8,128)S(1)}, f32[16,16]{1,0:T(8,128)}, u32[]{:S(2)}) copy-start(f32[16,16]{1,0:T(8,128)} %param.28) | copy-start | bytes 3076
  29.6 4.7 %copy-start.9 = (f32[16]{0:T(128)S(1)}, f32[16]{0:T(128)}, u32[]{:S(2)}) copy-start(f32[16]{0:T(128)} %param.29) | copy-start | bytes 196
  30.0 4.3 %collective-permute-start.2 = (f32[2,16,4,32]{3,1,2,0:T(8,128)S(1)}, f32[2,16,4,32]{3,1,2,0:T(8,128)S(1)}, u32[]{:S(2)}, u32[]{:S(2)}) collective-permute-start(f32[2,16,4,32]{3,1,2,0:T(8,128)S(1)} %dynamic-slice_bitcast_fusion), channel_id=1, source_target_pairs={{0,2},{2,0},{1,3},{3,1},{4,6},{6,4},{5,7},{7,5},{8,10},{10,8},{9,1... | collective-permute-start | bytes 49160 | tf_op jit(solution)/shard_map/ppermute | solution.py:70

commit v11 on v7

--- a/solution.py
+++ b/solution.py
@@ -130,13 +130,20 @@
     )
     full = jnp.concatenate([top, joined, bottom], axis=3)
     first = jnp.pad(full, ((0, 0), (0, 0), (0, 0), (0, 0), (2, 2)))
-    update = jax.nn.sigmoid(
-        apply_filter(first, w_update, 1, 3, row_count, column_count) + b_update[:, None, None]
-    )
+    gates = jax.nn.sigmoid(
+        apply_filter(
+            first,
+            jnp.concatenate([w_update, w_reset], axis=1),
+            1,
+            1,
+            row_count + 4,
+            column_count,
+        )
+        + jnp.concatenate([b_update, b_reset])[:, None, None]
+    )
+    update = gates[:, :, :chans, 2 : row_count + 2]
+    reset = gates[:, :, chans:]
     hidden_wide = first[:, :, inputs_count:, 1 : row_count + 5, 2 : column_count + 2]
-    reset = jax.nn.sigmoid(
-        apply_filter(first, w_reset, 1, 1, row_count + 4, column_count) + b_reset[:, None, None]
-    )
     gated = (reset * hidden_wide.astype(jnp.float32)).astype(jnp.bfloat16)
     gated_pad = jnp.pad(gated, ((0, 0), (0, 0), (0, 0), (0, 0), (2, 2)))
     second = jnp.concatenate([first[:, :, :inputs_count, 1 : row_count + 5, :], gated_pad], axis=2)

time: 35.4 us -> 34.8 us (0.983)
  matrix products: 12.8 us -> 11.6 us
  local copies, waits for them, and re-layouts: 6.74 us -> 7.14 us
    dot_general x27 -> x18, matrix products: 11.9 us -> 10.7 us  [apply_filter(): jnp.einsum('oi,bsirw->bsorw', filter_weight[(left_operand + 1) * 3 + (rig...]
    unnamed x30, local copies, waits for them, and re-layouts: 4.47 us -> 5.14 us
where the time goes in v11:
time: 34.8 us; the launch traced here: 34.5 us
  matrix products  11.6 us (33%)
  starting transfers between devices  8.87 us (25%)
  local copies, waits for them, and re-layouts  7.14 us (21%)
  other arithmetic  4.4 us (13%)
  waiting for transfers between devices  1.42 us (4%)
  between operations  1.08 us (3%)
    dot_general x18, matrix products, apply_filter(): jnp.einsum('oi,bsirw->bsorw', filter_weight[(left_operand + 1) * 3 + (rig...  10.7 us
    ppermute x1, starting transfers between devices, padded(): lax.ppermute(lax.slice_in_dim(block, block.shape[dim] - width, None, axis...  5.59 us
    unnamed x30, local copies, waits for them, and re-layouts  5.14 us
    ppermute x1, starting transfers between devices, exchange_sum(): chunk = lax.ppermute(chunk, 'band', perm)  1.99 us
    ppermute x1, waiting for transfers between devices, exchange_sum(): chunk = lax.ppermute(chunk, 'band', perm)  1.41 us
    ppermute x1, starting transfers between devices, padded(): lax.ppermute(lax.slice_in_dim(block, 0, width, axis=dim), axis, backward)  1.29 us
    concatenate x1, other arithmetic, shards(): jnp.concatenate([first[:, :, :inputs_count, 1:row_count + 5, :], gated_pa...  1.14 us
    and x1, other arithmetic, shards(): jnp.take(joined[:, :, :, row_count - 3:, :], jnp.clip(ups - base, 0, slot...  0.77 us
  transfers between devices with their start and end apart: 3, of which 1 were waited for; matrix products, arithmetic and copies ran while one was open for 8% of the time, Pallas kernels for 0%

profile of v11, /device:TPU:0, one launch (start us, length us, event | category | flops | bytes accessed | tf_op | source)
XLA Modules:
  0.0 34.5 jit_solution(15356934018668748838)
XLA Ops:
  0.6 0.0 copy-start
  0.6 0.0 copy-start.8
  0.7 0.7 %not_and_fusion = (pred[4]{0:T(512)(128)(4,1)S(1)}, pred[4]{0:T(512)(128)(4,1)S(1)}) fusion(s32[4]{0:T(128)} %param.19, s32[]{:T(128)S(6)} %add.160, s32[]{:T(128)S(6)} %mul.29, s32[4,2]{0,1:T(2,128)} %param.20), kind=kLoop, calls=%fused_computation.144 | loop fusion | flops 24 | bytes 48 | tf_op jit(solution)/shard_map/and | solution.py:101
  1.4 0.8 %compare_and_fusion.1 = (pred[4]{0:T(512)(128)(4,1)S(1)}, s32[4]{0:T(128)S(1)}, pred[4]{0:T(512)(128)(4,1)S(1)}, pred[4]{0:T(512)(128)(4,1)S(1)}, s32[4]{0:T(128...) fusion(s32[]{:T(128)S(6)} %mul.29, s32[4,2]{0,1:T(2,128)} %param.20, ...), kind=kLoop, calls=%fused_computation.139 | loop fusion | flops 124 | bytes 116 | tf_op jit(solution)/shard_map/jit(_take)/and | solution.py:116
  2.2 0.7 %fusion.89 = (f32[4]{0:T(128)S(1)}, pred[4]{0:T(512)(128)(4,1)S(1)}) fusion(s32[4]{0:T(128)} %param.19, pred[4]{0:T(512)(128)(4,1)S(1)} %get-tuple-element.27), kind=kLoop, calls=%fused_computation.153 | loop fusion | flops 16 | bytes 40 | tf_op jit(solution)/shard_map/convert_element_type | solution.py:153
  2.9 1.6 %copy.86 = bf16[2,4,16,16,128]{4,2,3,1,0:T(8,128)(2,1)S(1)} copy(f32[2,4,16,16,128]{4,3,2,1,0:T(8,128)} %param.18) | data formatting | bytes 1572864 | tf_op args[1]
  4.4 0.9 %copy.42 = bf16[2,4,2,16,128]{4,2,3,1,0:T(2,128)(2,1)S(1)} copy(bf16[2,4,2,16,128]{4,3,2,1,0:T(8,128)(2,1)} %param.17) | data formatting | bytes 131072 | tf_op args[0]
  5.3 0.2 select_reduce_fusion.1
  5.5 1.3 %collective-permute-start.1 = (bf16[2,18,3,128]{3,1,2,0:T(8,128)(2,1)S(1)}, bf16[2,18,3,128]{3,1,2,0:T(8,128)(2,1)S(1)}, u32[]{:S(2)}, u32[]{:S(2)}) collective-permute-start(bf16[2,18,3,128]{3,1,2,0:T(8,128)(2,1)S(1)} %get-tuple-element.21), channel_id=1, source_target_pairs={{4,0},{8,4},{12,8},{5,1},{9,5},{13,9},{6,2},{10,6},{14,10},{7,3},{... | collective-permute-start | bytes 82952 | tf_op jit(solution)/shard_map/ppermute | solution.py:15
  6.8 5.6 %collective-permute-start = (bf16[2,18,3,128]{3,1,2,0:T(8,128)(2,1)S(1)}, bf16[2,18,3,128]{3,1,2,0:T(8,128)(2,1)S(1)}, u32[]{:S(2)}, u32[]{:S(2)}) collective-permute-start(bf16[2,18,3,128]{3,1,2,0:T(8,128)(2,1)S(1)} %get-tuple-element.9), channel_id=1, source_target_pairs={{0,4},{4,8},{8,12},{1,5},{5,9},{9,13},{2,6},{6,10},{10,14},{3,7},{... | collective-permute-start | bytes 82952 | tf_op jit(solution)/shard_map/ppermute | solution.py:12
  12.5 0.1 pad_maximum_fusion.4
  12.6 0.1 copy.46
  12.7 0.1 copy.47
  12.9 0.6 %gather_fusion.2 = bf16[4,2,18,3,128]{4,2,3,1,0:T(8,128)(2,1)S(1)} fusion(bf16[2,4,18,3,128]{4,2,3,1,0:T(8,128)(2,1)S(1)} %get-tuple-element.22, s32[1024]{0:T(1024)S(1)} %pad_clamp_fusion.1), kind=kCustom, calls=%fused_computation.1.clone | custom fusion | bytes 221200 | tf_op jit(solution)/shard_map/jit(_take)/gather | solution.py:119
  13.5 0.6 %gather_fusion.1 = bf16[4,2,18,3,128]{4,2,3,1,0:T(8,128)(2,1)S(1)} fusion(bf16[2,4,18,3,128]{4,2,3,1,0:T(8,128)(2,1)S(1)} %get-tuple-element.10, s32[1024]{0:T(1024)S(1)} %pad_clamp_fusion.2), kind=kCustom, calls=%fused_computation.clone | custom fusion | bytes 221200 | tf_op jit(solution)/shard_map/jit(_take)/gather | solution.py:116
  14.1 0.1 copy_select_fusion
  14.2 0.4 %pad_maximum_fusion = bf16[2,4,18,22,128]{4,2,3,1,0:T(8,128)(2,1)S(1)} fusion(bf16[2,4,18,3,128]{4,2,3,1,0:T(8,128)(2,1)S(1)} %copy_select_fusion, bf16[2,4,16,16,128]{4,2,3,1,0:T(8,128)(2,1)S(1)} %copy.86, bf16[2,4,2,16,128]{4,2,3,1,0:T(2,128)(2,1)S(1)} %copy.42, bf16[4,2,18,3,128]{4,2,3,1,0:T(8,128)(2,1)S(1)} %gather_fusion.1, ...), kind=kLoop, calls=%fused_computation.32 | loop fusion | flops 3409920 | bytes 1649676 | tf_op jit(solution)/shard_map/concatenate | solution.py:131
  14.6 0.6 %fusion.13 = f32[2,4,20,128,32]{3,4,2,1,0:T(8,128)S(1)} fusion(bf16[2,4,18,22,128]{4,2,3,1,0:T(8,128)(2,1)S(1)} %pad_maximum_fusion, bf16[9,16,18]{1,2,0:T(8,128)(2,1)S(1)} %copy.46, bf16[9,16,18]{1,2,0:T(8,128)(2,1)S(1)} %copy.47), kind=kOutput, calls=%fused_computation.38 | convolution fusion | flops 23595264 | bytes 3442816 | tf_op jit(solution)/shard_map/oi,bsirw->bsorw/dot_general | solution.py:39
  15.2 0.6 %fusion.12 = f32[2,4,20,128,32]{3,4,2,1,0:T(8,128)S(1)} fusion(bf16[2,4,18,22,128]{4,2,3,1,0:T(8,128)(2,1)S(1)} %pad_maximum_fusion, bf16[9,16,18]{1,2,0:T(8,128)(2,1)S(1)} %copy.46, bf16[9,16,18]{1,2,0:T(8,128)(2,1)S(1)} %copy.47), kind=kOutput, calls=%fused_computation.37 | convolution fusion | flops 23595264 | bytes 3442816 | tf_op jit(solution)/shard_map/oi,bsirw->bsorw/dot_general | solution.py:39
  15.9 0.6 %fusion.11 = f32[2,4,20,128,32]{3,4,2,1,0:T(8,128)S(1)} fusion(bf16[2,4,18,22,128]{4,2,3,1,0:T(8,128)(2,1)S(1)} %pad_maximum_fusion, bf16[9,16,18]{1,2,0:T(8,128)(2,1)S(1)} %copy.46, bf16[9,16,18]{1,2,0:T(8,128)(2,1)S(1)} %copy.47), kind=kOutput, calls=%fused_computation.36 | convolution fusion | flops 23595264 | bytes 3442816 | tf_op jit(solution)/shard_map/oi,bsirw->bsorw/dot_general | solution.py:39
  16.5 0.6 %fusion.10 = f32[2,4,20,128,32]{3,4,2,1,0:T(8,128)S(1)} fusion(bf16[2,4,18,22,128]{4,2,3,1,0:T(8,128)(2,1)S(1)} %pad_maximum_fusion, bf16[9,16,18]{1,2,0:T(8,128)(2,1)S(1)} %copy.46, bf16[9,16,18]{1,2,0:T(8,128)(2,1)S(1)} %copy.47), kind=kOutput, calls=%fused_computation.35 | convolution fusion | flops 23595264 | bytes 3442816 | tf_op jit(solution)/shard_map/oi,bsirw->bsorw/dot_general | solution.py:39
  17.1 0.6 %fusion.9 = f32[2,4,20,128,32]{3,4,2,1,0:T(8,128)S(1)} fusion(bf16[2,4,18,22,128]{4,2,3,1,0:T(8,128)(2,1)S(1)} %pad_maximum_fusion, bf16[9,16,18]{1,2,0:T(8,128)(2,1)S(1)} %copy.46, bf16[9,16,18]{1,2,0:T(8,128)(2,1)S(1)} %copy.47), kind=kOutput, calls=%fused_computation.34 | convolution fusion | flops 23595264 | bytes 3442816 | tf_op jit(solution)/shard_map/oi,bsirw->bsorw/dot_general | solution.py:39
  17.7 0.2 pad_slice_fusion
  17.9 0.6 %fusion.51 = f32[2,4,20,128,32]{3,4,2,1,0:T(8,128)S(1)} fusion(bf16[9,16,18]{1,2,0:T(8,128)(2,1)S(1)} %copy.46, bf16[9,16,18]{1,2,0:T(8,128)(2,1)S(1)} %copy.47, bf16[2,4,18,3,128]{4,2,3,1,0:T(8,128)(2,1)S(1)} %copy_select_fusion, bf16[2,4,16,16,128]{4,2,3,1,0:T(8,128)(2,1)S(1)} %copy.86, bf16[2,4,2,16,128]{4,2,3,1,0:T(2,128)(2,1)S(1)} %copy.42, ...), kind=kOutput, calls=%fused_computation.100 | convolution fusion | flops 27005184 | bytes 3470476 | tf_op jit(solution)/shard_map/oi,bsirw->bsorw/dot_general | solution.py:39
  18.6 0.6 %fusion.55 = f32[2,4,20,128,32]{3,4,2,1,0:T(8,128)S(1)} fusion(bf16[9,16,18]{1,2,0:T(8,128)(2,1)S(1)} %copy.46, bf16[9,16,18]{1,2,0:T(8,128)(2,1)S(1)} %copy.47, bf16[2,4,18,3,128]{4,2,3,1,0:T(8,128)(2,1)S(1)} %copy_select_fusion, bf16[2,4,16,16,128]{4,2,3,1,0:T(8,128)(2,1)S(1)} %copy.86, bf16[2,4,2,16,128]{4,2,3,1,0:T(2,128)(2,1)S(1)} %copy.42, ...), kind=kOutput, calls=%fused_computation.104 | convolution fusion | flops 27005184 | bytes 3470476 | tf_op jit(solution)/shard_map/oi,bsirw->bsorw/dot_general | solution.py:39
  19.2 0.6 %fusion.59 = f32[2,4,20,128,32]{3,4,2,1,0:T(8,128)S(1)} fusion(bf16[9,16,18]{1,2,0:T(8,128)(2,1)S(1)} %copy.46, bf16[9,16,18]{1,2,0:T(8,128)(2,1)S(1)} %copy.47, bf16[2,4,18,3,128]{4,2,3,1,0:T(8,128)(2,1)S(1)} %copy_select_fusion, bf16[2,4,16,16,128]{4,2,3,1,0:T(8,128)(2,1)S(1)} %copy.86, bf16[2,4,2,16,128]{4,2,3,1,0:T(2,128)(2,1)S(1)} %copy.42, ...), kind=kOutput, calls=%fused_computation.108 | convolution fusion | flops 27005184 | bytes 3470476 | tf_op jit(solution)/shard_map/oi,bsirw->bsorw/dot_general | solution.py:39
  19.8 2.0 %divide_bitcast_fusion = f32[2,4,32,20,128]{4,2,3,1,0:T(8,128)S(1)} fusion(f32[2,4,20,128,32]{3,4,2,1,0:T(8,128)S(1)} %fusion.51, f32[2,4,20,128,32]{3,4,2,1,0:T(8,128)S(1)} %fusion.13, f32[2,4,20,128,32]{3,4,2,1,0:T(8,128)S(1)} %fusion.12, f32[2,4,20,128,32]{3,4,2,1,0:T(8,128)S(1)} %fusion.55, f32[2,4,20,128,32]{3,4,2,1,0:T(8,128)S(1)} %fusion.11, ...), kind=kOutput, calls=%fused_computation.12 | convolution fusion | flops 31459584 | bytes 24414464 | tf_op jit(solution)/shard_map/oi,bsirw->bsorw/dot_general | solution.py:39
  21.9 0.0 copy-start.5
  21.9 0.3 fusion.8
  22.2 1.1 %fusion.1 = bf16[2,4,18,20,132]{4,2,3,1,0:T(8,128)(2,1)S(1)} fusion(bf16[2,4,16,20,128]{4,2,3,1,0:T(8,128)(2,1)S(1)} %fusion.8, bf16[2,4,2,20,132]{4,2,3,1,0:T(2,128)(2,1)S(1)} %pad_slice_fusion), kind=kLoop, calls=%fused_computation.13 | loop fusion | flops 2280960 | bytes 1500160 | tf_op jit(solution)/shard_map/concatenate | solution.py:149
  23.3 0.3 fusion.22
  23.6 0.4 %convolution_add_fusion.7 = f32[2,4,16,128,16]{3,4,2,1,0:T(8,128)S(1)} fusion(f32[2,4,16,128,16]{3,4,2,1,0:T(8,128)S(1)} %fusion.22, bf16[2,4,18,20,132]{4,2,3,1,0:T(8,128)(2,1)S(1)} %fusion.1, bf16[9,16,18]{2,1,0:T(8,128)(2,1)S(1)} %copy-done.5), kind=kOutput, calls=%fused_computation.27 | convolution fusion | flops 9699328 | bytes 2887680 | tf_op jit(solution)/shard_map/oi,bsirw->bsorw/dot_general | solution.py:39
  24.0 0.4 %convolution_add_fusion.6 = f32[2,4,16,128,16]{3,4,2,1,0:T(8,128)S(1)} fusion(f32[2,4,16,128,16]{3,4,2,1,0:T(8,128)S(1)} %convolution_add_fusion.7, bf16[2,4,18,20,132]{4,2,3,1,0:T(8,128)(2,1)S(1)} %fusion.1, bf16[9,16,18]{2,1,0:T(8,128)(2,1)S(1)} %copy-done.5), kind=kOutput, calls=%fused_computation.26 | convolution fusion | flops 9699328 | bytes 2887680 | tf_op jit(solution)/shard_map/oi,bsirw->bsorw/dot_general | solution.py:39
  24.4 0.3 convolution_add_fusion.5
  24.7 0.4 %convolution_add_fusion.4 = f32[2,4,16,128,16]{3,4,2,1,0:T(8,128)S(1)} fusion(f32[2,4,16,128,16]{3,4,2,1,0:T(8,128)S(1)} %convolution_add_fusion.5, bf16[2,4,18,20,132]{4,2,3,1,0:T(8,128)(2,1)S(1)} %fusion.1, bf16[9,16,18]{2,1,0:T(8,128)(2,1)S(1)} %copy-done.5), kind=kOutput, calls=%fused_computation.24 | convolution fusion | flops 9699328 | bytes 2887680 | tf_op jit(solution)/shard_map/oi,bsirw->bsorw/dot_general | solution.py:39
  25.2 0.4 %convolution_add_fusion.3 = f32[2,4,16,128,16]{3,4,2,1,0:T(8,128)S(1)} fusion(f32[2,4,16,128,16]{3,4,2,1,0:T(8,128)S(1)} %convolution_add_fusion.4, bf16[2,4,18,20,132]{4,2,3,1,0:T(8,128)(2,1)S(1)} %fusion.1, bf16[9,16,18]{2,1,0:T(8,128)(2,1)S(1)} %copy-done.5), kind=kOutput, calls=%fused_computation.23 | convolution fusion | flops 9699328 | bytes 2887680 | tf_op jit(solution)/shard_map/oi,bsirw->bsorw/dot_general | solution.py:39
  25.6 0.3 convolution_add_fusion.2
  25.9 0.4 %convolution_add_fusion.1 = f32[2,4,16,128,16]{3,4,2,1,0:T(8,128)S(1)} fusion(f32[2,4,16,128,16]{3,4,2,1,0:T(8,128)S(1)} %convolution_add_fusion.2, bf16[2,4,18,20,132]{4,2,3,1,0:T(8,128)(2,1)S(1)} %fusion.1, bf16[9,16,18]{2,1,0:T(8,128)(2,1)S(1)} %copy-done.5), kind=kOutput, calls=%fused_computation.21 | convolution fusion | flops 9699328 | bytes 2887680 | tf_op jit(solution)/shard_map/oi,bsirw->bsorw/dot_general | solution.py:39
  26.3 0.8 %copy-done.1 = f32[2,4,16,16,128]{4,3,2,1,0:T(8,128)S(1)} copy-done((f32[2,4,16,16,128]{4,3,2,1,0:T(8,128)S(1)}, f32[2,4,16,16,128]{4,3,2,1,0:T(8,128)}, u32[]{:S(2)}) %copy-start.1) | copy-done | bytes 1048600
  27.1 0.8 %fusion.106 = (f32[4,16,16,128]{3,1,2,0:T(8,128)S(1)}, f32[2,4,16,16,128]{4,2,3,1,0:T(8,128)S(1)}) fusion(f32[4]{0:T(128)S(1)} %get-tuple-element.28, f32[16]{0:T(128)S(1)} %copy-done.9, f32[2,4,16,128,16]{3,4,2,1,0:T(8,128)S(1)} %convolution_add_fusion.1, bf16[9,16,18]{2,1,0:T(8,128)(2,1)S(1)} %copy-done.5, bf16[2,4,18,20,132]{4,2,3,1,0:T(8,128)(2,1)S(1)} %fusion.1, ...), kind=kOutput, calls=%fused_computation.170 | convolution fusion | flops 11403264 | bytes 5510144 | tf_op jit(solution)/shard_map/oi,bsirw->bsorw/dot_general | solution.py:39
  28.0 0.4 %convolution_reduce_fusion = f32[4,16,4,32]{3,1,2,0:T(8,128)S(1)} fusion(f32[4,16,4,4,128]{4,1,3,2,0:T(8,128)S(1)} %bitcast.209, s32[128]{0:T(128)S(1)} %and_select_fusion), kind=kOutput, calls=%fused_computation.30 | convolution fusion | flops 50360320 | bytes 557568 | tf_op jit(solution)/shard_map/schw,wj->schj/dot_general | solution.py:160
  28.3 0.6 %gather_fusion = f32[4,16,4,32]{3,1,2,0:T(8,128)S(1)} fusion(f32[4,16,4,32]{3,1,2,0:T(8,128)S(1)} %broadcast_multiply_fusion, s32[1024]{0:T(1024)S(1)} %pad_clamp_fusion), kind=kCustom, calls=%fused_computation.2 | custom fusion | bytes 65552 | tf_op jit(solution)/shard_map/jit(_take)/gather | solution.py:166
  28.9 0.3 fusion.24
  29.3 2.0 %collective-permute-start.2 = (f32[2,16,4,32]{3,1,2,0:T(8,128)S(1)}, f32[2,16,4,32]{3,1,2,0:T(8,128)S(1)}, u32[]{:S(2)}, u32[]{:S(2)}) collective-permute-start(f32[2,16,4,32]{3,1,2,0:T(8,128)S(1)} %dynamic-slice_bitcast_fusion), channel_id=1, source_target_pairs={{0,2},{2,0},{1,3},{3,1},{4,6},{6,4},{5,7},{7,5},{8,10},{10,8},{9,1... | collective-permute-start | bytes 49160 | tf_op jit(solution)/shard_map/ppermute | solution.py:63
  31.3 0.9 %copy.51 = f32[2,4,8,16,128]{4,3,2,1,0:T(8,128)} copy(f32[2,4,8,16,128]{4,2,3,1,0:T(8,128)S(1)} %constant_dynamic-slice_fusion) | data formatting | bytes 1048576
  32.2 1.4 %collective-permute-done.2 = f32[2,16,4,32]{3,1,2,0:T(8,128)S(1)} collective-permute-done((f32[2,16,4,32]{3,1,2,0:T(8,128)S(1)}, f32[2,16,4,32]{3,1,2,0:T(8,128)S(1)}, u32[]{:S(2)}, u32[]{:S(2)}) %collective-permute-start.2) | collective-permute-done | bytes 16416 | tf_op jit(solution)/shard_map/ppermute | solution.py:63
  33.6 0.2 fusion.29
  33.8 0.7 %copy.52 = f32[2,16,4,32]{3,2,1,0:T(4,128)} copy(f32[2,16,4,32]{3,1,2,0:T(8,128)S(1)} %fusion.29) | data formatting | bytes 32768
  (30 shorter events, 0.1 us)
Async XLA Ops:
  0.6 28.3 %copy-start = (f32[16,16]{1,0:T(8,128)S(1)}, f32[16,16]{1,0:T(8,128)}, u32[]{:S(2)}) copy-start(f32[16,16]{1,0:T(8,128)} %param.29) | copy-start | bytes 3076
  0.6 11.8 %copy-start.8 = (s32[1,4]{1,0:T(1,128)S(1)}, s32[1,4]{1,0:T(1,128)}, u32[]{:S(2)}) copy-start(s32[1,4]{1,0:T(1,128)} %param.21) | copy-start | bytes 52
  0.7 11.8 %copy-start.10 = (f32[16]{0:T(128)S(1)}, f32[16]{0:T(128)}, u32[]{:S(2)}) copy-start(f32[16]{0:T(128)} %param.26) | copy-start | bytes 196
  0.7 11.8 %copy-start.11 = (f32[16]{0:T(128)S(1)}, f32[16]{0:T(128)}, u32[]{:S(2)}) copy-start(f32[16]{0:T(128)} %param.24) | copy-start | bytes 196
  0.7 11.9 %copy-start.3 = (bf16[9,16,18]{2,1,0:T(8,128)(2,1)S(1)}, bf16[9,16,18]{2,1,0:T(8,128)(2,1)}, u32[]{:S(2)}) copy-start(bf16[9,16,18]{2,1,0:T(8,128)(2,1)} %param.23) | copy-start | bytes 15556
  0.7 12.0 %copy-start.4 = (bf16[9,16,18]{2,1,0:T(8,128)(2,1)S(1)}, bf16[9,16,18]{2,1,0:T(8,128)(2,1)}, u32[]{:S(2)}) copy-start(bf16[9,16,18]{2,1,0:T(8,128)(2,1)} %param.25) | copy-start | bytes 15556
  5.5 8.5 %collective-permute-start.1 = (bf16[2,18,3,128]{3,1,2,0:T(8,128)(2,1)S(1)}, bf16[2,18,3,128]{3,1,2,0:T(8,128)(2,1)S(1)}, u32[]{:S(2)}, u32[]{:S(2)}) collective-permute-start(bf16[2,18,3,128]{3,1,2,0:T(8,128)(2,1)S(1)} %get-tuple-element.21), channel_id=1, source_target_pairs={{4,0},{8,4},{12,8},{5,1},{9,5},{13,9},{6,2},{10,6},{14,10},{7,3},{... | collective-permute-start | bytes 82952 | tf_op jit(solution)/shard_map/ppermute | solution.py:15
  6.8 7.4 %collective-permute-start = (bf16[2,18,3,128]{3,1,2,0:T(8,128)(2,1)S(1)}, bf16[2,18,3,128]{3,1,2,0:T(8,128)(2,1)S(1)}, u32[]{:S(2)}, u32[]{:S(2)}) collective-permute-start(bf16[2,18,3,128]{3,1,2,0:T(8,128)(2,1)S(1)} %get-tuple-element.9), channel_id=1, source_target_pairs={{0,4},{4,8},{8,12},{1,5},{5,9},{9,13},{2,6},{6,10},{10,14},{3,7},{... | collective-permute-start | bytes 82952 | tf_op jit(solution)/shard_map/ppermute | solution.py:12
  21.9 1.4 %copy-start.5 = (bf16[9,16,18]{2,1,0:T(8,128)(2,1)S(1)}, bf16[9,16,18]{2,1,0:T(8,128)(2,1)}, u32[]{:S(2)}) copy-start(bf16[9,16,18]{2,1,0:T(8,128)(2,1)} %param.27) | copy-start | bytes 15556
  25.9 1.2 %copy-start.1 = (f32[2,4,16,16,128]{4,3,2,1,0:T(8,128)S(1)}, f32[2,4,16,16,128]{4,3,2,1,0:T(8,128)}, u32[]{:S(2)}) copy-start(f32[2,4,16,16,128]{4,3,2,1,0:T(8,128)} %param.18) | copy-start | bytes 3145732
  25.9 1.2 %copy-start.9 = (f32[16]{0:T(128)S(1)}, f32[16]{0:T(128)}, u32[]{:S(2)}) copy-start(f32[16]{0:T(128)} %param.28) | copy-start | bytes 196
  27.9 5.7 %copy-start.2 = (f32[2,16,4,32]{3,2,1,0:T(4,128)S(1)}, f32[2,16,4,32]{3,2,1,0:T(4,128)}, u32[]{:S(2)}) copy-start(f32[2,16,4,32]{3,2,1,0:T(4,128)} %param.22) | copy-start | bytes 49156
  27.9 5.7 %copy-start.6 = (f32[16,16]{1,0:T(8,128)S(1)}, f32[16,16]{1,0:T(8,128)}, u32[]{:S(2)}) copy-start(f32[16,16]{1,0:T(8,128)} %param.30) | copy-start | bytes 3076
  27.9 5.7 %copy-start.7 = (f32[16]{0:T(128)S(1)}, f32[16]{0:T(128)}, u32[]{:S(2)}) copy-start(f32[16]{0:T(128)} %param.31) | copy-start | bytes 196
  29.3 4.3 %collective-permute-start.2 = (f32[2,16,4,32]{3,1,2,0:T(8,128)S(1)}, f32[2,16,4,32]{3,1,2,0:T(8,128)S(1)}, u32[]{:S(2)}, u32[]{:S(2)}) collective-permute-start(f32[2,16,4,32]{3,1,2,0:T(8,128)S(1)} %dynamic-slice_bitcast_fusion), channel_id=1, source_target_pairs={{0,2},{2,0},{1,3},{3,1},{4,6},{6,4},{5,7},{7,5},{8,10},{10,8},{9,1... | collective-permute-start | bytes 49160 | tf_op jit(solution)/shard_map/ppermute | solution.py:63

commit v12 on v11

--- a/solution.py
+++ b/solution.py
@@ -49,6 +49,10 @@
 def choose_rows(block, select):
     masked = jnp.where(select[None, :, None, None, None], block, jnp.zeros_like(block))
     return jnp.sum(masked, axis=1)
+
+
+def logistic(value):
+    return 0.5 + 0.5 * jnp.tanh(0.5 * value)
 
 
 def exchange_sum(part, owned):
@@ -130,7 +134,7 @@
     )
     full = jnp.concatenate([top, joined, bottom], axis=3)
     first = jnp.pad(full, ((0, 0), (0, 0), (0, 0), (0, 0), (2, 2)))
-    gates = jax.nn.sigmoid(
+    gates = logistic(
         apply_filter(
             first,
             jnp.concatenate([w_update, w_reset], axis=1),

time: 34.8 us -> 34.8 us (level)
  no operation moved by 1% of the time
where the time goes in v12:
time: 34.8 us; the launch traced here: 34.4 us
  matrix products  11.5 us (33%)
  starting transfers between devices  8.87 us (25%)
  local copies, waits for them, and re-layouts  7.14 us (21%)
  other arithmetic  4.4 us (13%)
  waiting for transfers between devices  1.42 us (4%)
  between operations  1.08 us (3%)
    dot_general x18, matrix products, apply_filter(): jnp.einsum('oi,bsirw->bsorw', filter_weight[(left_operand + 1) * 3 + (rig...  10.7 us
    ppermute x1, starting transfers between devices, padded(): lax.ppermute(lax.slice_in_dim(block, block.shape[dim] - width, None, axis...  5.59 us
    unnamed x30, local copies, waits for them, and re-layouts  5.14 us
    ppermute x1, starting transfers between devices, exchange_sum(): chunk = lax.ppermute(chunk, 'band', perm)  1.99 us
    ppermute x1, waiting for transfers between devices, exchange_sum(): chunk = lax.ppermute(chunk, 'band', perm)  1.41 us
    ppermute x1, starting transfers between devices, padded(): lax.ppermute(lax.slice_in_dim(block, 0, width, axis=dim), axis, backward)  1.29 us
    concatenate x1, other arithmetic, shards(): jnp.concatenate([first[:, :, :inputs_count, 1:row_count + 5, :], gated_pa...  1.14 us
    and x1, other arithmetic, shards(): jnp.take(joined[:, :, :, row_count - 3:, :], jnp.clip(ups - base, 0, slot...  0.77 us
  transfers between devices with their start and end apart: 3, of which 1 were waited for; matrix products, arithmetic and copies ran while one was open for 8% of the time, Pallas kernels for 0%

profile of v12, /device:TPU:0, one launch (start us, length us, event | category | flops | bytes accessed | tf_op | source)
XLA Modules:
  0.0 34.4 jit_solution(2514145717497977590)
XLA Ops:
  0.6 0.0 copy-start
  0.6 0.0 copy-start.8
  0.7 0.7 %not_and_fusion = (pred[4]{0:T(512)(128)(4,1)S(1)}, pred[4]{0:T(512)(128)(4,1)S(1)}) fusion(s32[4]{0:T(128)} %param.19, s32[]{:T(128)S(6)} %add.160, s32[]{:T(128)S(6)} %mul.35, s32[4,2]{0,1:T(2,128)} %param.20), kind=kLoop, calls=%fused_computation.144 | loop fusion | flops 24 | bytes 48 | tf_op jit(solution)/shard_map/and | solution.py:105
  1.4 0.8 %compare_and_fusion.1 = (pred[4]{0:T(512)(128)(4,1)S(1)}, s32[4]{0:T(128)S(1)}, pred[4]{0:T(512)(128)(4,1)S(1)}, pred[4]{0:T(512)(128)(4,1)S(1)}, s32[4]{0:T(128...) fusion(s32[]{:T(128)S(6)} %mul.35, s32[4,2]{0,1:T(2,128)} %param.20, ...), kind=kLoop, calls=%fused_computation.139 | loop fusion | flops 124 | bytes 116 | tf_op jit(solution)/shard_map/jit(_take)/and | solution.py:120
  2.2 0.7 %fusion.89 = (f32[4]{0:T(128)S(1)}, pred[4]{0:T(512)(128)(4,1)S(1)}) fusion(s32[4]{0:T(128)} %param.19, pred[4]{0:T(512)(128)(4,1)S(1)} %get-tuple-element.27), kind=kLoop, calls=%fused_computation.153 | loop fusion | flops 16 | bytes 40 | tf_op jit(solution)/shard_map/convert_element_type | solution.py:157
  2.9 1.6 %copy.86 = bf16[2,4,16,16,128]{4,2,3,1,0:T(8,128)(2,1)S(1)} copy(f32[2,4,16,16,128]{4,3,2,1,0:T(8,128)} %param.18) | data formatting | bytes 1572864 | tf_op args[1]
  4.4 0.9 %copy.42 = bf16[2,4,2,16,128]{4,2,3,1,0:T(2,128)(2,1)S(1)} copy(bf16[2,4,2,16,128]{4,3,2,1,0:T(8,128)(2,1)} %param.17) | data formatting | bytes 131072 | tf_op args[0]
  5.3 0.2 select_reduce_fusion.1
  5.5 1.3 %collective-permute-start.1 = (bf16[2,18,3,128]{3,1,2,0:T(8,128)(2,1)S(1)}, bf16[2,18,3,128]{3,1,2,0:T(8,128)(2,1)S(1)}, u32[]{:S(2)}, u32[]{:S(2)}) collective-permute-start(bf16[2,18,3,128]{3,1,2,0:T(8,128)(2,1)S(1)} %get-tuple-element.21), channel_id=1, source_target_pairs={{4,0},{8,4},{12,8},{5,1},{9,5},{13,9},{6,2},{10,6},{14,10},{7,3},{... | collective-permute-start | bytes 82952 | tf_op jit(solution)/shard_map/ppermute | solution.py:15
  6.8 5.6 %collective-permute-start = (bf16[2,18,3,128]{3,1,2,0:T(8,128)(2,1)S(1)}, bf16[2,18,3,128]{3,1,2,0:T(8,128)(2,1)S(1)}, u32[]{:S(2)}, u32[]{:S(2)}) collective-permute-start(bf16[2,18,3,128]{3,1,2,0:T(8,128)(2,1)S(1)} %get-tuple-element.9), channel_id=1, source_target_pairs={{0,4},{4,8},{8,12},{1,5},{5,9},{9,13},{2,6},{6,10},{10,14},{3,7},{... | collective-permute-start | bytes 82952 | tf_op jit(solution)/shard_map/ppermute | solution.py:12
  12.5 0.1 pad_maximum_fusion.4
  12.6 0.1 copy.46
  12.7 0.1 copy.47
  12.9 0.6 %gather_fusion.2 = bf16[4,2,18,3,128]{4,2,3,1,0:T(8,128)(2,1)S(1)} fusion(bf16[2,4,18,3,128]{4,2,3,1,0:T(8,128)(2,1)S(1)} %get-tuple-element.22, s32[1024]{0:T(1024)S(1)} %pad_clamp_fusion.1), kind=kCustom, calls=%fused_computation.1.clone | custom fusion | bytes 221200 | tf_op jit(solution)/shard_map/jit(_take)/gather | solution.py:123
  13.5 0.6 %gather_fusion.1 = bf16[4,2,18,3,128]{4,2,3,1,0:T(8,128)(2,1)S(1)} fusion(bf16[2,4,18,3,128]{4,2,3,1,0:T(8,128)(2,1)S(1)} %get-tuple-element.10, s32[1024]{0:T(1024)S(1)} %pad_clamp_fusion.2), kind=kCustom, calls=%fused_computation.clone | custom fusion | bytes 221200 | tf_op jit(solution)/shard_map/jit(_take)/gather | solution.py:120
  14.1 0.1 copy_select_fusion
  14.2 0.4 %pad_maximum_fusion = bf16[2,4,18,22,128]{4,2,3,1,0:T(8,128)(2,1)S(1)} fusion(bf16[2,4,18,3,128]{4,2,3,1,0:T(8,128)(2,1)S(1)} %copy_select_fusion, bf16[2,4,16,16,128]{4,2,3,1,0:T(8,128)(2,1)S(1)} %copy.86, bf16[2,4,2,16,128]{4,2,3,1,0:T(2,128)(2,1)S(1)} %copy.42, bf16[4,2,18,3,128]{4,2,3,1,0:T(8,128)(2,1)S(1)} %gather_fusion.1, ...), kind=kLoop, calls=%fused_computation.32 | loop fusion | flops 3409920 | bytes 1649676 | tf_op jit(solution)/shard_map/concatenate | solution.py:135
  14.6 0.6 %fusion.13 = f32[2,4,20,128,32]{3,4,2,1,0:T(8,128)S(1)} fusion(bf16[2,4,18,22,128]{4,2,3,1,0:T(8,128)(2,1)S(1)} %pad_maximum_fusion, bf16[9,16,18]{1,2,0:T(8,128)(2,1)S(1)} %copy.46, bf16[9,16,18]{1,2,0:T(8,128)(2,1)S(1)} %copy.47), kind=kOutput, calls=%fused_computation.38 | convolution fusion | flops 23595264 | bytes 3442816 | tf_op jit(solution)/shard_map/oi,bsirw->bsorw/dot_general | solution.py:39
  15.2 0.6 %fusion.12 = f32[2,4,20,128,32]{3,4,2,1,0:T(8,128)S(1)} fusion(bf16[2,4,18,22,128]{4,2,3,1,0:T(8,128)(2,1)S(1)} %pad_maximum_fusion, bf16[9,16,18]{1,2,0:T(8,128)(2,1)S(1)} %copy.46, bf16[9,16,18]{1,2,0:T(8,128)(2,1)S(1)} %copy.47), kind=kOutput, calls=%fused_computation.37 | convolution fusion | flops 23595264 | bytes 3442816 | tf_op jit(solution)/shard_map/oi,bsirw->bsorw/dot_general | solution.py:39
  15.9 0.6 %fusion.11 = f32[2,4,20,128,32]{3,4,2,1,0:T(8,128)S(1)} fusion(bf16[2,4,18,22,128]{4,2,3,1,0:T(8,128)(2,1)S(1)} %pad_maximum_fusion, bf16[9,16,18]{1,2,0:T(8,128)(2,1)S(1)} %copy.46, bf16[9,16,18]{1,2,0:T(8,128)(2,1)S(1)} %copy.47), kind=kOutput, calls=%fused_computation.36 | convolution fusion | flops 23595264 | bytes 3442816 | tf_op jit(solution)/shard_map/oi,bsirw->bsorw/dot_general | solution.py:39
  16.5 0.6 %fusion.10 = f32[2,4,20,128,32]{3,4,2,1,0:T(8,128)S(1)} fusion(bf16[2,4,18,22,128]{4,2,3,1,0:T(8,128)(2,1)S(1)} %pad_maximum_fusion, bf16[9,16,18]{1,2,0:T(8,128)(2,1)S(1)} %copy.46, bf16[9,16,18]{1,2,0:T(8,128)(2,1)S(1)} %copy.47), kind=kOutput, calls=%fused_computation.35 | convolution fusion | flops 23595264 | bytes 3442816 | tf_op jit(solution)/shard_map/oi,bsirw->bsorw/dot_general | solution.py:39
  17.1 0.6 %fusion.9 = f32[2,4,20,128,32]{3,4,2,1,0:T(8,128)S(1)} fusion(bf16[2,4,18,22,128]{4,2,3,1,0:T(8,128)(2,1)S(1)} %pad_maximum_fusion, bf16[9,16,18]{1,2,0:T(8,128)(2,1)S(1)} %copy.46, bf16[9,16,18]{1,2,0:T(8,128)(2,1)S(1)} %copy.47), kind=kOutput, calls=%fused_computation.34 | convolution fusion | flops 23595264 | bytes 3442816 | tf_op jit(solution)/shard_map/oi,bsirw->bsorw/dot_general | solution.py:39
  17.7 0.2 pad_slice_fusion
  17.9 0.6 %fusion.51 = f32[2,4,20,128,32]{3,4,2,1,0:T(8,128)S(1)} fusion(bf16[9,16,18]{1,2,0:T(8,128)(2,1)S(1)} %copy.46, bf16[9,16,18]{1,2,0:T(8,128)(2,1)S(1)} %copy.47, bf16[2,4,18,3,128]{4,2,3,1,0:T(8,128)(2,1)S(1)} %copy_select_fusion, bf16[2,4,16,16,128]{4,2,3,1,0:T(8,128)(2,1)S(1)} %copy.86, bf16[2,4,2,16,128]{4,2,3,1,0:T(2,128)(2,1)S(1)} %copy.42, ...), kind=kOutput, calls=%fused_computation.100 | convolution fusion | flops 27005184 | bytes 3470476 | tf_op jit(solution)/shard_map/oi,bsirw->bsorw/dot_general | solution.py:39
  18.6 0.6 %fusion.55 = f32[2,4,20,128,32]{3,4,2,1,0:T(8,128)S(1)} fusion(bf16[9,16,18]{1,2,0:T(8,128)(2,1)S(1)} %copy.46, bf16[9,16,18]{1,2,0:T(8,128)(2,1)S(1)} %copy.47, bf16[2,4,18,3,128]{4,2,3,1,0:T(8,128)(2,1)S(1)} %copy_select_fusion, bf16[2,4,16,16,128]{4,2,3,1,0:T(8,128)(2,1)S(1)} %copy.86, bf16[2,4,2,16,128]{4,2,3,1,0:T(2,128)(2,1)S(1)} %copy.42, ...), kind=kOutput, calls=%fused_computation.104 | convolution fusion | flops 27005184 | bytes 3470476 | tf_op jit(solution)/shard_map/oi,bsirw->bsorw/dot_general | solution.py:39
  19.2 0.6 %fusion.59 = f32[2,4,20,128,32]{3,4,2,1,0:T(8,128)S(1)} fusion(bf16[9,16,18]{1,2,0:T(8,128)(2,1)S(1)} %copy.46, bf16[9,16,18]{1,2,0:T(8,128)(2,1)S(1)} %copy.47, bf16[2,4,18,3,128]{4,2,3,1,0:T(8,128)(2,1)S(1)} %copy_select_fusion, bf16[2,4,16,16,128]{4,2,3,1,0:T(8,128)(2,1)S(1)} %copy.86, bf16[2,4,2,16,128]{4,2,3,1,0:T(2,128)(2,1)S(1)} %copy.42, ...), kind=kOutput, calls=%fused_computation.108 | convolution fusion | flops 27005184 | bytes 3470476 | tf_op jit(solution)/shard_map/oi,bsirw->bsorw/dot_general | solution.py:39
  19.8 2.0 %add_bitcast_fusion = f32[2,4,32,20,128]{4,2,3,1,0:T(8,128)S(1)} fusion(f32[2,4,20,128,32]{3,4,2,1,0:T(8,128)S(1)} %fusion.51, f32[2,4,20,128,32]{3,4,2,1,0:T(8,128)S(1)} %fusion.13, f32[2,4,20,128,32]{3,4,2,1,0:T(8,128)S(1)} %fusion.12, f32[2,4,20,128,32]{3,4,2,1,0:T(8,128)S(1)} %fusion.55, f32[2,4,20,128,32]{3,4,2,1,0:T(8,128)S(1)} %fusion.11, ...), kind=kOutput, calls=%fused_computation.12 | convolution fusion | flops 31459584 | bytes 24414464 | tf_op jit(solution)/shard_map/oi,bsirw->bsorw/dot_general | solution.py:39
  21.8 0.0 copy-start.5
  21.8 0.3 fusion.8
  22.1 1.1 %fusion.1 = bf16[2,4,18,20,132]{4,2,3,1,0:T(8,128)(2,1)S(1)} fusion(bf16[2,4,16,20,128]{4,2,3,1,0:T(8,128)(2,1)S(1)} %fusion.8, bf16[2,4,2,20,132]{4,2,3,1,0:T(2,128)(2,1)S(1)} %pad_slice_fusion), kind=kLoop, calls=%fused_computation.13 | loop fusion | flops 2280960 | bytes 1500160 | tf_op jit(solution)/shard_map/concatenate | solution.py:153
  23.3 0.3 fusion.22
  23.6 0.4 %convolution_add_fusion.7 = f32[2,4,16,128,16]{3,4,2,1,0:T(8,128)S(1)} fusion(f32[2,4,16,128,16]{3,4,2,1,0:T(8,128)S(1)} %fusion.22, bf16[2,4,18,20,132]{4,2,3,1,0:T(8,128)(2,1)S(1)} %fusion.1, bf16[9,16,18]{2,1,0:T(8,128)(2,1)S(1)} %copy-done.5), kind=kOutput, calls=%fused_computation.27 | convolution fusion | flops 9699328 | bytes 2887680 | tf_op jit(solution)/shard_map/oi,bsirw->bsorw/dot_general | solution.py:39
  24.0 0.4 %convolution_add_fusion.6 = f32[2,4,16,128,16]{3,4,2,1,0:T(8,128)S(1)} fusion(f32[2,4,16,128,16]{3,4,2,1,0:T(8,128)S(1)} %convolution_add_fusion.7, bf16[2,4,18,20,132]{4,2,3,1,0:T(8,128)(2,1)S(1)} %fusion.1, bf16[9,16,18]{2,1,0:T(8,128)(2,1)S(1)} %copy-done.5), kind=kOutput, calls=%fused_computation.26 | convolution fusion | flops 9699328 | bytes 2887680 | tf_op jit(solution)/shard_map/oi,bsirw->bsorw/dot_general | solution.py:39
  24.4 0.3 convolution_add_fusion.5
  24.7 0.4 %convolution_add_fusion.4 = f32[2,4,16,128,16]{3,4,2,1,0:T(8,128)S(1)} fusion(f32[2,4,16,128,16]{3,4,2,1,0:T(8,128)S(1)} %convolution_add_fusion.5, bf16[2,4,18,20,132]{4,2,3,1,0:T(8,128)(2,1)S(1)} %fusion.1, bf16[9,16,18]{2,1,0:T(8,128)(2,1)S(1)} %copy-done.5), kind=kOutput, calls=%fused_computation.24 | convolution fusion | flops 9699328 | bytes 2887680 | tf_op jit(solution)/shard_map/oi,bsirw->bsorw/dot_general | solution.py:39
  25.1 0.4 %convolution_add_fusion.3 = f32[2,4,16,128,16]{3,4,2,1,0:T(8,128)S(1)} fusion(f32[2,4,16,128,16]{3,4,2,1,0:T(8,128)S(1)} %convolution_add_fusion.4, bf16[2,4,18,20,132]{4,2,3,1,0:T(8,128)(2,1)S(1)} %fusion.1, bf16[9,16,18]{2,1,0:T(8,128)(2,1)S(1)} %copy-done.5), kind=kOutput, calls=%fused_computation.23 | convolution fusion | flops 9699328 | bytes 2887680 | tf_op jit(solution)/shard_map/oi,bsirw->bsorw/dot_general | solution.py:39
  25.6 0.3 convolution_add_fusion.2
  25.9 0.4 %convolution_add_fusion.1 = f32[2,4,16,128,16]{3,4,2,1,0:T(8,128)S(1)} fusion(f32[2,4,16,128,16]{3,4,2,1,0:T(8,128)S(1)} %convolution_add_fusion.2, bf16[2,4,18,20,132]{4,2,3,1,0:T(8,128)(2,1)S(1)} %fusion.1, bf16[9,16,18]{2,1,0:T(8,128)(2,1)S(1)} %copy-done.5), kind=kOutput, calls=%fused_computation.21 | convolution fusion | flops 9699328 | bytes 2887680 | tf_op jit(solution)/shard_map/oi,bsirw->bsorw/dot_general | solution.py:39
  26.3 0.8 %copy-done.1 = f32[2,4,16,16,128]{4,3,2,1,0:T(8,128)S(1)} copy-done((f32[2,4,16,16,128]{4,3,2,1,0:T(8,128)S(1)}, f32[2,4,16,16,128]{4,3,2,1,0:T(8,128)}, u32[]{:S(2)}) %copy-start.1) | copy-done | bytes 1048600
  27.1 0.8 %fusion.106 = (f32[4,16,16,128]{3,1,2,0:T(8,128)S(1)}, f32[2,4,16,16,128]{4,2,3,1,0:T(8,128)S(1)}) fusion(f32[4]{0:T(128)S(1)} %get-tuple-element.28, f32[16]{0:T(128)S(1)} %copy-done.9, f32[2,4,16,128,16]{3,4,2,1,0:T(8,128)S(1)} %convolution_add_fusion.1, bf16[9,16,18]{2,1,0:T(8,128)(2,1)S(1)} %copy-done.5, bf16[2,4,18,20,132]{4,2,3,1,0:T(8,128)(2,1)S(1)} %fusion.1, ...), kind=kOutput, calls=%fused_computation.170 | convolution fusion | flops 11403264 | bytes 5510144 | tf_op jit(solution)/shard_map/oi,bsirw->bsorw/dot_general | solution.py:39
  27.9 0.4 %convolution_reduce_fusion = f32[4,16,4,32]{3,1,2,0:T(8,128)S(1)} fusion(f32[4,16,4,4,128]{4,1,3,2,0:T(8,128)S(1)} %bitcast.209, s32[128]{0:T(128)S(1)} %and_select_fusion), kind=kOutput, calls=%fused_computation.30 | convolution fusion | flops 50360320 | bytes 557568 | tf_op jit(solution)/shard_map/schw,wj->schj/dot_general | solution.py:164
  28.3 0.6 %gather_fusion = f32[4,16,4,32]{3,1,2,0:T(8,128)S(1)} fusion(f32[4,16,4,32]{3,1,2,0:T(8,128)S(1)} %broadcast_multiply_fusion, s32[1024]{0:T(1024)S(1)} %pad_clamp_fusion), kind=kCustom, calls=%fused_computation.2 | custom fusion | bytes 65552 | tf_op jit(solution)/shard_map/jit(_take)/gather | solution.py:170
  28.9 0.3 fusion.24
  29.2 2.0 %collective-permute-start.2 = (f32[2,16,4,32]{3,1,2,0:T(8,128)S(1)}, f32[2,16,4,32]{3,1,2,0:T(8,128)S(1)}, u32[]{:S(2)}, u32[]{:S(2)}) collective-permute-start(f32[2,16,4,32]{3,1,2,0:T(8,128)S(1)} %dynamic-slice_bitcast_fusion), channel_id=1, source_target_pairs={{0,2},{2,0},{1,3},{3,1},{4,6},{6,4},{5,7},{7,5},{8,10},{10,8},{9,1... | collective-permute-start | bytes 49160 | tf_op jit(solution)/shard_map/ppermute | solution.py:67
  31.3 0.9 %copy.51 = f32[2,4,8,16,128]{4,3,2,1,0:T(8,128)} copy(f32[2,4,8,16,128]{4,2,3,1,0:T(8,128)S(1)} %constant_dynamic-slice_fusion) | data formatting | bytes 1048576
  32.2 1.4 %collective-permute-done.2 = f32[2,16,4,32]{3,1,2,0:T(8,128)S(1)} collective-permute-done((f32[2,16,4,32]{3,1,2,0:T(8,128)S(1)}, f32[2,16,4,32]{3,1,2,0:T(8,128)S(1)}, u32[]{:S(2)}, u32[]{:S(2)}) %collective-permute-start.2) | collective-permute-done | bytes 16416 | tf_op jit(solution)/shard_map/ppermute | solution.py:67
  33.6 0.2 fusion.29
  33.8 0.7 %copy.52 = f32[2,16,4,32]{3,2,1,0:T(4,128)} copy(f32[2,16,4,32]{3,1,2,0:T(8,128)S(1)} %fusion.29) | data formatting | bytes 32768
  (30 shorter events, 0.1 us)
Async XLA Ops:
  0.6 28.2 %copy-start = (f32[16,16]{1,0:T(8,128)S(1)}, f32[16,16]{1,0:T(8,128)}, u32[]{:S(2)}) copy-start(f32[16,16]{1,0:T(8,128)} %param.29) | copy-start | bytes 3076
  0.6 11.8 %copy-start.8 = (s32[1,4]{1,0:T(1,128)S(1)}, s32[1,4]{1,0:T(1,128)}, u32[]{:S(2)}) copy-start(s32[1,4]{1,0:T(1,128)} %param.21) | copy-start | bytes 52
  0.7 11.8 %copy-start.10 = (f32[16]{0:T(128)S(1)}, f32[16]{0:T(128)}, u32[]{:S(2)}) copy-start(f32[16]{0:T(128)} %param.26) | copy-start | bytes 196
  0.7 11.8 %copy-start.11 = (f32[16]{0:T(128)S(1)}, f32[16]{0:T(128)}, u32[]{:S(2)}) copy-start(f32[16]{0:T(128)} %param.24) | copy-start | bytes 196
  0.7 11.9 %copy-start.3 = (bf16[9,16,18]{2,1,0:T(8,128)(2,1)S(1)}, bf16[9,16,18]{2,1,0:T(8,128)(2,1)}, u32[]{:S(2)}) copy-start(bf16[9,16,18]{2,1,0:T(8,128)(2,1)} %param.23) | copy-start | bytes 15556
  0.7 12.0 %copy-start.4 = (bf16[9,16,18]{2,1,0:T(8,128)(2,1)S(1)}, bf16[9,16,18]{2,1,0:T(8,128)(2,1)}, u32[]{:S(2)}) copy-start(bf16[9,16,18]{2,1,0:T(8,128)(2,1)} %param.25) | copy-start | bytes 15556
  5.5 8.5 %collective-permute-start.1 = (bf16[2,18,3,128]{3,1,2,0:T(8,128)(2,1)S(1)}, bf16[2,18,3,128]{3,1,2,0:T(8,128)(2,1)S(1)}, u32[]{:S(2)}, u32[]{:S(2)}) collective-permute-start(bf16[2,18,3,128]{3,1,2,0:T(8,128)(2,1)S(1)} %get-tuple-element.21), channel_id=1, source_target_pairs={{4,0},{8,4},{12,8},{5,1},{9,5},{13,9},{6,2},{10,6},{14,10},{7,3},{... | collective-permute-start | bytes 82952 | tf_op jit(solution)/shard_map/ppermute | solution.py:15
  6.8 7.4 %collective-permute-start = (bf16[2,18,3,128]{3,1,2,0:T(8,128)(2,1)S(1)}, bf16[2,18,3,128]{3,1,2,0:T(8,128)(2,1)S(1)}, u32[]{:S(2)}, u32[]{:S(2)}) collective-permute-start(bf16[2,18,3,128]{3,1,2,0:T(8,128)(2,1)S(1)} %get-tuple-element.9), channel_id=1, source_target_pairs={{0,4},{4,8},{8,12},{1,5},{5,9},{9,13},{2,6},{6,10},{10,14},{3,7},{... | collective-permute-start | bytes 82952 | tf_op jit(solution)/shard_map/ppermute | solution.py:12
  21.8 1.4 %copy-start.5 = (bf16[9,16,18]{2,1,0:T(8,128)(2,1)S(1)}, bf16[9,16,18]{2,1,0:T(8,128)(2,1)}, u32[]{:S(2)}) copy-start(bf16[9,16,18]{2,1,0:T(8,128)(2,1)} %param.27) | copy-start | bytes 15556
  25.8 1.2 %copy-start.1 = (f32[2,4,16,16,128]{4,3,2,1,0:T(8,128)S(1)}, f32[2,4,16,16,128]{4,3,2,1,0:T(8,128)}, u32[]{:S(2)}) copy-start(f32[2,4,16,16,128]{4,3,2,1,0:T(8,128)} %param.18) | copy-start | bytes 3145732
  25.9 1.2 %copy-start.9 = (f32[16]{0:T(128)S(1)}, f32[16]{0:T(128)}, u32[]{:S(2)}) copy-start(f32[16]{0:T(128)} %param.28) | copy-start | bytes 196
  27.9 5.7 %copy-start.2 = (f32[2,16,4,32]{3,2,1,0:T(4,128)S(1)}, f32[2,16,4,32]{3,2,1,0:T(4,128)}, u32[]{:S(2)}) copy-start(f32[2,16,4,32]{3,2,1,0:T(4,128)} %param.22) | copy-start | bytes 49156
  27.9 5.7 %copy-start.6 = (f32[16,16]{1,0:T(8,128)S(1)}, f32[16,16]{1,0:T(8,128)}, u32[]{:S(2)}) copy-start(f32[16,16]{1,0:T(8,128)} %param.30) | copy-start | bytes 3076
  27.9 5.7 %copy-start.7 = (f32[16]{0:T(128)S(1)}, f32[16]{0:T(128)}, u32[]{:S(2)}) copy-start(f32[16]{0:T(128)} %param.31) | copy-start | bytes 196
  29.2 4.3 %collective-permute-start.2 = (f32[2,16,4,32]{3,1,2,0:T(8,128)S(1)}, f32[2,16,4,32]{3,1,2,0:T(8,128)S(1)}, u32[]{:S(2)}, u32[]{:S(2)}) collective-permute-start(f32[2,16,4,32]{3,1,2,0:T(8,128)S(1)} %dynamic-slice_bitcast_fusion), channel_id=1, source_target_pairs={{0,2},{2,0},{1,3},{3,1},{4,6},{6,4},{5,7},{7,5},{8,10},{10,8},{9,1... | collective-permute-start | bytes 49160 | tf_op jit(solution)/shard_map/ppermute | solution.py:67

commit v13 on v12

--- a/solution.py
+++ b/solution.py
@@ -53,6 +53,10 @@
 
 def logistic(value):
     return 0.5 + 0.5 * jnp.tanh(0.5 * value)
+
+
+def channel_map(matrix, blocks):
+    return jnp.sum(matrix[None, :, :, None, None] * blocks[:, None], axis=2)
 
 
 def exchange_sum(part, owned):
@@ -167,10 +171,13 @@
     pooled = jnp.sum(
         cols.reshape(slots, chans, row_count // 4, 4, column_count // 4), axis=3
     ) / 16.0
-    ordered = jnp.take(pooled, coarse_perm[0], axis=0)
-    part = jnp.einsum("oc,kcij->koij", u_pool, ordered, precision=lax.Precision.HIGHEST)
+    hits = coarse_perm[0][:, None] == jnp.arange(slots)[None, :]
+    ordered = jnp.sum(
+        jnp.where(hits[:, :, None, None, None], pooled[None], jnp.zeros_like(pooled[None])), axis=1
+    )
+    part = channel_map(u_pool, ordered)
     pre = exchange_sum(part, coarse_state.shape[0])
-    pre = pre + jnp.einsum("oc,kcij->koij", u_state, coarse_state, precision=lax.Precision.HIGHEST)
+    pre = pre + channel_map(u_state, coarse_state)
     pre = pre + b_coarse[None, :, None, None]
     coarse_next = coarse_state + jnp.tanh(pre)
     return (new_half, coarse_next)

time: 34.8 us -> 34.9 us (level)
  other arithmetic: 4.4 us -> 6.29 us
  local copies, waits for them, and re-layouts: 7.14 us -> 5.92 us
  matrix products: 11.5 us -> 11 us
    reduce_sum x0 -> x3, other arithmetic: none -> 1.07 us  [the longest x2 0.96 us: channel_map(): return jnp.sum(matrix[None, :, :, None, None] * blocks[:, None], axis=2)]
    add x0 -> x1, other arithmetic: none -> 0.72 us  [shards(): coarse_next = coarse_state + jnp.tanh(pre)]
    unnamed x30, local copies, waits for them, and re-layouts: 5.14 us -> 4.47 us
    gather x1 -> x0, local copies, waits for them, and re-layouts: 0.56 us -> none  [shards(): ordered = jnp.take(pooled, coarse_perm[0], axis=0)]
    dot_general x2 -> x0, matrix products: 0.52 us -> none  [the longest x1 0.32 us: shards(): jnp.einsum('oc,kcij->koij', u_pool, ordered, precision=lax.Precision.HIGH...]
  transfers between devices with their start and end apart: 3 -> 3, of which waited for: 1 -> 1; matrix products, arithmetic and copies ran while one was open for 8% -> 9% of each run, Pallas kernels for 0% -> 0%
where the time goes in v13:
time: 34.9 us; the launch traced here: 34.6 us
  matrix products  11 us (32%)
  starting transfers between devices  8.87 us (25%)
  other arithmetic  6.29 us (18%)
  local copies, waits for them, and re-layouts  5.92 us (17%)
  waiting for transfers between devices  1.42 us (4%)
  between operations  1.06 us (3%)
    dot_general x18, matrix products, apply_filter(): jnp.einsum('oi,bsirw->bsorw', filter_weight[(left_operand + 1) * 3 + (rig...  10.6 us
    ppermute x1, starting transfers between devices, padded(): lax.ppermute(lax.slice_in_dim(block, block.shape[dim] - width, None, axis...  5.59 us
    unnamed x30, local copies, waits for them, and re-layouts  4.47 us
    ppermute x1, starting transfers between devices, exchange_sum(): chunk = lax.ppermute(chunk, 'band', perm)  1.99 us
    ppermute x1, waiting for transfers between devices, exchange_sum(): chunk = lax.ppermute(chunk, 'band', perm)  1.41 us
    ppermute x1, starting transfers between devices, padded(): lax.ppermute(lax.slice_in_dim(block, 0, width, axis=dim), axis, backward)  1.29 us
    concatenate x1, other arithmetic, shards(): jnp.concatenate([first[:, :, :inputs_count, 1:row_count + 5, :], gated_pa...  1.14 us
    reduce_sum x2, other arithmetic, channel_map(): return jnp.sum(matrix[None, :, :, None, None] * blocks[:, None], axis=2)  0.96 us
  transfers between devices with their start and end apart: 3, of which 1 were waited for; matrix products, arithmetic and copies ran while one was open for 9% of the time, Pallas kernels for 0%

profile of v13, /device:TPU:0, one launch (start us, length us, event | category | flops | bytes accessed | tf_op | source)
XLA Modules:
  0.0 34.6 jit_solution(4190788494784752519)
XLA Ops:
  0.7 0.8 %not_and_fusion = (pred[4]{0:T(512)(128)(4,1)S(1)}, pred[4]{0:T(512)(128)(4,1)S(1)}) fusion(s32[4]{0:T(128)} %param.19, s32[]{:T(128)S(6)} %add.145, s32[]{:T(128)S(6)} %mul.61, s32[4,2]{0,1:T(2,128)} %param.20), kind=kLoop, calls=%fused_computation.130 | loop fusion | flops 24 | bytes 48 | tf_op jit(solution)/shard_map/and | solution.py:109
  1.5 0.8 %compare_and_fusion.1 = (pred[4]{0:T(512)(128)(4,1)S(1)}, s32[4]{0:T(128)S(1)}, pred[4]{0:T(512)(128)(4,1)S(1)}, pred[4]{0:T(512)(128)(4,1)S(1)}, s32[4]{0:T(128...) fusion(s32[]{:T(128)S(6)} %mul.61, s32[4,2]{0,1:T(2,128)} %param.20, pred[4]{0:T(512)(128)(4,1)S(1)} %get-tuple-element.12, ...), kind=kLoop, calls=%fused_computation.126 | loop fusion | flops 100 | bytes 96 | tf_op jit(solution)/shard_map/jit(_take)/and | solution.py:124
  2.2 0.7 %fusion.75 = (f32[4]{0:T(128)S(1)}, pred[4]{0:T(512)(128)(4,1)S(1)}) fusion(s32[4]{0:T(128)} %param.19, pred[4]{0:T(512)(128)(4,1)S(1)} %get-tuple-element.27), kind=kLoop, calls=%fused_computation.139 | loop fusion | flops 16 | bytes 40 | tf_op jit(solution)/shard_map/convert_element_type | solution.py:161
  2.9 1.6 %copy.72 = bf16[2,4,16,16,128]{4,2,3,1,0:T(8,128)(2,1)S(1)} copy(f32[2,4,16,16,128]{4,3,2,1,0:T(8,128)} %param.18) | data formatting | bytes 1572864 | tf_op args[1]
  4.5 0.9 %copy.37 = bf16[2,4,2,16,128]{4,2,3,1,0:T(2,128)(2,1)S(1)} copy(bf16[2,4,2,16,128]{4,3,2,1,0:T(8,128)(2,1)} %param.17) | data formatting | bytes 131072 | tf_op args[0]
  5.4 0.2 select_reduce_fusion.2
  5.5 1.3 %collective-permute-start.1 = (bf16[2,18,3,128]{3,1,2,0:T(8,128)(2,1)S(1)}, bf16[2,18,3,128]{3,1,2,0:T(8,128)(2,1)S(1)}, u32[]{:S(2)}, u32[]{:S(2)}) collective-permute-start(bf16[2,18,3,128]{3,1,2,0:T(8,128)(2,1)S(1)} %get-tuple-element.21), channel_id=1, source_target_pairs={{4,0},{8,4},{12,8},{5,1},{9,5},{13,9},{6,2},{10,6},{14,10},{7,3},{... | collective-permute-start | bytes 82952 | tf_op jit(solution)/shard_map/ppermute | solution.py:15
  6.8 5.6 %collective-permute-start = (bf16[2,18,3,128]{3,1,2,0:T(8,128)(2,1)S(1)}, bf16[2,18,3,128]{3,1,2,0:T(8,128)(2,1)S(1)}, u32[]{:S(2)}, u32[]{:S(2)}) collective-permute-start(bf16[2,18,3,128]{3,1,2,0:T(8,128)(2,1)S(1)} %get-tuple-element.9), channel_id=1, source_target_pairs={{0,4},{4,8},{8,12},{1,5},{5,9},{9,13},{2,6},{6,10},{10,14},{3,7},{... | collective-permute-start | bytes 82952 | tf_op jit(solution)/shard_map/ppermute | solution.py:12
  12.5 0.1 iota_compare_fusion.2
  12.6 0.3 multiply_reduce_fusion.1
  12.9 0.1 pad_maximum_fusion.4
  13.0 0.1 copy.41
  13.1 0.1 copy.42
  13.3 0.6 %gather_fusion.1 = bf16[4,2,18,3,128]{4,2,3,1,0:T(8,128)(2,1)S(1)} fusion(bf16[2,4,18,3,128]{4,2,3,1,0:T(8,128)(2,1)S(1)} %get-tuple-element.22, s32[1024]{0:T(1024)S(1)} %pad_clamp_fusion), kind=kCustom, calls=%fused_computation.1.clone | custom fusion | bytes 221200 | tf_op jit(solution)/shard_map/jit(_take)/gather | solution.py:127
  13.9 0.6 %gather_fusion = bf16[4,2,18,3,128]{4,2,3,1,0:T(8,128)(2,1)S(1)} fusion(bf16[2,4,18,3,128]{4,2,3,1,0:T(8,128)(2,1)S(1)} %get-tuple-element.10, s32[1024]{0:T(1024)S(1)} %pad_clamp_fusion.1), kind=kCustom, calls=%fused_computation.clone | custom fusion | bytes 221200 | tf_op jit(solution)/shard_map/jit(_take)/gather | solution.py:124
  14.5 0.1 copy_select_fusion
  14.6 0.4 %pad_maximum_fusion = bf16[2,4,18,22,128]{4,2,3,1,0:T(8,128)(2,1)S(1)} fusion(bf16[2,4,18,3,128]{4,2,3,1,0:T(8,128)(2,1)S(1)} %copy_select_fusion, bf16[2,4,16,16,128]{4,2,3,1,0:T(8,128)(2,1)S(1)} %copy.72, bf16[2,4,2,16,128]{4,2,3,1,0:T(2,128)(2,1)S(1)} %copy.37, bf16[4,2,18,3,128]{4,2,3,1,0:T(8,128)(2,1)S(1)} %gather_fusion, ...), kind=kLoop, calls=%fused_computation.31 | loop fusion | flops 3409920 | bytes 1649676 | tf_op jit(solution)/shard_map/concatenate | solution.py:139
  15.0 0.6 %fusion.13 = f32[2,4,20,128,32]{3,4,2,1,0:T(8,128)S(1)} fusion(bf16[2,4,18,22,128]{4,2,3,1,0:T(8,128)(2,1)S(1)} %pad_maximum_fusion, bf16[9,16,18]{1,2,0:T(8,128)(2,1)S(1)} %copy.41, bf16[9,16,18]{1,2,0:T(8,128)(2,1)S(1)} %copy.42), kind=kOutput, calls=%fused_computation.38 | convolution fusion | flops 23595264 | bytes 3442816 | tf_op jit(solution)/shard_map/oi,bsirw->bsorw/dot_general | solution.py:39
  15.7 0.6 %fusion.12 = f32[2,4,20,128,32]{3,4,2,1,0:T(8,128)S(1)} fusion(bf16[2,4,18,22,128]{4,2,3,1,0:T(8,128)(2,1)S(1)} %pad_maximum_fusion, bf16[9,16,18]{1,2,0:T(8,128)(2,1)S(1)} %copy.41, bf16[9,16,18]{1,2,0:T(8,128)(2,1)S(1)} %copy.42), kind=kOutput, calls=%fused_computation.37 | convolution fusion | flops 23595264 | bytes 3442816 | tf_op jit(solution)/shard_map/oi,bsirw->bsorw/dot_general | solution.py:39
  16.3 0.6 %fusion.11 = f32[2,4,20,128,32]{3,4,2,1,0:T(8,128)S(1)} fusion(bf16[2,4,18,22,128]{4,2,3,1,0:T(8,128)(2,1)S(1)} %pad_maximum_fusion, bf16[9,16,18]{1,2,0:T(8,128)(2,1)S(1)} %copy.41, bf16[9,16,18]{1,2,0:T(8,128)(2,1)S(1)} %copy.42), kind=kOutput, calls=%fused_computation.36 | convolution fusion | flops 23595264 | bytes 3442816 | tf_op jit(solution)/shard_map/oi,bsirw->bsorw/dot_general | solution.py:39
  16.9 0.6 %fusion.10 = f32[2,4,20,128,32]{3,4,2,1,0:T(8,128)S(1)} fusion(bf16[2,4,18,22,128]{4,2,3,1,0:T(8,128)(2,1)S(1)} %pad_maximum_fusion, bf16[9,16,18]{1,2,0:T(8,128)(2,1)S(1)} %copy.41, bf16[9,16,18]{1,2,0:T(8,128)(2,1)S(1)} %copy.42), kind=kOutput, calls=%fused_computation.35 | convolution fusion | flops 23595264 | bytes 3442816 | tf_op jit(solution)/shard_map/oi,bsirw->bsorw/dot_general | solution.py:39
  17.5 0.6 %fusion.9 = f32[2,4,20,128,32]{3,4,2,1,0:T(8,128)S(1)} fusion(bf16[2,4,18,22,128]{4,2,3,1,0:T(8,128)(2,1)S(1)} %pad_maximum_fusion, bf16[9,16,18]{1,2,0:T(8,128)(2,1)S(1)} %copy.41, bf16[9,16,18]{1,2,0:T(8,128)(2,1)S(1)} %copy.42), kind=kOutput, calls=%fused_computation.34 | convolution fusion | flops 23595264 | bytes 3442816 | tf_op jit(solution)/shard_map/oi,bsirw->bsorw/dot_general | solution.py:39
  18.1 0.2 pad_slice_fusion
  18.4 0.6 %fusion.38 = f32[2,4,20,128,32]{3,4,2,1,0:T(8,128)S(1)} fusion(bf16[9,16,18]{1,2,0:T(8,128)(2,1)S(1)} %copy.41, bf16[9,16,18]{1,2,0:T(8,128)(2,1)S(1)} %copy.42, bf16[2,4,18,3,128]{4,2,3,1,0:T(8,128)(2,1)S(1)} %copy_select_fusion, bf16[2,4,16,16,128]{4,2,3,1,0:T(8,128)(2,1)S(1)} %copy.72, bf16[2,4,2,16,128]{4,2,3,1,0:T(2,128)(2,1)S(1)} %copy.37, ...), kind=kOutput, calls=%fused_computation.89 | convolution fusion | flops 27005184 | bytes 3470476 | tf_op jit(solution)/shard_map/oi,bsirw->bsorw/dot_general | solution.py:39
  19.0 0.6 %fusion.42 = f32[2,4,20,128,32]{3,4,2,1,0:T(8,128)S(1)} fusion(bf16[9,16,18]{1,2,0:T(8,128)(2,1)S(1)} %copy.41, bf16[9,16,18]{1,2,0:T(8,128)(2,1)S(1)} %copy.42, bf16[2,4,18,3,128]{4,2,3,1,0:T(8,128)(2,1)S(1)} %copy_select_fusion, bf16[2,4,16,16,128]{4,2,3,1,0:T(8,128)(2,1)S(1)} %copy.72, bf16[2,4,2,16,128]{4,2,3,1,0:T(2,128)(2,1)S(1)} %copy.37, ...), kind=kOutput, calls=%fused_computation.93 | convolution fusion | flops 27005184 | bytes 3470476 | tf_op jit(solution)/shard_map/oi,bsirw->bsorw/dot_general | solution.py:39
  19.6 0.6 %fusion.46 = f32[2,4,20,128,32]{3,4,2,1,0:T(8,128)S(1)} fusion(bf16[9,16,18]{1,2,0:T(8,128)(2,1)S(1)} %copy.41, bf16[9,16,18]{1,2,0:T(8,128)(2,1)S(1)} %copy.42, bf16[2,4,18,3,128]{4,2,3,1,0:T(8,128)(2,1)S(1)} %copy_select_fusion, bf16[2,4,16,16,128]{4,2,3,1,0:T(8,128)(2,1)S(1)} %copy.72, bf16[2,4,2,16,128]{4,2,3,1,0:T(2,128)(2,1)S(1)} %copy.37, ...), kind=kOutput, calls=%fused_computation.97 | convolution fusion | flops 27005184 | bytes 3470476 | tf_op jit(solution)/shard_map/oi,bsirw->bsorw/dot_general | solution.py:39
  20.2 2.0 %add_bitcast_fusion = f32[2,4,32,20,128]{4,2,3,1,0:T(8,128)S(1)} fusion(f32[2,4,20,128,32]{3,4,2,1,0:T(8,128)S(1)} %fusion.38, f32[2,4,20,128,32]{3,4,2,1,0:T(8,128)S(1)} %fusion.13, f32[2,4,20,128,32]{3,4,2,1,0:T(8,128)S(1)} %fusion.12, f32[2,4,20,128,32]{3,4,2,1,0:T(8,128)S(1)} %fusion.42, f32[2,4,20,128,32]{3,4,2,1,0:T(8,128)S(1)} %fusion.11, ...), kind=kOutput, calls=%fused_computation.11 | convolution fusion | flops 31459584 | bytes 24414464 | tf_op jit(solution)/shard_map/oi,bsirw->bsorw/dot_general | solution.py:39
  22.3 0.0 copy-start.4
  22.3 0.3 fusion.8
  22.6 1.1 %fusion.1 = bf16[2,4,18,20,132]{4,2,3,1,0:T(8,128)(2,1)S(1)} fusion(bf16[2,4,16,20,128]{4,2,3,1,0:T(8,128)(2,1)S(1)} %fusion.8, bf16[2,4,2,20,132]{4,2,3,1,0:T(2,128)(2,1)S(1)} %pad_slice_fusion), kind=kLoop, calls=%fused_computation.13 | loop fusion | flops 2280960 | bytes 1500160 | tf_op jit(solution)/shard_map/concatenate | solution.py:157
  23.7 0.3 fusion.22
  24.0 0.4 %convolution_add_fusion.7 = f32[2,4,16,128,16]{3,4,2,1,0:T(8,128)S(1)} fusion(f32[2,4,16,128,16]{3,4,2,1,0:T(8,128)S(1)} %fusion.22, bf16[2,4,18,20,132]{4,2,3,1,0:T(8,128)(2,1)S(1)} %fusion.1, bf16[9,16,18]{2,1,0:T(8,128)(2,1)S(1)} %copy-done.4), kind=kOutput, calls=%fused_computation.27 | convolution fusion | flops 9699328 | bytes 2887680 | tf_op jit(solution)/shard_map/oi,bsirw->bsorw/dot_general | solution.py:39
  24.4 0.4 %convolution_add_fusion.6 = f32[2,4,16,128,16]{3,4,2,1,0:T(8,128)S(1)} fusion(f32[2,4,16,128,16]{3,4,2,1,0:T(8,128)S(1)} %convolution_add_fusion.7, bf16[2,4,18,20,132]{4,2,3,1,0:T(8,128)(2,1)S(1)} %fusion.1, bf16[9,16,18]{2,1,0:T(8,128)(2,1)S(1)} %copy-done.4), kind=kOutput, calls=%fused_computation.26 | convolution fusion | flops 9699328 | bytes 2887680 | tf_op jit(solution)/shard_map/oi,bsirw->bsorw/dot_general | solution.py:39
  24.8 0.3 convolution_add_fusion.5
  25.1 0.4 %convolution_add_fusion.4 = f32[2,4,16,128,16]{3,4,2,1,0:T(8,128)S(1)} fusion(f32[2,4,16,128,16]{3,4,2,1,0:T(8,128)S(1)} %convolution_add_fusion.5, bf16[2,4,18,20,132]{4,2,3,1,0:T(8,128)(2,1)S(1)} %fusion.1, bf16[9,16,18]{2,1,0:T(8,128)(2,1)S(1)} %copy-done.4), kind=kOutput, calls=%fused_computation.24 | convolution fusion | flops 9699328 | bytes 2887680 | tf_op jit(solution)/shard_map/oi,bsirw->bsorw/dot_general | solution.py:39
  25.6 0.4 %convolution_add_fusion.3 = f32[2,4,16,128,16]{3,4,2,1,0:T(8,128)S(1)} fusion(f32[2,4,16,128,16]{3,4,2,1,0:T(8,128)S(1)} %convolution_add_fusion.4, bf16[2,4,18,20,132]{4,2,3,1,0:T(8,128)(2,1)S(1)} %fusion.1, bf16[9,16,18]{2,1,0:T(8,128)(2,1)S(1)} %copy-done.4), kind=kOutput, calls=%fused_computation.23 | convolution fusion | flops 9699328 | bytes 2887680 | tf_op jit(solution)/shard_map/oi,bsirw->bsorw/dot_general | solution.py:39
  26.0 0.3 convolution_add_fusion.2
  26.3 0.4 %convolution_add_fusion.1 = f32[2,4,16,128,16]{3,4,2,1,0:T(8,128)S(1)} fusion(f32[2,4,16,128,16]{3,4,2,1,0:T(8,128)S(1)} %convolution_add_fusion.2, bf16[2,4,18,20,132]{4,2,3,1,0:T(8,128)(2,1)S(1)} %fusion.1, bf16[9,16,18]{2,1,0:T(8,128)(2,1)S(1)} %copy-done.4), kind=kOutput, calls=%fused_computation.21 | convolution fusion | flops 9699328 | bytes 2887680 | tf_op jit(solution)/shard_map/oi,bsirw->bsorw/dot_general | solution.py:39
  26.7 0.8 %copy-done = f32[2,4,16,16,128]{4,3,2,1,0:T(8,128)S(1)} copy-done((f32[2,4,16,16,128]{4,3,2,1,0:T(8,128)S(1)}, f32[2,4,16,16,128]{4,3,2,1,0:T(8,128)}, u32[]{:S(2)}) %copy-start) | copy-done | bytes 1048600
  27.5 0.8 %fusion.91 = (f32[4,16,16,128]{3,1,2,0:T(8,128)S(1)}, f32[2,4,16,16,128]{4,2,3,1,0:T(8,128)S(1)}) fusion(f32[4]{0:T(128)S(1)} %get-tuple-element.28, f32[16]{0:T(128)S(1)} %copy-done.8, f32[2,4,16,128,16]{3,4,2,1,0:T(8,128)S(1)} %convolution_add_fusion.1, bf16[9,16,18]{2,1,0:T(8,128)(2,1)S(1)} %copy-done.4, bf16[2,4,18,20,132]{4,2,3,1,0:T(8,128)(2,1)S(1)} %fusion.1, ...), kind=kOutput, calls=%fused_computation.155 | convolution fusion | flops 11403264 | bytes 5510144 | tf_op jit(solution)/shard_map/oi,bsirw->bsorw/dot_general | solution.py:39
  28.3 0.0 copy-start.7
  28.3 0.4 %convolution_reduce_fusion = f32[4,16,4,32]{3,1,2,0:T(8,128)S(1)} fusion(f32[4,16,4,4,128]{4,1,3,2,0:T(8,128)S(1)} %bitcast.178, s32[128]{0:T(128)S(1)} %and_select_fusion), kind=kOutput, calls=%fused_computation.30 | convolution fusion | flops 50360320 | bytes 557568 | tf_op jit(solution)/shard_map/schw,wj->schj/dot_general | solution.py:168
  28.7 0.1 select_reduce_fusion
  28.8 0.6 %multiply_reduce_fusion = f32[4,16,4,32]{3,2,1,0:T(4,128)S(1)} fusion(f32[4,16,4,32]{3,1,2,0:T(8,128)S(1)} %select_reduce_fusion, f32[16,16]{1,0:T(8,128)S(1)} %copy-done.6), kind=kLoop, calls=%fused_computation.12 | loop fusion | flops 253952 | bytes 66560 | tf_op jit(solution)/shard_map/reduce_sum | solution.py:59
  29.5 2.0 %collective-permute-start.2 = (f32[2,16,4,32]{3,2,1,0:T(4,128)S(1)}, f32[2,16,4,32]{3,2,1,0:T(4,128)S(1)}, u32[]{:S(2)}, u32[]{:S(2)}) collective-permute-start(f32[2,16,4,32]{3,2,1,0:T(4,128)S(1)} %constant_dynamic-slice_fusion), channel_id=1, source_target_pairs={{0,2},{2,0},{1,3},{3,1},{4,6},{6,4},{5,7},{7,5},{8,10},{10,8},{9,1... | collective-permute-start | bytes 49160 | tf_op jit(solution)/shard_map/ppermute | solution.py:71
  31.5 0.9 %copy.45 = f32[2,4,8,16,128]{4,3,2,1,0:T(8,128)} copy(f32[2,4,8,16,128]{4,2,3,1,0:T(8,128)S(1)} %constant_dynamic-slice_fusion.1) | data formatting | bytes 1048576
  32.4 1.4 %collective-permute-done.2 = f32[2,16,4,32]{3,2,1,0:T(4,128)S(1)} collective-permute-done((f32[2,16,4,32]{3,2,1,0:T(4,128)S(1)}, f32[2,16,4,32]{3,2,1,0:T(4,128)S(1)}, u32[]{:S(2)}, u32[]{:S(2)}) %collective-permute-start.2) | collective-permute-done | bytes 16416 | tf_op jit(solution)/shard_map/ppermute | solution.py:71
  33.8 0.7 %tanh_add_fusion = f32[2,16,4,32]{3,2,1,0:T(4,128)} fusion(f32[2,16,4,32]{3,2,1,0:T(4,128)S(1)} %copy-done.1, f32[2,16,4,32]{3,2,1,0:T(4,128)S(1)} %multiply_reduce_fusion.1, f32[2,16,4,32]{3,2,1,0:T(4,128)S(1)} %collective-permute-done.2, f32[4,16,4,32]{3,2,1,0:T(4,128)S(1)} %multiply_reduce_fusion, s32[]{:T(128)S(6)} %select_n.70, f32[16]{0:T(128)S(1)} %copy-done.7), kind=kLoop, calls=%fused_computation.57 | loop fusion | flops 16384 | bytes 81988 | tf_op jit(solution)/shard_map/add | solution.py:182
  (30 shorter events, 0.1 us)
Async XLA Ops:
  0.6 11.8 %copy-start.1 = (f32[2,16,4,32]{3,2,1,0:T(4,128)S(1)}, f32[2,16,4,32]{3,2,1,0:T(4,128)}, u32[]{:S(2)}) copy-start(f32[2,16,4,32]{3,2,1,0:T(4,128)} %param.22) | copy-start | bytes 49156
  0.6 11.9 %copy-start.9 = (s32[1,4]{1,0:T(1,128)S(1)}, s32[1,4]{1,0:T(1,128)}, u32[]{:S(2)}) copy-start(s32[1,4]{1,0:T(1,128)} %param.21) | copy-start | bytes 52
  0.7 11.9 %copy-start.5 = (f32[16,16]{1,0:T(8,128)S(1)}, f32[16,16]{1,0:T(8,128)}, u32[]{:S(2)}) copy-start(f32[16,16]{1,0:T(8,128)} %param.30) | copy-start | bytes 3076
  0.7 12.2 %copy-start.10 = (f32[16]{0:T(128)S(1)}, f32[16]{0:T(128)}, u32[]{:S(2)}) copy-start(f32[16]{0:T(128)} %param.26) | copy-start | bytes 196
  0.7 12.2 %copy-start.11 = (f32[16]{0:T(128)S(1)}, f32[16]{0:T(128)}, u32[]{:S(2)}) copy-start(f32[16]{0:T(128)} %param.24) | copy-start | bytes 196
  0.7 12.3 %copy-start.2 = (bf16[9,16,18]{2,1,0:T(8,128)(2,1)S(1)}, bf16[9,16,18]{2,1,0:T(8,128)(2,1)}, u32[]{:S(2)}) copy-start(bf16[9,16,18]{2,1,0:T(8,128)(2,1)} %param.23) | copy-start | bytes 15556
  0.7 12.4 %copy-start.3 = (bf16[9,16,18]{2,1,0:T(8,128)(2,1)S(1)}, bf16[9,16,18]{2,1,0:T(8,128)(2,1)}, u32[]{:S(2)}) copy-start(bf16[9,16,18]{2,1,0:T(8,128)(2,1)} %param.25) | copy-start | bytes 15556
  5.5 8.9 %collective-permute-start.1 = (bf16[2,18,3,128]{3,1,2,0:T(8,128)(2,1)S(1)}, bf16[2,18,3,128]{3,1,2,0:T(8,128)(2,1)S(1)}, u32[]{:S(2)}, u32[]{:S(2)}) collective-permute-start(bf16[2,18,3,128]{3,1,2,0:T(8,128)(2,1)S(1)} %get-tuple-element.21), channel_id=1, source_target_pairs={{4,0},{8,4},{12,8},{5,1},{9,5},{13,9},{6,2},{10,6},{14,10},{7,3},{... | collective-permute-start | bytes 82952 | tf_op jit(solution)/shard_map/ppermute | solution.py:15
  6.8 7.8 %collective-permute-start = (bf16[2,18,3,128]{3,1,2,0:T(8,128)(2,1)S(1)}, bf16[2,18,3,128]{3,1,2,0:T(8,128)(2,1)S(1)}, u32[]{:S(2)}, u32[]{:S(2)}) collective-permute-start(bf16[2,18,3,128]{3,1,2,0:T(8,128)(2,1)S(1)} %get-tuple-element.9), channel_id=1, source_target_pairs={{0,4},{4,8},{8,12},{1,5},{5,9},{9,13},{2,6},{6,10},{10,14},{3,7},{... | collective-permute-start | bytes 82952 | tf_op jit(solution)/shard_map/ppermute | solution.py:12
  22.3 1.4 %copy-start.4 = (bf16[9,16,18]{2,1,0:T(8,128)(2,1)S(1)}, bf16[9,16,18]{2,1,0:T(8,128)(2,1)}, u32[]{:S(2)}) copy-start(bf16[9,16,18]{2,1,0:T(8,128)(2,1)} %param.27) | copy-start | bytes 15556
  26.3 1.2 %copy-start = (f32[2,4,16,16,128]{4,3,2,1,0:T(8,128)S(1)}, f32[2,4,16,16,128]{4,3,2,1,0:T(8,128)}, u32[]{:S(2)}) copy-start(f32[2,4,16,16,128]{4,3,2,1,0:T(8,128)} %param.18) | copy-start | bytes 3145732
  26.3 1.2 %copy-start.8 = (f32[16]{0:T(128)S(1)}, f32[16]{0:T(128)}, u32[]{:S(2)}) copy-start(f32[16]{0:T(128)} %param.28) | copy-start | bytes 196
  27.5 1.3 %copy-start.6 = (f32[16,16]{1,0:T(8,128)S(1)}, f32[16,16]{1,0:T(8,128)}, u32[]{:S(2)}) copy-start(f32[16,16]{1,0:T(8,128)} %param.29) | copy-start | bytes 3076
  28.3 5.5 %copy-start.7 = (f32[16]{0:T(128)S(1)}, f32[16]{0:T(128)}, u32[]{:S(2)}) copy-start(f32[16]{0:T(128)} %param.31) | copy-start | bytes 196
  29.5 4.3 %collective-permute-start.2 = (f32[2,16,4,32]{3,2,1,0:T(4,128)S(1)}, f32[2,16,4,32]{3,2,1,0:T(4,128)S(1)}, u32[]{:S(2)}, u32[]{:S(2)}) collective-permute-start(f32[2,16,4,32]{3,2,1,0:T(4,128)S(1)} %constant_dynamic-slice_fusion), channel_id=1, source_target_pairs={{0,2},{2,0},{1,3},{3,1},{4,6},{6,4},{5,7},{7,5},{8,10},{10,8},{9,1... | collective-permute-start | bytes 49160 | tf_op jit(solution)/shard_map/ppermute | solution.py:71

commit v14 on v12

--- a/solution.py
+++ b/solution.py
@@ -57,15 +57,23 @@
 
 def exchange_sum(part, owned):
     bands = lax.axis_size("band")
+    reps = lax.axis_size("rep")
     band = lax.axis_index("band")
     total = None
     for shift in range(bands):
-        target = (band + shift) % bands
-        chunk = lax.dynamic_slice_in_dim(part, target * owned, owned, 0)
-        if shift:
-            perm = [(b, (b + shift) % bands) for b in range(bands)]
-            chunk = lax.ppermute(chunk, "band", perm)
-        total = chunk if total is None else total + chunk
+        pair = None
+        for step in range(reps):
+            target = (band + shift) % bands
+            chunk = lax.dynamic_slice_in_dim(part, target * owned, owned, 0)
+            if shift or step:
+                perm = [
+                    (b * reps + r, ((b + shift) % bands) * reps + (r + step) % reps)
+                    for b in range(bands)
+                    for r in range(reps)
+                ]
+                chunk = lax.ppermute(chunk, ("band", "rep"), perm)
+            pair = chunk if pair is None else pair + chunk
+        total = pair if total is None else total + pair
     return total
 
 
@@ -86,6 +94,11 @@
     u_state,
     b_coarse,
 ):
+    reps = lax.axis_size("rep")
+    rep = lax.axis_index("rep")
+    per_core = features.shape[0] // reps
+    features = lax.dynamic_slice_in_dim(features, rep * per_core, per_core, 0)
+    state = lax.dynamic_slice_in_dim(state, rep * per_core, per_core, 0)
     slots = state.shape[1]
     chans = state.shape[2]
     row_count = state.shape[3]
@@ -156,7 +169,22 @@
     )
     live_scale = alive.astype(jnp.float32)[None, :, None, None, None]
     new_state = ((1.0 - update) * state + update * candidate) * live_scale
-    new_half = lax.dynamic_slice_in_dim(new_state, start, half, 2)
+    groups = []
+    for step in range(reps):
+        piece = lax.dynamic_slice_in_dim(new_state, ((rep + step) % reps) * half, half, 2)
+        if step:
+            piece = lax.ppermute(piece, "rep", [(r, (r + step) % reps) for r in range(reps)])
+        groups.append(piece)
+    new_half = jnp.concatenate(
+        [
+            sum(
+                jnp.where((rep - step) % reps == owner, piece, jnp.zeros_like(piece))
+                for step, piece in enumerate(groups)
+            )
+            for owner in range(reps)
+        ],
+        axis=0,
+    )
     summed = jnp.sum(new_state, axis=0)
     column_pool = (
         jnp.arange(column_count)[:, None] // 4 == jnp.arange(column_count // 4)[None, :]

time: 34.8 us -> 31.3 us (0.90)
  waiting for transfers between devices: 1.42 us -> 7 us
  matrix products: 11.5 us -> 7.74 us
  other arithmetic: 4.4 us -> 1.36 us
  local copies, waits for them, and re-layouts: 7.14 us -> 5.39 us
  starting transfers between devices: 8.87 us -> 8.38 us
    dot_general x18, matrix products: 10.7 us -> 6.85 us  [apply_filter(): jnp.einsum('oi,bsirw->bsorw', filter_weight[(left_operand + 1) * 3 + (rig...]
    ppermute x1 -> x4, waiting for transfers between devices: 1.41 us -> 4.37 us  [the longest x3 4.37 us: exchange_sum(): chunk = lax.ppermute(chunk, ('band', 'rep'), perm)]
    ppermute x1, waiting for transfers between devices: 0.01 us -> 2.63 us  [padded(): lax.ppermute(lax.slice_in_dim(block, 0, width, axis=dim), axis, backward)]
    unnamed x30 -> x36, local copies, waits for them, and re-layouts: 5.14 us -> 3.44 us
    and x1, other arithmetic: 0.77 us -> 0.02 us  [shards(): jnp.take(joined[:, :, :, row_count - 3:, :], jnp.clip(ups - base, 0, slot...]
    and x1, other arithmetic: 0.73 us -> 0.02 us  [shards(): last_sel = alive & jnp.logical_not(down_here)]
    convert_element_type x1, other arithmetic: 0.67 us -> 0.01 us  [shards(): live_scale = alive.astype(jnp.float32)[None, :, None, None, None]]
    ppermute x1, starting transfers between devices: 5.59 us -> 4.96 us  [padded(): lax.ppermute(lax.slice_in_dim(block, block.shape[dim] - width, None, axis...]
  transfers between devices with their start and end apart: 3 -> 6, of which waited for: 1 -> 3; matrix products, arithmetic and copies ran while one was open for 8% -> 11% of each run, Pallas kernels for 0% -> 0%
where the time goes in v14:
time: 31.3 us; the launch traced here: 31.1 us
  starting transfers between devices  8.38 us (27%)
  matrix products  7.74 us (25%)
  waiting for transfers between devices  7 us (22%)
  local copies, waits for them, and re-layouts  5.39 us (17%)
  other arithmetic  1.36 us (4%)
  between operations  1.2 us (4%)
    dot_general x18, matrix products, apply_filter(): jnp.einsum('oi,bsirw->bsorw', filter_weight[(left_operand + 1) * 3 + (rig...  6.85 us
    ppermute x1, starting transfers between devices, padded(): lax.ppermute(lax.slice_in_dim(block, block.shape[dim] - width, None, axis...  4.96 us
    ppermute x3, waiting for transfers between devices, exchange_sum(): chunk = lax.ppermute(chunk, ('band', 'rep'), perm)  4.37 us
    unnamed x36, local copies, waits for them, and re-layouts  3.44 us
    ppermute x1, waiting for transfers between devices, padded(): lax.ppermute(lax.slice_in_dim(block, 0, width, axis=dim), axis, backward)  2.63 us
    ppermute x3, starting transfers between devices, exchange_sum(): chunk = lax.ppermute(chunk, ('band', 'rep'), perm)  2.05 us
    ppermute x1, starting transfers between devices, padded(): lax.ppermute(lax.slice_in_dim(block, 0, width, axis=dim), axis, backward)  1.29 us
  transfers between devices with their start and end apart: 6, of which 3 were waited for; matrix products, arithmetic and copies ran while one was open for 11% of the time, Pallas kernels for 0%

profile of v14, /device:TPU:0, one launch (start us, length us, event | category | flops | bytes accessed | tf_op | source)
XLA Modules:
  0.0 31.1 jit_solution(15341940319645983333)
XLA Ops:
  0.7 1.1 %copy-done = f32[2,4,16,16,128]{4,3,2,1,0:T(8,128)S(1)} copy-done((f32[2,4,16,16,128]{4,3,2,1,0:T(8,128)S(1)}, f32[2,4,16,16,128]{4,3,2,1,0:T(8,128)}, u32[]{:S(2)}) %copy-start) | copy-done | bytes 1048600
  1.9 0.2 copy.71
  2.2 0.1 select_reduce_fusion.1
  2.3 5.0 %collective-permute-start = (bf16[1,18,3,128]{3,1,2,0:T(8,128)(2,1)S(1)}, bf16[1,18,3,128]{3,1,2,0:T(8,128)(2,1)S(1)}, u32[]{:S(2)}, u32[]{:S(2)}) collective-permute-start(bf16[1,18,3,128]{3,1,2,0:T(8,128)(2,1)S(1)} %bitcast.285), channel_id=1, source_target_pairs={{0,4},{4,8},{8,12},{1,5},{5,9},{9,13},{2,6},{6,10},{10,14},{3,7},{... | collective-permute-start | bytes 41480 | tf_op jit(solution)/shard_map/ppermute | solution.py:12
  7.3 1.3 %collective-permute-start.1 = (bf16[1,18,3,128]{3,1,2,0:T(8,128)(2,1)S(1)}, bf16[1,18,3,128]{3,1,2,0:T(8,128)(2,1)S(1)}, u32[]{:S(2)}, u32[]{:S(2)}) collective-permute-start(bf16[1,18,3,128]{3,1,2,0:T(8,128)(2,1)S(1)} %bitcast.284), channel_id=1, source_target_pairs={{4,0},{8,4},{12,8},{5,1},{9,5},{13,9},{6,2},{10,6},{14,10},{7,3},{... | collective-permute-start | bytes 41480 | tf_op jit(solution)/shard_map/ppermute | solution.py:15
  8.7 0.1 pad_maximum_fusion.5
  8.8 0.1 copy.35
  8.9 0.1 copy.36
  9.1 0.6 %gather_fusion.1 = bf16[4,18,3,128]{3,1,2,0:T(8,128)(2,1)S(1)} fusion(bf16[4,18,3,128]{3,1,2,0:T(8,128)(2,1)S(1)} %bitcast.281, s32[1024]{0:T(1024)S(1)} %pad_clamp_fusion.2), kind=kCustom, calls=%fused_computation.clone | custom fusion | bytes 110608 | tf_op jit(solution)/shard_map/jit(_take)/gather | solution.py:133
  9.6 0.6 %gather_fusion.2 = bf16[4,18,3,128]{3,1,2,0:T(8,128)(2,1)S(1)} fusion(bf16[4,18,3,128]{3,1,2,0:T(8,128)(2,1)S(1)} %bitcast.280, s32[1024]{0:T(1024)S(1)} %pad_clamp_fusion.1), kind=kCustom, calls=%fused_computation.1.clone | custom fusion | bytes 110608 | tf_op jit(solution)/shard_map/jit(_take)/gather | solution.py:136
  10.2 0.1 fusion.34
  10.3 2.6 %collective-permute-done.1 = bf16[1,18,3,128]{3,1,2,0:T(8,128)(2,1)S(1)} collective-permute-done((bf16[1,18,3,128]{3,1,2,0:T(8,128)(2,1)S(1)}, bf16[1,18,3,128]{3,1,2,0:T(8,128)(2,1)S(1)}, u32[]{:S(2)}, u32[]{:S(2)}) %collective-permute-start.1) | collective-permute-done | bytes 13856 | tf_op jit(solution)/shard_map/ppermute | solution.py:15
  13.0 0.1 fusion.33
  13.1 0.2 pad_maximum_fusion
  13.2 0.2 pad_slice_fusion
  13.4 0.5 %fusion.18 = f32[4,20,128,32]{2,3,1,0:T(8,128)S(1)} fusion(bf16[1,4,18,22,128]{4,2,3,1,0:T(8,128)(2,1)S(1)} %pad_maximum_fusion, bf16[9,16,18]{1,2,0:T(8,128)(2,1)S(1)} %copy.35, bf16[9,16,18]{1,2,0:T(8,128)(2,1)S(1)} %copy.36), kind=kOutput, calls=%fused_computation.51 | convolution fusion | flops 11798784 | bytes 1726592 | tf_op jit(solution)/shard_map/oi,bsirw->bsorw/dot_general | solution.py:39
  13.9 0.4 %convolution_add_fusion.7 = f32[4,20,128,32]{2,3,1,0:T(8,128)S(1)} fusion(f32[4,20,128,32]{2,3,1,0:T(8,128)S(1)} %fusion.18, bf16[1,4,18,22,128]{4,2,3,1,0:T(8,128)(2,1)S(1)} %pad_maximum_fusion, bf16[9,16,18]{1,2,0:T(8,128)(2,1)S(1)} %copy.35, bf16[9,16,18]{1,2,0:T(8,128)(2,1)S(1)} %copy.36), kind=kOutput, calls=%fused_computation.19 | convolution fusion | flops 12126464 | bytes 3223552 | tf_op jit(solution)/shard_map/oi,bsirw->bsorw/dot_general | solution.py:39
  14.3 0.5 %convolution_add_fusion.6 = f32[4,20,128,32]{2,3,1,0:T(8,128)S(1)} fusion(f32[4,20,128,32]{2,3,1,0:T(8,128)S(1)} %convolution_add_fusion.7, bf16[1,4,18,22,128]{4,2,3,1,0:T(8,128)(2,1)S(1)} %pad_maximum_fusion, bf16[9,16,18]{1,2,0:T(8,128)(2,1)S(1)} %copy.35, bf16[9,16,18]{1,2,0:T(8,128)(2,1)S(1)} %copy.36), kind=kOutput, calls=%fused_computation.18 | convolution fusion | flops 12126464 | bytes 3037312 | tf_op jit(solution)/shard_map/oi,bsirw->bsorw/dot_general | solution.py:39
  14.8 0.5 %convolution_add_fusion.5 = f32[4,20,128,32]{2,3,1,0:T(8,128)S(1)} fusion(f32[4,20,128,32]{2,3,1,0:T(8,128)S(1)} %convolution_add_fusion.6, bf16[1,4,18,22,128]{4,2,3,1,0:T(8,128)(2,1)S(1)} %pad_maximum_fusion, bf16[9,16,18]{1,2,0:T(8,128)(2,1)S(1)} %copy.35, bf16[9,16,18]{1,2,0:T(8,128)(2,1)S(1)} %copy.36), kind=kOutput, calls=%fused_computation.17 | convolution fusion | flops 12126464 | bytes 3037312 | tf_op jit(solution)/shard_map/oi,bsirw->bsorw/dot_general | solution.py:39
  15.3 0.5 %convolution_add_fusion.4 = f32[4,20,128,32]{2,3,1,0:T(8,128)S(1)} fusion(f32[4,20,128,32]{2,3,1,0:T(8,128)S(1)} %convolution_add_fusion.5, bf16[1,4,18,22,128]{4,2,3,1,0:T(8,128)(2,1)S(1)} %pad_maximum_fusion, bf16[9,16,18]{1,2,0:T(8,128)(2,1)S(1)} %copy.35, bf16[9,16,18]{1,2,0:T(8,128)(2,1)S(1)} %copy.36), kind=kOutput, calls=%fused_computation.16 | convolution fusion | flops 12126464 | bytes 3223552 | tf_op jit(solution)/shard_map/oi,bsirw->bsorw/dot_general | solution.py:39
  15.8 0.5 %convolution_add_fusion.3 = f32[4,20,128,32]{2,3,1,0:T(8,128)S(1)} fusion(f32[4,20,128,32]{2,3,1,0:T(8,128)S(1)} %convolution_add_fusion.4, bf16[1,4,18,22,128]{4,2,3,1,0:T(8,128)(2,1)S(1)} %pad_maximum_fusion, bf16[9,16,18]{1,2,0:T(8,128)(2,1)S(1)} %copy.35, bf16[9,16,18]{1,2,0:T(8,128)(2,1)S(1)} %copy.36), kind=kOutput, calls=%fused_computation.15 | convolution fusion | flops 12126464 | bytes 3037312 | tf_op jit(solution)/shard_map/oi,bsirw->bsorw/dot_general | solution.py:39
  16.3 0.5 %convolution_add_fusion.2 = f32[4,20,128,32]{2,3,1,0:T(8,128)S(1)} fusion(f32[4,20,128,32]{2,3,1,0:T(8,128)S(1)} %convolution_add_fusion.3, bf16[1,4,18,22,128]{4,2,3,1,0:T(8,128)(2,1)S(1)} %pad_maximum_fusion, bf16[9,16,18]{1,2,0:T(8,128)(2,1)S(1)} %copy.35, bf16[9,16,18]{1,2,0:T(8,128)(2,1)S(1)} %copy.36), kind=kOutput, calls=%fused_computation.14 | convolution fusion | flops 12126464 | bytes 3037312 | tf_op jit(solution)/shard_map/oi,bsirw->bsorw/dot_general | solution.py:39
  16.8 0.4 %convolution_add_fusion.1 = f32[4,20,128,32]{2,3,1,0:T(8,128)S(1)} fusion(f32[4,20,128,32]{2,3,1,0:T(8,128)S(1)} %convolution_add_fusion.2, bf16[1,4,18,22,128]{4,2,3,1,0:T(8,128)(2,1)S(1)} %pad_maximum_fusion, bf16[9,16,18]{1,2,0:T(8,128)(2,1)S(1)} %copy.35, bf16[9,16,18]{1,2,0:T(8,128)(2,1)S(1)} %copy.36), kind=kOutput, calls=%fused_computation.13 | convolution fusion | flops 12126464 | bytes 3223552 | tf_op jit(solution)/shard_map/oi,bsirw->bsorw/dot_general | solution.py:39
  17.2 0.6 %fusion.7 = f32[1,4,32,20,128]{4,2,3,1,0:T(8,128)S(1)} fusion(f32[4,20,128,32]{2,3,1,0:T(8,128)S(1)} %convolution_add_fusion.1, f32[32]{0:T(128)S(1)} %pad_maximum_fusion.5, bf16[1,4,18,22,128]{4,2,3,1,0:T(8,128)(2,1)S(1)} %pad_maximum_fusion, bf16[9,16,18]{1,2,0:T(8,128)(2,1)S(1)} %copy.36, bf16[9,16,18]{1,2,0:T(8,128)(2,1)S(1)} %copy.35), kind=kOutput, calls=%fused_computation.26 | convolution fusion | flops 13437184 | bytes 3037440 | tf_op jit(solution)/shard_map/oi,bsirw->bsorw/dot_general | solution.py:39
  17.8 0.1 fusion.16
  17.9 0.5 %fusion.15 = bf16[1,4,18,20,132]{4,2,3,1,0:T(8,128)(2,1)S(1)} fusion(bf16[1,4,16,20,128]{4,2,3,1,0:T(8,128)(2,1)S(1)} %fusion.16, bf16[1,4,2,20,132]{4,2,3,1,0:T(2,128)(2,1)S(1)} %pad_slice_fusion), kind=kLoop, calls=%fused_computation.44 | loop fusion | flops 1140480 | bytes 750080 | tf_op jit(solution)/shard_map/concatenate | solution.py:166
  18.5 0.1 copy-done.2
  18.6 0.2 fusion.30
  18.8 0.3 convolution_add_fusion.15
  19.1 0.3 convolution_add_fusion.14
  19.4 0.2 convolution_add_fusion.13
  19.6 0.3 convolution_add_fusion.12
  19.9 0.3 convolution_add_fusion.11
  20.2 0.2 convolution_add_fusion.10
  20.4 0.3 convolution_add_fusion.9
  20.7 0.1 copy-done.10
  20.9 0.4 %fusion.14 = f32[1,4,16,16,128]{4,2,3,1,0:T(8,128)S(1)} fusion(f32[4,16,128,16]{2,3,1,0:T(8,128)S(1)} %convolution_add_fusion.9, f32[1,4,32,20,128]{4,2,3,1,0:T(8,128)S(1)} %fusion.7, f32[1,4,16,16,128]{4,3,2,1,0:T(8,128)S(1)} %constant_dynamic-slice_fusion.1, bf16[1,4,18,20,132]{4,2,3,1,0:T(8,128)(2,1)S(1)} %fusion.15, f32[16]{0:T(128)S(1)} %copy-done.10, ...), kind=kOutput, calls=%fused_computation.41 | convolution fusion | flops 5636096 | bytes 2495488 | tf_op jit(solution)/shard_map/oi,bsirw->bsorw/dot_general | solution.py:39
  21.3 0.4 %convolution_reduce_fusion = f32[4,16,4,32]{3,1,2,0:T(8,128)S(1)} fusion(f32[4,16,4,4,128]{4,1,3,2,0:T(8,128)S(1)} %bitcast.279, s32[128]{0:T(128)S(1)} %and_select_fusion), kind=kOutput, calls=%fused_computation.42 | convolution fusion | flops 50360320 | bytes 557568 | tf_op jit(solution)/shard_map/schw,wj->schj/dot_general | solution.py:192
  21.8 0.1 collective-permute-start.2
  21.8 0.6 %gather_fusion = f32[4,16,4,32]{3,1,2,0:T(8,128)S(1)} fusion(f32[4,16,4,32]{3,1,2,0:T(8,128)S(1)} %broadcast_multiply_fusion, s32[1024]{0:T(1024)S(1)} %pad_clamp_fusion), kind=kCustom, calls=%fused_computation.2 | custom fusion | bytes 65552 | tf_op jit(solution)/shard_map/jit(_take)/gather | solution.py:198
  22.4 0.3 %fusion.31 = f32[4,4,32,16]{2,3,1,0:T(8,128)S(1)} fusion(f32[4,16,4,32]{3,1,2,0:T(8,128)S(1)} %gather_fusion, pred[4]{0:T(512)(128)(4,1)S(1)} %get-tuple-element.34, f32[16,16]{1,0:T(8,128)S(1)} %copy-done.6), kind=kOutput, calls=%fused_computation.72 | convolution fusion | flops 1581056 | bytes 66564 | tf_op jit(solution)/shard_map/oc,kcij->koij/dot_general | solution.py:199
  22.8 0.6 %collective-permute-start.3 = (f32[2,16,4,32]{3,1,2,0:T(8,128)S(1)}, f32[2,16,4,32]{3,1,2,0:T(8,128)S(1)}, u32[]{:S(2)}, u32[]{:S(2)}) collective-permute-start(f32[2,16,4,32]{3,1,2,0:T(8,128)S(1)} %get-tuple-element.25), channel_id=1, source_target_pairs={{0,1},{1,0},{2,3},{3,2},{4,5},{5,4},{6,7},{7,6},{8,9},{9,8},{10,11... | collective-permute-start | bytes 49160 | tf_op jit(solution)/shard_map/ppermute | solution.py:74
  23.3 1.5 %collective-permute-start.4 = (f32[2,16,4,32]{3,1,2,0:T(8,128)S(1)}, f32[2,16,4,32]{3,1,2,0:T(8,128)S(1)}, u32[]{:S(2)}, u32[]{:S(2)}) collective-permute-start(f32[2,16,4,32]{3,1,2,0:T(8,128)S(1)} %get-tuple-element.26), channel_id=1, source_target_pairs={{0,2},{1,3},{2,0},{3,1},{4,6},{5,7},{6,4},{7,5},{8,10},{9,11},{10,... | collective-permute-start | bytes 49160 | tf_op jit(solution)/shard_map/ppermute | solution.py:74
  24.8 2.8 %collective-permute-done.4 = f32[2,16,4,32]{3,1,2,0:T(8,128)S(1)} collective-permute-done((f32[2,16,4,32]{3,1,2,0:T(8,128)S(1)}, f32[2,16,4,32]{3,1,2,0:T(8,128)S(1)}, u32[]{:S(2)}, u32[]{:S(2)}) %collective-permute-start.4) | collective-permute-done | bytes 16416 | tf_op jit(solution)/shard_map/ppermute | solution.py:74
  27.6 1.6 %collective-permute-done.5 = f32[2,16,4,32]{3,1,2,0:T(8,128)S(1)} collective-permute-done((f32[2,16,4,32]{3,1,2,0:T(8,128)S(1)}, f32[2,16,4,32]{3,1,2,0:T(8,128)S(1)}, u32[]{:S(2)}, u32[]{:S(2)}) %collective-permute-start.5) | collective-permute-done | bytes 16416 | tf_op jit(solution)/shard_map/ppermute | solution.py:74
  29.2 0.2 tanh_add_fusion
  29.4 0.7 %copy.40 = f32[2,16,4,32]{3,2,1,0:T(4,128)} copy(f32[2,16,4,32]{3,1,2,0:T(8,128)S(1)} %tanh_add_fusion) | data formatting | bytes 32768
  30.2 0.9 %copy.39 = f32[2,4,8,16,128]{4,3,2,1,0:T(8,128)} copy(f32[2,4,8,16,128]{4,2,3,1,0:T(8,128)S(1)} %pad_maximum_fusion.1) | data formatting | bytes 1048576
  (47 shorter events, 0.4 us)
Async XLA Ops:
  0.6 1.2 %copy-start = (f32[2,4,16,16,128]{4,3,2,1,0:T(8,128)S(1)}, f32[2,4,16,16,128]{4,3,2,1,0:T(8,128)}, u32[]{:S(2)}) copy-start(f32[2,4,16,16,128]{4,3,2,1,0:T(8,128)} %param.18) | copy-start | bytes 3145732
  0.6 1.4 %copy-start.9 = (s32[4]{0:T(128)S(1)}, s32[4]{0:T(128)}, u32[]{:S(2)}) copy-start(s32[4]{0:T(128)} %param.19) | copy-start | bytes 52
  0.7 1.4 %copy-start.8 = (s32[4,2]{0,1:T(2,128)S(1)}, s32[4,2]{0,1:T(2,128)}, u32[]{:S(2)}) copy-start(s32[4,2]{0,1:T(2,128)} %param.20) | copy-start | bytes 100
  0.7 1.5 %copy-start.12 = (s32[1,4]{1,0:T(1,128)S(1)}, s32[1,4]{1,0:T(1,128)}, u32[]{:S(2)}) copy-start(s32[1,4]{1,0:T(1,128)} %param.21) | copy-start | bytes 52
  0.7 1.5 %copy-start.5 = (bf16[2,4,2,16,128]{4,3,2,1,0:T(8,128)(2,1)S(1)}, bf16[2,4,2,16,128]{4,3,2,1,0:T(8,128)(2,1)}, u32[]{:S(2)}) copy-start(bf16[2,4,2,16,128]{4,3,2,1,0:T(8,128)(2,1)} %param.17) | copy-start | bytes 196612
  0.7 8.0 %copy-start.14 = (f32[16]{0:T(128)S(1)}, f32[16]{0:T(128)}, u32[]{:S(2)}) copy-start(f32[16]{0:T(128)} %param.24) | copy-start | bytes 196
  0.7 8.0 %copy-start.13 = (f32[16]{0:T(128)S(1)}, f32[16]{0:T(128)}, u32[]{:S(2)}) copy-start(f32[16]{0:T(128)} %param.26) | copy-start | bytes 196
  0.7 8.1 %copy-start.3 = (bf16[9,16,18]{2,1,0:T(8,128)(2,1)S(1)}, bf16[9,16,18]{2,1,0:T(8,128)(2,1)}, u32[]{:S(2)}) copy-start(bf16[9,16,18]{2,1,0:T(8,128)(2,1)} %param.23) | copy-start | bytes 15556
  1.9 7.1 %copy-start.4 = (bf16[9,16,18]{2,1,0:T(8,128)(2,1)S(1)}, bf16[9,16,18]{2,1,0:T(8,128)(2,1)}, u32[]{:S(2)}) copy-start(bf16[9,16,18]{2,1,0:T(8,128)(2,1)} %param.25) | copy-start | bytes 15556
  2.3 7.9 %collective-permute-start = (bf16[1,18,3,128]{3,1,2,0:T(8,128)(2,1)S(1)}, bf16[1,18,3,128]{3,1,2,0:T(8,128)(2,1)S(1)}, u32[]{:S(2)}, u32[]{:S(2)}) collective-permute-start(bf16[1,18,3,128]{3,1,2,0:T(8,128)(2,1)S(1)} %bitcast.285), channel_id=1, source_target_pairs={{0,4},{4,8},{8,12},{1,5},{5,9},{9,13},{2,6},{6,10},{10,14},{3,7},{... | collective-permute-start | bytes 41480 | tf_op jit(solution)/shard_map/ppermute | solution.py:12
  7.3 5.7 %collective-permute-start.1 = (bf16[1,18,3,128]{3,1,2,0:T(8,128)(2,1)S(1)}, bf16[1,18,3,128]{3,1,2,0:T(8,128)(2,1)S(1)}, u32[]{:S(2)}, u32[]{:S(2)}) collective-permute-start(bf16[1,18,3,128]{3,1,2,0:T(8,128)(2,1)S(1)} %bitcast.284), channel_id=1, source_target_pairs={{4,0},{8,4},{12,8},{5,1},{9,5},{13,9},{6,2},{10,6},{14,10},{7,3},{... | collective-permute-start | bytes 41480 | tf_op jit(solution)/shard_map/ppermute | solution.py:15
  17.8 0.8 %copy-start.2 = (bf16[9,16,18]{2,1,0:T(8,128)(2,1)S(1)}, bf16[9,16,18]{2,1,0:T(8,128)(2,1)}, u32[]{:S(2)}) copy-start(bf16[9,16,18]{2,1,0:T(8,128)(2,1)} %param.27) | copy-start | bytes 15556
  20.2 0.7 %copy-start.10 = (f32[16]{0:T(128)S(1)}, f32[16]{0:T(128)}, u32[]{:S(2)}) copy-start(f32[16]{0:T(128)} %param.28) | copy-start | bytes 196
  21.3 1.1 %copy-start.6 = (f32[16,16]{1,0:T(8,128)S(1)}, f32[16,16]{1,0:T(8,128)}, u32[]{:S(2)}) copy-start(f32[16,16]{1,0:T(8,128)} %param.29) | copy-start | bytes 3076
  21.3 7.9 %copy-start.1 = (f32[2,16,4,32]{3,2,1,0:T(4,128)S(1)}, f32[2,16,4,32]{3,2,1,0:T(4,128)}, u32[]{:S(2)}) copy-start(f32[2,16,4,32]{3,2,1,0:T(4,128)} %param.22) | copy-start | bytes 49156
  21.3 7.9 %copy-start.7 = (f32[16,16]{1,0:T(8,128)S(1)}, f32[16,16]{1,0:T(8,128)}, u32[]{:S(2)}) copy-start(f32[16,16]{1,0:T(8,128)} %param.30) | copy-start | bytes 3076
  21.3 7.9 %copy-start.11 = (f32[16]{0:T(128)S(1)}, f32[16]{0:T(128)}, u32[]{:S(2)}) copy-start(f32[16]{0:T(128)} %param.31) | copy-start | bytes 196
  21.8 8.3 %collective-permute-start.2 = (f32[1,4,8,16,128]{4,2,3,1,0:T(8,128)S(1)}, f32[1,4,8,16,128]{4,2,3,1,0:T(8,128)S(1)}, u32[]{:S(2)}, u32[]{:S(2)}) collective-permute-start(f32[1,4,8,16,128]{4,2,3,1,0:T(8,128)S(1)} %constant_dynamic-slice_fusion), channel_id=1, source_target_pairs={{0,1},{1,0},{2,3},{3,2},{4,5},{5,4},{6,7},{7,6},{8,9},{9,8},{10,11... | collective-permute-start | bytes 786440 | tf_op jit(solution)/shard_map/ppermute | solution.py:176
  22.8 2.1 %collective-permute-start.3 = (f32[2,16,4,32]{3,1,2,0:T(8,128)S(1)}, f32[2,16,4,32]{3,1,2,0:T(8,128)S(1)}, u32[]{:S(2)}, u32[]{:S(2)}) collective-permute-start(f32[2,16,4,32]{3,1,2,0:T(8,128)S(1)} %get-tuple-element.25), channel_id=1, source_target_pairs={{0,1},{1,0},{2,3},{3,2},{4,5},{5,4},{6,7},{7,6},{8,9},{9,8},{10,11... | collective-permute-start | bytes 49160 | tf_op jit(solution)/shard_map/ppermute | solution.py:74
  23.3 4.3 %collective-permute-start.4 = (f32[2,16,4,32]{3,1,2,0:T(8,128)S(1)}, f32[2,16,4,32]{3,1,2,0:T(8,128)S(1)}, u32[]{:S(2)}, u32[]{:S(2)}) collective-permute-start(f32[2,16,4,32]{3,1,2,0:T(8,128)S(1)} %get-tuple-element.26), channel_id=1, source_target_pairs={{0,2},{1,3},{2,0},{3,1},{4,6},{5,7},{6,4},{7,5},{8,10},{9,11},{10,... | collective-permute-start | bytes 49160 | tf_op jit(solution)/shard_map/ppermute | solution.py:74
  24.8 4.4 %collective-permute-start.5 = (f32[2,16,4,32]{3,1,2,0:T(8,128)S(1)}, f32[2,16,4,32]{3,1,2,0:T(8,128)S(1)}, u32[]{:S(2)}, u32[]{:S(2)}) collective-permute-start(f32[2,16,4,32]{3,1,2,0:T(8,128)S(1)} %get-tuple-element.26), channel_id=1, source_target_pairs={{0,3},{1,2},{2,1},{3,0},{4,7},{5,6},{6,5},{7,4},{8,11},{9,10},{10,... | collective-permute-start | bytes 49160 | tf_op jit(solution)/shard_map/ppermute | solution.py:74

commit v15 on v14

--- a/solution.py
+++ b/solution.py
@@ -55,25 +55,25 @@
     return 0.5 + 0.5 * jnp.tanh(0.5 * value)
 
 
+def rep_sum(part):
+    reps = lax.axis_size("rep")
+    total = part
+    for step in range(1, reps):
+        total = total + lax.ppermute(part, "rep", [(r, (r + step) % reps) for r in range(reps)])
+    return total
+
+
 def exchange_sum(part, owned):
     bands = lax.axis_size("band")
-    reps = lax.axis_size("rep")
     band = lax.axis_index("band")
     total = None
     for shift in range(bands):
-        pair = None
-        for step in range(reps):
-            target = (band + shift) % bands
-            chunk = lax.dynamic_slice_in_dim(part, target * owned, owned, 0)
-            if shift or step:
-                perm = [
-                    (b * reps + r, ((b + shift) % bands) * reps + (r + step) % reps)
-                    for b in range(bands)
-                    for r in range(reps)
-                ]
-                chunk = lax.ppermute(chunk, ("band", "rep"), perm)
-            pair = chunk if pair is None else pair + chunk
-        total = pair if total is None else total + pair
+        target = (band + shift) % bands
+        chunk = lax.dynamic_slice_in_dim(part, target * owned, owned, 0)
+        if shift:
+            perm = [(b, (b + shift) % bands) for b in range(bands)]
+            chunk = lax.ppermute(chunk, "band", perm)
+        total = chunk if total is None else total + chunk
     return total
 
 
@@ -197,7 +197,7 @@
     ) / 16.0
     ordered = jnp.take(pooled, coarse_perm[0], axis=0)
     part = jnp.einsum("oc,kcij->koij", u_pool, ordered, precision=lax.Precision.HIGHEST)
-    pre = exchange_sum(part, coarse_state.shape[0])
+    pre = exchange_sum(rep_sum(part), coarse_state.shape[0])
     pre = pre + jnp.einsum("oc,kcij->koij", u_state, coarse_state, precision=lax.Precision.HIGHEST)
     pre = pre + b_coarse[None, :, None, None]
     coarse_next = coarse_state + jnp.tanh(pre)

time: 31.3 us -> 30.4 us (0.971)
  waiting for transfers between devices: 7 us -> 5.92 us
    ppermute x3 -> x2, waiting for transfers between devices: 4.37 us -> 3.27 us  [the longest x1 2.52 us: exchange_sum(): chunk = lax.ppermute(chunk, 'band', perm)]
    ppermute x1, starting transfers between devices: 0.07 us -> 0.55 us  [shards(): lax.ppermute(piece, 'rep', [(r, (r + step) % reps) for r in range(reps)])]
    ppermute x3 -> x2, starting transfers between devices: 2.05 us -> 1.63 us  [the longest x1 1.55 us: exchange_sum(): chunk = lax.ppermute(chunk, 'band', perm)]
  transfers between devices with their start and end apart: 6 -> 5, of which waited for: 3 -> 3; matrix products, arithmetic and copies ran while one was open for 11% -> 9% of each run, Pallas kernels for 0% -> 0%
where the time goes in v15:
time: 30.4 us; the launch traced here: 30.1 us
  starting transfers between devices  8.42 us (28%)
  matrix products  7.73 us (25%)
  waiting for transfers between devices  5.92 us (19%)
  local copies, waits for them, and re-layouts  5.38 us (18%)
  other arithmetic  1.46 us (5%)
  between operations  1.24 us (4%)
    dot_general x18, matrix products, apply_filter(): jnp.einsum('oi,bsirw->bsorw', filter_weight[(left_operand + 1) * 3 + (rig...  6.86 us
    ppermute x1, starting transfers between devices, padded(): lax.ppermute(lax.slice_in_dim(block, block.shape[dim] - width, None, axis...  4.96 us
    unnamed x36, local copies, waits for them, and re-layouts  3.44 us
    ppermute x1, waiting for transfers between devices, padded(): lax.ppermute(lax.slice_in_dim(block, 0, width, axis=dim), axis, backward)  2.64 us
    ppermute x1, waiting for transfers between devices, exchange_sum(): chunk = lax.ppermute(chunk, 'band', perm)  2.52 us
    ppermute x1, starting transfers between devices, exchange_sum(): chunk = lax.ppermute(chunk, 'band', perm)  1.55 us
    ppermute x1, starting transfers between devices, padded(): lax.ppermute(lax.slice_in_dim(block, 0, width, axis=dim), axis, backward)  1.29 us
    ppermute x1, waiting for transfers between devices, rep_sum(): lax.ppermute(part, 'rep', [(r, (r + step) % reps) for r in range(reps)])  0.75 us
  transfers between devices with their start and end apart: 5, of which 3 were waited for; matrix products, arithmetic and copies ran while one was open for 9% of the time, Pallas kernels for 0%

profile of v15, /device:TPU:0, one launch (start us, length us, event | category | flops | bytes accessed | tf_op | source)
XLA Modules:
  0.0 30.1 jit_solution(235932004270464677)
XLA Ops:
  0.7 1.1 %copy-done = f32[2,4,16,16,128]{4,3,2,1,0:T(8,128)S(1)} copy-done((f32[2,4,16,16,128]{4,3,2,1,0:T(8,128)S(1)}, f32[2,4,16,16,128]{4,3,2,1,0:T(8,128)}, u32[]{:S(2)}) %copy-start) | copy-done | bytes 1048600
  1.9 0.2 copy.69
  2.2 0.1 select_reduce_fusion.1
  2.3 5.0 %collective-permute-start = (bf16[1,18,3,128]{3,1,2,0:T(8,128)(2,1)S(1)}, bf16[1,18,3,128]{3,1,2,0:T(8,128)(2,1)S(1)}, u32[]{:S(2)}, u32[]{:S(2)}) collective-permute-start(bf16[1,18,3,128]{3,1,2,0:T(8,128)(2,1)S(1)} %bitcast.281), channel_id=1, source_target_pairs={{0,4},{4,8},{8,12},{1,5},{5,9},{9,13},{2,6},{6,10},{10,14},{3,7},{... | collective-permute-start | bytes 41480 | tf_op jit(solution)/shard_map/ppermute | solution.py:12
  7.3 1.3 %collective-permute-start.1 = (bf16[1,18,3,128]{3,1,2,0:T(8,128)(2,1)S(1)}, bf16[1,18,3,128]{3,1,2,0:T(8,128)(2,1)S(1)}, u32[]{:S(2)}, u32[]{:S(2)}) collective-permute-start(bf16[1,18,3,128]{3,1,2,0:T(8,128)(2,1)S(1)} %bitcast.280), channel_id=1, source_target_pairs={{4,0},{8,4},{12,8},{5,1},{9,5},{13,9},{6,2},{10,6},{14,10},{7,3},{... | collective-permute-start | bytes 41480 | tf_op jit(solution)/shard_map/ppermute | solution.py:15
  8.7 0.1 pad_maximum_fusion.5
  8.8 0.1 copy.35
  8.9 0.1 copy.36
  9.1 0.6 %gather_fusion.1 = bf16[4,18,3,128]{3,1,2,0:T(8,128)(2,1)S(1)} fusion(bf16[4,18,3,128]{3,1,2,0:T(8,128)(2,1)S(1)} %bitcast.277, s32[1024]{0:T(1024)S(1)} %pad_clamp_fusion.2), kind=kCustom, calls=%fused_computation.clone | custom fusion | bytes 110608 | tf_op jit(solution)/shard_map/jit(_take)/gather | solution.py:133
  9.6 0.6 %gather_fusion.2 = bf16[4,18,3,128]{3,1,2,0:T(8,128)(2,1)S(1)} fusion(bf16[4,18,3,128]{3,1,2,0:T(8,128)(2,1)S(1)} %bitcast.276, s32[1024]{0:T(1024)S(1)} %pad_clamp_fusion.1), kind=kCustom, calls=%fused_computation.1.clone | custom fusion | bytes 110608 | tf_op jit(solution)/shard_map/jit(_take)/gather | solution.py:136
  10.2 0.1 fusion.33
  10.3 2.6 %collective-permute-done.1 = bf16[1,18,3,128]{3,1,2,0:T(8,128)(2,1)S(1)} collective-permute-done((bf16[1,18,3,128]{3,1,2,0:T(8,128)(2,1)S(1)}, bf16[1,18,3,128]{3,1,2,0:T(8,128)(2,1)S(1)}, u32[]{:S(2)}, u32[]{:S(2)}) %collective-permute-start.1) | collective-permute-done | bytes 13856 | tf_op jit(solution)/shard_map/ppermute | solution.py:15
  13.0 0.1 fusion.32
  13.1 0.2 pad_maximum_fusion
  13.2 0.2 pad_slice_fusion
  13.4 0.5 %fusion.18 = f32[4,20,128,32]{2,3,1,0:T(8,128)S(1)} fusion(bf16[1,4,18,22,128]{4,2,3,1,0:T(8,128)(2,1)S(1)} %pad_maximum_fusion, bf16[9,16,18]{1,2,0:T(8,128)(2,1)S(1)} %copy.35, bf16[9,16,18]{1,2,0:T(8,128)(2,1)S(1)} %copy.36), kind=kOutput, calls=%fused_computation.52 | convolution fusion | flops 11798784 | bytes 1726592 | tf_op jit(solution)/shard_map/oi,bsirw->bsorw/dot_general | solution.py:39
  13.9 0.4 %convolution_add_fusion.7 = f32[4,20,128,32]{2,3,1,0:T(8,128)S(1)} fusion(f32[4,20,128,32]{2,3,1,0:T(8,128)S(1)} %fusion.18, bf16[1,4,18,22,128]{4,2,3,1,0:T(8,128)(2,1)S(1)} %pad_maximum_fusion, bf16[9,16,18]{1,2,0:T(8,128)(2,1)S(1)} %copy.35, bf16[9,16,18]{1,2,0:T(8,128)(2,1)S(1)} %copy.36), kind=kOutput, calls=%fused_computation.19 | convolution fusion | flops 12126464 | bytes 3223552 | tf_op jit(solution)/shard_map/oi,bsirw->bsorw/dot_general | solution.py:39
  14.3 0.5 %convolution_add_fusion.6 = f32[4,20,128,32]{2,3,1,0:T(8,128)S(1)} fusion(f32[4,20,128,32]{2,3,1,0:T(8,128)S(1)} %convolution_add_fusion.7, bf16[1,4,18,22,128]{4,2,3,1,0:T(8,128)(2,1)S(1)} %pad_maximum_fusion, bf16[9,16,18]{1,2,0:T(8,128)(2,1)S(1)} %copy.35, bf16[9,16,18]{1,2,0:T(8,128)(2,1)S(1)} %copy.36), kind=kOutput, calls=%fused_computation.18 | convolution fusion | flops 12126464 | bytes 3037312 | tf_op jit(solution)/shard_map/oi,bsirw->bsorw/dot_general | solution.py:39
  14.8 0.5 %convolution_add_fusion.5 = f32[4,20,128,32]{2,3,1,0:T(8,128)S(1)} fusion(f32[4,20,128,32]{2,3,1,0:T(8,128)S(1)} %convolution_add_fusion.6, bf16[1,4,18,22,128]{4,2,3,1,0:T(8,128)(2,1)S(1)} %pad_maximum_fusion, bf16[9,16,18]{1,2,0:T(8,128)(2,1)S(1)} %copy.35, bf16[9,16,18]{1,2,0:T(8,128)(2,1)S(1)} %copy.36), kind=kOutput, calls=%fused_computation.17 | convolution fusion | flops 12126464 | bytes 3037312 | tf_op jit(solution)/shard_map/oi,bsirw->bsorw/dot_general | solution.py:39
  15.3 0.5 %convolution_add_fusion.4 = f32[4,20,128,32]{2,3,1,0:T(8,128)S(1)} fusion(f32[4,20,128,32]{2,3,1,0:T(8,128)S(1)} %convolution_add_fusion.5, bf16[1,4,18,22,128]{4,2,3,1,0:T(8,128)(2,1)S(1)} %pad_maximum_fusion, bf16[9,16,18]{1,2,0:T(8,128)(2,1)S(1)} %copy.35, bf16[9,16,18]{1,2,0:T(8,128)(2,1)S(1)} %copy.36), kind=kOutput, calls=%fused_computation.16 | convolution fusion | flops 12126464 | bytes 3223552 | tf_op jit(solution)/shard_map/oi,bsirw->bsorw/dot_general | solution.py:39
  15.8 0.5 %convolution_add_fusion.3 = f32[4,20,128,32]{2,3,1,0:T(8,128)S(1)} fusion(f32[4,20,128,32]{2,3,1,0:T(8,128)S(1)} %convolution_add_fusion.4, bf16[1,4,18,22,128]{4,2,3,1,0:T(8,128)(2,1)S(1)} %pad_maximum_fusion, bf16[9,16,18]{1,2,0:T(8,128)(2,1)S(1)} %copy.35, bf16[9,16,18]{1,2,0:T(8,128)(2,1)S(1)} %copy.36), kind=kOutput, calls=%fused_computation.15 | convolution fusion | flops 12126464 | bytes 3037312 | tf_op jit(solution)/shard_map/oi,bsirw->bsorw/dot_general | solution.py:39
  16.3 0.5 %convolution_add_fusion.2 = f32[4,20,128,32]{2,3,1,0:T(8,128)S(1)} fusion(f32[4,20,128,32]{2,3,1,0:T(8,128)S(1)} %convolution_add_fusion.3, bf16[1,4,18,22,128]{4,2,3,1,0:T(8,128)(2,1)S(1)} %pad_maximum_fusion, bf16[9,16,18]{1,2,0:T(8,128)(2,1)S(1)} %copy.35, bf16[9,16,18]{1,2,0:T(8,128)(2,1)S(1)} %copy.36), kind=kOutput, calls=%fused_computation.14 | convolution fusion | flops 12126464 | bytes 3037312 | tf_op jit(solution)/shard_map/oi,bsirw->bsorw/dot_general | solution.py:39
  16.8 0.4 %convolution_add_fusion.1 = f32[4,20,128,32]{2,3,1,0:T(8,128)S(1)} fusion(f32[4,20,128,32]{2,3,1,0:T(8,128)S(1)} %convolution_add_fusion.2, bf16[1,4,18,22,128]{4,2,3,1,0:T(8,128)(2,1)S(1)} %pad_maximum_fusion, bf16[9,16,18]{1,2,0:T(8,128)(2,1)S(1)} %copy.35, bf16[9,16,18]{1,2,0:T(8,128)(2,1)S(1)} %copy.36), kind=kOutput, calls=%fused_computation.13 | convolution fusion | flops 12126464 | bytes 3223552 | tf_op jit(solution)/shard_map/oi,bsirw->bsorw/dot_general | solution.py:39
  17.2 0.6 %fusion.7 = f32[1,4,32,20,128]{4,2,3,1,0:T(8,128)S(1)} fusion(f32[4,20,128,32]{2,3,1,0:T(8,128)S(1)} %convolution_add_fusion.1, f32[32]{0:T(128)S(1)} %pad_maximum_fusion.5, bf16[1,4,18,22,128]{4,2,3,1,0:T(8,128)(2,1)S(1)} %pad_maximum_fusion, bf16[9,16,18]{1,2,0:T(8,128)(2,1)S(1)} %copy.36, bf16[9,16,18]{1,2,0:T(8,128)(2,1)S(1)} %copy.35), kind=kOutput, calls=%fused_computation.26 | convolution fusion | flops 13437184 | bytes 3037440 | tf_op jit(solution)/shard_map/oi,bsirw->bsorw/dot_general | solution.py:39
  17.8 0.1 fusion.16
  17.9 0.5 %fusion.15 = bf16[1,4,18,20,132]{4,2,3,1,0:T(8,128)(2,1)S(1)} fusion(bf16[1,4,16,20,128]{4,2,3,1,0:T(8,128)(2,1)S(1)} %fusion.16, bf16[1,4,2,20,132]{4,2,3,1,0:T(2,128)(2,1)S(1)} %pad_slice_fusion), kind=kLoop, calls=%fused_computation.45 | loop fusion | flops 1140480 | bytes 750080 | tf_op jit(solution)/shard_map/concatenate | solution.py:166
  18.5 0.1 copy-done.2
  18.6 0.2 fusion.30
  18.8 0.3 %convolution_add_fusion.15 = f32[4,16,128,16]{2,3,1,0:T(8,128)S(1)} fusion(f32[4,16,128,16]{2,3,1,0:T(8,128)S(1)} %fusion.30, bf16[1,4,18,20,132]{4,2,3,1,0:T(8,128)(2,1)S(1)} %fusion.15, bf16[9,16,18]{2,1,0:T(8,128)(2,1)S(1)} %copy-done.2), kind=kOutput, calls=%fused_computation.35 | convolution fusion | flops 4849664 | bytes 1445888 | tf_op jit(solution)/shard_map/oi,bsirw->bsorw/dot_general | solution.py:39
  19.1 0.3 %convolution_add_fusion.14 = f32[4,16,128,16]{2,3,1,0:T(8,128)S(1)} fusion(f32[4,16,128,16]{2,3,1,0:T(8,128)S(1)} %convolution_add_fusion.15, bf16[1,4,18,20,132]{4,2,3,1,0:T(8,128)(2,1)S(1)} %fusion.15, bf16[9,16,18]{2,1,0:T(8,128)(2,1)S(1)} %copy-done.2), kind=kOutput, calls=%fused_computation.34 | convolution fusion | flops 4849664 | bytes 1445888 | tf_op jit(solution)/shard_map/oi,bsirw->bsorw/dot_general | solution.py:39
  19.4 0.2 convolution_add_fusion.13
  19.6 0.3 %convolution_add_fusion.12 = f32[4,16,128,16]{2,3,1,0:T(8,128)S(1)} fusion(f32[4,16,128,16]{2,3,1,0:T(8,128)S(1)} %convolution_add_fusion.13, bf16[1,4,18,20,132]{4,2,3,1,0:T(8,128)(2,1)S(1)} %fusion.15, bf16[9,16,18]{2,1,0:T(8,128)(2,1)S(1)} %copy-done.2), kind=kOutput, calls=%fused_computation.32 | convolution fusion | flops 4849664 | bytes 1445888 | tf_op jit(solution)/shard_map/oi,bsirw->bsorw/dot_general | solution.py:39
  19.9 0.3 convolution_add_fusion.11
  20.2 0.2 convolution_add_fusion.10
  20.4 0.3 %convolution_add_fusion.9 = f32[4,16,128,16]{2,3,1,0:T(8,128)S(1)} fusion(f32[4,16,128,16]{2,3,1,0:T(8,128)S(1)} %convolution_add_fusion.10, bf16[1,4,18,20,132]{4,2,3,1,0:T(8,128)(2,1)S(1)} %fusion.15, bf16[9,16,18]{2,1,0:T(8,128)(2,1)S(1)} %copy-done.2), kind=kOutput, calls=%fused_computation.29 | convolution fusion | flops 4849664 | bytes 1445888 | tf_op jit(solution)/shard_map/oi,bsirw->bsorw/dot_general | solution.py:39
  20.8 0.1 copy-done.10
  20.9 0.4 %fusion.14 = f32[1,4,16,16,128]{4,2,3,1,0:T(8,128)S(1)} fusion(f32[4,16,128,16]{2,3,1,0:T(8,128)S(1)} %convolution_add_fusion.9, f32[1,4,32,20,128]{4,2,3,1,0:T(8,128)S(1)} %fusion.7, f32[1,4,16,16,128]{4,3,2,1,0:T(8,128)S(1)} %constant_dynamic-slice_fusion.2, bf16[1,4,18,20,132]{4,2,3,1,0:T(8,128)(2,1)S(1)} %fusion.15, f32[16]{0:T(128)S(1)} %copy-done.10, ...), kind=kOutput, calls=%fused_computation.41 | convolution fusion | flops 5636096 | bytes 2495488 | tf_op jit(solution)/shard_map/oi,bsirw->bsorw/dot_general | solution.py:39
  21.3 0.4 %convolution_reduce_fusion = f32[4,16,4,32]{3,1,2,0:T(8,128)S(1)} fusion(f32[4,16,4,4,128]{4,1,3,2,0:T(8,128)S(1)} %bitcast.275, s32[128]{0:T(128)S(1)} %and_select_fusion), kind=kOutput, calls=%fused_computation.42 | convolution fusion | flops 50360320 | bytes 557568 | tf_op jit(solution)/shard_map/schw,wj->schj/dot_general | solution.py:192
  21.7 0.6 %gather_fusion = f32[4,16,4,32]{3,1,2,0:T(8,128)S(1)} fusion(f32[4,16,4,32]{3,1,2,0:T(8,128)S(1)} %broadcast_multiply_fusion, s32[1024]{0:T(1024)S(1)} %pad_clamp_fusion), kind=kCustom, calls=%fused_computation.2 | custom fusion | bytes 65552 | tf_op jit(solution)/shard_map/jit(_take)/gather | solution.py:198
  22.3 0.3 %convolution_bitcast_fusion = f32[4,16,4,32]{3,1,2,0:T(8,128)S(1)} fusion(f32[4,16,4,32]{3,1,2,0:T(8,128)S(1)} %gather_fusion, pred[4]{0:T(512)(128)(4,1)S(1)} %get-tuple-element.32, f32[16,16]{1,0:T(8,128)S(1)} %copy-done.6), kind=kOutput, calls=%fused_computation.43 | convolution fusion | flops 1581056 | bytes 66564 | tf_op jit(solution)/shard_map/oc,kcij->koij/dot_general | solution.py:199
  22.7 0.5 %collective-permute-start.2 = (f32[1,4,8,16,128]{4,2,3,1,0:T(8,128)S(1)}, f32[1,4,8,16,128]{4,2,3,1,0:T(8,128)S(1)}, u32[]{:S(2)}, u32[]{:S(2)}) collective-permute-start(f32[1,4,8,16,128]{4,2,3,1,0:T(8,128)S(1)} %constant_dynamic-slice_fusion.1), channel_id=1, source_target_pairs={{0,1},{1,0},{2,3},{3,2},{4,5},{5,4},{6,7},{7,6},{8,9},{9,8},{10,11... | collective-permute-start | bytes 786440 | tf_op jit(solution)/shard_map/ppermute | solution.py:176
  23.3 0.8 %collective-permute-done.3 = f32[4,16,4,32]{3,1,2,0:T(8,128)S(1)} collective-permute-done((f32[4,16,4,32]{3,1,2,0:T(8,128)S(1)}, f32[4,16,4,32]{3,1,2,0:T(8,128)S(1)}, u32[]{:S(2)}, u32[]{:S(2)}) %collective-permute-start.3) | collective-permute-done | bytes 32800 | tf_op jit(solution)/shard_map/ppermute | solution.py:62
  24.1 1.6 %collective-permute-start.4 = (f32[2,16,4,32]{3,1,2,0:T(8,128)S(1)}, f32[2,16,4,32]{3,1,2,0:T(8,128)S(1)}, u32[]{:S(2)}, u32[]{:S(2)}) collective-permute-start(f32[2,16,4,32]{3,1,2,0:T(8,128)S(1)} %constant_dynamic-slice_fusion), channel_id=1, source_target_pairs={{0,2},{2,0},{1,3},{3,1},{4,6},{6,4},{5,7},{7,5},{8,10},{10,8},{9,1... | collective-permute-start | bytes 49160 | tf_op jit(solution)/shard_map/ppermute | solution.py:75
  25.6 0.2 convolution_bitcast_fusion.1
  25.9 2.5 %collective-permute-done.4 = f32[2,16,4,32]{3,1,2,0:T(8,128)S(1)} collective-permute-done((f32[2,16,4,32]{3,1,2,0:T(8,128)S(1)}, f32[2,16,4,32]{3,1,2,0:T(8,128)S(1)}, u32[]{:S(2)}, u32[]{:S(2)}) %collective-permute-start.4) | collective-permute-done | bytes 16416 | tf_op jit(solution)/shard_map/ppermute | solution.py:75
  28.4 0.1 tanh_add_fusion
  28.5 0.7 %copy.40 = f32[2,16,4,32]{3,2,1,0:T(4,128)} copy(f32[2,16,4,32]{3,1,2,0:T(8,128)S(1)} %tanh_add_fusion) | data formatting | bytes 32768
  29.3 0.9 %copy.39 = f32[2,4,8,16,128]{4,3,2,1,0:T(8,128)} copy(f32[2,4,8,16,128]{4,2,3,1,0:T(8,128)S(1)} %pad_maximum_fusion.1) | data formatting | bytes 1048576
  (47 shorter events, 0.5 us)
Async XLA Ops:
  0.6 1.2 %copy-start = (f32[2,4,16,16,128]{4,3,2,1,0:T(8,128)S(1)}, f32[2,4,16,16,128]{4,3,2,1,0:T(8,128)}, u32[]{:S(2)}) copy-start(f32[2,4,16,16,128]{4,3,2,1,0:T(8,128)} %param.18) | copy-start | bytes 3145732
  0.6 1.4 %copy-start.9 = (s32[4]{0:T(128)S(1)}, s32[4]{0:T(128)}, u32[]{:S(2)}) copy-start(s32[4]{0:T(128)} %param.19) | copy-start | bytes 52
  0.7 1.4 %copy-start.8 = (s32[4,2]{0,1:T(2,128)S(1)}, s32[4,2]{0,1:T(2,128)}, u32[]{:S(2)}) copy-start(s32[4,2]{0,1:T(2,128)} %param.20) | copy-start | bytes 100
  0.7 1.5 %copy-start.12 = (s32[1,4]{1,0:T(1,128)S(1)}, s32[1,4]{1,0:T(1,128)}, u32[]{:S(2)}) copy-start(s32[1,4]{1,0:T(1,128)} %param.21) | copy-start | bytes 52
  0.7 1.5 %copy-start.5 = (bf16[2,4,2,16,128]{4,3,2,1,0:T(8,128)(2,1)S(1)}, bf16[2,4,2,16,128]{4,3,2,1,0:T(8,128)(2,1)}, u32[]{:S(2)}) copy-start(bf16[2,4,2,16,128]{4,3,2,1,0:T(8,128)(2,1)} %param.17) | copy-start | bytes 196612
  0.7 8.0 %copy-start.14 = (f32[16]{0:T(128)S(1)}, f32[16]{0:T(128)}, u32[]{:S(2)}) copy-start(f32[16]{0:T(128)} %param.24) | copy-start | bytes 196
  0.7 8.0 %copy-start.13 = (f32[16]{0:T(128)S(1)}, f32[16]{0:T(128)}, u32[]{:S(2)}) copy-start(f32[16]{0:T(128)} %param.26) | copy-start | bytes 196
  0.7 8.1 %copy-start.3 = (bf16[9,16,18]{2,1,0:T(8,128)(2,1)S(1)}, bf16[9,16,18]{2,1,0:T(8,128)(2,1)}, u32[]{:S(2)}) copy-start(bf16[9,16,18]{2,1,0:T(8,128)(2,1)} %param.23) | copy-start | bytes 15556
  1.9 7.1 %copy-start.4 = (bf16[9,16,18]{2,1,0:T(8,128)(2,1)S(1)}, bf16[9,16,18]{2,1,0:T(8,128)(2,1)}, u32[]{:S(2)}) copy-start(bf16[9,16,18]{2,1,0:T(8,128)(2,1)} %param.25) | copy-start | bytes 15556
  2.3 7.9 %collective-permute-start = (bf16[1,18,3,128]{3,1,2,0:T(8,128)(2,1)S(1)}, bf16[1,18,3,128]{3,1,2,0:T(8,128)(2,1)S(1)}, u32[]{:S(2)}, u32[]{:S(2)}) collective-permute-start(bf16[1,18,3,128]{3,1,2,0:T(8,128)(2,1)S(1)} %bitcast.281), channel_id=1, source_target_pairs={{0,4},{4,8},{8,12},{1,5},{5,9},{9,13},{2,6},{6,10},{10,14},{3,7},{... | collective-permute-start | bytes 41480 | tf_op jit(solution)/shard_map/ppermute | solution.py:12
  7.3 5.7 %collective-permute-start.1 = (bf16[1,18,3,128]{3,1,2,0:T(8,128)(2,1)S(1)}, bf16[1,18,3,128]{3,1,2,0:T(8,128)(2,1)S(1)}, u32[]{:S(2)}, u32[]{:S(2)}) collective-permute-start(bf16[1,18,3,128]{3,1,2,0:T(8,128)(2,1)S(1)} %bitcast.280), channel_id=1, source_target_pairs={{4,0},{8,4},{12,8},{5,1},{9,5},{13,9},{6,2},{10,6},{14,10},{7,3},{... | collective-permute-start | bytes 41480 | tf_op jit(solution)/shard_map/ppermute | solution.py:15
  17.8 0.8 %copy-start.2 = (bf16[9,16,18]{2,1,0:T(8,128)(2,1)S(1)}, bf16[9,16,18]{2,1,0:T(8,128)(2,1)}, u32[]{:S(2)}) copy-start(bf16[9,16,18]{2,1,0:T(8,128)(2,1)} %param.27) | copy-start | bytes 15556
  20.2 0.7 %copy-start.10 = (f32[16]{0:T(128)S(1)}, f32[16]{0:T(128)}, u32[]{:S(2)}) copy-start(f32[16]{0:T(128)} %param.28) | copy-start | bytes 196
  20.9 1.4 %copy-start.6 = (f32[16,16]{1,0:T(8,128)S(1)}, f32[16,16]{1,0:T(8,128)}, u32[]{:S(2)}) copy-start(f32[16,16]{1,0:T(8,128)} %param.29) | copy-start | bytes 3076
  21.3 4.3 %copy-start.1 = (f32[2,16,4,32]{3,2,1,0:T(4,128)S(1)}, f32[2,16,4,32]{3,2,1,0:T(4,128)}, u32[]{:S(2)}) copy-start(f32[2,16,4,32]{3,2,1,0:T(4,128)} %param.22) | copy-start | bytes 49156
  21.3 4.3 %copy-start.7 = (f32[16,16]{1,0:T(8,128)S(1)}, f32[16,16]{1,0:T(8,128)}, u32[]{:S(2)}) copy-start(f32[16,16]{1,0:T(8,128)} %param.30) | copy-start | bytes 3076
  21.3 7.1 %copy-start.11 = (f32[16]{0:T(128)S(1)}, f32[16]{0:T(128)}, u32[]{:S(2)}) copy-start(f32[16]{0:T(128)} %param.31) | copy-start | bytes 196
  22.6 1.4 %collective-permute-start.3 = (f32[4,16,4,32]{3,1,2,0:T(8,128)S(1)}, f32[4,16,4,32]{3,1,2,0:T(8,128)S(1)}, u32[]{:S(2)}, u32[]{:S(2)}) collective-permute-start(f32[4,16,4,32]{3,1,2,0:T(8,128)S(1)} %convolution_bitcast_fusion), channel_id=1, source_target_pairs={{0,1},{1,0},{2,3},{3,2},{4,5},{5,4},{6,7},{7,6},{8,9},{9,8},{10,11... | collective-permute-start | bytes 98312 | tf_op jit(solution)/shard_map/ppermute | solution.py:62
  22.7 6.4 %collective-permute-start.2 = (f32[1,4,8,16,128]{4,2,3,1,0:T(8,128)S(1)}, f32[1,4,8,16,128]{4,2,3,1,0:T(8,128)S(1)}, u32[]{:S(2)}, u32[]{:S(2)}) collective-permute-start(f32[1,4,8,16,128]{4,2,3,1,0:T(8,128)S(1)} %constant_dynamic-slice_fusion.1), channel_id=1, source_target_pairs={{0,1},{1,0},{2,3},{3,2},{4,5},{5,4},{6,7},{7,6},{8,9},{9,8},{10,11... | collective-permute-start | bytes 786440 | tf_op jit(solution)/shard_map/ppermute | solution.py:176
  24.1 4.3 %collective-permute-start.4 = (f32[2,16,4,32]{3,1,2,0:T(8,128)S(1)}, f32[2,16,4,32]{3,1,2,0:T(8,128)S(1)}, u32[]{:S(2)}, u32[]{:S(2)}) collective-permute-start(f32[2,16,4,32]{3,1,2,0:T(8,128)S(1)} %constant_dynamic-slice_fusion), channel_id=1, source_target_pairs={{0,2},{2,0},{1,3},{3,1},{4,6},{6,4},{5,7},{7,5},{8,10},{10,8},{9,1... | collective-permute-start | bytes 49160 | tf_op jit(solution)/shard_map/ppermute | solution.py:75

commit v16 on v15

--- a/solution.py
+++ b/solution.py
@@ -197,7 +197,8 @@
     ) / 16.0
     ordered = jnp.take(pooled, coarse_perm[0], axis=0)
     part = jnp.einsum("oc,kcij->koij", u_pool, ordered, precision=lax.Precision.HIGHEST)
-    pre = exchange_sum(rep_sum(part), coarse_state.shape[0])
+    new_half, chip_part = lax.optimization_barrier((new_half, rep_sum(part)))
+    pre = exchange_sum(chip_part, coarse_state.shape[0])
     pre = pre + jnp.einsum("oc,kcij->koij", u_state, coarse_state, precision=lax.Precision.HIGHEST)
     pre = pre + b_coarse[None, :, None, None]
     coarse_next = coarse_state + jnp.tanh(pre)

time: 30.4 us -> 30 us (0.987)
    ppermute x1, waiting for transfers between devices: 2.52 us -> 1.99 us  [exchange_sum(): chunk = lax.ppermute(chunk, 'band', perm)]
    ppermute x1, starting transfers between devices: 0.07 us -> 0.56 us  [rep_sum(): lax.ppermute(part, 'rep', [(r, (r + step) % reps) for r in range(reps)])]
    ppermute x1, starting transfers between devices: 0.55 us -> 0.07 us  [shards(): lax.ppermute(piece, 'rep', [(r, (r + step) % reps) for r in range(reps)])]
  transfers between devices with their start and end apart: 5 -> 5, of which waited for: 3 -> 3; matrix products, arithmetic and copies ran while one was open for 9% -> 11% of each run, Pallas kernels for 0% -> 0%
where the time goes in v16:
time: 30 us; the launch traced here: 29.8 us
  starting transfers between devices  8.43 us (28%)
  matrix products  7.74 us (26%)
  waiting for transfers between devices  5.62 us (19%)
  local copies, waits for them, and re-layouts  5.37 us (18%)
  other arithmetic  1.38 us (5%)
  between operations  1.2 us (4%)
    dot_general x18, matrix products, apply_filter(): jnp.einsum('oi,bsirw->bsorw', filter_weight[(left_operand + 1) * 3 + (rig...  6.86 us
    ppermute x1, starting transfers between devices, padded(): lax.ppermute(lax.slice_in_dim(block, block.shape[dim] - width, None, axis...  4.96 us
    unnamed x36, local copies, waits for them, and re-layouts  3.43 us
    ppermute x1, waiting for transfers between devices, padded(): lax.ppermute(lax.slice_in_dim(block, 0, width, axis=dim), axis, backward)  2.64 us
    ppermute x1, waiting for transfers between devices, exchange_sum(): chunk = lax.ppermute(chunk, 'band', perm)  1.99 us
    ppermute x1, starting transfers between devices, exchange_sum(): chunk = lax.ppermute(chunk, 'band', perm)  1.55 us
    ppermute x1, starting transfers between devices, padded(): lax.ppermute(lax.slice_in_dim(block, 0, width, axis=dim), axis, backward)  1.29 us
    ppermute x1, waiting for transfers between devices, rep_sum(): lax.ppermute(part, 'rep', [(r, (r + step) % reps) for r in range(reps)])  0.99 us
  transfers between devices with their start and end apart: 5, of which 3 were waited for; matrix products, arithmetic and copies ran while one was open for 11% of the time, Pallas kernels for 0%

profile of v16, /device:TPU:0, one launch (start us, length us, event | category | flops | bytes accessed | tf_op | source)
XLA Modules:
  0.0 29.8 jit_solution(9680979057536887110)
XLA Ops:
  0.7 1.1 %copy-done = f32[2,4,16,16,128]{4,3,2,1,0:T(8,128)S(1)} copy-done((f32[2,4,16,16,128]{4,3,2,1,0:T(8,128)S(1)}, f32[2,4,16,16,128]{4,3,2,1,0:T(8,128)}, u32[]{:S(2)}) %copy-start) | copy-done | bytes 1048600
  1.9 0.2 copy.71
  2.2 0.1 select_reduce_fusion.1
  2.3 5.0 %collective-permute-start = (bf16[1,18,3,128]{3,1,2,0:T(8,128)(2,1)S(1)}, bf16[1,18,3,128]{3,1,2,0:T(8,128)(2,1)S(1)}, u32[]{:S(2)}, u32[]{:S(2)}) collective-permute-start(bf16[1,18,3,128]{3,1,2,0:T(8,128)(2,1)S(1)} %bitcast.283), channel_id=1, source_target_pairs={{0,4},{4,8},{8,12},{1,5},{5,9},{9,13},{2,6},{6,10},{10,14},{3,7},{... | collective-permute-start | bytes 41480 | tf_op jit(solution)/shard_map/ppermute | solution.py:12
  7.3 1.3 %collective-permute-start.1 = (bf16[1,18,3,128]{3,1,2,0:T(8,128)(2,1)S(1)}, bf16[1,18,3,128]{3,1,2,0:T(8,128)(2,1)S(1)}, u32[]{:S(2)}, u32[]{:S(2)}) collective-permute-start(bf16[1,18,3,128]{3,1,2,0:T(8,128)(2,1)S(1)} %bitcast.282), channel_id=1, source_target_pairs={{4,0},{8,4},{12,8},{5,1},{9,5},{13,9},{6,2},{10,6},{14,10},{7,3},{... | collective-permute-start | bytes 41480 | tf_op jit(solution)/shard_map/ppermute | solution.py:15
  8.7 0.1 pad_maximum_fusion.5
  8.8 0.1 copy.35
  8.9 0.1 copy.36
  9.1 0.6 %gather_fusion.1 = bf16[4,18,3,128]{3,1,2,0:T(8,128)(2,1)S(1)} fusion(bf16[4,18,3,128]{3,1,2,0:T(8,128)(2,1)S(1)} %bitcast.279, s32[1024]{0:T(1024)S(1)} %pad_clamp_fusion.2), kind=kCustom, calls=%fused_computation.clone | custom fusion | bytes 110608 | tf_op jit(solution)/shard_map/jit(_take)/gather | solution.py:133
  9.6 0.6 %gather_fusion.2 = bf16[4,18,3,128]{3,1,2,0:T(8,128)(2,1)S(1)} fusion(bf16[4,18,3,128]{3,1,2,0:T(8,128)(2,1)S(1)} %bitcast.278, s32[1024]{0:T(1024)S(1)} %pad_clamp_fusion.1), kind=kCustom, calls=%fused_computation.1.clone | custom fusion | bytes 110608 | tf_op jit(solution)/shard_map/jit(_take)/gather | solution.py:136
  10.2 0.1 fusion.33
  10.3 2.6 %collective-permute-done.1 = bf16[1,18,3,128]{3,1,2,0:T(8,128)(2,1)S(1)} collective-permute-done((bf16[1,18,3,128]{3,1,2,0:T(8,128)(2,1)S(1)}, bf16[1,18,3,128]{3,1,2,0:T(8,128)(2,1)S(1)}, u32[]{:S(2)}, u32[]{:S(2)}) %collective-permute-start.1) | collective-permute-done | bytes 13856 | tf_op jit(solution)/shard_map/ppermute | solution.py:15
  13.0 0.1 fusion.32
  13.1 0.2 pad_maximum_fusion
  13.2 0.2 pad_slice_fusion
  13.4 0.5 %fusion.18 = f32[4,20,128,32]{2,3,1,0:T(8,128)S(1)} fusion(bf16[1,4,18,22,128]{4,2,3,1,0:T(8,128)(2,1)S(1)} %pad_maximum_fusion, bf16[9,16,18]{1,2,0:T(8,128)(2,1)S(1)} %copy.35, bf16[9,16,18]{1,2,0:T(8,128)(2,1)S(1)} %copy.36), kind=kOutput, calls=%fused_computation.52 | convolution fusion | flops 11798784 | bytes 1726592 | tf_op jit(solution)/shard_map/oi,bsirw->bsorw/dot_general | solution.py:39
  13.9 0.5 %convolution_add_fusion.7 = f32[4,20,128,32]{2,3,1,0:T(8,128)S(1)} fusion(f32[4,20,128,32]{2,3,1,0:T(8,128)S(1)} %fusion.18, bf16[1,4,18,22,128]{4,2,3,1,0:T(8,128)(2,1)S(1)} %pad_maximum_fusion, bf16[9,16,18]{1,2,0:T(8,128)(2,1)S(1)} %copy.35, bf16[9,16,18]{1,2,0:T(8,128)(2,1)S(1)} %copy.36), kind=kOutput, calls=%fused_computation.19 | convolution fusion | flops 12126464 | bytes 3223552 | tf_op jit(solution)/shard_map/oi,bsirw->bsorw/dot_general | solution.py:39
  14.3 0.5 %convolution_add_fusion.6 = f32[4,20,128,32]{2,3,1,0:T(8,128)S(1)} fusion(f32[4,20,128,32]{2,3,1,0:T(8,128)S(1)} %convolution_add_fusion.7, bf16[1,4,18,22,128]{4,2,3,1,0:T(8,128)(2,1)S(1)} %pad_maximum_fusion, bf16[9,16,18]{1,2,0:T(8,128)(2,1)S(1)} %copy.35, bf16[9,16,18]{1,2,0:T(8,128)(2,1)S(1)} %copy.36), kind=kOutput, calls=%fused_computation.18 | convolution fusion | flops 12126464 | bytes 3037312 | tf_op jit(solution)/shard_map/oi,bsirw->bsorw/dot_general | solution.py:39
  14.8 0.5 %convolution_add_fusion.5 = f32[4,20,128,32]{2,3,1,0:T(8,128)S(1)} fusion(f32[4,20,128,32]{2,3,1,0:T(8,128)S(1)} %convolution_add_fusion.6, bf16[1,4,18,22,128]{4,2,3,1,0:T(8,128)(2,1)S(1)} %pad_maximum_fusion, bf16[9,16,18]{1,2,0:T(8,128)(2,1)S(1)} %copy.35, bf16[9,16,18]{1,2,0:T(8,128)(2,1)S(1)} %copy.36), kind=kOutput, calls=%fused_computation.17 | convolution fusion | flops 12126464 | bytes 3037312 | tf_op jit(solution)/shard_map/oi,bsirw->bsorw/dot_general | solution.py:39
  15.3 0.4 %convolution_add_fusion.4 = f32[4,20,128,32]{2,3,1,0:T(8,128)S(1)} fusion(f32[4,20,128,32]{2,3,1,0:T(8,128)S(1)} %convolution_add_fusion.5, bf16[1,4,18,22,128]{4,2,3,1,0:T(8,128)(2,1)S(1)} %pad_maximum_fusion, bf16[9,16,18]{1,2,0:T(8,128)(2,1)S(1)} %copy.35, bf16[9,16,18]{1,2,0:T(8,128)(2,1)S(1)} %copy.36), kind=kOutput, calls=%fused_computation.16 | convolution fusion | flops 12126464 | bytes 3223552 | tf_op jit(solution)/shard_map/oi,bsirw->bsorw/dot_general | solution.py:39
  15.8 0.5 %convolution_add_fusion.3 = f32[4,20,128,32]{2,3,1,0:T(8,128)S(1)} fusion(f32[4,20,128,32]{2,3,1,0:T(8,128)S(1)} %convolution_add_fusion.4, bf16[1,4,18,22,128]{4,2,3,1,0:T(8,128)(2,1)S(1)} %pad_maximum_fusion, bf16[9,16,18]{1,2,0:T(8,128)(2,1)S(1)} %copy.35, bf16[9,16,18]{1,2,0:T(8,128)(2,1)S(1)} %copy.36), kind=kOutput, calls=%fused_computation.15 | convolution fusion | flops 12126464 | bytes 3037312 | tf_op jit(solution)/shard_map/oi,bsirw->bsorw/dot_general | solution.py:39
  16.3 0.5 %convolution_add_fusion.2 = f32[4,20,128,32]{2,3,1,0:T(8,128)S(1)} fusion(f32[4,20,128,32]{2,3,1,0:T(8,128)S(1)} %convolution_add_fusion.3, bf16[1,4,18,22,128]{4,2,3,1,0:T(8,128)(2,1)S(1)} %pad_maximum_fusion, bf16[9,16,18]{1,2,0:T(8,128)(2,1)S(1)} %copy.35, bf16[9,16,18]{1,2,0:T(8,128)(2,1)S(1)} %copy.36), kind=kOutput, calls=%fused_computation.14 | convolution fusion | flops 12126464 | bytes 3037312 | tf_op jit(solution)/shard_map/oi,bsirw->bsorw/dot_general | solution.py:39
  16.8 0.5 %convolution_add_fusion.1 = f32[4,20,128,32]{2,3,1,0:T(8,128)S(1)} fusion(f32[4,20,128,32]{2,3,1,0:T(8,128)S(1)} %convolution_add_fusion.2, bf16[1,4,18,22,128]{4,2,3,1,0:T(8,128)(2,1)S(1)} %pad_maximum_fusion, bf16[9,16,18]{1,2,0:T(8,128)(2,1)S(1)} %copy.35, bf16[9,16,18]{1,2,0:T(8,128)(2,1)S(1)} %copy.36), kind=kOutput, calls=%fused_computation.13 | convolution fusion | flops 12126464 | bytes 3223552 | tf_op jit(solution)/shard_map/oi,bsirw->bsorw/dot_general | solution.py:39
  17.2 0.6 %fusion.7 = f32[1,4,32,20,128]{4,2,3,1,0:T(8,128)S(1)} fusion(f32[4,20,128,32]{2,3,1,0:T(8,128)S(1)} %convolution_add_fusion.1, f32[32]{0:T(128)S(1)} %pad_maximum_fusion.5, bf16[1,4,18,22,128]{4,2,3,1,0:T(8,128)(2,1)S(1)} %pad_maximum_fusion, bf16[9,16,18]{1,2,0:T(8,128)(2,1)S(1)} %copy.36, bf16[9,16,18]{1,2,0:T(8,128)(2,1)S(1)} %copy.35), kind=kOutput, calls=%fused_computation.26 | convolution fusion | flops 13437184 | bytes 3037440 | tf_op jit(solution)/shard_map/oi,bsirw->bsorw/dot_general | solution.py:39
  17.8 0.1 fusion.16
  17.9 0.5 %fusion.15 = bf16[1,4,18,20,132]{4,2,3,1,0:T(8,128)(2,1)S(1)} fusion(bf16[1,4,16,20,128]{4,2,3,1,0:T(8,128)(2,1)S(1)} %fusion.16, bf16[1,4,2,20,132]{4,2,3,1,0:T(2,128)(2,1)S(1)} %pad_slice_fusion), kind=kLoop, calls=%fused_computation.45 | loop fusion | flops 1140480 | bytes 750080 | tf_op jit(solution)/shard_map/concatenate | solution.py:166
  18.5 0.1 copy-done.2
  18.6 0.2 fusion.30
  18.8 0.3 %convolution_add_fusion.15 = f32[4,16,128,16]{2,3,1,0:T(8,128)S(1)} fusion(f32[4,16,128,16]{2,3,1,0:T(8,128)S(1)} %fusion.30, bf16[1,4,18,20,132]{4,2,3,1,0:T(8,128)(2,1)S(1)} %fusion.15, bf16[9,16,18]{2,1,0:T(8,128)(2,1)S(1)} %copy-done.2), kind=kOutput, calls=%fused_computation.35 | convolution fusion | flops 4849664 | bytes 1445888 | tf_op jit(solution)/shard_map/oi,bsirw->bsorw/dot_general | solution.py:39
  19.1 0.3 %convolution_add_fusion.14 = f32[4,16,128,16]{2,3,1,0:T(8,128)S(1)} fusion(f32[4,16,128,16]{2,3,1,0:T(8,128)S(1)} %convolution_add_fusion.15, bf16[1,4,18,20,132]{4,2,3,1,0:T(8,128)(2,1)S(1)} %fusion.15, bf16[9,16,18]{2,1,0:T(8,128)(2,1)S(1)} %copy-done.2), kind=kOutput, calls=%fused_computation.34 | convolution fusion | flops 4849664 | bytes 1445888 | tf_op jit(solution)/shard_map/oi,bsirw->bsorw/dot_general | solution.py:39
  19.4 0.2 convolution_add_fusion.13
  19.6 0.3 %convolution_add_fusion.12 = f32[4,16,128,16]{2,3,1,0:T(8,128)S(1)} fusion(f32[4,16,128,16]{2,3,1,0:T(8,128)S(1)} %convolution_add_fusion.13, bf16[1,4,18,20,132]{4,2,3,1,0:T(8,128)(2,1)S(1)} %fusion.15, bf16[9,16,18]{2,1,0:T(8,128)(2,1)S(1)} %copy-done.2), kind=kOutput, calls=%fused_computation.32 | convolution fusion | flops 4849664 | bytes 1445888 | tf_op jit(solution)/shard_map/oi,bsirw->bsorw/dot_general | solution.py:39
  19.9 0.3 %convolution_add_fusion.11 = f32[4,16,128,16]{2,3,1,0:T(8,128)S(1)} fusion(f32[4,16,128,16]{2,3,1,0:T(8,128)S(1)} %convolution_add_fusion.12, bf16[1,4,18,20,132]{4,2,3,1,0:T(8,128)(2,1)S(1)} %fusion.15, bf16[9,16,18]{2,1,0:T(8,128)(2,1)S(1)} %copy-done.2), kind=kOutput, calls=%fused_computation.31 | convolution fusion | flops 4849664 | bytes 1445888 | tf_op jit(solution)/shard_map/oi,bsirw->bsorw/dot_general | solution.py:39
  20.2 0.2 convolution_add_fusion.10
  20.4 0.3 %convolution_add_fusion.9 = f32[4,16,128,16]{2,3,1,0:T(8,128)S(1)} fusion(f32[4,16,128,16]{2,3,1,0:T(8,128)S(1)} %convolution_add_fusion.10, bf16[1,4,18,20,132]{4,2,3,1,0:T(8,128)(2,1)S(1)} %fusion.15, bf16[9,16,18]{2,1,0:T(8,128)(2,1)S(1)} %copy-done.2), kind=kOutput, calls=%fused_computation.29 | convolution fusion | flops 4849664 | bytes 1445888 | tf_op jit(solution)/shard_map/oi,bsirw->bsorw/dot_general | solution.py:39
  20.8 0.1 copy-done.10
  20.9 0.4 %fusion.14 = f32[1,4,16,16,128]{4,2,3,1,0:T(8,128)S(1)} fusion(f32[4,16,128,16]{2,3,1,0:T(8,128)S(1)} %convolution_add_fusion.9, f32[1,4,32,20,128]{4,2,3,1,0:T(8,128)S(1)} %fusion.7, f32[1,4,16,16,128]{4,3,2,1,0:T(8,128)S(1)} %constant_dynamic-slice_fusion.2, bf16[1,4,18,20,132]{4,2,3,1,0:T(8,128)(2,1)S(1)} %fusion.15, f32[16]{0:T(128)S(1)} %copy-done.10, ...), kind=kOutput, calls=%fused_computation.41 | convolution fusion | flops 5636096 | bytes 2495488 | tf_op jit(solution)/shard_map/oi,bsirw->bsorw/dot_general | solution.py:39
  21.3 0.4 %convolution_reduce_fusion = f32[4,16,4,32]{3,1,2,0:T(8,128)S(1)} fusion(f32[4,16,4,4,128]{4,1,3,2,0:T(8,128)S(1)} %bitcast.277, s32[128]{0:T(128)S(1)} %and_select_fusion), kind=kOutput, calls=%fused_computation.42 | convolution fusion | flops 50360320 | bytes 557568 | tf_op jit(solution)/shard_map/schw,wj->schj/dot_general | solution.py:192
  21.7 0.1 collective-permute-start.2
  21.8 0.6 %gather_fusion = f32[4,16,4,32]{3,1,2,0:T(8,128)S(1)} fusion(f32[4,16,4,32]{3,1,2,0:T(8,128)S(1)} %broadcast_multiply_fusion, s32[1024]{0:T(1024)S(1)} %pad_clamp_fusion), kind=kCustom, calls=%fused_computation.2 | custom fusion | bytes 65552 | tf_op jit(solution)/shard_map/jit(_take)/gather | solution.py:198
  22.4 0.3 %convolution_bitcast_fusion = f32[4,16,4,32]{3,1,2,0:T(8,128)S(1)} fusion(f32[4,16,4,32]{3,1,2,0:T(8,128)S(1)} %gather_fusion, pred[4]{0:T(512)(128)(4,1)S(1)} %get-tuple-element.36, f32[16,16]{1,0:T(8,128)S(1)} %copy-done.6), kind=kOutput, calls=%fused_computation.43 | convolution fusion | flops 1581056 | bytes 66564 | tf_op jit(solution)/shard_map/oc,kcij->koij/dot_general | solution.py:199
  22.7 0.6 %collective-permute-start.3 = (f32[4,16,4,32]{3,1,2,0:T(8,128)S(1)}, f32[4,16,4,32]{3,1,2,0:T(8,128)S(1)}, u32[]{:S(2)}, u32[]{:S(2)}) collective-permute-start(f32[4,16,4,32]{3,1,2,0:T(8,128)S(1)} %convolution_bitcast_fusion), channel_id=1, source_target_pairs={{0,1},{1,0},{2,3},{3,2},{4,5},{5,4},{6,7},{7,6},{8,9},{9,8},{10,11... | collective-permute-start | bytes 98312 | tf_op jit(solution)/shard_map/ppermute | solution.py:62
  23.3 1.0 %collective-permute-done.3 = f32[4,16,4,32]{3,1,2,0:T(8,128)S(1)} collective-permute-done((f32[4,16,4,32]{3,1,2,0:T(8,128)S(1)}, f32[4,16,4,32]{3,1,2,0:T(8,128)S(1)}, u32[]{:S(2)}, u32[]{:S(2)}) %collective-permute-start.3) | collective-permute-done | bytes 32800 | tf_op jit(solution)/shard_map/ppermute | solution.py:62
  24.4 1.6 %collective-permute-start.4 = (f32[2,16,4,32]{3,1,2,0:T(8,128)S(1)}, f32[2,16,4,32]{3,1,2,0:T(8,128)S(1)}, u32[]{:S(2)}, u32[]{:S(2)}) collective-permute-start(f32[2,16,4,32]{3,1,2,0:T(8,128)S(1)} %constant_dynamic-slice_fusion), channel_id=1, source_target_pairs={{0,2},{2,0},{1,3},{3,1},{4,6},{6,4},{5,7},{7,5},{8,10},{10,8},{9,1... | collective-permute-start | bytes 49160 | tf_op jit(solution)/shard_map/ppermute | solution.py:75
  26.0 0.9 %copy.39 = f32[2,4,8,16,128]{4,3,2,1,0:T(8,128)} copy(f32[2,4,8,16,128]{4,2,3,1,0:T(8,128)S(1)} %pad_maximum_fusion.1) | data formatting | bytes 1048576
  26.9 2.0 %collective-permute-done.4 = f32[2,16,4,32]{3,1,2,0:T(8,128)S(1)} collective-permute-done((f32[2,16,4,32]{3,1,2,0:T(8,128)S(1)}, f32[2,16,4,32]{3,1,2,0:T(8,128)S(1)}, u32[]{:S(2)}, u32[]{:S(2)}) %collective-permute-start.4) | collective-permute-done | bytes 16416 | tf_op jit(solution)/shard_map/ppermute | solution.py:75
  28.9 0.2 tanh_add_fusion
  29.1 0.7 %copy.40 = f32[2,16,4,32]{3,2,1,0:T(4,128)} copy(f32[2,16,4,32]{3,1,2,0:T(8,128)S(1)} %tanh_add_fusion) | data formatting | bytes 32768
  (46 shorter events, 0.4 us)
Async XLA Ops:
  0.6 1.2 %copy-start = (f32[2,4,16,16,128]{4,3,2,1,0:T(8,128)S(1)}, f32[2,4,16,16,128]{4,3,2,1,0:T(8,128)}, u32[]{:S(2)}) copy-start(f32[2,4,16,16,128]{4,3,2,1,0:T(8,128)} %param.18) | copy-start | bytes 3145732
  0.6 1.4 %copy-start.9 = (s32[4]{0:T(128)S(1)}, s32[4]{0:T(128)}, u32[]{:S(2)}) copy-start(s32[4]{0:T(128)} %param.19) | copy-start | bytes 52
  0.7 1.4 %copy-start.8 = (s32[4,2]{0,1:T(2,128)S(1)}, s32[4,2]{0,1:T(2,128)}, u32[]{:S(2)}) copy-start(s32[4,2]{0,1:T(2,128)} %param.20) | copy-start | bytes 100
  0.7 1.5 %copy-start.12 = (s32[1,4]{1,0:T(1,128)S(1)}, s32[1,4]{1,0:T(1,128)}, u32[]{:S(2)}) copy-start(s32[1,4]{1,0:T(1,128)} %param.21) | copy-start | bytes 52
  0.7 1.5 %copy-start.5 = (bf16[2,4,2,16,128]{4,3,2,1,0:T(8,128)(2,1)S(1)}, bf16[2,4,2,16,128]{4,3,2,1,0:T(8,128)(2,1)}, u32[]{:S(2)}) copy-start(bf16[2,4,2,16,128]{4,3,2,1,0:T(8,128)(2,1)} %param.17) | copy-start | bytes 196612
  0.7 8.0 %copy-start.14 = (f32[16]{0:T(128)S(1)}, f32[16]{0:T(128)}, u32[]{:S(2)}) copy-start(f32[16]{0:T(128)} %param.24) | copy-start | bytes 196
  0.7 8.0 %copy-start.13 = (f32[16]{0:T(128)S(1)}, f32[16]{0:T(128)}, u32[]{:S(2)}) copy-start(f32[16]{0:T(128)} %param.26) | copy-start | bytes 196
  0.7 8.1 %copy-start.3 = (bf16[9,16,18]{2,1,0:T(8,128)(2,1)S(1)}, bf16[9,16,18]{2,1,0:T(8,128)(2,1)}, u32[]{:S(2)}) copy-start(bf16[9,16,18]{2,1,0:T(8,128)(2,1)} %param.23) | copy-start | bytes 15556
  0.7 8.2 %copy-start.4 = (bf16[9,16,18]{2,1,0:T(8,128)(2,1)S(1)}, bf16[9,16,18]{2,1,0:T(8,128)(2,1)}, u32[]{:S(2)}) copy-start(bf16[9,16,18]{2,1,0:T(8,128)(2,1)} %param.25) | copy-start | bytes 15556
  2.3 7.9 %collective-permute-start = (bf16[1,18,3,128]{3,1,2,0:T(8,128)(2,1)S(1)}, bf16[1,18,3,128]{3,1,2,0:T(8,128)(2,1)S(1)}, u32[]{:S(2)}, u32[]{:S(2)}) collective-permute-start(bf16[1,18,3,128]{3,1,2,0:T(8,128)(2,1)S(1)} %bitcast.283), channel_id=1, source_target_pairs={{0,4},{4,8},{8,12},{1,5},{5,9},{9,13},{2,6},{6,10},{10,14},{3,7},{... | collective-permute-start | bytes 41480 | tf_op jit(solution)/shard_map/ppermute | solution.py:12
  7.3 5.7 %collective-permute-start.1 = (bf16[1,18,3,128]{3,1,2,0:T(8,128)(2,1)S(1)}, bf16[1,18,3,128]{3,1,2,0:T(8,128)(2,1)S(1)}, u32[]{:S(2)}, u32[]{:S(2)}) collective-permute-start(bf16[1,18,3,128]{3,1,2,0:T(8,128)(2,1)S(1)} %bitcast.282), channel_id=1, source_target_pairs={{4,0},{8,4},{12,8},{5,1},{9,5},{13,9},{6,2},{10,6},{14,10},{7,3},{... | collective-permute-start | bytes 41480 | tf_op jit(solution)/shard_map/ppermute | solution.py:15
  17.8 0.8 %copy-start.2 = (bf16[9,16,18]{2,1,0:T(8,128)(2,1)S(1)}, bf16[9,16,18]{2,1,0:T(8,128)(2,1)}, u32[]{:S(2)}) copy-start(bf16[9,16,18]{2,1,0:T(8,128)(2,1)} %param.27) | copy-start | bytes 15556
  20.2 0.7 %copy-start.10 = (f32[16]{0:T(128)S(1)}, f32[16]{0:T(128)}, u32[]{:S(2)}) copy-start(f32[16]{0:T(128)} %param.28) | copy-start | bytes 196
  21.3 1.1 %copy-start.6 = (f32[16,16]{1,0:T(8,128)S(1)}, f32[16,16]{1,0:T(8,128)}, u32[]{:S(2)}) copy-start(f32[16,16]{1,0:T(8,128)} %param.29) | copy-start | bytes 3076
  21.7 2.5 %collective-permute-start.2 = (f32[1,4,8,16,128]{4,2,3,1,0:T(8,128)S(1)}, f32[1,4,8,16,128]{4,2,3,1,0:T(8,128)S(1)}, u32[]{:S(2)}, u32[]{:S(2)}) collective-permute-start(f32[1,4,8,16,128]{4,2,3,1,0:T(8,128)S(1)} %constant_dynamic-slice_fusion.1), channel_id=1, source_target_pairs={{0,1},{1,0},{2,3},{3,2},{4,5},{5,4},{6,7},{7,6},{8,9},{9,8},{10,11... | collective-permute-start | bytes 786440 | tf_op jit(solution)/shard_map/ppermute | solution.py:176
  22.7 1.5 %collective-permute-start.3 = (f32[4,16,4,32]{3,1,2,0:T(8,128)S(1)}, f32[4,16,4,32]{3,1,2,0:T(8,128)S(1)}, u32[]{:S(2)}, u32[]{:S(2)}) collective-permute-start(f32[4,16,4,32]{3,1,2,0:T(8,128)S(1)} %convolution_bitcast_fusion), channel_id=1, source_target_pairs={{0,1},{1,0},{2,3},{3,2},{4,5},{5,4},{6,7},{7,6},{8,9},{9,8},{10,11... | collective-permute-start | bytes 98312 | tf_op jit(solution)/shard_map/ppermute | solution.py:62
  24.3 4.5 %copy-start.1 = (f32[2,16,4,32]{3,2,1,0:T(4,128)S(1)}, f32[2,16,4,32]{3,2,1,0:T(4,128)}, u32[]{:S(2)}) copy-start(f32[2,16,4,32]{3,2,1,0:T(4,128)} %param.22) | copy-start | bytes 49156
  24.4 4.5 %copy-start.7 = (f32[16,16]{1,0:T(8,128)S(1)}, f32[16,16]{1,0:T(8,128)}, u32[]{:S(2)}) copy-start(f32[16,16]{1,0:T(8,128)} %param.30) | copy-start | bytes 3076
  24.4 4.5 %copy-start.11 = (f32[16]{0:T(128)S(1)}, f32[16]{0:T(128)}, u32[]{:S(2)}) copy-start(f32[16]{0:T(128)} %param.31) | copy-start | bytes 196
  24.4 4.4 %collective-permute-start.4 = (f32[2,16,4,32]{3,1,2,0:T(8,128)S(1)}, f32[2,16,4,32]{3,1,2,0:T(8,128)S(1)}, u32[]{:S(2)}, u32[]{:S(2)}) collective-permute-start(f32[2,16,4,32]{3,1,2,0:T(8,128)S(1)} %constant_dynamic-slice_fusion), channel_id=1, source_target_pairs={{0,2},{2,0},{1,3},{3,1},{4,6},{6,4},{5,7},{7,5},{8,10},{10,8},{9,1... | collective-permute-start | bytes 49160 | tf_op jit(solution)/shard_map/ppermute | solution.py:75

commit v17 on v8

--- a/solution.py
+++ b/solution.py
@@ -57,6 +57,18 @@
 def choose_rows(block, select):
     masked = jnp.where(select[None, :, None, None, None], block, jnp.zeros_like(block))
     return jnp.sum(masked, axis=1)
+
+
+def logistic(value):
+    return 0.5 + 0.5 * jnp.tanh(0.5 * value)
+
+
+def rep_sum(part):
+    reps = lax.axis_size("rep")
+    total = part
+    for step in range(1, reps):
+        total = total + lax.ppermute(part, "rep", [(r, (r + step) % reps) for r in range(reps)])
+    return total
 
 
 def exchange_sum(part, owned):
@@ -90,6 +102,11 @@
     u_state,
     b_coarse,
 ):
+    reps = lax.axis_size("rep")
+    rep = lax.axis_index("rep")
+    per_core = features.shape[0] // reps
+    features = lax.dynamic_slice_in_dim(features, rep * per_core, per_core, 0)
+    state = lax.dynamic_slice_in_dim(state, rep * per_core, per_core, 0)
     slots = state.shape[1]
     chans = state.shape[2]
     row_count = state.shape[3]
@@ -138,7 +155,7 @@
     )
     full = jnp.concatenate([top, joined, bottom], axis=3)
     first = jnp.pad(full, ((0, 0), (0, 0), (0, 0), (0, 0), (2, 2)))
-    gates = jax.nn.sigmoid(
+    gates = logistic(
         apply_filter(
             first,
             jnp.concatenate([w_update, w_reset], axis=1),
@@ -160,7 +177,22 @@
     )
     live_scale = alive.astype(jnp.float32)[None, :, None, None, None]
     new_state = ((1.0 - update) * state + update * candidate) * live_scale
-    new_half = lax.dynamic_slice_in_dim(new_state, start, half, 2)
+    groups = []
+    for step in range(reps):
+        piece = lax.dynamic_slice_in_dim(new_state, ((rep + step) % reps) * half, half, 2)
+        if step:
+            piece = lax.ppermute(piece, "rep", [(r, (r + step) % reps) for r in range(reps)])
+        groups.append(piece)
+    new_half = jnp.concatenate(
+        [
+            sum(
+                jnp.where((rep - step) % reps == owner, piece, jnp.zeros_like(piece))
+                for step, piece in enumerate(groups)
+            )
+            for owner in range(reps)
+        ],
+        axis=0,
+    )
     summed = jnp.sum(new_state, axis=0)
     column_pool = (
         jnp.arange(column_count)[:, None] // 4 == jnp.arange(column_count // 4)[None, :]
@@ -173,7 +205,8 @@
     ) / 16.0
     ordered = jnp.take(pooled, coarse_perm[0], axis=0)
     part = jnp.einsum("oc,kcij->koij", u_pool, ordered, precision=lax.Precision.HIGHEST)
-    pre = exchange_sum(part, coarse_state.shape[0])
+    new_half, chip_part = lax.optimization_barrier((new_half, rep_sum(part)))
+    pre = exchange_sum(chip_part, coarse_state.shape[0])
     pre = pre + jnp.einsum("oc,kcij->koij", u_state, coarse_state, precision=lax.Precision.HIGHEST)
     pre = pre + b_coarse[None, :, None, None]
     coarse_next = coarse_state + jnp.tanh(pre)

time: 35.9 us -> 28.8 us (0.80)
  other arithmetic: 9.01 us -> 3.32 us
  waiting for transfers between devices: 1.44 us -> 5.83 us
  local copies, waits for them, and re-layouts: 8.68 us -> 5.95 us
  matrix products: 6.55 us -> 3.99 us
  starting transfers between devices: 8.87 us -> 8.43 us
    ppermute x1, waiting for transfers between devices: 0.01 us -> 2.86 us  [padded(): lax.ppermute(lax.slice_in_dim(block, 0, width, axis=dim), axis, backward)]
    concatenate x2, other arithmetic: 4.6 us -> 1.93 us  [apply_filter(): jnp.concatenate([padded_input[:, :, :, first_row_index + row_offset * dil...]
    dot_general x6, matrix products: 5.67 us -> 3.1 us  [apply_filter(): jnp.einsum('oi,bsirw->bsorw', weight, window_slice, preferred_element_typ...]
    slice x2, local copies, waits for them, and re-layouts: 2.57 us -> 1.05 us  [apply_filter(): padded_input[:, :, :, first_row_index + row_offset * dilation_rate:first_...]
    unnamed x29 -> x35, local copies, waits for them, and re-layouts: 4.08 us -> 2.94 us
    ppermute x0 -> x2, waiting for transfers between devices: none -> 0.98 us  [the longest x1 0.98 us: rep_sum(): lax.ppermute(part, 'rep', [(r, (r + step) % reps) for r in range(reps)])]
    and x1, other arithmetic: 0.77 us -> 0.02 us  [shards(): jnp.take(joined[:, :, :, row_count - 3:, :], jnp.clip(ups - base, 0, slot...]
    and x1, other arithmetic: 0.74 us -> 0.01 us  [shards(): last_sel = alive & jnp.logical_not(down_here)]
  transfers between devices with their start and end apart: 3 -> 5, of which waited for: 1 -> 3; matrix products, arithmetic and copies ran while one was open for 7% -> 11% of each run, Pallas kernels for 0% -> 0%
where the time goes in v17:
time: 28.8 us; the launch traced here: 28.7 us
  starting transfers between devices  8.43 us (29%)
  local copies, waits for them, and re-layouts  5.95 us (21%)
  waiting for transfers between devices  5.83 us (20%)
  matrix products  3.99 us (14%)
  other arithmetic  3.32 us (12%)
  between operations  1.14 us (4%)
    ppermute x1, starting transfers between devices, padded(): lax.ppermute(lax.slice_in_dim(block, block.shape[dim] - width, None, axis...  4.96 us
    dot_general x6, matrix products, apply_filter(): jnp.einsum('oi,bsirw->bsorw', weight, window_slice, preferred_element_typ...  3.1 us
    unnamed x35, local copies, waits for them, and re-layouts  2.94 us
    ppermute x1, waiting for transfers between devices, padded(): lax.ppermute(lax.slice_in_dim(block, 0, width, axis=dim), axis, backward)  2.86 us
    ppermute x1, waiting for transfers between devices, exchange_sum(): chunk = lax.ppermute(chunk, 'band', perm)  1.98 us
    concatenate x2, other arithmetic, apply_filter(): jnp.concatenate([padded_input[:, :, :, first_row_index + row_offset * dil...  1.93 us
    ppermute x1, starting transfers between devices, exchange_sum(): chunk = lax.ppermute(chunk, 'band', perm)  1.56 us
    ppermute x1, starting transfers between devices, padded(): lax.ppermute(lax.slice_in_dim(block, 0, width, axis=dim), axis, backward)  1.29 us
  transfers between devices with their start and end apart: 5, of which 3 were waited for; matrix products, arithmetic and copies ran while one was open for 11% of the time, Pallas kernels for 0%

profile of v17, /device:TPU:0, one launch (start us, length us, event | category | flops | bytes accessed | tf_op | source)
XLA Modules:
  0.0 28.7 jit_solution(2245198031415952167)
XLA Ops:
  0.6 0.0 copy-start
  0.6 0.0 copy-start.9
  0.7 0.0 copy-start.8
  0.7 0.0 copy-start.11
  0.7 1.1 %copy-done = f32[2,4,16,16,128]{4,3,2,1,0:T(8,128)S(1)} copy-done((f32[2,4,16,16,128]{4,3,2,1,0:T(8,128)S(1)}, f32[2,4,16,16,128]{4,3,2,1,0:T(8,128)}, u32[]{:S(2)}) %copy-start) | copy-done | bytes 1048600
  1.9 0.2 copy.53
  2.1 0.0 copy-done.11
  2.2 0.1 select_reduce_fusion.1
  2.3 5.0 %collective-permute-start = (bf16[1,18,3,128]{3,1,2,0:T(8,128)(2,1)S(1)}, bf16[1,18,3,128]{3,1,2,0:T(8,128)(2,1)S(1)}, u32[]{:S(2)}, u32[]{:S(2)}) collective-permute-start(bf16[1,18,3,128]{3,1,2,0:T(8,128)(2,1)S(1)} %bitcast.187), channel_id=1, source_target_pairs={{0,4},{4,8},{8,12},{1,5},{5,9},{9,13},{2,6},{6,10},{10,14},{3,7},{... | collective-permute-start | bytes 41480 | tf_op jit(solution)/shard_map/ppermute | solution.py:12
  7.3 1.3 %collective-permute-start.1 = (bf16[1,18,3,128]{3,1,2,0:T(8,128)(2,1)S(1)}, bf16[1,18,3,128]{3,1,2,0:T(8,128)(2,1)S(1)}, u32[]{:S(2)}, u32[]{:S(2)}) collective-permute-start(bf16[1,18,3,128]{3,1,2,0:T(8,128)(2,1)S(1)} %bitcast.186), channel_id=1, source_target_pairs={{4,0},{8,4},{12,8},{5,1},{9,5},{13,9},{6,2},{10,6},{14,10},{7,3},{... | collective-permute-start | bytes 41480 | tf_op jit(solution)/shard_map/ppermute | solution.py:15
  8.7 0.0 copy-done.4
  8.8 0.0 copy-done.14
  8.8 0.0 copy-done.13
  8.8 0.1 pad_maximum_fusion.6
  8.9 0.6 %gather_fusion.1 = bf16[4,18,3,128]{3,1,2,0:T(8,128)(2,1)S(1)} fusion(bf16[4,18,3,128]{3,1,2,0:T(8,128)(2,1)S(1)} %bitcast.183, s32[1024]{0:T(1024)S(1)} %pad_clamp_fusion.2), kind=kCustom, calls=%fused_computation.clone | custom fusion | bytes 110608 | tf_op jit(solution)/shard_map/jit(_take)/gather | solution.py:141
  9.4 0.6 %gather_fusion.2 = bf16[4,18,3,128]{3,1,2,0:T(8,128)(2,1)S(1)} fusion(bf16[4,18,3,128]{3,1,2,0:T(8,128)(2,1)S(1)} %bitcast.182, s32[1024]{0:T(1024)S(1)} %pad_clamp_fusion.1), kind=kCustom, calls=%fused_computation.1.clone | custom fusion | bytes 110608 | tf_op jit(solution)/shard_map/jit(_take)/gather | solution.py:144
  10.0 0.0 collective-permute-done
  10.0 0.1 fusion.21
  10.1 2.9 %collective-permute-done.1 = bf16[1,18,3,128]{3,1,2,0:T(8,128)(2,1)S(1)} collective-permute-done((bf16[1,18,3,128]{3,1,2,0:T(8,128)(2,1)S(1)}, bf16[1,18,3,128]{3,1,2,0:T(8,128)(2,1)S(1)}, u32[]{:S(2)}, u32[]{:S(2)}) %collective-permute-start.1) | collective-permute-done | bytes 13856 | tf_op jit(solution)/shard_map/ppermute | solution.py:15
  13.0 0.1 fusion.20
  13.1 0.2 pad_maximum_fusion.2
  13.2 0.9 %pad_slice_fusion.3 = (bf16[1,4,18,20,132]{4,2,3,1,0:T(8,128)(2,1)S(1)}, bf16[1,4,18,20,132]{4,2,3,1,0:T(8,128)(2,1)S(1)}, bf16[1,4,18,20,132]{4,2,3,1,0:T(8,128)(2,1)S(1)}) fusion(bf16[1,4,18,22,128]{4,2,3,1,0:T(8,128)(2,1)S(1)} %pad_maximum_fusion.2), kind=kLoop, calls=%fused_computation.10 | loop fusion | bytes 1545984 | tf_op jit(solution)/shard_map/slice | solution.py:26
  14.1 0.2 pad_slice_fusion
  14.3 1.1 %pad_maximum_fusion = bf16[1,4,54,20,132]{4,2,3,1,0:T(8,128)(2,1)S(1)} fusion(bf16[1,4,18,20,132]{4,2,3,1,0:T(8,128)(2,1)S(1)} %get-tuple-element.32, bf16[1,4,18,20,132]{4,2,3,1,0:T(8,128)(2,1)S(1)} %get-tuple-element.31, bf16[1,4,18,20,132]{4,2,3,1,0:T(8,128)(2,1)S(1)} %get-tuple-element.30), kind=kLoop, calls=%fused_computation.3 | loop fusion | flops 3421440 | bytes 2280960 | tf_op jit(solution)/shard_map/concatenate | solution.py:24
  15.4 0.5 %fusion.15 = f32[4,20,128,32]{2,3,1,0:T(8,128)S(1)} fusion(bf16[1,4,54,20,132]{4,2,3,1,0:T(8,128)(2,1)S(1)} %pad_maximum_fusion, bf16[32,18]{1,0:T(8,128)(2,1)S(1)} %get-tuple-element.41, bf16[32,18]{1,0:T(8,128)(2,1)S(1)} %get-tuple-element.42, bf16[32,18]{1,0:T(8,128)(2,1)S(1)} %get-tuple-element.43), kind=kOutput, calls=%fused_computation.33 | convolution fusion | flops 35399808 | bytes 2482176 | tf_op jit(solution)/shard_map/oi,bsirw->bsorw/dot_general | solution.py:50
  15.9 0.6 %convolution_add_fusion.1 = f32[4,20,128,32]{2,3,1,0:T(8,128)S(1)} fusion(f32[4,20,128,32]{2,3,1,0:T(8,128)S(1)} %fusion.15, bf16[1,4,54,20,132]{4,2,3,1,0:T(8,128)(2,1)S(1)} %pad_maximum_fusion, bf16[32,18]{1,0:T(8,128)(2,1)S(1)} %get-tuple-element.38, bf16[32,18]{1,0:T(8,128)(2,1)S(1)} %get-tuple-element.39, bf16[32,18]{1,0:T(8,128)(2,1)S(1)} %get-tuple-element.40), kind=kOutput, calls=%fused_computation.13 | convolution fusion | flops 35727488 | bytes 3792896 | tf_op jit(solution)/shard_map/oi,bsirw->bsorw/dot_general | solution.py:50
  16.5 0.7 %fusion.7 = f32[1,4,32,20,128]{4,2,3,1,0:T(8,128)S(1)} fusion(f32[4,20,128,32]{2,3,1,0:T(8,128)S(1)} %convolution_add_fusion.1, bf16[1,4,54,20,132]{4,2,3,1,0:T(8,128)(2,1)S(1)} %pad_maximum_fusion, f32[32]{0:T(128)S(1)} %pad_maximum_fusion.6, bf16[32,18]{1,0:T(8,128)(2,1)S(1)} %get-tuple-element.36, bf16[32,18]{1,0:T(8,128)(2,1)S(1)} %get-tuple-element.37, ...), kind=kOutput, calls=%fused_computation.19 | convolution fusion | flops 37038208 | bytes 3793408 | tf_op jit(solution)/shard_map/oi,bsirw->bsorw/dot_general | solution.py:50
  17.2 0.1 fusion.18
  17.3 0.6 %fusion.16 = bf16[1,4,18,20,132]{4,2,3,1,0:T(8,128)(2,1)S(1)} fusion(bf16[1,4,16,20,128]{4,2,3,1,0:T(8,128)(2,1)S(1)} %fusion.18, bf16[1,4,2,20,132]{4,2,3,1,0:T(2,128)(2,1)S(1)} %pad_slice_fusion), kind=kLoop, calls=%fused_computation.36 | loop fusion | flops 1140480 | bytes 750080 | tf_op jit(solution)/shard_map/concatenate | solution.py:174
  17.9 0.2 fusion.65
  18.1 0.8 %pad_maximum_fusion.1 = bf16[1,4,54,16,132]{4,2,3,1,0:T(8,128)(2,1)S(1)} fusion(bf16[1,4,18,16,132]{4,2,3,1,0:T(8,128)(2,1)S(1)} %get-tuple-element.26, bf16[1,4,18,16,132]{4,2,3,1,0:T(8,128)(2,1)S(1)} %get-tuple-element.27, bf16[1,4,18,16,132]{4,2,3,1,0:T(8,128)(2,1)S(1)} %get-tuple-element.25), kind=kLoop, calls=%fused_computation.6 | loop fusion | flops 2737152 | bytes 1824768 | tf_op jit(solution)/shard_map/concatenate | solution.py:24
  18.9 0.0 copy-start.12
  18.9 0.3 %fusion.17 = f32[4,16,128,16]{2,3,1,0:T(8,128)S(1)} fusion(bf16[1,4,54,16,132]{4,2,3,1,0:T(8,128)(2,1)S(1)} %pad_maximum_fusion.1, bf16[16,18]{1,0:T(8,128)(2,1)S(1)} %get-tuple-element.48, bf16[16,18]{1,0:T(8,128)(2,1)S(1)} %get-tuple-element.49, bf16[16,18]{1,0:T(8,128)(2,1)S(1)} %get-tuple-element.50), kind=kOutput, calls=%fused_computation.40 | convolution fusion | flops 14160960 | bytes 1454080 | tf_op jit(solution)/shard_map/oi,bsirw->bsorw/dot_general | solution.py:50
  19.2 0.5 %convolution_add_fusion.3 = f32[4,16,128,16]{2,3,1,0:T(8,128)S(1)} fusion(f32[4,16,128,16]{2,3,1,0:T(8,128)S(1)} %fusion.17, bf16[1,4,54,16,132]{4,2,3,1,0:T(8,128)(2,1)S(1)} %pad_maximum_fusion.1, bf16[16,18]{1,0:T(8,128)(2,1)S(1)} %get-tuple-element.45, bf16[16,18]{1,0:T(8,128)(2,1)S(1)} %get-tuple-element.46, bf16[16,18]{1,0:T(8,128)(2,1)S(1)} %get-tuple-element.47), kind=kOutput, calls=%fused_computation.22 | convolution fusion | flops 14292032 | bytes 1978368 | tf_op jit(solution)/shard_map/oi,bsirw->bsorw/dot_general | solution.py:50
  19.7 0.5 %fusion.14 = f32[1,4,16,16,128]{4,2,3,1,0:T(8,128)S(1)} fusion(f32[4,16,128,16]{2,3,1,0:T(8,128)S(1)} %convolution_add_fusion.3, bf16[1,4,54,16,132]{4,2,3,1,0:T(8,128)(2,1)S(1)} %pad_maximum_fusion.1, f32[1,4,32,20,128]{4,2,3,1,0:T(8,128)S(1)} %fusion.7, f32[1,4,16,16,128]{4,3,2,1,0:T(8,128)S(1)} %constant_dynamic-slice_fusion.2, ...), kind=kOutput, calls=%fused_computation.28 | convolution fusion | flops 15078464 | bytes 3027968 | tf_op jit(solution)/shard_map/oi,bsirw->bsorw/dot_general | solution.py:50
  20.2 0.4 %convolution_reduce_fusion = f32[4,16,4,32]{3,1,2,0:T(8,128)S(1)} fusion(f32[4,16,4,4,128]{4,1,3,2,0:T(8,128)S(1)} %bitcast.181, s32[128]{0:T(128)S(1)} %and_select_fusion), kind=kOutput, calls=%fused_computation.29 | convolution fusion | flops 50360320 | bytes 557568 | tf_op jit(solution)/shard_map/schw,wj->schj/dot_general | solution.py:200
  20.7 0.1 collective-permute-start.2
  20.7 0.6 %gather_fusion = f32[4,16,4,32]{3,1,2,0:T(8,128)S(1)} fusion(f32[4,16,4,32]{3,1,2,0:T(8,128)S(1)} %broadcast_multiply_fusion, s32[1024]{0:T(1024)S(1)} %pad_clamp_fusion), kind=kCustom, calls=%fused_computation.2 | custom fusion | bytes 65552 | tf_op jit(solution)/shard_map/jit(_take)/gather | solution.py:206
  21.3 0.3 %convolution_bitcast_fusion = f32[4,16,4,32]{3,1,2,0:T(8,128)S(1)} fusion(f32[4,16,4,32]{3,1,2,0:T(8,128)S(1)} %gather_fusion, pred[4]{0:T(512)(128)(4,1)S(1)} %get-tuple-element.60, f32[16,16]{1,0:T(8,128)S(1)} %copy-done.6), kind=kOutput, calls=%fused_computation.34 | convolution fusion | flops 1581056 | bytes 66564 | tf_op jit(solution)/shard_map/oc,kcij->koij/dot_general | solution.py:207
  21.6 0.6 %collective-permute-start.3 = (f32[4,16,4,32]{3,1,2,0:T(8,128)S(1)}, f32[4,16,4,32]{3,1,2,0:T(8,128)S(1)}, u32[]{:S(2)}, u32[]{:S(2)}) collective-permute-start(f32[4,16,4,32]{3,1,2,0:T(8,128)S(1)} %convolution_bitcast_fusion), channel_id=1, source_target_pairs={{0,1},{1,0},{2,3},{3,2},{4,5},{5,4},{6,7},{7,6},{8,9},{9,8},{10,11... | collective-permute-start | bytes 98312 | tf_op jit(solution)/shard_map/ppermute | solution.py:70
  22.2 1.0 %collective-permute-done.3 = f32[4,16,4,32]{3,1,2,0:T(8,128)S(1)} collective-permute-done((f32[4,16,4,32]{3,1,2,0:T(8,128)S(1)}, f32[4,16,4,32]{3,1,2,0:T(8,128)S(1)}, u32[]{:S(2)}, u32[]{:S(2)}) %collective-permute-start.3) | collective-permute-done | bytes 32800 | tf_op jit(solution)/shard_map/ppermute | solution.py:70
  23.2 0.0 collective-permute-done.2
  23.2 0.1 select_add_fusion.1
  23.3 1.6 %collective-permute-start.4 = (f32[2,16,4,32]{3,1,2,0:T(8,128)S(1)}, f32[2,16,4,32]{3,1,2,0:T(8,128)S(1)}, u32[]{:S(2)}, u32[]{:S(2)}) collective-permute-start(f32[2,16,4,32]{3,1,2,0:T(8,128)S(1)} %constant_dynamic-slice_fusion), channel_id=1, source_target_pairs={{0,2},{2,0},{1,3},{3,1},{4,6},{6,4},{5,7},{7,5},{8,10},{10,8},{9,1... | collective-permute-start | bytes 49160 | tf_op jit(solution)/shard_map/ppermute | solution.py:83
  24.9 0.9 %copy.33 = f32[2,4,8,16,128]{4,3,2,1,0:T(8,128)} copy(f32[2,4,8,16,128]{4,2,3,1,0:T(8,128)S(1)} %pad_maximum_fusion.3) | data formatting | bytes 1048576
  25.8 2.0 %collective-permute-done.4 = f32[2,16,4,32]{3,1,2,0:T(8,128)S(1)} collective-permute-done((f32[2,16,4,32]{3,1,2,0:T(8,128)S(1)}, f32[2,16,4,32]{3,1,2,0:T(8,128)S(1)}, u32[]{:S(2)}, u32[]{:S(2)}) %collective-permute-start.4) | collective-permute-done | bytes 16416 | tf_op jit(solution)/shard_map/ppermute | solution.py:83
  27.8 0.2 tanh_add_fusion
  28.0 0.7 %copy.34 = f32[2,16,4,32]{3,2,1,0:T(4,128)} copy(f32[2,16,4,32]{3,1,2,0:T(8,128)S(1)} %tanh_add_fusion) | data formatting | bytes 32768
  (40 shorter events, 0.3 us)
Async XLA Ops:
  0.6 1.2 %copy-start = (f32[2,4,16,16,128]{4,3,2,1,0:T(8,128)S(1)}, f32[2,4,16,16,128]{4,3,2,1,0:T(8,128)}, u32[]{:S(2)}) copy-start(f32[2,4,16,16,128]{4,3,2,1,0:T(8,128)} %param.18) | copy-start | bytes 3145732
  0.6 1.4 %copy-start.9 = (s32[4]{0:T(128)S(1)}, s32[4]{0:T(128)}, u32[]{:S(2)}) copy-start(s32[4]{0:T(128)} %param.19) | copy-start | bytes 52
  0.7 1.4 %copy-start.8 = (s32[4,2]{0,1:T(2,128)S(1)}, s32[4,2]{0,1:T(2,128)}, u32[]{:S(2)}) copy-start(s32[4,2]{0,1:T(2,128)} %param.20) | copy-start | bytes 100
  0.7 1.5 %copy-start.11 = (s32[1,4]{1,0:T(1,128)S(1)}, s32[1,4]{1,0:T(1,128)}, u32[]{:S(2)}) copy-start(s32[1,4]{1,0:T(1,128)} %param.21) | copy-start | bytes 52
  0.7 1.5 %copy-start.5 = (bf16[2,4,2,16,128]{4,3,2,1,0:T(8,128)(2,1)S(1)}, bf16[2,4,2,16,128]{4,3,2,1,0:T(8,128)(2,1)}, u32[]{:S(2)}) copy-start(bf16[2,4,2,16,128]{4,3,2,1,0:T(8,128)(2,1)} %param.17) | copy-start | bytes 196612
  0.7 8.0 %copy-start.2 = (bf16[9,16,18]{2,1,0:T(8,128)(2,1)S(1)}, bf16[9,16,18]{2,1,0:T(8,128)(2,1)}, u32[]{:S(2)}) copy-start(bf16[9,16,18]{2,1,0:T(8,128)(2,1)} %param.23) | copy-start | bytes 15556
  0.7 8.0 %copy-start.3 = (bf16[9,16,18]{2,1,0:T(8,128)(2,1)S(1)}, bf16[9,16,18]{2,1,0:T(8,128)(2,1)}, u32[]{:S(2)}) copy-start(bf16[9,16,18]{2,1,0:T(8,128)(2,1)} %param.25) | copy-start | bytes 15556
  0.7 8.0 %copy-start.4 = (bf16[9,16,18]{2,1,0:T(8,128)(2,1)S(1)}, bf16[9,16,18]{2,1,0:T(8,128)(2,1)}, u32[]{:S(2)}) copy-start(bf16[9,16,18]{2,1,0:T(8,128)(2,1)} %param.27) | copy-start | bytes 15556
  0.7 8.0 %copy-start.14 = (f32[16]{0:T(128)S(1)}, f32[16]{0:T(128)}, u32[]{:S(2)}) copy-start(f32[16]{0:T(128)} %param.24) | copy-start | bytes 196
  0.7 8.0 %copy-start.13 = (f32[16]{0:T(128)S(1)}, f32[16]{0:T(128)}, u32[]{:S(2)}) copy-start(f32[16]{0:T(128)} %param.26) | copy-start | bytes 196
  2.3 7.7 %collective-permute-start = (bf16[1,18,3,128]{3,1,2,0:T(8,128)(2,1)S(1)}, bf16[1,18,3,128]{3,1,2,0:T(8,128)(2,1)S(1)}, u32[]{:S(2)}, u32[]{:S(2)}) collective-permute-start(bf16[1,18,3,128]{3,1,2,0:T(8,128)(2,1)S(1)} %bitcast.187), channel_id=1, source_target_pairs={{0,4},{4,8},{8,12},{1,5},{5,9},{9,13},{2,6},{6,10},{10,14},{3,7},{... | collective-permute-start | bytes 41480 | tf_op jit(solution)/shard_map/ppermute | solution.py:12
  7.3 5.7 %collective-permute-start.1 = (bf16[1,18,3,128]{3,1,2,0:T(8,128)(2,1)S(1)}, bf16[1,18,3,128]{3,1,2,0:T(8,128)(2,1)S(1)}, u32[]{:S(2)}, u32[]{:S(2)}) collective-permute-start(bf16[1,18,3,128]{3,1,2,0:T(8,128)(2,1)S(1)} %bitcast.186), channel_id=1, source_target_pairs={{4,0},{8,4},{12,8},{5,1},{9,5},{13,9},{6,2},{10,6},{14,10},{7,3},{... | collective-permute-start | bytes 41480 | tf_op jit(solution)/shard_map/ppermute | solution.py:15
  18.9 0.8 %copy-start.12 = (f32[16]{0:T(128)S(1)}, f32[16]{0:T(128)}, u32[]{:S(2)}) copy-start(f32[16]{0:T(128)} %param.28) | copy-start | bytes 196
  19.7 1.6 %copy-start.6 = (f32[16,16]{1,0:T(8,128)S(1)}, f32[16,16]{1,0:T(8,128)}, u32[]{:S(2)}) copy-start(f32[16,16]{1,0:T(8,128)} %param.29) | copy-start | bytes 3076
  20.7 2.5 %collective-permute-start.2 = (f32[1,4,8,16,128]{4,2,3,1,0:T(8,128)S(1)}, f32[1,4,8,16,128]{4,2,3,1,0:T(8,128)S(1)}, u32[]{:S(2)}, u32[]{:S(2)}) collective-permute-start(f32[1,4,8,16,128]{4,2,3,1,0:T(8,128)S(1)} %constant_dynamic-slice_fusion.1), channel_id=1, source_target_pairs={{0,1},{1,0},{2,3},{3,2},{4,5},{5,4},{6,7},{7,6},{8,9},{9,8},{10,11... | collective-permute-start | bytes 786440 | tf_op jit(solution)/shard_map/ppermute | solution.py:184
  21.6 1.5 %collective-permute-start.3 = (f32[4,16,4,32]{3,1,2,0:T(8,128)S(1)}, f32[4,16,4,32]{3,1,2,0:T(8,128)S(1)}, u32[]{:S(2)}, u32[]{:S(2)}) collective-permute-start(f32[4,16,4,32]{3,1,2,0:T(8,128)S(1)} %convolution_bitcast_fusion), channel_id=1, source_target_pairs={{0,1},{1,0},{2,3},{3,2},{4,5},{5,4},{6,7},{7,6},{8,9},{9,8},{10,11... | collective-permute-start | bytes 98312 | tf_op jit(solution)/shard_map/ppermute | solution.py:70
  22.2 5.6 %copy-start.1 = (f32[2,16,4,32]{3,2,1,0:T(4,128)S(1)}, f32[2,16,4,32]{3,2,1,0:T(4,128)}, u32[]{:S(2)}) copy-start(f32[2,16,4,32]{3,2,1,0:T(4,128)} %param.22) | copy-start | bytes 49156
  22.2 5.6 %copy-start.7 = (f32[16,16]{1,0:T(8,128)S(1)}, f32[16,16]{1,0:T(8,128)}, u32[]{:S(2)}) copy-start(f32[16,16]{1,0:T(8,128)} %param.30) | copy-start | bytes 3076
  22.2 5.6 %copy-start.10 = (f32[16]{0:T(128)S(1)}, f32[16]{0:T(128)}, u32[]{:S(2)}) copy-start(f32[16]{0:T(128)} %param.31) | copy-start | bytes 196
  23.3 4.4 %collective-permute-start.4 = (f32[2,16,4,32]{3,1,2,0:T(8,128)S(1)}, f32[2,16,4,32]{3,1,2,0:T(8,128)S(1)}, u32[]{:S(2)}, u32[]{:S(2)}) collective-permute-start(f32[2,16,4,32]{3,1,2,0:T(8,128)S(1)} %constant_dynamic-slice_fusion), channel_id=1, source_target_pairs={{0,2},{2,0},{1,3},{3,1},{4,6},{6,4},{5,7},{7,5},{8,10},{10,8},{9,1... | collective-permute-start | bytes 49160 | tf_op jit(solution)/shard_map/ppermute | solution.py:83

commit v18 on v17

--- a/solution.py
+++ b/solution.py
@@ -17,11 +17,8 @@
     return block
 
 
-def apply_filter(
-    padded_input, filter_weight, dilation_rate, first_row_index, row_count, column_count
-):
-    offsets = (-1, 0, 1)
-    stacked = jnp.concatenate(
+def row_stack(padded_input, dilation_rate, first_row_index, row_count):
+    return jnp.concatenate(
         [
             padded_input[
                 :,
@@ -33,10 +30,14 @@
                 + row_count,
                 :,
             ]
-            for row_offset in offsets
+            for row_offset in (-1, 0, 1)
         ],
         axis=2,
     )
+
+
+def apply_stacked(stacked, filter_weight, dilation_rate, column_count):
+    offsets = (-1, 0, 1)
     total = None
     for column_offset in offsets:
         weight = jnp.concatenate(
@@ -52,6 +53,13 @@
         )
         total = term if total is None else total + term
     return total
+
+
+def apply_filter(
+    padded_input, filter_weight, dilation_rate, first_row_index, row_count, column_count
+):
+    stacked = row_stack(padded_input, dilation_rate, first_row_index, row_count)
+    return apply_stacked(stacked, filter_weight, dilation_rate, column_count)
 
 
 def choose_rows(block, select):
@@ -155,15 +163,18 @@
     )
     full = jnp.concatenate([top, joined, bottom], axis=3)
     first = jnp.pad(full, ((0, 0), (0, 0), (0, 0), (0, 0), (2, 2)))
+    cols_pad = ((0, 0), (0, 0), (0, 0), (0, 0), (2, 2))
+    stacked = row_stack(
+        jnp.pad(joined, ((0, 0), (0, 0), (0, 0), (3, 3), (2, 2))), 1, 1, row_count + 4
+    )
+    edge_top = jnp.pad(jnp.concatenate([top, joined[:, :, :, :2]], axis=3), cols_pad)
+    edge_bottom = jnp.pad(
+        jnp.concatenate([joined[:, :, :, row_count - 2 :], bottom], axis=3), cols_pad
+    )
+    stacked = stacked.at[:, :, :, :3].set(row_stack(edge_top, 1, 1, 3))
+    stacked = stacked.at[:, :, :, row_count + 1 :].set(row_stack(edge_bottom, 1, 1, 3))
     gates = logistic(
-        apply_filter(
-            first,
-            jnp.concatenate([w_update, w_reset], axis=1),
-            1,
-            1,
-            row_count + 4,
-            column_count,
-        )
+        apply_stacked(stacked, jnp.concatenate([w_update, w_reset], axis=1), 1, column_count)
         + jnp.concatenate([b_update, b_reset])[:, None, None]
     )
     update = gates[:, :, :chans, 2 : row_count + 2]

time: 28.8 us -> 40.4 us (1.40)
  other arithmetic: 3.32 us -> 13.1 us
  local copies, waits for them, and re-layouts: 5.95 us -> 9.5 us
  waiting for transfers between devices: 5.83 us -> 2.97 us
  starting transfers between devices: 8.43 us -> 9 us
    ppermute x1, waiting for transfers between devices: 2.86 us -> 0.01 us  [padded(): lax.ppermute(lax.slice_in_dim(block, 0, width, axis=dim), axis, backward)]
    concatenate x2 -> x6, other arithmetic: 1.93 us -> 3.82 us  [the longest x2 1.94 us: row_stack(): jnp.concatenate([padded_input[:, :, :, first_row_index + row_offset * dil...]
    squeeze x2, local copies, waits for them, and re-layouts: 0.02 us -> 1.25 us  [apply_stacked(): filter_weight[(row_offset + 1) * 3 + (column_offset + 1)]]
    reduce_sum x1, other arithmetic: 0.1 us -> 1.3 us  [choose_rows(): return jnp.sum(masked, axis=1)]
    gather x2, other arithmetic: 0.01 us -> 1.19 us
    and x1 -> x2, other arithmetic: 0.02 us -> 1.18 us  [the longest x1 0.6 us: shards(): jnp.take(joined[:, :, :, :3, :], jnp.clip(downs - base, 0, slots - 1), ax...]
    gather x1, local copies, waits for them, and re-layouts: 0.57 us -> 1.57 us  [shards(): jnp.take(joined[:, :, :, :3, :], jnp.clip(downs - base, 0, slots - 1), ax...]
    concatenate x1, other arithmetic: 0.17 us -> 1.12 us  [shards(): full = jnp.concatenate([top, joined, bottom], axis=3)]
  transfers between devices with their start and end apart: 5 -> 5, of which waited for: 3 -> 2; matrix products, arithmetic and copies ran while one was open for 11% -> 33% of each run, Pallas kernels for 0% -> 0%
where the time goes in v18:
time: 40.4 us; the launch traced here: 39.9 us
  other arithmetic  13.1 us (32%)
  local copies, waits for them, and re-layouts  9.5 us (24%)
  starting transfers between devices  9 us (22%)
  matrix products  3.98 us (10%)
  waiting for transfers between devices  2.97 us (7%)
  between operations  1.31 us (3%)
    ppermute x1, starting transfers between devices, padded(): lax.ppermute(lax.slice_in_dim(block, block.shape[dim] - width, None, axis...  5.54 us
    unnamed x81, local copies, waits for them, and re-layouts  3.24 us
    dot_general x6, matrix products, apply_stacked(): jnp.einsum('oi,bsirw->bsorw', weight, window_slice, preferred_element_typ...  3.1 us
    ppermute x1, waiting for transfers between devices, exchange_sum(): chunk = lax.ppermute(chunk, 'band', perm)  1.98 us
    concatenate x2, other arithmetic, row_stack(): jnp.concatenate([padded_input[:, :, :, first_row_index + row_offset * dil...  1.94 us
    gather x1, local copies, waits for them, and re-layouts, shards(): jnp.take(joined[:, :, :, :3, :], jnp.clip(downs - base, 0, slots - 1), ax...  1.57 us
    ppermute x1, starting transfers between devices, exchange_sum(): chunk = lax.ppermute(chunk, 'band', perm)  1.56 us
    reduce_sum x1, other arithmetic, choose_rows(): return jnp.sum(masked, axis=1)  1.3 us
  transfers between devices with their start and end apart: 5, of which 2 were waited for; matrix products, arithmetic and copies ran while one was open for 33% of the time, Pallas kernels for 0%

profile of v18, /device:TPU:0, one launch (start us, length us, event | category | flops | bytes accessed | tf_op | source)
XLA Modules:
  0.0 39.9 jit_solution(2033501351269781909)
XLA Ops:
  0.7 0.8 %constant_dynamic-slice_fusion.3 = bf16[1,4,2,16,128]{4,3,2,1,0:T(8,128)(2,1)S(1)} fusion(bf16[2,4,2,16,128]{4,3,2,1,0:T(8,128)(2,1)} %param.21, s32[]{:T(128)S(6)} %select_n.152), kind=kLoop, calls=%fused_computation.147 | loop fusion | bytes 65540 | tf_op jit(solution)/shard_map/dynamic_slice | solution.py:116
  1.6 0.3 copy-done
  1.9 0.8 %copy-done.2 = f32[1,4,16,16,128]{4,3,2,1,0:T(8,128)} copy-done((f32[1,4,16,16,128]{4,3,2,1,0:T(8,128)}, f32[1,4,16,16,128]{4,3,2,1,0:T(8,128)S(1)}, u32[]{:S(2)}) %copy-start.2) | copy-done | bytes 524312
  2.7 0.2 copy.53
  2.9 0.6 %not_and_fusion.1 = (pred[4]{0:T(512)(128)(4,1)S(1)}, pred[4]{0:T(512)(128)(4,1)S(1)}, f32[4]{0:T(128)}) fusion(s32[4]{0:T(128)S(1)} %copy-done.33, s32[]{:T(128)S(6)} %add.174, s32[]{:T(128)S(6)} %mul.41, s32[4,2]{0,1:T(2,128)S(1)} %copy-done.26), kind=kLoop, calls=%fused_computation.157 | loop fusion | flops 28 | bytes 64 | tf_op jit(solution)/shard_map/and | solution.py:133
  3.5 0.6 %compare_and_fusion = (pred[4]{0:T(512)(128)(4,1)}, s32[4]{0:T(128)S(1)}, pred[4]{0:T(512)(128)(4,1)}, pred[4]{0:T(512)(128)(4,1)}, s32[4]{0:T(128)S(1)}, /*inde...) fusion(s32[]{:T(128)S(6)} %mul.41, s32[4,2]{0,1:T(2,128)S(1)} %copy-done.26, ...), kind=kLoop, calls=%fused_computation.150 | loop fusion | flops 124 | bytes 116 | tf_op jit(solution)/shard_map/jit(_take)/and | solution.py:152
  4.1 1.3 %select_reduce_fusion = (bf16[18,3,128]{2,0,1:T(8,128)(2,1)}, bf16[1,4,18,3,128]{4,2,3,1,0:T(8,128)(2,1)}, bf16[18,3,128]{2,0,1:T(8,128)(2,1)}, bf16[1,4,18,3,128]{4,2,3,1,0:T(8,128)(2,1)S(1)}) fusion(pred[4]{0:T(512)(128)(4,1)S(1)} %get-tuple-element.39, bf16[1,4,16,16,128]{4,2,3,1,0:T(8,128)(2,1)S(1)} %copy.53, bf16[1,4,2,16,128]{4,2,3,1,0:T(2,128)(2,1)S(1)} %copy.44, ...), kind=kLoop, calls=%fused_computation.73 | loop fusion | flops 317952 | bytes 433160 | tf_op jit(solution)/shard_map/reduce_sum | solution.py:67
  5.4 5.5 %collective-permute-start = (bf16[1,18,3,128]{3,1,2,0:T(8,128)(2,1)}, bf16[1,18,3,128]{3,1,2,0:T(8,128)(2,1)}, u32[]{:S(2)}, u32[]{:S(2)}) collective-permute-start(bf16[1,18,3,128]{3,1,2,0:T(8,128)(2,1)} %bitcast.6), channel_id=1, source_target_pairs={{0,4},{4,8},{8,12},{1,5},{5,9},{9,13},{2,6},{6,10},{10,14},{3,7},{... | collective-permute-start | bytes 41480 | tf_op jit(solution)/shard_map/ppermute | solution.py:12
  11.0 1.3 %collective-permute-start.1 = (bf16[1,18,3,128]{3,1,2,0:T(8,128)(2,1)}, bf16[1,18,3,128]{3,1,2,0:T(8,128)(2,1)}, u32[]{:S(2)}, u32[]{:S(2)}) collective-permute-start(bf16[1,18,3,128]{3,1,2,0:T(8,128)(2,1)} %bitcast.12), channel_id=1, source_target_pairs={{4,0},{8,4},{12,8},{5,1},{9,5},{13,9},{6,2},{10,6},{14,10},{7,3},{... | collective-permute-start | bytes 41480 | tf_op jit(solution)/shard_map/ppermute | solution.py:15
  12.3 0.1 pad_maximum_fusion.2
  12.4 0.7 %fusion.34 = (bf16[1,4,18,2,128]{4,2,3,1,0:T(8,128)(2,1)}, bf16[1,4,18,2,128]{4,2,3,1,0:T(8,128)(2,1)}) fusion(bf16[1,4,16,16,128]{4,2,3,1,0:T(8,128)(2,1)S(1)} %copy.53, bf16[1,4,2,16,128]{4,2,3,1,0:T(2,128)(2,1)S(1)} %copy.44), kind=kLoop, calls=%fused_computation.81 | loop fusion | flops 147456 | bytes 368640 | tf_op jit(solution)/shard_map/concatenate | solution.py:143
  13.1 0.6 %and_select_fusion = s32[128]{0:T(128)} fusion(), kind=kLoop, calls=%fused_computation.152 | loop fusion | flops 1024 | bytes 512 | tf_op jit(solution)/shard_map/jit(floor_divide)/jit(_where)/select_n | solution.py:209
  13.7 0.8 %pad_slice_fusion.2 = (bf16[1,4,18,20,132]{4,2,3,1,0:T(8,128)(2,1)S(1)}, bf16[1,4,18,20,132]{4,2,3,1,0:T(8,128)(2,1)S(1)}, bf16[1,4,18,20,132]{4,2,3,1,0:T(8,128)(2,1)S(1)}) fusion(bf16[1,4,18,16,128]{4,2,3,1,0:T(8,128)(2,1)S(1)} %pad_maximum_fusion.2), kind=kLoop, calls=%fused_computation.9 | loop fusion | bytes 1435392 | tf_op jit(solution)/shard_map/slice | solution.py:23
  14.5 0.6 %pad_clamp_fusion.2 = s32[1024]{0:T(1024)} fusion(s32[4]{0:T(128)S(1)} %get-tuple-element.87), kind=kLoop, calls=%fused_computation.113 | loop fusion | flops 1024 | bytes 4112 | tf_op gather
  15.1 0.6 %pad_clamp_fusion.1 = s32[1024]{0:T(1024)} fusion(s32[4]{0:T(128)S(1)} %get-tuple-element.44), kind=kLoop, calls=%fused_computation.112 | loop fusion | flops 1024 | bytes 4112 | tf_op gather
  15.7 0.6 %slice_bitcast_fusion.14 = (bf16[32,18]{1,0:T(8,128)(2,1)S(1)}, bf16[32,18]{1,0:T(8,128)(2,1)S(1)}, bf16[32,18]{1,0:T(8,128)(2,1)S(1)}, bf16[32,18]{1,0:T(8,128)...) fusion(bf16[9,32,18]{2,1,0:T(8,128)(2,1)S(1)} %constant_dynamic, ...), kind=kLoop, calls=%fused_computation.86 | loop fusion | bytes 20736 | tf_op jit(solution)/shard_map/squeeze | solution.py:44
  16.3 0.6 %slice_bitcast_fusion.23 = (bf16[16,18]{1,0:T(8,128)(2,1)}, bf16[16,18]{1,0:T(8,128)(2,1)}, bf16[16,18]{1,0:T(8,128)(2,1)}, bf16[16,18]{1,0:T(8,128)(2,1)}, bf16...) fusion(bf16[9,16,18]{2,1,0:T(8,128)(2,1)S(1)} %copy-done.8), kind=kLoop, calls=%fused_computation.133 | loop fusion | bytes 10368 | tf_op jit(solution)/shard_map/squeeze | solution.py:44
  16.9 0.6 %pad_clamp_fusion = s32[1024]{0:T(1024)} fusion(s32[4]{0:T(128)S(1)} %fusion.64), kind=kLoop, calls=%fused_computation.111 | loop fusion | flops 1024 | bytes 4112 | tf_op jit(solution)/shard_map/jit(_take)/gather | solution.py:217
  17.5 1.1 %pad_maximum_fusion = bf16[1,4,54,20,132]{4,2,3,1,0:T(8,128)(2,1)S(1)} fusion(bf16[1,4,18,20,132]{4,2,3,1,0:T(8,128)(2,1)S(1)} %get-tuple-element.56, bf16[1,4,18,20,132]{4,2,3,1,0:T(8,128)(2,1)S(1)} %get-tuple-element.55, bf16[1,4,18,20,132]{4,2,3,1,0:T(8,128)(2,1)S(1)} %get-tuple-element.54), kind=kLoop, calls=%fused_computation.3 | loop fusion | flops 3421440 | bytes 2280960 | tf_op jit(solution)/shard_map/concatenate | solution.py:21
  18.7 0.6 %pad_maximum_fusion.5 = f32[32]{0:T(128)} fusion(f32[16]{0:T(128)S(1)} %copy-done.36, f32[16]{0:T(128)S(1)} %copy-done.37), kind=kLoop, calls=%fused_computation.162 | loop fusion | flops 32 | bytes 256 | tf_op jit(solution)/shard_map/concatenate | solution.py:178
  19.3 0.7 %gather_fusion.1 = bf16[4,18,3,128]{3,1,2,0:T(8,128)(2,1)S(1)} fusion(bf16[4,18,3,128]{3,1,2,0:T(8,128)(2,1)S(1)} %bitcast.183, s32[1024]{0:T(1024)} %pad_clamp_fusion.2), kind=kCustom, calls=%fused_computation.clone | custom fusion | bytes 110608 | tf_op jit(solution)/shard_map/jit(_take)/gather | solution.py:149
  20.0 1.6 %gather_fusion.2 = bf16[4,18,3,128]{3,1,2,0:T(8,128)(2,1)S(1)} fusion(bf16[4,18,3,128]{3,1,2,0:T(8,128)(2,1)} %bitcast.182, s32[1024]{0:T(1024)} %pad_clamp_fusion.1), kind=kCustom, calls=%fused_computation.1.clone | custom fusion | bytes 110608 | tf_op jit(solution)/shard_map/jit(_take)/gather | solution.py:152
  21.6 0.8 %fusion.27 = bf16[1,4,18,3,128]{4,2,3,1,0:T(8,128)(2,1)S(1)} fusion(bf16[4,18,3,128]{3,1,2,0:T(8,128)(2,1)S(1)} %gather_fusion.1, pred[4]{0:T(512)(128)(4,1)} %get-tuple-element.86, pred[4]{0:T(512)(128)(4,1)} %get-tuple-element.85, pred[4]{0:T(512)(128)(4,1)} %copy-done.25, bf16[18,3,128]{2,0,1:T(8,128)(2,1)} %bitcast.7), kind=kLoop, calls=%fused_computation.72 | loop fusion | flops 82944 | bytes 124428 | tf_op jit(solution)/shard_map/jit(_where)/select_n | solution.py:154
  22.4 0.9 %fusion.22 = bf16[1,4,18,5,132]{4,2,3,1,0:T(8,128)(2,1)S(1)} fusion(bf16[1,4,18,2,128]{4,2,3,1,0:T(8,128)(2,1)} %get-tuple-element.58, bf16[1,4,18,3,128]{4,2,3,1,0:T(8,128)(2,1)S(1)} %fusion.27), kind=kLoop, calls=%fused_computation.65 | loop fusion | flops 427680 | bytes 187200 | tf_op jit(solution)/shard_map/concatenate | solution.py:170
  23.4 0.8 %fusion.26 = bf16[1,4,18,3,128]{4,2,3,1,0:T(8,128)(2,1)S(1)} fusion(bf16[4,18,3,128]{3,1,2,0:T(8,128)(2,1)S(1)} %gather_fusion.2, pred[4]{0:T(512)(128)(4,1)} %get-tuple-element.43, pred[4]{0:T(512)(128)(4,1)} %get-tuple-element.88, pred[4]{0:T(512)(128)(4,1)} %copy-done.28, bf16[18,3,128]{2,0,1:T(8,128)(2,1)} %bitcast.13), kind=kLoop, calls=%fused_computation.70 | loop fusion | flops 82944 | bytes 124428 | tf_op jit(solution)/shard_map/jit(_where)/select_n | solution.py:159
  24.2 1.1 %pad_maximum_fusion.3 = bf16[1,4,18,22,128]{4,2,3,1,0:T(8,128)(2,1)S(1)} fusion(bf16[1,4,18,3,128]{4,2,3,1,0:T(8,128)(2,1)S(1)} %fusion.26, bf16[1,4,16,16,128]{4,2,3,1,0:T(8,128)(2,1)} %copy-done.1, bf16[1,4,2,16,128]{4,2,3,1,0:T(2,128)(2,1)S(1)} %copy.44, bf16[1,4,18,3,128]{4,2,3,1,0:T(8,128)(2,1)S(1)} %fusion.27), kind=kLoop, calls=%fused_computation.50 | loop fusion | flops 1622016 | bytes 811008 | tf_op jit(solution)/shard_map/concatenate | solution.py:164
  25.4 0.1 select_maximum_fusion
  25.6 0.2 pad_slice_fusion.3
  26.1 0.5 %fusion.15 = f32[4,20,128,32]{2,3,1,0:T(8,128)S(1)} fusion(bf16[1,4,54,20,132]{4,2,3,1,0:T(8,128)(2,1)S(1)} %maximum_dynamic-update-slice_fusion.1, bf16[32,18]{1,0:T(8,128)(2,1)S(1)} %copy-done.11, bf16[32,18]{1,0:T(8,128)(2,1)S(1)} %copy-done.12, bf16[32,18]{1,0:T(8,128)(2,1)S(1)} %copy-done.13), kind=kOutput, calls=%fused_computation.32 | convolution fusion | flops 35399808 | bytes 2482176 | tf_op jit(solution)/shard_map/oi,bsirw->bsorw/dot_general | solution.py:51
  26.6 0.6 %convolution_add_fusion.1 = f32[4,20,128,32]{2,3,1,0:T(8,128)S(1)} fusion(f32[4,20,128,32]{2,3,1,0:T(8,128)S(1)} %fusion.15, bf16[1,4,54,20,132]{4,2,3,1,0:T(8,128)(2,1)S(1)} %maximum_dynamic-update-slice_fusion.1, bf16[32,18]{1,0:T(8,128)(2,1)S(1)} %get-tuple-element.70, bf16[32,18]{1,0:T(8,128)(2,1)S(1)} %copy-done.9, bf16[32,18]{1,0:T(8,128)(2,1)S(1)} %copy-done.10), kind=kOutput, calls=%fused_computation.12 | convolution fusion | flops 35727488 | bytes 3792896 | tf_op jit(solution)/shard_map/oi,bsirw->bsorw/dot_general | solution.py:51
  27.3 0.7 %fusion.7 = f32[1,4,32,20,128]{4,2,3,1,0:T(8,128)S(1)} fusion(f32[4,20,128,32]{2,3,1,0:T(8,128)S(1)} %convolution_add_fusion.1, bf16[1,4,54,20,132]{4,2,3,1,0:T(8,128)(2,1)S(1)} %maximum_dynamic-update-slice_fusion.1, f32[32]{0:T(128)S(1)} %copy-done.31, bf16[32,18]{1,0:T(8,128)(2,1)S(1)} %get-tuple-element.68, bf16[32,18]{1,0:T(8,128)(2,1)S(1)} %get-tuple-element.69, ...), kind=kOutput, calls=%fused_computation.18 | convolution fusion | flops 37038208 | bytes 3793408 | tf_op jit(solution)/shard_map/oi,bsirw->bsorw/dot_general | solution.py:51
  28.1 0.5 %fusion.16 = bf16[1,4,18,20,132]{4,2,3,1,0:T(8,128)(2,1)S(1)} fusion(bf16[1,4,16,20,128]{4,2,3,1,0:T(8,128)(2,1)S(1)} %fusion.18, bf16[1,4,2,20,132]{4,2,3,1,0:T(2,128)(2,1)S(1)} %pad_slice_fusion.3), kind=kLoop, calls=%fused_computation.36 | loop fusion | flops 1140480 | bytes 750080 | tf_op jit(solution)/shard_map/concatenate | solution.py:185
  28.6 0.2 fusion.75
  28.9 0.8 %pad_maximum_fusion.1 = bf16[1,4,54,16,132]{4,2,3,1,0:T(8,128)(2,1)S(1)} fusion(bf16[1,4,18,16,132]{4,2,3,1,0:T(8,128)(2,1)S(1)} %get-tuple-element.50, bf16[1,4,18,16,132]{4,2,3,1,0:T(8,128)(2,1)S(1)} %get-tuple-element.51, bf16[1,4,18,16,132]{4,2,3,1,0:T(8,128)(2,1)S(1)} %get-tuple-element.49), kind=kLoop, calls=%fused_computation.6 | loop fusion | flops 2737152 | bytes 1824768 | tf_op jit(solution)/shard_map/concatenate | solution.py:21
  29.8 0.3 fusion.17
  30.1 0.5 %convolution_add_fusion.3 = f32[4,16,128,16]{2,3,1,0:T(8,128)S(1)} fusion(f32[4,16,128,16]{2,3,1,0:T(8,128)S(1)} %fusion.17, bf16[1,4,54,16,132]{4,2,3,1,0:T(8,128)(2,1)S(1)} %pad_maximum_fusion.1, bf16[16,18]{1,0:T(8,128)(2,1)S(1)} %copy-done.17, bf16[16,18]{1,0:T(8,128)(2,1)S(1)} %copy-done.18, bf16[16,18]{1,0:T(8,128)(2,1)S(1)} %copy-done.19), kind=kOutput, calls=%fused_computation.21 | convolution fusion | flops 14292032 | bytes 1978368 | tf_op jit(solution)/shard_map/oi,bsirw->bsorw/dot_general | solution.py:51
  30.6 0.1 copy-done.3
  30.8 0.5 %fusion.14 = f32[1,4,16,16,128]{4,2,3,1,0:T(8,128)S(1)} fusion(f32[4,16,128,16]{2,3,1,0:T(8,128)S(1)} %convolution_add_fusion.3, bf16[1,4,54,16,132]{4,2,3,1,0:T(8,128)(2,1)S(1)} %pad_maximum_fusion.1, f32[1,4,32,20,128]{4,2,3,1,0:T(8,128)S(1)} %fusion.7, f32[1,4,16,16,128]{4,3,2,1,0:T(8,128)S(1)} %copy-done.3, f32[4]{0:T(128)S(1)} %copy-done.29, ...), kind=kOutput, calls=%fused_computation.27 | convolution fusion | flops 15078464 | bytes 3027968 | tf_op jit(solution)/shard_map/oi,bsirw->bsorw/dot_general | solution.py:51
  31.5 0.4 convolution_reduce_fusion
  31.9 0.7 %gather_fusion = f32[4,16,4,32]{3,1,2,0:T(8,128)S(1)} fusion(f32[4,16,4,32]{3,1,2,0:T(8,128)S(1)} %broadcast_multiply_fusion, s32[1024]{0:T(1024)} %pad_clamp_fusion), kind=kCustom, calls=%fused_computation.2 | custom fusion | bytes 65552 | tf_op jit(solution)/shard_map/jit(_take)/gather | solution.py:217
  32.6 0.3 convolution_bitcast_fusion
  32.9 0.6 %collective-permute-start.3 = (f32[4,16,4,32]{3,1,2,0:T(8,128)S(1)}, f32[4,16,4,32]{3,1,2,0:T(8,128)S(1)}, u32[]{:S(2)}, u32[]{:S(2)}) collective-permute-start(f32[4,16,4,32]{3,1,2,0:T(8,128)S(1)} %convolution_bitcast_fusion), channel_id=1, source_target_pairs={{0,1},{1,0},{2,3},{3,2},{4,5},{5,4},{6,7},{7,6},{8,9},{9,8},{10,11... | collective-permute-start | bytes 98312 | tf_op jit(solution)/shard_map/ppermute | solution.py:78
  33.4 1.0 %collective-permute-done.3 = f32[4,16,4,32]{3,1,2,0:T(8,128)S(1)} collective-permute-done((f32[4,16,4,32]{3,1,2,0:T(8,128)S(1)}, f32[4,16,4,32]{3,1,2,0:T(8,128)S(1)}, u32[]{:S(2)}, u32[]{:S(2)}) %collective-permute-start.3) | collective-permute-done | bytes 32800 | tf_op jit(solution)/shard_map/ppermute | solution.py:78
  34.6 1.6 %collective-permute-start.4 = (f32[2,16,4,32]{3,1,2,0:T(8,128)S(1)}, f32[2,16,4,32]{3,1,2,0:T(8,128)S(1)}, u32[]{:S(2)}, u32[]{:S(2)}) collective-permute-start(f32[2,16,4,32]{3,1,2,0:T(8,128)S(1)} %constant_dynamic-slice_fusion), channel_id=1, source_target_pairs={{0,2},{2,0},{1,3},{3,1},{4,6},{6,4},{5,7},{7,5},{8,10},{10,8},{9,1... | collective-permute-start | bytes 49160 | tf_op jit(solution)/shard_map/ppermute | solution.py:91
  36.1 0.9 %copy.33 = f32[2,4,8,16,128]{4,3,2,1,0:T(8,128)} copy(f32[2,4,8,16,128]{4,2,3,1,0:T(8,128)S(1)} %pad_maximum_fusion.4) | data formatting | bytes 1048576
  37.0 2.0 %collective-permute-done.4 = f32[2,16,4,32]{3,1,2,0:T(8,128)S(1)} collective-permute-done((f32[2,16,4,32]{3,1,2,0:T(8,128)S(1)}, f32[2,16,4,32]{3,1,2,0:T(8,128)S(1)}, u32[]{:S(2)}, u32[]{:S(2)}) %collective-permute-start.4) | collective-permute-done | bytes 16416 | tf_op jit(solution)/shard_map/ppermute | solution.py:91
  39.0 0.2 tanh_add_fusion
  39.2 0.7 %copy.34 = f32[2,16,4,32]{3,2,1,0:T(4,128)} copy(f32[2,16,4,32]{3,1,2,0:T(8,128)S(1)} %tanh_add_fusion) | data formatting | bytes 32768
  (94 shorter events, 1.0 us)
Async XLA Ops:
  0.6 1.2 %copy-start = (f32[2,4,16,16,128]{4,3,2,1,0:T(8,128)S(1)}, f32[2,4,16,16,128]{4,3,2,1,0:T(8,128)}, u32[]{:S(2)}) copy-start(f32[2,4,16,16,128]{4,3,2,1,0:T(8,128)} %param.22) | copy-start | bytes 3145732
  0.6 2.3 %copy-start.33 = (s32[4]{0:T(128)S(1)}, s32[4]{0:T(128)}, u32[]{:S(2)}) copy-start(s32[4]{0:T(128)} %param.23) | copy-start | bytes 52
  0.7 2.3 %copy-start.26 = (s32[4,2]{0,1:T(2,128)S(1)}, s32[4,2]{0,1:T(2,128)}, u32[]{:S(2)}) copy-start(s32[4,2]{0,1:T(2,128)} %param.24) | copy-start | bytes 100
  0.7 2.8 %copy-start.32 = (s32[1,4]{1,0:T(1,128)S(1)}, s32[1,4]{1,0:T(1,128)}, u32[]{:S(2)}) copy-start(s32[1,4]{1,0:T(1,128)} %param.25) | copy-start | bytes 52
  1.9 0.8 %copy-start.2 = (f32[1,4,16,16,128]{4,3,2,1,0:T(8,128)}, f32[1,4,16,16,128]{4,3,2,1,0:T(8,128)S(1)}, u32[]{:S(2)}) copy-start(f32[1,4,16,16,128]{4,3,2,1,0:T(8,128)S(1)} %constant_dynamic-slice_fusion.2) | copy-start | bytes 1572868
  2.9 11.6 %copy-start.1 = (bf16[1,4,16,16,128]{4,2,3,1,0:T(8,128)(2,1)}, bf16[1,4,16,16,128]{4,2,3,1,0:T(8,128)(2,1)S(1)}, u32[]{:S(2)}) copy-start(bf16[1,4,16,16,128]{4,2,3,1,0:T(8,128)(2,1)S(1)} %copy.53) | copy-start | bytes 786436
  3.5 7.5 %copy-start.25 = (pred[4]{0:T(512)(128)(4,1)}, pred[4]{0:T(512)(128)(4,1)S(1)}, u32[]{:S(2)}) copy-start(pred[4]{0:T(512)(128)(4,1)S(1)} %get-tuple-element.40) | copy-start | bytes 16
  4.1 6.9 %copy-start.28 = (pred[4]{0:T(512)(128)(4,1)}, pred[4]{0:T(512)(128)(4,1)S(1)}, u32[]{:S(2)}) copy-start(pred[4]{0:T(512)(128)(4,1)S(1)} %get-tuple-element.89) | copy-start | bytes 16
  5.4 16.1 %collective-permute-start = (bf16[1,18,3,128]{3,1,2,0:T(8,128)(2,1)}, bf16[1,18,3,128]{3,1,2,0:T(8,128)(2,1)}, u32[]{:S(2)}, u32[]{:S(2)}) collective-permute-start(bf16[1,18,3,128]{3,1,2,0:T(8,128)(2,1)} %bitcast.6), channel_id=1, source_target_pairs={{0,4},{4,8},{8,12},{1,5},{5,9},{9,13},{2,6},{6,10},{10,14},{3,7},{... | collective-permute-start | bytes 41480 | tf_op jit(solution)/shard_map/ppermute | solution.py:12
  11.0 12.4 %collective-permute-start.1 = (bf16[1,18,3,128]{3,1,2,0:T(8,128)(2,1)}, bf16[1,18,3,128]{3,1,2,0:T(8,128)(2,1)}, u32[]{:S(2)}, u32[]{:S(2)}) collective-permute-start(bf16[1,18,3,128]{3,1,2,0:T(8,128)(2,1)} %bitcast.12), channel_id=1, source_target_pairs={{4,0},{8,4},{12,8},{5,1},{9,5},{13,9},{6,2},{10,6},{14,10},{7,3},{... | collective-permute-start | bytes 41480 | tf_op jit(solution)/shard_map/ppermute | solution.py:15
  12.4 3.2 %copy-start.6 = (bf16[9,16,18]{2,1,0:T(8,128)(2,1)S(1)}, bf16[9,16,18]{2,1,0:T(8,128)(2,1)}, u32[]{:S(2)}) copy-start(bf16[9,16,18]{2,1,0:T(8,128)(2,1)} %param.27) | copy-start | bytes 15556
  12.4 3.2 %copy-start.7 = (bf16[9,16,18]{2,1,0:T(8,128)(2,1)S(1)}, bf16[9,16,18]{2,1,0:T(8,128)(2,1)}, u32[]{:S(2)}) copy-start(bf16[9,16,18]{2,1,0:T(8,128)(2,1)} %param.29) | copy-start | bytes 15556
  13.1 3.2 %copy-start.8 = (bf16[9,16,18]{2,1,0:T(8,128)(2,1)S(1)}, bf16[9,16,18]{2,1,0:T(8,128)(2,1)}, u32[]{:S(2)}) copy-start(bf16[9,16,18]{2,1,0:T(8,128)(2,1)} %param.31) | copy-start | bytes 15556
  17.5 1.1 %copy-start.36 = (f32[16]{0:T(128)S(1)}, f32[16]{0:T(128)}, u32[]{:S(2)}) copy-start(f32[16]{0:T(128)} %param.30) | copy-start | bytes 196
  17.5 1.1 %copy-start.37 = (f32[16]{0:T(128)S(1)}, f32[16]{0:T(128)}, u32[]{:S(2)}) copy-start(f32[16]{0:T(128)} %param.28) | copy-start | bytes 196
  21.5 3.8 %copy-start.4 = (bf16[1,4,18,2,128]{4,2,3,1,0:T(8,128)(2,1)S(1)}, bf16[1,4,18,2,128]{4,2,3,1,0:T(8,128)(2,1)}, u32[]{:S(2)}) copy-start(bf16[1,4,18,2,128]{4,2,3,1,0:T(8,128)(2,1)} %get-tuple-element.57) | copy-start | bytes 110596
  25.3 0.7 %copy-start.11 = (bf16[32,18]{1,0:T(8,128)(2,1)S(1)}, bf16[32,18]{1,0:T(8,128)(2,1)}, u32[]{:S(2)}) copy-start(bf16[32,18]{1,0:T(8,128)(2,1)} %get-tuple-element.73) | copy-start | bytes 3460
  25.3 0.7 %copy-start.12 = (bf16[32,18]{1,0:T(8,128)(2,1)S(1)}, bf16[32,18]{1,0:T(8,128)(2,1)}, u32[]{:S(2)}) copy-start(bf16[32,18]{1,0:T(8,128)(2,1)} %get-tuple-element.74) | copy-start | bytes 3460
  25.4 0.7 %copy-start.13 = (bf16[32,18]{1,0:T(8,128)(2,1)S(1)}, bf16[32,18]{1,0:T(8,128)(2,1)}, u32[]{:S(2)}) copy-start(bf16[32,18]{1,0:T(8,128)(2,1)} %get-tuple-element.75) | copy-start | bytes 3460
  25.9 0.7 %copy-start.9 = (bf16[32,18]{1,0:T(8,128)(2,1)S(1)}, bf16[32,18]{1,0:T(8,128)(2,1)}, u32[]{:S(2)}) copy-start(bf16[32,18]{1,0:T(8,128)(2,1)} %get-tuple-element.71) | copy-start | bytes 3460
  25.9 0.7 %copy-start.10 = (bf16[32,18]{1,0:T(8,128)(2,1)S(1)}, bf16[32,18]{1,0:T(8,128)(2,1)}, u32[]{:S(2)}) copy-start(bf16[32,18]{1,0:T(8,128)(2,1)} %get-tuple-element.72) | copy-start | bytes 3460
  26.6 0.6 %copy-start.31 = (f32[32]{0:T(128)S(1)}, f32[32]{0:T(128)}, u32[]{:S(2)}) copy-start(f32[32]{0:T(128)} %pad_maximum_fusion.5) | copy-start | bytes 388
  28.8 1.0 %copy-start.20 = (bf16[16,18]{1,0:T(8,128)(2,1)S(1)}, bf16[16,18]{1,0:T(8,128)(2,1)}, u32[]{:S(2)}) copy-start(bf16[16,18]{1,0:T(8,128)(2,1)} %get-tuple-element.80) | copy-start | bytes 1732
  28.8 1.0 %copy-start.21 = (bf16[16,18]{1,0:T(8,128)(2,1)S(1)}, bf16[16,18]{1,0:T(8,128)(2,1)}, u32[]{:S(2)}) copy-start(bf16[16,18]{1,0:T(8,128)(2,1)} %get-tuple-element.81) | copy-start | bytes 1732
  28.8 1.0 %copy-start.22 = (bf16[16,18]{1,0:T(8,128)(2,1)S(1)}, bf16[16,18]{1,0:T(8,128)(2,1)}, u32[]{:S(2)}) copy-start(bf16[16,18]{1,0:T(8,128)(2,1)} %get-tuple-element.82) | copy-start | bytes 1732
  28.8 1.3 %copy-start.17 = (bf16[16,18]{1,0:T(8,128)(2,1)S(1)}, bf16[16,18]{1,0:T(8,128)(2,1)}, u32[]{:S(2)}) copy-start(bf16[16,18]{1,0:T(8,128)(2,1)} %get-tuple-element.77) | copy-start | bytes 1732
  28.9 1.3 %copy-start.18 = (bf16[16,18]{1,0:T(8,128)(2,1)S(1)}, bf16[16,18]{1,0:T(8,128)(2,1)}, u32[]{:S(2)}) copy-start(bf16[16,18]{1,0:T(8,128)(2,1)} %get-tuple-element.78) | copy-start | bytes 1732
  28.9 1.3 %copy-start.19 = (bf16[16,18]{1,0:T(8,128)(2,1)S(1)}, bf16[16,18]{1,0:T(8,128)(2,1)}, u32[]{:S(2)}) copy-start(bf16[16,18]{1,0:T(8,128)(2,1)} %get-tuple-element.79) | copy-start | bytes 1732
  29.7 1.0 %copy-start.3 = (f32[1,4,16,16,128]{4,3,2,1,0:T(8,128)S(1)}, f32[1,4,16,16,128]{4,3,2,1,0:T(8,128)}, u32[]{:S(2)}) copy-start(f32[1,4,16,16,128]{4,3,2,1,0:T(8,128)} %copy-done.2) | copy-start | bytes 1572868
  29.7 1.0 %copy-start.14 = (bf16[16,18]{1,0:T(8,128)(2,1)S(1)}, bf16[16,18]{1,0:T(8,128)(2,1)}, u32[]{:S(2)}) copy-start(bf16[16,18]{1,0:T(8,128)(2,1)} %get-tuple-element.76) | copy-start | bytes 1732
  29.7 1.0 %copy-start.15 = (bf16[16,18]{1,0:T(8,128)(2,1)S(1)}, bf16[16,18]{1,0:T(8,128)(2,1)}, u32[]{:S(2)}) copy-start(bf16[16,18]{1,0:T(8,128)(2,1)} %get-tuple-element.83) | copy-start | bytes 1732
  29.8 1.0 %copy-start.16 = (bf16[16,18]{1,0:T(8,128)(2,1)S(1)}, bf16[16,18]{1,0:T(8,128)(2,1)}, u32[]{:S(2)}) copy-start(bf16[16,18]{1,0:T(8,128)(2,1)} %get-tuple-element.84) | copy-start | bytes 1732
  29.8 1.0 %copy-start.29 = (f32[4]{0:T(128)S(1)}, f32[4]{0:T(128)}, u32[]{:S(2)}) copy-start(f32[4]{0:T(128)} %get-tuple-element.90) | copy-start | bytes 52
  29.8 1.0 %copy-start.35 = (f32[16]{0:T(128)S(1)}, f32[16]{0:T(128)}, u32[]{:S(2)}) copy-start(f32[16]{0:T(128)} %param.32) | copy-start | bytes 196
  30.6 0.8 %copy-start.34 = (s32[128]{0:T(128)S(1)}, s32[128]{0:T(128)}, u32[]{:S(2)}) copy-start(s32[128]{0:T(128)} %and_select_fusion) | copy-start | bytes 1540
  30.8 1.8 %copy-start.23 = (f32[16,16]{1,0:T(8,128)S(1)}, f32[16,16]{1,0:T(8,128)}, u32[]{:S(2)}) copy-start(f32[16,16]{1,0:T(8,128)} %param.33) | copy-start | bytes 3076
  30.8 1.8 %copy-start.27 = (pred[4]{0:T(512)(128)(4,1)S(1)}, pred[4]{0:T(512)(128)(4,1)}, u32[]{:S(2)}) copy-start(pred[4]{0:T(512)(128)(4,1)} %get-tuple-element.91) | copy-start | bytes 16
  31.4 3.1 %collective-permute-start.2 = (f32[1,4,8,16,128]{4,2,3,1,0:T(8,128)S(1)}, f32[1,4,8,16,128]{4,2,3,1,0:T(8,128)S(1)}, u32[]{:S(2)}, u32[]{:S(2)}) collective-permute-start(f32[1,4,8,16,128]{4,2,3,1,0:T(8,128)S(1)} %constant_dynamic-slice_fusion.1), channel_id=1, source_target_pairs={{0,1},{1,0},{2,3},{3,2},{4,5},{5,4},{6,7},{7,6},{8,9},{9,8},{10,11... | collective-permute-start | bytes 786440 | tf_op jit(solution)/shard_map/ppermute | solution.py:195
  32.9 1.5 %collective-permute-start.3 = (f32[4,16,4,32]{3,1,2,0:T(8,128)S(1)}, f32[4,16,4,32]{3,1,2,0:T(8,128)S(1)}, u32[]{:S(2)}, u32[]{:S(2)}) collective-permute-start(f32[4,16,4,32]{3,1,2,0:T(8,128)S(1)} %convolution_bitcast_fusion), channel_id=1, source_target_pairs={{0,1},{1,0},{2,3},{3,2},{4,5},{5,4},{6,7},{7,6},{8,9},{9,8},{10,11... | collective-permute-start | bytes 98312 | tf_op jit(solution)/shard_map/ppermute | solution.py:78
  33.4 5.6 %copy-start.5 = (f32[2,16,4,32]{3,2,1,0:T(4,128)S(1)}, f32[2,16,4,32]{3,2,1,0:T(4,128)}, u32[]{:S(2)}) copy-start(f32[2,16,4,32]{3,2,1,0:T(4,128)} %param.26) | copy-start | bytes 49156
  33.4 5.6 %copy-start.24 = (f32[16,16]{1,0:T(8,128)S(1)}, f32[16,16]{1,0:T(8,128)}, u32[]{:S(2)}) copy-start(f32[16,16]{1,0:T(8,128)} %param.34) | copy-start | bytes 3076
  33.4 5.6 %copy-start.30 = (f32[16]{0:T(128)S(1)}, f32[16]{0:T(128)}, u32[]{:S(2)}) copy-start(f32[16]{0:T(128)} %param.35) | copy-start | bytes 196
  34.6 4.4 %collective-permute-start.4 = (f32[2,16,4,32]{3,1,2,0:T(8,128)S(1)}, f32[2,16,4,32]{3,1,2,0:T(8,128)S(1)}, u32[]{:S(2)}, u32[]{:S(2)}) collective-permute-start(f32[2,16,4,32]{3,1,2,0:T(8,128)S(1)} %constant_dynamic-slice_fusion), channel_id=1, source_target_pairs={{0,2},{2,0},{1,3},{3,1},{4,6},{6,4},{5,7},{7,5},{8,10},{10,8},{9,1... | collective-permute-start | bytes 49160 | tf_op jit(solution)/shard_map/ppermute | solution.py:91

commit v19 on v17

--- a/solution.py
+++ b/solution.py
@@ -203,10 +203,10 @@
     pooled = jnp.sum(
         cols.reshape(slots, chans, row_count // 4, 4, column_count // 4), axis=3
     ) / 16.0
-    ordered = jnp.take(pooled, coarse_perm[0], axis=0)
+    new_half, chip_pooled = lax.optimization_barrier((new_half, rep_sum(pooled)))
+    ordered = jnp.take(chip_pooled, coarse_perm[0], axis=0)
     part = jnp.einsum("oc,kcij->koij", u_pool, ordered, precision=lax.Precision.HIGHEST)
-    new_half, chip_part = lax.optimization_barrier((new_half, rep_sum(part)))
-    pre = exchange_sum(chip_part, coarse_state.shape[0])
+    pre = exchange_sum(part, coarse_state.shape[0])
     pre = pre + jnp.einsum("oc,kcij->koij", u_state, coarse_state, precision=lax.Precision.HIGHEST)
     pre = pre + b_coarse[None, :, None, None]
     coarse_next = coarse_state + jnp.tanh(pre)

time: 28.8 us -> 29 us (level)
    ppermute x1, starting transfers between devices: 0.56 us -> 0.07 us  [rep_sum(): lax.ppermute(part, 'rep', [(r, (r + step) % reps) for r in range(reps)])]
    ppermute x1, starting transfers between devices: 0.07 us -> 0.55 us  [shards(): lax.ppermute(piece, 'rep', [(r, (r + step) % reps) for r in range(reps)])]
    ppermute x1, waiting for transfers between devices: 0.01 us -> 0.35 us  [shards(): lax.ppermute(piece, 'rep', [(r, (r + step) % reps) for r in range(reps)])]
  transfers between devices with their start and end apart: 5 -> 5, of which waited for: 3 -> 4; matrix products, arithmetic and copies ran while one was open for 11% -> 8% of each run, Pallas kernels for 0% -> 0%
where the time goes in v19:
time: 29 us; the launch traced here: 28.8 us
  starting transfers between devices  8.42 us (29%)
  waiting for transfers between devices  5.97 us (21%)
  local copies, waits for them, and re-layouts  5.96 us (21%)
  matrix products  3.99 us (14%)
  other arithmetic  3.32 us (11%)
  between operations  1.15 us (4%)
    ppermute x1, starting transfers between devices, padded(): lax.ppermute(lax.slice_in_dim(block, block.shape[dim] - width, None, axis...  4.96 us
    dot_general x6, matrix products, apply_filter(): jnp.einsum('oi,bsirw->bsorw', weight, window_slice, preferred_element_typ...  3.1 us
    unnamed x35, local copies, waits for them, and re-layouts  2.95 us
    ppermute x1, waiting for transfers between devices, padded(): lax.ppermute(lax.slice_in_dim(block, 0, width, axis=dim), axis, backward)  2.87 us
    ppermute x1, waiting for transfers between devices, exchange_sum(): chunk = lax.ppermute(chunk, 'band', perm)  2 us
    concatenate x2, other arithmetic, apply_filter(): jnp.concatenate([padded_input[:, :, :, first_row_index + row_offset * dil...  1.93 us
    ppermute x1, starting transfers between devices, exchange_sum(): chunk = lax.ppermute(chunk, 'band', perm)  1.55 us
    ppermute x1, starting transfers between devices, padded(): lax.ppermute(lax.slice_in_dim(block, 0, width, axis=dim), axis, backward)  1.29 us
  transfers between devices with their start and end apart: 5, of which 4 were waited for; matrix products, arithmetic and copies ran while one was open for 8% of the time, Pallas kernels for 0%

profile of v19, /device:TPU:0, one launch (start us, length us, event | category | flops | bytes accessed | tf_op | source)
XLA Modules:
  0.0 28.8 jit_solution(5977633294681308621)
XLA Ops:
  0.6 0.0 copy-start
  0.6 0.0 copy-start.9
  0.7 0.0 copy-start.8
  0.7 0.0 copy-start.11
  0.7 1.1 %copy-done = f32[2,4,16,16,128]{4,3,2,1,0:T(8,128)S(1)} copy-done((f32[2,4,16,16,128]{4,3,2,1,0:T(8,128)S(1)}, f32[2,4,16,16,128]{4,3,2,1,0:T(8,128)}, u32[]{:S(2)}) %copy-start) | copy-done | bytes 1048600
  1.9 0.2 copy.47
  2.2 0.1 select_reduce_fusion.1
  2.3 5.0 %collective-permute-start = (bf16[1,18,3,128]{3,1,2,0:T(8,128)(2,1)S(1)}, bf16[1,18,3,128]{3,1,2,0:T(8,128)(2,1)S(1)}, u32[]{:S(2)}, u32[]{:S(2)}) collective-permute-start(bf16[1,18,3,128]{3,1,2,0:T(8,128)(2,1)S(1)} %bitcast.197), channel_id=1, source_target_pairs={{0,4},{4,8},{8,12},{1,5},{5,9},{9,13},{2,6},{6,10},{10,14},{3,7},{... | collective-permute-start | bytes 41480 | tf_op jit(solution)/shard_map/ppermute | solution.py:12
  7.3 1.3 %collective-permute-start.1 = (bf16[1,18,3,128]{3,1,2,0:T(8,128)(2,1)S(1)}, bf16[1,18,3,128]{3,1,2,0:T(8,128)(2,1)S(1)}, u32[]{:S(2)}, u32[]{:S(2)}) collective-permute-start(bf16[1,18,3,128]{3,1,2,0:T(8,128)(2,1)S(1)} %bitcast.196), channel_id=1, source_target_pairs={{4,0},{8,4},{12,8},{5,1},{9,5},{13,9},{6,2},{10,6},{14,10},{7,3},{... | collective-permute-start | bytes 41480 | tf_op jit(solution)/shard_map/ppermute | solution.py:15
  8.8 0.1 pad_maximum_fusion.6
  8.8 0.6 %gather_fusion.1 = bf16[4,18,3,128]{3,1,2,0:T(8,128)(2,1)S(1)} fusion(bf16[4,18,3,128]{3,1,2,0:T(8,128)(2,1)S(1)} %bitcast.193, s32[1024]{0:T(1024)S(1)} %pad_clamp_fusion.2), kind=kCustom, calls=%fused_computation.clone | custom fusion | bytes 110608 | tf_op jit(solution)/shard_map/jit(_take)/gather | solution.py:141
  9.4 0.6 %gather_fusion.2 = bf16[4,18,3,128]{3,1,2,0:T(8,128)(2,1)S(1)} fusion(bf16[4,18,3,128]{3,1,2,0:T(8,128)(2,1)S(1)} %bitcast.192, s32[1024]{0:T(1024)S(1)} %pad_clamp_fusion.1), kind=kCustom, calls=%fused_computation.1.clone | custom fusion | bytes 110608 | tf_op jit(solution)/shard_map/jit(_take)/gather | solution.py:144
  10.0 0.0 collective-permute-done
  10.0 0.1 fusion.22
  10.1 2.9 %collective-permute-done.1 = bf16[1,18,3,128]{3,1,2,0:T(8,128)(2,1)S(1)} collective-permute-done((bf16[1,18,3,128]{3,1,2,0:T(8,128)(2,1)S(1)}, bf16[1,18,3,128]{3,1,2,0:T(8,128)(2,1)S(1)}, u32[]{:S(2)}, u32[]{:S(2)}) %collective-permute-start.1) | collective-permute-done | bytes 13856 | tf_op jit(solution)/shard_map/ppermute | solution.py:15
  13.0 0.1 fusion.21
  13.1 0.2 pad_maximum_fusion.2
  13.2 0.9 %pad_slice_fusion.3 = (bf16[1,4,18,20,132]{4,2,3,1,0:T(8,128)(2,1)S(1)}, bf16[1,4,18,20,132]{4,2,3,1,0:T(8,128)(2,1)S(1)}, bf16[1,4,18,20,132]{4,2,3,1,0:T(8,128)(2,1)S(1)}) fusion(bf16[1,4,18,22,128]{4,2,3,1,0:T(8,128)(2,1)S(1)} %pad_maximum_fusion.2), kind=kLoop, calls=%fused_computation.10 | loop fusion | bytes 1545984 | tf_op jit(solution)/shard_map/slice | solution.py:26
  14.1 0.2 pad_slice_fusion
  14.3 1.1 %pad_maximum_fusion = bf16[1,4,54,20,132]{4,2,3,1,0:T(8,128)(2,1)S(1)} fusion(bf16[1,4,18,20,132]{4,2,3,1,0:T(8,128)(2,1)S(1)} %get-tuple-element.30, bf16[1,4,18,20,132]{4,2,3,1,0:T(8,128)(2,1)S(1)} %get-tuple-element.29, bf16[1,4,18,20,132]{4,2,3,1,0:T(8,128)(2,1)S(1)} %get-tuple-element.28), kind=kLoop, calls=%fused_computation.3 | loop fusion | flops 3421440 | bytes 2280960 | tf_op jit(solution)/shard_map/concatenate | solution.py:24
  15.4 0.5 %fusion.15 = f32[4,20,128,32]{2,3,1,0:T(8,128)S(1)} fusion(bf16[1,4,54,20,132]{4,2,3,1,0:T(8,128)(2,1)S(1)} %pad_maximum_fusion, bf16[32,18]{1,0:T(8,128)(2,1)S(1)} %get-tuple-element.39, bf16[32,18]{1,0:T(8,128)(2,1)S(1)} %get-tuple-element.40, bf16[32,18]{1,0:T(8,128)(2,1)S(1)} %get-tuple-element.41), kind=kOutput, calls=%fused_computation.33 | convolution fusion | flops 35399808 | bytes 2482176 | tf_op jit(solution)/shard_map/oi,bsirw->bsorw/dot_general | solution.py:50
  15.9 0.6 %convolution_add_fusion.1 = f32[4,20,128,32]{2,3,1,0:T(8,128)S(1)} fusion(f32[4,20,128,32]{2,3,1,0:T(8,128)S(1)} %fusion.15, bf16[1,4,54,20,132]{4,2,3,1,0:T(8,128)(2,1)S(1)} %pad_maximum_fusion, bf16[32,18]{1,0:T(8,128)(2,1)S(1)} %get-tuple-element.36, bf16[32,18]{1,0:T(8,128)(2,1)S(1)} %get-tuple-element.37, bf16[32,18]{1,0:T(8,128)(2,1)S(1)} %get-tuple-element.38), kind=kOutput, calls=%fused_computation.13 | convolution fusion | flops 35727488 | bytes 3792896 | tf_op jit(solution)/shard_map/oi,bsirw->bsorw/dot_general | solution.py:50
  16.5 0.7 %fusion.7 = f32[1,4,32,20,128]{4,2,3,1,0:T(8,128)S(1)} fusion(f32[4,20,128,32]{2,3,1,0:T(8,128)S(1)} %convolution_add_fusion.1, bf16[1,4,54,20,132]{4,2,3,1,0:T(8,128)(2,1)S(1)} %pad_maximum_fusion, f32[32]{0:T(128)S(1)} %pad_maximum_fusion.6, bf16[32,18]{1,0:T(8,128)(2,1)S(1)} %get-tuple-element.34, bf16[32,18]{1,0:T(8,128)(2,1)S(1)} %get-tuple-element.35, ...), kind=kOutput, calls=%fused_computation.19 | convolution fusion | flops 37038208 | bytes 3793408 | tf_op jit(solution)/shard_map/oi,bsirw->bsorw/dot_general | solution.py:50
  17.2 0.1 fusion.18
  17.3 0.6 %fusion.16 = bf16[1,4,18,20,132]{4,2,3,1,0:T(8,128)(2,1)S(1)} fusion(bf16[1,4,16,20,128]{4,2,3,1,0:T(8,128)(2,1)S(1)} %fusion.18, bf16[1,4,2,20,132]{4,2,3,1,0:T(2,128)(2,1)S(1)} %pad_slice_fusion), kind=kLoop, calls=%fused_computation.35 | loop fusion | flops 1140480 | bytes 750080 | tf_op jit(solution)/shard_map/concatenate | solution.py:174
  17.9 0.2 fusion.71
  18.1 0.8 %pad_maximum_fusion.1 = bf16[1,4,54,16,132]{4,2,3,1,0:T(8,128)(2,1)S(1)} fusion(bf16[1,4,18,16,132]{4,2,3,1,0:T(8,128)(2,1)S(1)} %get-tuple-element.24, bf16[1,4,18,16,132]{4,2,3,1,0:T(8,128)(2,1)S(1)} %get-tuple-element.25, bf16[1,4,18,16,132]{4,2,3,1,0:T(8,128)(2,1)S(1)} %get-tuple-element.23), kind=kLoop, calls=%fused_computation.6 | loop fusion | flops 2737152 | bytes 1824768 | tf_op jit(solution)/shard_map/concatenate | solution.py:24
  18.9 0.0 copy-start.12
  18.9 0.3 %fusion.17 = f32[4,16,128,16]{2,3,1,0:T(8,128)S(1)} fusion(bf16[1,4,54,16,132]{4,2,3,1,0:T(8,128)(2,1)S(1)} %pad_maximum_fusion.1, bf16[16,18]{1,0:T(8,128)(2,1)S(1)} %get-tuple-element.46, bf16[16,18]{1,0:T(8,128)(2,1)S(1)} %get-tuple-element.47, bf16[16,18]{1,0:T(8,128)(2,1)S(1)} %get-tuple-element.48), kind=kOutput, calls=%fused_computation.39 | convolution fusion | flops 14160960 | bytes 1454080 | tf_op jit(solution)/shard_map/oi,bsirw->bsorw/dot_general | solution.py:50
  19.2 0.5 %convolution_add_fusion.3 = f32[4,16,128,16]{2,3,1,0:T(8,128)S(1)} fusion(f32[4,16,128,16]{2,3,1,0:T(8,128)S(1)} %fusion.17, bf16[1,4,54,16,132]{4,2,3,1,0:T(8,128)(2,1)S(1)} %pad_maximum_fusion.1, bf16[16,18]{1,0:T(8,128)(2,1)S(1)} %get-tuple-element.43, bf16[16,18]{1,0:T(8,128)(2,1)S(1)} %get-tuple-element.44, bf16[16,18]{1,0:T(8,128)(2,1)S(1)} %get-tuple-element.45), kind=kOutput, calls=%fused_computation.22 | convolution fusion | flops 14292032 | bytes 1978368 | tf_op jit(solution)/shard_map/oi,bsirw->bsorw/dot_general | solution.py:50
  19.7 0.5 %fusion.14 = f32[1,4,16,16,128]{4,2,3,1,0:T(8,128)S(1)} fusion(f32[4,16,128,16]{2,3,1,0:T(8,128)S(1)} %convolution_add_fusion.3, bf16[1,4,54,16,132]{4,2,3,1,0:T(8,128)(2,1)S(1)} %pad_maximum_fusion.1, f32[1,4,32,20,128]{4,2,3,1,0:T(8,128)S(1)} %fusion.7, f32[1,4,16,16,128]{4,3,2,1,0:T(8,128)S(1)} %constant_dynamic-slice_fusion.1, ...), kind=kOutput, calls=%fused_computation.28 | convolution fusion | flops 15078464 | bytes 3027968 | tf_op jit(solution)/shard_map/oi,bsirw->bsorw/dot_general | solution.py:50
  20.2 0.4 %convolution_reduce_fusion = f32[4,16,4,32]{3,1,2,0:T(8,128)S(1)} fusion(f32[4,16,4,4,128]{4,1,3,2,0:T(8,128)S(1)} %bitcast.191, s32[128]{0:T(128)S(1)} %and_select_fusion), kind=kOutput, calls=%fused_computation.29 | convolution fusion | flops 50360320 | bytes 557568 | tf_op jit(solution)/shard_map/schw,wj->schj/dot_general | solution.py:200
  20.6 0.0 copy-start.6
  20.6 0.1 collective-permute-start.3
  20.7 0.5 %collective-permute-start.2 = (f32[1,4,8,16,128]{4,2,3,1,0:T(8,128)S(1)}, f32[1,4,8,16,128]{4,2,3,1,0:T(8,128)S(1)}, u32[]{:S(2)}, u32[]{:S(2)}) collective-permute-start(f32[1,4,8,16,128]{4,2,3,1,0:T(8,128)S(1)} %constant_dynamic-slice_fusion), channel_id=1, source_target_pairs={{0,1},{1,0},{2,3},{3,2},{4,5},{5,4},{6,7},{7,6},{8,9},{9,8},{10,11... | collective-permute-start | bytes 786440 | tf_op jit(solution)/shard_map/ppermute | solution.py:184
  21.3 0.7 %collective-permute-done.3 = f32[4,16,4,32]{3,1,2,0:T(8,128)S(1)} collective-permute-done((f32[4,16,4,32]{3,1,2,0:T(8,128)S(1)}, f32[4,16,4,32]{3,1,2,0:T(8,128)S(1)}, u32[]{:S(2)}, u32[]{:S(2)}) %collective-permute-start.3) | collective-permute-done | bytes 32800 | tf_op jit(solution)/shard_map/ppermute | solution.py:70
  22.1 0.0 copy-start.1
  22.1 0.0 copy-start.7
  22.1 0.0 copy-start.10
  22.1 0.4 %collective-permute-done.2 = f32[1,4,8,16,128]{4,2,3,1,0:T(8,128)S(1)} collective-permute-done((f32[1,4,8,16,128]{4,2,3,1,0:T(8,128)S(1)}, f32[1,4,8,16,128]{4,2,3,1,0:T(8,128)S(1)}, u32[]{:S(2)}, u32[]{:S(2)}) %collective-permute-start.2) | collective-permute-done | bytes 262176 | tf_op jit(solution)/shard_map/ppermute | solution.py:184
  22.5 0.1 select_add_fusion.1
  22.6 0.6 %gather_fusion = f32[4,16,4,32]{3,1,2,0:T(8,128)S(1)} fusion(f32[4,16,4,32]{3,1,2,0:T(8,128)S(1)} %fusion.70, s32[1024]{0:T(1024)S(1)} %pad_clamp_fusion), kind=kCustom, calls=%fused_computation.2 | custom fusion | bytes 65552 | tf_op jit(solution)/shard_map/jit(_take)/gather | solution.py:207
  23.1 0.3 %fusion.19 = f32[4,4,32,16]{2,3,1,0:T(8,128)S(1)} fusion(f32[4,16,4,32]{3,1,2,0:T(8,128)S(1)} %gather_fusion, pred[4]{0:T(512)(128)(4,1)S(1)} %get-tuple-element.58, f32[16,16]{1,0:T(8,128)S(1)} %copy-done.6), kind=kOutput, calls=%fused_computation.47 | convolution fusion | flops 1581056 | bytes 66564 | tf_op jit(solution)/shard_map/oc,kcij->koij/dot_general | solution.py:208
  23.5 1.6 %collective-permute-start.4 = (f32[2,16,4,32]{3,1,2,0:T(8,128)S(1)}, f32[2,16,4,32]{3,1,2,0:T(8,128)S(1)}, u32[]{:S(2)}, u32[]{:S(2)}) collective-permute-start(f32[2,16,4,32]{3,1,2,0:T(8,128)S(1)} %dynamic-slice_bitcast_fusion), channel_id=1, source_target_pairs={{0,2},{2,0},{1,3},{3,1},{4,6},{6,4},{5,7},{7,5},{8,10},{10,8},{9,1... | collective-permute-start | bytes 49160 | tf_op jit(solution)/shard_map/ppermute | solution.py:83
  25.0 0.9 %copy.27 = f32[2,4,8,16,128]{4,3,2,1,0:T(8,128)} copy(f32[2,4,8,16,128]{4,2,3,1,0:T(8,128)S(1)} %pad_maximum_fusion.3) | data formatting | bytes 1048576
  25.9 2.0 %collective-permute-done.4 = f32[2,16,4,32]{3,1,2,0:T(8,128)S(1)} collective-permute-done((f32[2,16,4,32]{3,1,2,0:T(8,128)S(1)}, f32[2,16,4,32]{3,1,2,0:T(8,128)S(1)}, u32[]{:S(2)}, u32[]{:S(2)}) %collective-permute-start.4) | collective-permute-done | bytes 16416 | tf_op jit(solution)/shard_map/ppermute | solution.py:83
  27.9 0.2 fusion.26
  28.1 0.7 %copy.28 = f32[2,16,4,32]{3,2,1,0:T(4,128)} copy(f32[2,16,4,32]{3,1,2,0:T(8,128)S(1)} %fusion.26) | data formatting | bytes 32768
  (40 shorter events, 0.3 us)
Async XLA Ops:
  0.6 1.2 %copy-start = (f32[2,4,16,16,128]{4,3,2,1,0:T(8,128)S(1)}, f32[2,4,16,16,128]{4,3,2,1,0:T(8,128)}, u32[]{:S(2)}) copy-start(f32[2,4,16,16,128]{4,3,2,1,0:T(8,128)} %param.18) | copy-start | bytes 3145732
  0.6 1.4 %copy-start.9 = (s32[4]{0:T(128)S(1)}, s32[4]{0:T(128)}, u32[]{:S(2)}) copy-start(s32[4]{0:T(128)} %param.19) | copy-start | bytes 52
  0.7 1.4 %copy-start.8 = (s32[4,2]{0,1:T(2,128)S(1)}, s32[4,2]{0,1:T(2,128)}, u32[]{:S(2)}) copy-start(s32[4,2]{0,1:T(2,128)} %param.20) | copy-start | bytes 100
  0.7 1.5 %copy-start.11 = (s32[1,4]{1,0:T(1,128)S(1)}, s32[1,4]{1,0:T(1,128)}, u32[]{:S(2)}) copy-start(s32[1,4]{1,0:T(1,128)} %param.21) | copy-start | bytes 52
  0.7 1.5 %copy-start.5 = (bf16[2,4,2,16,128]{4,3,2,1,0:T(8,128)(2,1)S(1)}, bf16[2,4,2,16,128]{4,3,2,1,0:T(8,128)(2,1)}, u32[]{:S(2)}) copy-start(bf16[2,4,2,16,128]{4,3,2,1,0:T(8,128)(2,1)} %param.17) | copy-start | bytes 196612
  0.7 8.0 %copy-start.2 = (bf16[9,16,18]{2,1,0:T(8,128)(2,1)S(1)}, bf16[9,16,18]{2,1,0:T(8,128)(2,1)}, u32[]{:S(2)}) copy-start(bf16[9,16,18]{2,1,0:T(8,128)(2,1)} %param.23) | copy-start | bytes 15556
  0.7 8.0 %copy-start.3 = (bf16[9,16,18]{2,1,0:T(8,128)(2,1)S(1)}, bf16[9,16,18]{2,1,0:T(8,128)(2,1)}, u32[]{:S(2)}) copy-start(bf16[9,16,18]{2,1,0:T(8,128)(2,1)} %param.25) | copy-start | bytes 15556
  0.7 8.0 %copy-start.4 = (bf16[9,16,18]{2,1,0:T(8,128)(2,1)S(1)}, bf16[9,16,18]{2,1,0:T(8,128)(2,1)}, u32[]{:S(2)}) copy-start(bf16[9,16,18]{2,1,0:T(8,128)(2,1)} %param.27) | copy-start | bytes 15556
  0.7 8.0 %copy-start.14 = (f32[16]{0:T(128)S(1)}, f32[16]{0:T(128)}, u32[]{:S(2)}) copy-start(f32[16]{0:T(128)} %param.24) | copy-start | bytes 196
  0.7 8.0 %copy-start.13 = (f32[16]{0:T(128)S(1)}, f32[16]{0:T(128)}, u32[]{:S(2)}) copy-start(f32[16]{0:T(128)} %param.26) | copy-start | bytes 196
  2.3 7.6 %collective-permute-start = (bf16[1,18,3,128]{3,1,2,0:T(8,128)(2,1)S(1)}, bf16[1,18,3,128]{3,1,2,0:T(8,128)(2,1)S(1)}, u32[]{:S(2)}, u32[]{:S(2)}) collective-permute-start(bf16[1,18,3,128]{3,1,2,0:T(8,128)(2,1)S(1)} %bitcast.197), channel_id=1, source_target_pairs={{0,4},{4,8},{8,12},{1,5},{5,9},{9,13},{2,6},{6,10},{10,14},{3,7},{... | collective-permute-start | bytes 41480 | tf_op jit(solution)/shard_map/ppermute | solution.py:12
  7.3 5.7 %collective-permute-start.1 = (bf16[1,18,3,128]{3,1,2,0:T(8,128)(2,1)S(1)}, bf16[1,18,3,128]{3,1,2,0:T(8,128)(2,1)S(1)}, u32[]{:S(2)}, u32[]{:S(2)}) collective-permute-start(bf16[1,18,3,128]{3,1,2,0:T(8,128)(2,1)S(1)} %bitcast.196), channel_id=1, source_target_pairs={{4,0},{8,4},{12,8},{5,1},{9,5},{13,9},{6,2},{10,6},{14,10},{7,3},{... | collective-permute-start | bytes 41480 | tf_op jit(solution)/shard_map/ppermute | solution.py:15
  18.9 0.8 %copy-start.12 = (f32[16]{0:T(128)S(1)}, f32[16]{0:T(128)}, u32[]{:S(2)}) copy-start(f32[16]{0:T(128)} %param.28) | copy-start | bytes 196
  20.6 2.5 %copy-start.6 = (f32[16,16]{1,0:T(8,128)S(1)}, f32[16,16]{1,0:T(8,128)}, u32[]{:S(2)}) copy-start(f32[16,16]{1,0:T(8,128)} %param.29) | copy-start | bytes 3076
  20.6 1.4 %collective-permute-start.3 = (f32[4,16,4,32]{3,1,2,0:T(8,128)S(1)}, f32[4,16,4,32]{3,1,2,0:T(8,128)S(1)}, u32[]{:S(2)}, u32[]{:S(2)}) collective-permute-start(f32[4,16,4,32]{3,1,2,0:T(8,128)S(1)} %broadcast_multiply_fusion), channel_id=1, source_target_pairs={{0,1},{1,0},{2,3},{3,2},{4,5},{5,4},{6,7},{7,6},{8,9},{9,8},{10,11... | collective-permute-start | bytes 98312 | tf_op jit(solution)/shard_map/ppermute | solution.py:70
  20.7 1.7 %collective-permute-start.2 = (f32[1,4,8,16,128]{4,2,3,1,0:T(8,128)S(1)}, f32[1,4,8,16,128]{4,2,3,1,0:T(8,128)S(1)}, u32[]{:S(2)}, u32[]{:S(2)}) collective-permute-start(f32[1,4,8,16,128]{4,2,3,1,0:T(8,128)S(1)} %constant_dynamic-slice_fusion), channel_id=1, source_target_pairs={{0,1},{1,0},{2,3},{3,2},{4,5},{5,4},{6,7},{7,6},{8,9},{9,8},{10,11... | collective-permute-start | bytes 786440 | tf_op jit(solution)/shard_map/ppermute | solution.py:184
  22.1 5.9 %copy-start.1 = (f32[2,16,4,32]{3,2,1,0:T(4,128)S(1)}, f32[2,16,4,32]{3,2,1,0:T(4,128)}, u32[]{:S(2)}) copy-start(f32[2,16,4,32]{3,2,1,0:T(4,128)} %param.22) | copy-start | bytes 49156
  22.1 5.9 %copy-start.7 = (f32[16,16]{1,0:T(8,128)S(1)}, f32[16,16]{1,0:T(8,128)}, u32[]{:S(2)}) copy-start(f32[16,16]{1,0:T(8,128)} %param.30) | copy-start | bytes 3076
  22.1 5.8 %copy-start.10 = (f32[16]{0:T(128)S(1)}, f32[16]{0:T(128)}, u32[]{:S(2)}) copy-start(f32[16]{0:T(128)} %param.31) | copy-start | bytes 196
  23.5 4.4 %collective-permute-start.4 = (f32[2,16,4,32]{3,1,2,0:T(8,128)S(1)}, f32[2,16,4,32]{3,1,2,0:T(8,128)S(1)}, u32[]{:S(2)}, u32[]{:S(2)}) collective-permute-start(f32[2,16,4,32]{3,1,2,0:T(8,128)S(1)} %dynamic-slice_bitcast_fusion), channel_id=1, source_target_pairs={{0,2},{2,0},{1,3},{3,1},{4,6},{6,4},{5,7},{7,5},{8,10},{10,8},{9,1... | collective-permute-start | bytes 49160 | tf_op jit(solution)/shard_map/ppermute | solution.py:83

commit v20 on v17

--- a/solution.py
+++ b/solution.py
@@ -205,8 +205,10 @@
     ) / 16.0
     ordered = jnp.take(pooled, coarse_perm[0], axis=0)
     part = jnp.einsum("oc,kcij->koij", u_pool, ordered, precision=lax.Precision.HIGHEST)
-    new_half, chip_part = lax.optimization_barrier((new_half, rep_sum(part)))
-    pre = exchange_sum(chip_part, coarse_state.shape[0])
+    new_half, band_part = lax.optimization_barrier(
+        (new_half, exchange_sum(part, coarse_state.shape[0]))
+    )
+    pre = rep_sum(band_part)
     pre = pre + jnp.einsum("oc,kcij->koij", u_state, coarse_state, precision=lax.Precision.HIGHEST)
     pre = pre + b_coarse[None, :, None, None]
     coarse_next = coarse_state + jnp.tanh(pre)

time: 28.8 us -> 28.6 us (level)
  starting transfers between devices: 8.43 us -> 7.95 us
    ppermute x1, waiting for transfers between devices: 1.98 us -> 3 us  [exchange_sum(): chunk = lax.ppermute(chunk, 'band', perm)]
    ppermute x1, waiting for transfers between devices: 0.98 us -> 0.13 us  [rep_sum(): lax.ppermute(part, 'rep', [(r, (r + step) % reps) for r in range(reps)])]
    ppermute x1, starting transfers between devices: 0.56 us -> 0.07 us  [rep_sum(): lax.ppermute(part, 'rep', [(r, (r + step) % reps) for r in range(reps)])]
  transfers between devices with their start and end apart: 5 -> 5, of which waited for: 3 -> 3; matrix products, arithmetic and copies ran while one was open for 11% -> 12% of each run, Pallas kernels for 0% -> 0%
where the time goes in v20:
time: 28.6 us; the launch traced here: 28.5 us
  starting transfers between devices  7.95 us (28%)
  waiting for transfers between devices  5.99 us (21%)
  local copies, waits for them, and re-layouts  5.96 us (21%)
  matrix products  3.98 us (14%)
  other arithmetic  3.4 us (12%)
  between operations  1.19 us (4%)
    ppermute x1, starting transfers between devices, padded(): lax.ppermute(lax.slice_in_dim(block, block.shape[dim] - width, None, axis...  4.96 us
    dot_general x6, matrix products, apply_filter(): jnp.einsum('oi,bsirw->bsorw', weight, window_slice, preferred_element_typ...  3.1 us
    ppermute x1, waiting for transfers between devices, exchange_sum(): chunk = lax.ppermute(chunk, 'band', perm)  3 us
    unnamed x35, local copies, waits for them, and re-layouts  2.95 us
    ppermute x1, waiting for transfers between devices, padded(): lax.ppermute(lax.slice_in_dim(block, 0, width, axis=dim), axis, backward)  2.85 us
    concatenate x2, other arithmetic, apply_filter(): jnp.concatenate([padded_input[:, :, :, first_row_index + row_offset * dil...  1.93 us
    ppermute x1, starting transfers between devices, exchange_sum(): chunk = lax.ppermute(chunk, 'band', perm)  1.56 us
    ppermute x1, starting transfers between devices, padded(): lax.ppermute(lax.slice_in_dim(block, 0, width, axis=dim), axis, backward)  1.29 us
  transfers between devices with their start and end apart: 5, of which 3 were waited for; matrix products, arithmetic and copies ran while one was open for 12% of the time, Pallas kernels for 0%

profile of v20, /device:TPU:0, one launch (start us, length us, event | category | flops | bytes accessed | tf_op | source)
XLA Modules:
  0.0 28.5 jit_solution(13610556435394136660)
XLA Ops:
  0.6 0.0 copy-start
  0.6 0.0 copy-start.9
  0.7 1.1 %copy-done = f32[2,4,16,16,128]{4,3,2,1,0:T(8,128)S(1)} copy-done((f32[2,4,16,16,128]{4,3,2,1,0:T(8,128)S(1)}, f32[2,4,16,16,128]{4,3,2,1,0:T(8,128)}, u32[]{:S(2)}) %copy-start) | copy-done | bytes 1048600
  1.9 0.2 copy.51
  2.1 0.0 copy-done.11
  2.2 0.1 select_reduce_fusion.1
  2.3 5.0 %collective-permute-start = (bf16[1,18,3,128]{3,1,2,0:T(8,128)(2,1)S(1)}, bf16[1,18,3,128]{3,1,2,0:T(8,128)(2,1)S(1)}, u32[]{:S(2)}, u32[]{:S(2)}) collective-permute-start(bf16[1,18,3,128]{3,1,2,0:T(8,128)(2,1)S(1)} %bitcast.187), channel_id=1, source_target_pairs={{0,4},{4,8},{8,12},{1,5},{5,9},{9,13},{2,6},{6,10},{10,14},{3,7},{... | collective-permute-start | bytes 41480 | tf_op jit(solution)/shard_map/ppermute | solution.py:12
  7.3 1.3 %collective-permute-start.1 = (bf16[1,18,3,128]{3,1,2,0:T(8,128)(2,1)S(1)}, bf16[1,18,3,128]{3,1,2,0:T(8,128)(2,1)S(1)}, u32[]{:S(2)}, u32[]{:S(2)}) collective-permute-start(bf16[1,18,3,128]{3,1,2,0:T(8,128)(2,1)S(1)} %bitcast.186), channel_id=1, source_target_pairs={{4,0},{8,4},{12,8},{5,1},{9,5},{13,9},{6,2},{10,6},{14,10},{7,3},{... | collective-permute-start | bytes 41480 | tf_op jit(solution)/shard_map/ppermute | solution.py:15
  8.7 0.0 copy-done.4
  8.8 0.1 pad_maximum_fusion.6
  8.9 0.6 %gather_fusion.1 = bf16[4,18,3,128]{3,1,2,0:T(8,128)(2,1)S(1)} fusion(bf16[4,18,3,128]{3,1,2,0:T(8,128)(2,1)S(1)} %bitcast.183, s32[1024]{0:T(1024)S(1)} %pad_clamp_fusion.2), kind=kCustom, calls=%fused_computation.clone | custom fusion | bytes 110608 | tf_op jit(solution)/shard_map/jit(_take)/gather | solution.py:141
  9.4 0.6 %gather_fusion.2 = bf16[4,18,3,128]{3,1,2,0:T(8,128)(2,1)S(1)} fusion(bf16[4,18,3,128]{3,1,2,0:T(8,128)(2,1)S(1)} %bitcast.182, s32[1024]{0:T(1024)S(1)} %pad_clamp_fusion.1), kind=kCustom, calls=%fused_computation.1.clone | custom fusion | bytes 110608 | tf_op jit(solution)/shard_map/jit(_take)/gather | solution.py:144
  10.0 0.0 collective-permute-done
  10.0 0.1 fusion.22
  10.1 2.9 %collective-permute-done.1 = bf16[1,18,3,128]{3,1,2,0:T(8,128)(2,1)S(1)} collective-permute-done((bf16[1,18,3,128]{3,1,2,0:T(8,128)(2,1)S(1)}, bf16[1,18,3,128]{3,1,2,0:T(8,128)(2,1)S(1)}, u32[]{:S(2)}, u32[]{:S(2)}) %collective-permute-start.1) | collective-permute-done | bytes 13856 | tf_op jit(solution)/shard_map/ppermute | solution.py:15
  13.0 0.1 fusion.21
  13.1 0.2 pad_maximum_fusion.2
  13.2 0.9 %pad_slice_fusion.3 = (bf16[1,4,18,20,132]{4,2,3,1,0:T(8,128)(2,1)S(1)}, bf16[1,4,18,20,132]{4,2,3,1,0:T(8,128)(2,1)S(1)}, bf16[1,4,18,20,132]{4,2,3,1,0:T(8,128)(2,1)S(1)}) fusion(bf16[1,4,18,22,128]{4,2,3,1,0:T(8,128)(2,1)S(1)} %pad_maximum_fusion.2), kind=kLoop, calls=%fused_computation.10 | loop fusion | bytes 1545984 | tf_op jit(solution)/shard_map/slice | solution.py:26
  14.1 0.2 pad_slice_fusion
  14.3 1.1 %pad_maximum_fusion = bf16[1,4,54,20,132]{4,2,3,1,0:T(8,128)(2,1)S(1)} fusion(bf16[1,4,18,20,132]{4,2,3,1,0:T(8,128)(2,1)S(1)} %get-tuple-element.32, bf16[1,4,18,20,132]{4,2,3,1,0:T(8,128)(2,1)S(1)} %get-tuple-element.31, bf16[1,4,18,20,132]{4,2,3,1,0:T(8,128)(2,1)S(1)} %get-tuple-element.30), kind=kLoop, calls=%fused_computation.3 | loop fusion | flops 3421440 | bytes 2280960 | tf_op jit(solution)/shard_map/concatenate | solution.py:24
  15.4 0.5 %fusion.15 = f32[4,20,128,32]{2,3,1,0:T(8,128)S(1)} fusion(bf16[1,4,54,20,132]{4,2,3,1,0:T(8,128)(2,1)S(1)} %pad_maximum_fusion, bf16[32,18]{1,0:T(8,128)(2,1)S(1)} %get-tuple-element.41, bf16[32,18]{1,0:T(8,128)(2,1)S(1)} %get-tuple-element.42, bf16[32,18]{1,0:T(8,128)(2,1)S(1)} %get-tuple-element.43), kind=kOutput, calls=%fused_computation.33 | convolution fusion | flops 35399808 | bytes 2482176 | tf_op jit(solution)/shard_map/oi,bsirw->bsorw/dot_general | solution.py:50
  15.9 0.6 %convolution_add_fusion.1 = f32[4,20,128,32]{2,3,1,0:T(8,128)S(1)} fusion(f32[4,20,128,32]{2,3,1,0:T(8,128)S(1)} %fusion.15, bf16[1,4,54,20,132]{4,2,3,1,0:T(8,128)(2,1)S(1)} %pad_maximum_fusion, bf16[32,18]{1,0:T(8,128)(2,1)S(1)} %get-tuple-element.38, bf16[32,18]{1,0:T(8,128)(2,1)S(1)} %get-tuple-element.39, bf16[32,18]{1,0:T(8,128)(2,1)S(1)} %get-tuple-element.40), kind=kOutput, calls=%fused_computation.13 | convolution fusion | flops 35727488 | bytes 3792896 | tf_op jit(solution)/shard_map/oi,bsirw->bsorw/dot_general | solution.py:50
  16.5 0.7 %fusion.7 = f32[1,4,32,20,128]{4,2,3,1,0:T(8,128)S(1)} fusion(f32[4,20,128,32]{2,3,1,0:T(8,128)S(1)} %convolution_add_fusion.1, bf16[1,4,54,20,132]{4,2,3,1,0:T(8,128)(2,1)S(1)} %pad_maximum_fusion, f32[32]{0:T(128)S(1)} %pad_maximum_fusion.6, bf16[32,18]{1,0:T(8,128)(2,1)S(1)} %get-tuple-element.36, bf16[32,18]{1,0:T(8,128)(2,1)S(1)} %get-tuple-element.37, ...), kind=kOutput, calls=%fused_computation.19 | convolution fusion | flops 37038208 | bytes 3793408 | tf_op jit(solution)/shard_map/oi,bsirw->bsorw/dot_general | solution.py:50
  17.2 0.1 fusion.18
  17.3 0.6 %fusion.16 = bf16[1,4,18,20,132]{4,2,3,1,0:T(8,128)(2,1)S(1)} fusion(bf16[1,4,16,20,128]{4,2,3,1,0:T(8,128)(2,1)S(1)} %fusion.18, bf16[1,4,2,20,132]{4,2,3,1,0:T(2,128)(2,1)S(1)} %pad_slice_fusion), kind=kLoop, calls=%fused_computation.35 | loop fusion | flops 1140480 | bytes 750080 | tf_op jit(solution)/shard_map/concatenate | solution.py:174
  17.9 0.2 fusion.64
  18.1 0.8 %pad_maximum_fusion.1 = bf16[1,4,54,16,132]{4,2,3,1,0:T(8,128)(2,1)S(1)} fusion(bf16[1,4,18,16,132]{4,2,3,1,0:T(8,128)(2,1)S(1)} %get-tuple-element.26, bf16[1,4,18,16,132]{4,2,3,1,0:T(8,128)(2,1)S(1)} %get-tuple-element.27, bf16[1,4,18,16,132]{4,2,3,1,0:T(8,128)(2,1)S(1)} %get-tuple-element.25), kind=kLoop, calls=%fused_computation.6 | loop fusion | flops 2737152 | bytes 1824768 | tf_op jit(solution)/shard_map/concatenate | solution.py:24
  18.9 0.0 copy-start.12
  18.9 0.3 %fusion.17 = f32[4,16,128,16]{2,3,1,0:T(8,128)S(1)} fusion(bf16[1,4,54,16,132]{4,2,3,1,0:T(8,128)(2,1)S(1)} %pad_maximum_fusion.1, bf16[16,18]{1,0:T(8,128)(2,1)S(1)} %get-tuple-element.48, bf16[16,18]{1,0:T(8,128)(2,1)S(1)} %get-tuple-element.49, bf16[16,18]{1,0:T(8,128)(2,1)S(1)} %get-tuple-element.50), kind=kOutput, calls=%fused_computation.39 | convolution fusion | flops 14160960 | bytes 1454080 | tf_op jit(solution)/shard_map/oi,bsirw->bsorw/dot_general | solution.py:50
  19.2 0.5 %convolution_add_fusion.3 = f32[4,16,128,16]{2,3,1,0:T(8,128)S(1)} fusion(f32[4,16,128,16]{2,3,1,0:T(8,128)S(1)} %fusion.17, bf16[1,4,54,16,132]{4,2,3,1,0:T(8,128)(2,1)S(1)} %pad_maximum_fusion.1, bf16[16,18]{1,0:T(8,128)(2,1)S(1)} %get-tuple-element.45, bf16[16,18]{1,0:T(8,128)(2,1)S(1)} %get-tuple-element.46, bf16[16,18]{1,0:T(8,128)(2,1)S(1)} %get-tuple-element.47), kind=kOutput, calls=%fused_computation.22 | convolution fusion | flops 14292032 | bytes 1978368 | tf_op jit(solution)/shard_map/oi,bsirw->bsorw/dot_general | solution.py:50
  19.7 0.5 %fusion.14 = f32[1,4,16,16,128]{4,2,3,1,0:T(8,128)S(1)} fusion(f32[4,16,128,16]{2,3,1,0:T(8,128)S(1)} %convolution_add_fusion.3, bf16[1,4,54,16,132]{4,2,3,1,0:T(8,128)(2,1)S(1)} %pad_maximum_fusion.1, f32[1,4,32,20,128]{4,2,3,1,0:T(8,128)S(1)} %fusion.7, f32[1,4,16,16,128]{4,3,2,1,0:T(8,128)S(1)} %constant_dynamic-slice_fusion.1, ...), kind=kOutput, calls=%fused_computation.28 | convolution fusion | flops 15078464 | bytes 3027968 | tf_op jit(solution)/shard_map/oi,bsirw->bsorw/dot_general | solution.py:50
  20.2 0.4 %convolution_reduce_fusion = f32[4,16,4,32]{3,1,2,0:T(8,128)S(1)} fusion(f32[4,16,4,4,128]{4,1,3,2,0:T(8,128)S(1)} %bitcast.181, s32[128]{0:T(128)S(1)} %and_select_fusion), kind=kOutput, calls=%fused_computation.29 | convolution fusion | flops 50360320 | bytes 557568 | tf_op jit(solution)/shard_map/schw,wj->schj/dot_general | solution.py:200
  20.6 0.0 copy-start.1
  20.6 0.0 copy-start.7
  20.7 0.1 collective-permute-start.2
  20.8 0.6 %gather_fusion = f32[4,16,4,32]{3,1,2,0:T(8,128)S(1)} fusion(f32[4,16,4,32]{3,1,2,0:T(8,128)S(1)} %broadcast_multiply_fusion, s32[1024]{0:T(1024)S(1)} %pad_clamp_fusion), kind=kCustom, calls=%fused_computation.2 | custom fusion | bytes 65552 | tf_op jit(solution)/shard_map/jit(_take)/gather | solution.py:206
  21.3 0.3 %fusion.19 = f32[4,4,32,16]{2,3,1,0:T(8,128)S(1)} fusion(f32[4,16,4,32]{3,1,2,0:T(8,128)S(1)} %gather_fusion, pred[4]{0:T(512)(128)(4,1)S(1)} %get-tuple-element.60, f32[16,16]{1,0:T(8,128)S(1)} %copy-done.6), kind=kOutput, calls=%fused_computation.47 | convolution fusion | flops 1581056 | bytes 66564 | tf_op jit(solution)/shard_map/oc,kcij->koij/dot_general | solution.py:207
  21.7 0.0 copy-start.10
  21.7 1.6 %collective-permute-start.3 = (f32[2,16,4,32]{3,1,2,0:T(8,128)S(1)}, f32[2,16,4,32]{3,1,2,0:T(8,128)S(1)}, u32[]{:S(2)}, u32[]{:S(2)}) collective-permute-start(f32[2,16,4,32]{3,1,2,0:T(8,128)S(1)} %dynamic-slice_bitcast_fusion), channel_id=1, source_target_pairs={{0,2},{2,0},{1,3},{3,1},{4,6},{6,4},{5,7},{7,5},{8,10},{10,8},{9,1... | collective-permute-start | bytes 49160 | tf_op jit(solution)/shard_map/ppermute | solution.py:83
  23.2 3.0 %collective-permute-done.3 = f32[2,16,4,32]{3,1,2,0:T(8,128)S(1)} collective-permute-done((f32[2,16,4,32]{3,1,2,0:T(8,128)S(1)}, f32[2,16,4,32]{3,1,2,0:T(8,128)S(1)}, u32[]{:S(2)}, u32[]{:S(2)}) %collective-permute-start.3) | collective-permute-done | bytes 16416 | tf_op jit(solution)/shard_map/ppermute | solution.py:83
  26.3 0.0 collective-permute-done.2
  26.3 0.1 select_add_fusion.1
  26.4 0.1 collective-permute-start.4
  26.5 0.2 convolution_bitcast_fusion
  26.7 0.9 %copy.33 = f32[2,4,8,16,128]{4,3,2,1,0:T(8,128)} copy(f32[2,4,8,16,128]{4,2,3,1,0:T(8,128)S(1)} %pad_maximum_fusion.3) | data formatting | bytes 1048576
  27.6 0.1 collective-permute-done.4
  27.7 0.1 tanh_add_fusion
  27.8 0.7 %copy.34 = f32[2,16,4,32]{3,2,1,0:T(4,128)} copy(f32[2,16,4,32]{3,1,2,0:T(8,128)S(1)} %tanh_add_fusion) | data formatting | bytes 32768
  (41 shorter events, 0.3 us)
Async XLA Ops:
  0.6 1.2 %copy-start = (f32[2,4,16,16,128]{4,3,2,1,0:T(8,128)S(1)}, f32[2,4,16,16,128]{4,3,2,1,0:T(8,128)}, u32[]{:S(2)}) copy-start(f32[2,4,16,16,128]{4,3,2,1,0:T(8,128)} %param.18) | copy-start | bytes 3145732
  0.6 1.4 %copy-start.9 = (s32[4]{0:T(128)S(1)}, s32[4]{0:T(128)}, u32[]{:S(2)}) copy-start(s32[4]{0:T(128)} %param.19) | copy-start | bytes 52
  0.7 1.4 %copy-start.8 = (s32[4,2]{0,1:T(2,128)S(1)}, s32[4,2]{0,1:T(2,128)}, u32[]{:S(2)}) copy-start(s32[4,2]{0,1:T(2,128)} %param.20) | copy-start | bytes 100
  0.7 1.5 %copy-start.11 = (s32[1,4]{1,0:T(1,128)S(1)}, s32[1,4]{1,0:T(1,128)}, u32[]{:S(2)}) copy-start(s32[1,4]{1,0:T(1,128)} %param.21) | copy-start | bytes 52
  0.7 1.5 %copy-start.5 = (bf16[2,4,2,16,128]{4,3,2,1,0:T(8,128)(2,1)S(1)}, bf16[2,4,2,16,128]{4,3,2,1,0:T(8,128)(2,1)}, u32[]{:S(2)}) copy-start(bf16[2,4,2,16,128]{4,3,2,1,0:T(8,128)(2,1)} %param.17) | copy-start | bytes 196612
  0.7 8.0 %copy-start.2 = (bf16[9,16,18]{2,1,0:T(8,128)(2,1)S(1)}, bf16[9,16,18]{2,1,0:T(8,128)(2,1)}, u32[]{:S(2)}) copy-start(bf16[9,16,18]{2,1,0:T(8,128)(2,1)} %param.23) | copy-start | bytes 15556
  0.7 8.0 %copy-start.3 = (bf16[9,16,18]{2,1,0:T(8,128)(2,1)S(1)}, bf16[9,16,18]{2,1,0:T(8,128)(2,1)}, u32[]{:S(2)}) copy-start(bf16[9,16,18]{2,1,0:T(8,128)(2,1)} %param.25) | copy-start | bytes 15556
  0.7 8.0 %copy-start.4 = (bf16[9,16,18]{2,1,0:T(8,128)(2,1)S(1)}, bf16[9,16,18]{2,1,0:T(8,128)(2,1)}, u32[]{:S(2)}) copy-start(bf16[9,16,18]{2,1,0:T(8,128)(2,1)} %param.27) | copy-start | bytes 15556
  0.7 8.0 %copy-start.14 = (f32[16]{0:T(128)S(1)}, f32[16]{0:T(128)}, u32[]{:S(2)}) copy-start(f32[16]{0:T(128)} %param.24) | copy-start | bytes 196
  0.7 8.0 %copy-start.13 = (f32[16]{0:T(128)S(1)}, f32[16]{0:T(128)}, u32[]{:S(2)}) copy-start(f32[16]{0:T(128)} %param.26) | copy-start | bytes 196
  2.3 7.7 %collective-permute-start = (bf16[1,18,3,128]{3,1,2,0:T(8,128)(2,1)S(1)}, bf16[1,18,3,128]{3,1,2,0:T(8,128)(2,1)S(1)}, u32[]{:S(2)}, u32[]{:S(2)}) collective-permute-start(bf16[1,18,3,128]{3,1,2,0:T(8,128)(2,1)S(1)} %bitcast.187), channel_id=1, source_target_pairs={{0,4},{4,8},{8,12},{1,5},{5,9},{9,13},{2,6},{6,10},{10,14},{3,7},{... | collective-permute-start | bytes 41480 | tf_op jit(solution)/shard_map/ppermute | solution.py:12
  7.3 5.7 %collective-permute-start.1 = (bf16[1,18,3,128]{3,1,2,0:T(8,128)(2,1)S(1)}, bf16[1,18,3,128]{3,1,2,0:T(8,128)(2,1)S(1)}, u32[]{:S(2)}, u32[]{:S(2)}) collective-permute-start(bf16[1,18,3,128]{3,1,2,0:T(8,128)(2,1)S(1)} %bitcast.186), channel_id=1, source_target_pairs={{4,0},{8,4},{12,8},{5,1},{9,5},{13,9},{6,2},{10,6},{14,10},{7,3},{... | collective-permute-start | bytes 41480 | tf_op jit(solution)/shard_map/ppermute | solution.py:15
  18.9 0.8 %copy-start.12 = (f32[16]{0:T(128)S(1)}, f32[16]{0:T(128)}, u32[]{:S(2)}) copy-start(f32[16]{0:T(128)} %param.28) | copy-start | bytes 196
  19.7 1.6 %copy-start.6 = (f32[16,16]{1,0:T(8,128)S(1)}, f32[16,16]{1,0:T(8,128)}, u32[]{:S(2)}) copy-start(f32[16,16]{1,0:T(8,128)} %param.29) | copy-start | bytes 3076
  20.6 5.8 %copy-start.1 = (f32[2,16,4,32]{3,2,1,0:T(4,128)S(1)}, f32[2,16,4,32]{3,2,1,0:T(4,128)}, u32[]{:S(2)}) copy-start(f32[2,16,4,32]{3,2,1,0:T(4,128)} %param.22) | copy-start | bytes 49156
  20.6 5.8 %copy-start.7 = (f32[16,16]{1,0:T(8,128)S(1)}, f32[16,16]{1,0:T(8,128)}, u32[]{:S(2)}) copy-start(f32[16,16]{1,0:T(8,128)} %param.30) | copy-start | bytes 3076
  20.7 5.6 %collective-permute-start.2 = (f32[1,4,8,16,128]{4,2,3,1,0:T(8,128)S(1)}, f32[1,4,8,16,128]{4,2,3,1,0:T(8,128)S(1)}, u32[]{:S(2)}, u32[]{:S(2)}) collective-permute-start(f32[1,4,8,16,128]{4,2,3,1,0:T(8,128)S(1)} %constant_dynamic-slice_fusion), channel_id=1, source_target_pairs={{0,1},{1,0},{2,3},{3,2},{4,5},{5,4},{6,7},{7,6},{8,9},{9,8},{10,11... | collective-permute-start | bytes 786440 | tf_op jit(solution)/shard_map/ppermute | solution.py:184
  21.7 6.1 %copy-start.10 = (f32[16]{0:T(128)S(1)}, f32[16]{0:T(128)}, u32[]{:S(2)}) copy-start(f32[16]{0:T(128)} %param.31) | copy-start | bytes 196
  21.7 4.6 %collective-permute-start.3 = (f32[2,16,4,32]{3,1,2,0:T(8,128)S(1)}, f32[2,16,4,32]{3,1,2,0:T(8,128)S(1)}, u32[]{:S(2)}, u32[]{:S(2)}) collective-permute-start(f32[2,16,4,32]{3,1,2,0:T(8,128)S(1)} %dynamic-slice_bitcast_fusion), channel_id=1, source_target_pairs={{0,2},{2,0},{1,3},{3,1},{4,6},{6,4},{5,7},{7,5},{8,10},{10,8},{9,1... | collective-permute-start | bytes 49160 | tf_op jit(solution)/shard_map/ppermute | solution.py:83
  26.4 1.3 %collective-permute-start.4 = (f32[2,16,4,32]{3,1,2,0:T(8,128)S(1)}, f32[2,16,4,32]{3,1,2,0:T(8,128)S(1)}, u32[]{:S(2)}, u32[]{:S(2)}) collective-permute-start(f32[2,16,4,32]{3,1,2,0:T(8,128)S(1)} %bitcast_add_fusion), channel_id=1, source_target_pairs={{0,1},{1,0},{2,3},{3,2},{4,5},{5,4},{6,7},{7,6},{8,9},{9,8},{10,11... | collective-permute-start | bytes 49160 | tf_op jit(solution)/shard_map/ppermute | solution.py:70

commit v21 on v19

--- a/solution.py
+++ b/solution.py
@@ -203,10 +203,18 @@
     pooled = jnp.sum(
         cols.reshape(slots, chans, row_count // 4, 4, column_count // 4), axis=3
     ) / 16.0
-    new_half, chip_pooled = lax.optimization_barrier((new_half, rep_sum(pooled)))
-    ordered = jnp.take(chip_pooled, coarse_perm[0], axis=0)
+    bands = lax.axis_size("band")
+    band_pooled = pooled
+    for shift in range(1, bands):
+        band_pooled = band_pooled + lax.ppermute(
+            pooled, "band", [(b, (b + shift) % bands) for b in range(bands)]
+        )
+    owned = coarse_state.shape[0]
+    mine = lax.dynamic_slice_in_dim(coarse_perm[0], lax.axis_index("band") * owned, owned, 0)
+    ordered = jnp.take(band_pooled, mine, axis=0)
     part = jnp.einsum("oc,kcij->koij", u_pool, ordered, precision=lax.Precision.HIGHEST)
-    pre = exchange_sum(part, coarse_state.shape[0])
+    new_half, part = lax.optimization_barrier((new_half, part))
+    pre = rep_sum(part)
     pre = pre + jnp.einsum("oc,kcij->koij", u_state, coarse_state, precision=lax.Precision.HIGHEST)
     pre = pre + b_coarse[None, :, None, None]
     coarse_next = coarse_state + jnp.tanh(pre)

time: 29 us -> 29 us (level)
  starting transfers between devices: 8.42 us -> 7.95 us
  waiting for transfers between devices: 5.97 us -> 6.4 us
    ppermute x1, waiting for transfers between devices: 2 us -> 3.34 us  [shards(): lax.ppermute(pooled, 'band', [(b, (b + shift) % bands) for b in range(ban...]
    ppermute x1, starting transfers between devices: 0.55 us -> 0.07 us  [shards(): lax.ppermute(piece, 'rep', [(r, (r + step) % reps) for r in range(reps)])]
    ppermute x1, waiting for transfers between devices: 0.75 us -> 0.35 us  [rep_sum(): lax.ppermute(part, 'rep', [(r, (r + step) % reps) for r in range(reps)])]
    ppermute x1, waiting for transfers between devices: 0.35 us -> 0.01 us  [shards(): lax.ppermute(piece, 'rep', [(r, (r + step) % reps) for r in range(reps)])]
  transfers between devices with their start and end apart: 5 -> 5, of which waited for: 4 -> 3; matrix products, arithmetic and copies ran while one was open for 8% -> 11% of each run, Pallas kernels for 0% -> 0%
where the time goes in v21:
time: 29 us; the launch traced here: 28.8 us
  starting transfers between devices  7.95 us (27%)
  waiting for transfers between devices  6.4 us (22%)
  local copies, waits for them, and re-layouts  5.93 us (20%)
  matrix products  3.93 us (14%)
  other arithmetic  3.48 us (12%)
  between operations  1.15 us (4%)
    ppermute x1, starting transfers between devices, padded(): lax.ppermute(lax.slice_in_dim(block, block.shape[dim] - width, None, axis...  4.96 us
    ppermute x1, waiting for transfers between devices, shards(): lax.ppermute(pooled, 'band', [(b, (b + shift) % bands) for b in range(ban...  3.34 us
    dot_general x6, matrix products, apply_filter(): jnp.einsum('oi,bsirw->bsorw', weight, window_slice, preferred_element_typ...  3.11 us
    unnamed x35, local copies, waits for them, and re-layouts  2.95 us
    ppermute x1, waiting for transfers between devices, padded(): lax.ppermute(lax.slice_in_dim(block, 0, width, axis=dim), axis, backward)  2.7 us
    concatenate x2, other arithmetic, apply_filter(): jnp.concatenate([padded_input[:, :, :, first_row_index + row_offset * dil...  1.93 us
    ppermute x1, starting transfers between devices, shards(): lax.ppermute(pooled, 'band', [(b, (b + shift) % bands) for b in range(ban...  1.56 us
    ppermute x1, starting transfers between devices, padded(): lax.ppermute(lax.slice_in_dim(block, 0, width, axis=dim), axis, backward)  1.29 us
  transfers between devices with their start and end apart: 5, of which 3 were waited for; matrix products, arithmetic and copies ran while one was open for 11% of the time, Pallas kernels for 0%

profile of v21, /device:TPU:0, one launch (start us, length us, event | category | flops | bytes accessed | tf_op | source)
XLA Modules:
  0.0 28.8 jit_solution(7045985866895830656)
XLA Ops:
  0.6 0.0 copy-start
  0.7 1.1 %copy-done = f32[2,4,16,16,128]{4,3,2,1,0:T(8,128)S(1)} copy-done((f32[2,4,16,16,128]{4,3,2,1,0:T(8,128)S(1)}, f32[2,4,16,16,128]{4,3,2,1,0:T(8,128)}, u32[]{:S(2)}) %copy-start) | copy-done | bytes 1048600
  1.9 0.2 copy.47
  2.2 0.0 copy-done.9
  2.2 0.0 copy-done.8
  2.2 0.1 select_reduce_fusion.1
  2.3 5.0 %collective-permute-start = (bf16[1,18,3,128]{3,1,2,0:T(8,128)(2,1)S(1)}, bf16[1,18,3,128]{3,1,2,0:T(8,128)(2,1)S(1)}, u32[]{:S(2)}, u32[]{:S(2)}) collective-permute-start(bf16[1,18,3,128]{3,1,2,0:T(8,128)(2,1)S(1)} %bitcast.187), channel_id=1, source_target_pairs={{0,4},{4,8},{8,12},{1,5},{5,9},{9,13},{2,6},{6,10},{10,14},{3,7},{... | collective-permute-start | bytes 41480 | tf_op jit(solution)/shard_map/ppermute | solution.py:12
  7.3 1.3 %collective-permute-start.1 = (bf16[1,18,3,128]{3,1,2,0:T(8,128)(2,1)S(1)}, bf16[1,18,3,128]{3,1,2,0:T(8,128)(2,1)S(1)}, u32[]{:S(2)}, u32[]{:S(2)}) collective-permute-start(bf16[1,18,3,128]{3,1,2,0:T(8,128)(2,1)S(1)} %bitcast.186), channel_id=1, source_target_pairs={{4,0},{8,4},{12,8},{5,1},{9,5},{13,9},{6,2},{10,6},{14,10},{7,3},{... | collective-permute-start | bytes 41480 | tf_op jit(solution)/shard_map/ppermute | solution.py:15
  8.6 0.1 fusion.56
  8.7 0.1 compare_and_fusion.2
  8.9 0.1 pad_maximum_fusion.6
  9.0 0.6 %gather_fusion.1 = bf16[4,18,3,128]{3,1,2,0:T(8,128)(2,1)S(1)} fusion(bf16[4,18,3,128]{3,1,2,0:T(8,128)(2,1)S(1)} %bitcast.183, s32[1024]{0:T(1024)S(1)} %pad_clamp_fusion.2), kind=kCustom, calls=%fused_computation.clone | custom fusion | bytes 110608 | tf_op jit(solution)/shard_map/jit(_take)/gather | solution.py:141
  9.6 0.6 %gather_fusion.2 = bf16[4,18,3,128]{3,1,2,0:T(8,128)(2,1)S(1)} fusion(bf16[4,18,3,128]{3,1,2,0:T(8,128)(2,1)S(1)} %bitcast.182, s32[1024]{0:T(1024)S(1)} %pad_clamp_fusion.1), kind=kCustom, calls=%fused_computation.1.clone | custom fusion | bytes 110608 | tf_op jit(solution)/shard_map/jit(_take)/gather | solution.py:144
  10.2 0.0 collective-permute-done
  10.2 0.1 fusion.20
  10.3 2.7 %collective-permute-done.1 = bf16[1,18,3,128]{3,1,2,0:T(8,128)(2,1)S(1)} collective-permute-done((bf16[1,18,3,128]{3,1,2,0:T(8,128)(2,1)S(1)}, bf16[1,18,3,128]{3,1,2,0:T(8,128)(2,1)S(1)}, u32[]{:S(2)}, u32[]{:S(2)}) %collective-permute-start.1) | collective-permute-done | bytes 13856 | tf_op jit(solution)/shard_map/ppermute | solution.py:15
  13.0 0.1 fusion.19
  13.0 0.2 pad_maximum_fusion.2
  13.2 0.9 %pad_slice_fusion.3 = (bf16[1,4,18,20,132]{4,2,3,1,0:T(8,128)(2,1)S(1)}, bf16[1,4,18,20,132]{4,2,3,1,0:T(8,128)(2,1)S(1)}, bf16[1,4,18,20,132]{4,2,3,1,0:T(8,128)(2,1)S(1)}) fusion(bf16[1,4,18,22,128]{4,2,3,1,0:T(8,128)(2,1)S(1)} %pad_maximum_fusion.2), kind=kLoop, calls=%fused_computation.10 | loop fusion | bytes 1545984 | tf_op jit(solution)/shard_map/slice | solution.py:26
  14.1 0.2 pad_slice_fusion
  14.3 1.1 %pad_maximum_fusion = bf16[1,4,54,20,132]{4,2,3,1,0:T(8,128)(2,1)S(1)} fusion(bf16[1,4,18,20,132]{4,2,3,1,0:T(8,128)(2,1)S(1)} %get-tuple-element.30, bf16[1,4,18,20,132]{4,2,3,1,0:T(8,128)(2,1)S(1)} %get-tuple-element.29, bf16[1,4,18,20,132]{4,2,3,1,0:T(8,128)(2,1)S(1)} %get-tuple-element.28), kind=kLoop, calls=%fused_computation.3 | loop fusion | flops 3421440 | bytes 2280960 | tf_op jit(solution)/shard_map/concatenate | solution.py:24
  15.4 0.5 %fusion.15 = f32[4,20,128,32]{2,3,1,0:T(8,128)S(1)} fusion(bf16[1,4,54,20,132]{4,2,3,1,0:T(8,128)(2,1)S(1)} %pad_maximum_fusion, bf16[32,18]{1,0:T(8,128)(2,1)S(1)} %get-tuple-element.39, bf16[32,18]{1,0:T(8,128)(2,1)S(1)} %get-tuple-element.40, bf16[32,18]{1,0:T(8,128)(2,1)S(1)} %get-tuple-element.41), kind=kOutput, calls=%fused_computation.33 | convolution fusion | flops 35399808 | bytes 2482176 | tf_op jit(solution)/shard_map/oi,bsirw->bsorw/dot_general | solution.py:50
  15.9 0.6 %convolution_add_fusion.1 = f32[4,20,128,32]{2,3,1,0:T(8,128)S(1)} fusion(f32[4,20,128,32]{2,3,1,0:T(8,128)S(1)} %fusion.15, bf16[1,4,54,20,132]{4,2,3,1,0:T(8,128)(2,1)S(1)} %pad_maximum_fusion, bf16[32,18]{1,0:T(8,128)(2,1)S(1)} %get-tuple-element.36, bf16[32,18]{1,0:T(8,128)(2,1)S(1)} %get-tuple-element.37, bf16[32,18]{1,0:T(8,128)(2,1)S(1)} %get-tuple-element.38), kind=kOutput, calls=%fused_computation.13 | convolution fusion | flops 35727488 | bytes 3792896 | tf_op jit(solution)/shard_map/oi,bsirw->bsorw/dot_general | solution.py:50
  16.5 0.7 %fusion.7 = f32[1,4,32,20,128]{4,2,3,1,0:T(8,128)S(1)} fusion(f32[4,20,128,32]{2,3,1,0:T(8,128)S(1)} %convolution_add_fusion.1, bf16[1,4,54,20,132]{4,2,3,1,0:T(8,128)(2,1)S(1)} %pad_maximum_fusion, f32[32]{0:T(128)S(1)} %pad_maximum_fusion.6, bf16[32,18]{1,0:T(8,128)(2,1)S(1)} %get-tuple-element.34, bf16[32,18]{1,0:T(8,128)(2,1)S(1)} %get-tuple-element.35, ...), kind=kOutput, calls=%fused_computation.19 | convolution fusion | flops 37038208 | bytes 3793408 | tf_op jit(solution)/shard_map/oi,bsirw->bsorw/dot_general | solution.py:50
  17.2 0.1 fusion.18
  17.3 0.6 %fusion.16 = bf16[1,4,18,20,132]{4,2,3,1,0:T(8,128)(2,1)S(1)} fusion(bf16[1,4,16,20,128]{4,2,3,1,0:T(8,128)(2,1)S(1)} %fusion.18, bf16[1,4,2,20,132]{4,2,3,1,0:T(2,128)(2,1)S(1)} %pad_slice_fusion), kind=kLoop, calls=%fused_computation.36 | loop fusion | flops 1140480 | bytes 750080 | tf_op jit(solution)/shard_map/concatenate | solution.py:174
  17.9 0.2 fusion.66
  18.1 0.8 %pad_maximum_fusion.1 = bf16[1,4,54,16,132]{4,2,3,1,0:T(8,128)(2,1)S(1)} fusion(bf16[1,4,18,16,132]{4,2,3,1,0:T(8,128)(2,1)S(1)} %get-tuple-element.24, bf16[1,4,18,16,132]{4,2,3,1,0:T(8,128)(2,1)S(1)} %get-tuple-element.25, bf16[1,4,18,16,132]{4,2,3,1,0:T(8,128)(2,1)S(1)} %get-tuple-element.23), kind=kLoop, calls=%fused_computation.6 | loop fusion | flops 2737152 | bytes 1824768 | tf_op jit(solution)/shard_map/concatenate | solution.py:24
  18.9 0.0 copy-start.11
  18.9 0.3 %fusion.17 = f32[4,16,128,16]{2,3,1,0:T(8,128)S(1)} fusion(bf16[1,4,54,16,132]{4,2,3,1,0:T(8,128)(2,1)S(1)} %pad_maximum_fusion.1, bf16[16,18]{1,0:T(8,128)(2,1)S(1)} %get-tuple-element.46, bf16[16,18]{1,0:T(8,128)(2,1)S(1)} %get-tuple-element.47, bf16[16,18]{1,0:T(8,128)(2,1)S(1)} %get-tuple-element.48), kind=kOutput, calls=%fused_computation.40 | convolution fusion | flops 14160960 | bytes 1454080 | tf_op jit(solution)/shard_map/oi,bsirw->bsorw/dot_general | solution.py:50
  19.2 0.5 %convolution_add_fusion.3 = f32[4,16,128,16]{2,3,1,0:T(8,128)S(1)} fusion(f32[4,16,128,16]{2,3,1,0:T(8,128)S(1)} %fusion.17, bf16[1,4,54,16,132]{4,2,3,1,0:T(8,128)(2,1)S(1)} %pad_maximum_fusion.1, bf16[16,18]{1,0:T(8,128)(2,1)S(1)} %get-tuple-element.43, bf16[16,18]{1,0:T(8,128)(2,1)S(1)} %get-tuple-element.44, bf16[16,18]{1,0:T(8,128)(2,1)S(1)} %get-tuple-element.45), kind=kOutput, calls=%fused_computation.22 | convolution fusion | flops 14292032 | bytes 1978368 | tf_op jit(solution)/shard_map/oi,bsirw->bsorw/dot_general | solution.py:50
  19.7 0.5 %fusion.14 = f32[1,4,16,16,128]{4,2,3,1,0:T(8,128)S(1)} fusion(f32[4,16,128,16]{2,3,1,0:T(8,128)S(1)} %convolution_add_fusion.3, bf16[1,4,54,16,132]{4,2,3,1,0:T(8,128)(2,1)S(1)} %pad_maximum_fusion.1, f32[1,4,32,20,128]{4,2,3,1,0:T(8,128)S(1)} %fusion.7, f32[1,4,16,16,128]{4,3,2,1,0:T(8,128)S(1)} %constant_dynamic-slice_fusion.2, ...), kind=kOutput, calls=%fused_computation.28 | convolution fusion | flops 15078464 | bytes 3027968 | tf_op jit(solution)/shard_map/oi,bsirw->bsorw/dot_general | solution.py:50
  20.2 0.4 %convolution_reduce_fusion = f32[4,16,4,32]{3,1,2,0:T(8,128)S(1)} fusion(f32[4,16,4,4,128]{4,1,3,2,0:T(8,128)S(1)} %bitcast.181, s32[128]{0:T(128)S(1)} %and_select_fusion), kind=kOutput, calls=%fused_computation.29 | convolution fusion | flops 50360320 | bytes 557568 | tf_op jit(solution)/shard_map/schw,wj->schj/dot_general | solution.py:200
  20.6 1.6 %collective-permute-start.3 = (f32[4,16,4,32]{3,1,2,0:T(8,128)S(1)}, f32[4,16,4,32]{3,1,2,0:T(8,128)S(1)}, u32[]{:S(2)}, u32[]{:S(2)}) collective-permute-start(f32[4,16,4,32]{3,1,2,0:T(8,128)S(1)} %broadcast_multiply_fusion), channel_id=1, source_target_pairs={{0,2},{2,0},{1,3},{3,1},{4,6},{6,4},{5,7},{7,5},{8,10},{10,8},{9,1... | collective-permute-start | bytes 98312 | tf_op jit(solution)/shard_map/ppermute | solution.py:209
  22.2 0.0 copy-start.1
  22.2 0.0 copy-start.7
  22.2 0.0 copy-start.10
  22.2 0.1 collective-permute-start.2
  22.3 3.3 %collective-permute-done.3 = f32[4,16,4,32]{3,1,2,0:T(8,128)S(1)} collective-permute-done((f32[4,16,4,32]{3,1,2,0:T(8,128)S(1)}, f32[4,16,4,32]{3,1,2,0:T(8,128)S(1)}, u32[]{:S(2)}, u32[]{:S(2)}) %collective-permute-start.3) | collective-permute-done | bytes 32800 | tf_op jit(solution)/shard_map/ppermute | solution.py:209
  25.7 0.6 %gather_fusion = f32[2,16,4,32]{3,1,2,0:T(8,128)S(1)} fusion(f32[4,16,4,32]{3,1,2,0:T(8,128)S(1)} %fusion.65, s32[1024]{0:T(1024)S(1)} %pad_clamp_fusion), kind=kCustom, calls=%fused_computation.2 | custom fusion | bytes 32776 | tf_op jit(solution)/shard_map/jit(_take)/gather | solution.py:214
  26.2 0.3 convolution_bitcast_fusion.1
  26.5 0.0 collective-permute-done.2
  26.5 0.1 select_add_fusion.1
  26.6 0.1 collective-permute-start.4
  26.7 0.9 %copy.27 = f32[2,4,8,16,128]{4,3,2,1,0:T(8,128)} copy(f32[2,4,8,16,128]{4,2,3,1,0:T(8,128)S(1)} %pad_maximum_fusion.3) | data formatting | bytes 1048576
  27.6 0.4 %collective-permute-done.4 = f32[2,16,4,32]{3,1,2,0:T(8,128)S(1)} collective-permute-done((f32[2,16,4,32]{3,1,2,0:T(8,128)S(1)}, f32[2,16,4,32]{3,1,2,0:T(8,128)S(1)}, u32[]{:S(2)}, u32[]{:S(2)}) %collective-permute-start.4) | collective-permute-done | bytes 16416 | tf_op jit(solution)/shard_map/ppermute | solution.py:70
  28.0 0.2 tanh_add_fusion
  28.2 0.7 %copy.28 = f32[2,16,4,32]{3,2,1,0:T(4,128)} copy(f32[2,16,4,32]{3,1,2,0:T(8,128)S(1)} %tanh_add_fusion) | data formatting | bytes 32768
  (40 shorter events, 0.3 us)
Async XLA Ops:
  0.6 1.2 %copy-start = (f32[2,4,16,16,128]{4,3,2,1,0:T(8,128)S(1)}, f32[2,4,16,16,128]{4,3,2,1,0:T(8,128)}, u32[]{:S(2)}) copy-start(f32[2,4,16,16,128]{4,3,2,1,0:T(8,128)} %param.18) | copy-start | bytes 3145732
  0.6 1.4 %copy-start.5 = (bf16[2,4,2,16,128]{4,3,2,1,0:T(8,128)(2,1)S(1)}, bf16[2,4,2,16,128]{4,3,2,1,0:T(8,128)(2,1)}, u32[]{:S(2)}) copy-start(bf16[2,4,2,16,128]{4,3,2,1,0:T(8,128)(2,1)} %param.17) | copy-start | bytes 196612
  0.7 1.5 %copy-start.9 = (s32[4]{0:T(128)S(1)}, s32[4]{0:T(128)}, u32[]{:S(2)}) copy-start(s32[4]{0:T(128)} %param.19) | copy-start | bytes 52
  0.7 1.5 %copy-start.8 = (s32[4,2]{0,1:T(2,128)S(1)}, s32[4,2]{0,1:T(2,128)}, u32[]{:S(2)}) copy-start(s32[4,2]{0,1:T(2,128)} %param.20) | copy-start | bytes 100
  0.7 7.9 %copy-start.12 = (s32[1,4]{1,0:T(1,128)S(1)}, s32[1,4]{1,0:T(1,128)}, u32[]{:S(2)}) copy-start(s32[1,4]{1,0:T(1,128)} %param.21) | copy-start | bytes 52
  0.7 8.1 %copy-start.2 = (bf16[9,16,18]{2,1,0:T(8,128)(2,1)S(1)}, bf16[9,16,18]{2,1,0:T(8,128)(2,1)}, u32[]{:S(2)}) copy-start(bf16[9,16,18]{2,1,0:T(8,128)(2,1)} %param.23) | copy-start | bytes 15556
  0.7 8.1 %copy-start.3 = (bf16[9,16,18]{2,1,0:T(8,128)(2,1)S(1)}, bf16[9,16,18]{2,1,0:T(8,128)(2,1)}, u32[]{:S(2)}) copy-start(bf16[9,16,18]{2,1,0:T(8,128)(2,1)} %param.25) | copy-start | bytes 15556
  0.7 8.2 %copy-start.4 = (bf16[9,16,18]{2,1,0:T(8,128)(2,1)S(1)}, bf16[9,16,18]{2,1,0:T(8,128)(2,1)}, u32[]{:S(2)}) copy-start(bf16[9,16,18]{2,1,0:T(8,128)(2,1)} %param.27) | copy-start | bytes 15556
  0.7 8.2 %copy-start.14 = (f32[16]{0:T(128)S(1)}, f32[16]{0:T(128)}, u32[]{:S(2)}) copy-start(f32[16]{0:T(128)} %param.24) | copy-start | bytes 196
  0.7 8.2 %copy-start.13 = (f32[16]{0:T(128)S(1)}, f32[16]{0:T(128)}, u32[]{:S(2)}) copy-start(f32[16]{0:T(128)} %param.26) | copy-start | bytes 196
  2.3 7.8 %collective-permute-start = (bf16[1,18,3,128]{3,1,2,0:T(8,128)(2,1)S(1)}, bf16[1,18,3,128]{3,1,2,0:T(8,128)(2,1)S(1)}, u32[]{:S(2)}, u32[]{:S(2)}) collective-permute-start(bf16[1,18,3,128]{3,1,2,0:T(8,128)(2,1)S(1)} %bitcast.187), channel_id=1, source_target_pairs={{0,4},{4,8},{8,12},{1,5},{5,9},{9,13},{2,6},{6,10},{10,14},{3,7},{... | collective-permute-start | bytes 41480 | tf_op jit(solution)/shard_map/ppermute | solution.py:12
  7.3 5.7 %collective-permute-start.1 = (bf16[1,18,3,128]{3,1,2,0:T(8,128)(2,1)S(1)}, bf16[1,18,3,128]{3,1,2,0:T(8,128)(2,1)S(1)}, u32[]{:S(2)}, u32[]{:S(2)}) collective-permute-start(bf16[1,18,3,128]{3,1,2,0:T(8,128)(2,1)S(1)} %bitcast.186), channel_id=1, source_target_pairs={{4,0},{8,4},{12,8},{5,1},{9,5},{13,9},{6,2},{10,6},{14,10},{7,3},{... | collective-permute-start | bytes 41480 | tf_op jit(solution)/shard_map/ppermute | solution.py:15
  18.9 0.8 %copy-start.11 = (f32[16]{0:T(128)S(1)}, f32[16]{0:T(128)}, u32[]{:S(2)}) copy-start(f32[16]{0:T(128)} %param.28) | copy-start | bytes 196
  19.7 6.5 %copy-start.6 = (f32[16,16]{1,0:T(8,128)S(1)}, f32[16,16]{1,0:T(8,128)}, u32[]{:S(2)}) copy-start(f32[16,16]{1,0:T(8,128)} %param.29) | copy-start | bytes 3076
  20.6 5.0 %collective-permute-start.3 = (f32[4,16,4,32]{3,1,2,0:T(8,128)S(1)}, f32[4,16,4,32]{3,1,2,0:T(8,128)S(1)}, u32[]{:S(2)}, u32[]{:S(2)}) collective-permute-start(f32[4,16,4,32]{3,1,2,0:T(8,128)S(1)} %broadcast_multiply_fusion), channel_id=1, source_target_pairs={{0,2},{2,0},{1,3},{3,1},{4,6},{6,4},{5,7},{7,5},{8,10},{10,8},{9,1... | collective-permute-start | bytes 98312 | tf_op jit(solution)/shard_map/ppermute | solution.py:209
  22.2 5.8 %copy-start.1 = (f32[2,16,4,32]{3,2,1,0:T(4,128)S(1)}, f32[2,16,4,32]{3,2,1,0:T(4,128)}, u32[]{:S(2)}) copy-start(f32[2,16,4,32]{3,2,1,0:T(4,128)} %param.22) | copy-start | bytes 49156
  22.2 5.8 %copy-start.7 = (f32[16,16]{1,0:T(8,128)S(1)}, f32[16,16]{1,0:T(8,128)}, u32[]{:S(2)}) copy-start(f32[16,16]{1,0:T(8,128)} %param.30) | copy-start | bytes 3076
  22.2 5.7 %copy-start.10 = (f32[16]{0:T(128)S(1)}, f32[16]{0:T(128)}, u32[]{:S(2)}) copy-start(f32[16]{0:T(128)} %param.31) | copy-start | bytes 196
  22.2 4.3 %collective-permute-start.2 = (f32[1,4,8,16,128]{4,2,3,1,0:T(8,128)S(1)}, f32[1,4,8,16,128]{4,2,3,1,0:T(8,128)S(1)}, u32[]{:S(2)}, u32[]{:S(2)}) collective-permute-start(f32[1,4,8,16,128]{4,2,3,1,0:T(8,128)S(1)} %constant_dynamic-slice_fusion.1), channel_id=1, source_target_pairs={{0,1},{1,0},{2,3},{3,2},{4,5},{5,4},{6,7},{7,6},{8,9},{9,8},{10,11... | collective-permute-start | bytes 786440 | tf_op jit(solution)/shard_map/ppermute | solution.py:184
  26.6 1.3 %collective-permute-start.4 = (f32[2,16,4,32]{3,1,2,0:T(8,128)S(1)}, f32[2,16,4,32]{3,1,2,0:T(8,128)S(1)}, u32[]{:S(2)}, u32[]{:S(2)}) collective-permute-start(f32[2,16,4,32]{3,1,2,0:T(8,128)S(1)} %convolution_bitcast_fusion.1), channel_id=1, source_target_pairs={{0,1},{1,0},{2,3},{3,2},{4,5},{5,4},{6,7},{7,6},{8,9},{9,8},{10,11... | collective-permute-start | bytes 49160 | tf_op jit(solution)/shard_map/ppermute | solution.py:70

commit v22 on v20

--- a/solution.py
+++ b/solution.py
@@ -71,13 +71,12 @@
     return total
 
 
-def exchange_sum(part, owned):
+def exchange_sum(make_chunk):
     bands = lax.axis_size("band")
     band = lax.axis_index("band")
     total = None
-    for shift in range(bands):
-        target = (band + shift) % bands
-        chunk = lax.dynamic_slice_in_dim(part, target * owned, owned, 0)
+    for shift in list(range(1, bands)) + [0]:
+        chunk = make_chunk((band + shift) % bands)
         if shift:
             perm = [(b, (b + shift) % bands) for b in range(bands)]
             chunk = lax.ppermute(chunk, "band", perm)
@@ -203,11 +202,14 @@
     pooled = jnp.sum(
         cols.reshape(slots, chans, row_count // 4, 4, column_count // 4), axis=3
     ) / 16.0
-    ordered = jnp.take(pooled, coarse_perm[0], axis=0)
-    part = jnp.einsum("oc,kcij->koij", u_pool, ordered, precision=lax.Precision.HIGHEST)
-    new_half, band_part = lax.optimization_barrier(
-        (new_half, exchange_sum(part, coarse_state.shape[0]))
-    )
+    owned = coarse_state.shape[0]
+
+    def make_chunk(target):
+        picked = lax.dynamic_slice_in_dim(coarse_perm[0], target * owned, owned, 0)
+        ordered = jnp.take(pooled, picked, axis=0)
+        return jnp.einsum("oc,kcij->koij", u_pool, ordered, precision=lax.Precision.HIGHEST)
+
+    new_half, band_part = lax.optimization_barrier((new_half, exchange_sum(make_chunk)))
     pre = rep_sum(band_part)
     pre = pre + jnp.einsum("oc,kcij->koij", u_state, coarse_state, precision=lax.Precision.HIGHEST)
     pre = pre + b_coarse[None, :, None, None]

time: 28.6 us -> 28.4 us (level)
  waiting for transfers between devices: 5.99 us -> 4.93 us
  local copies, waits for them, and re-layouts: 5.96 us -> 6.48 us
    ppermute x1, waiting for transfers between devices: 3 us -> 2.05 us  [exchange_sum(): chunk = lax.ppermute(chunk, 'band', perm)]
    gather x1 -> x2, local copies, waits for them, and re-layouts: 0.56 us -> 1.11 us  [make_chunk(): ordered = jnp.take(pooled, picked, axis=0)]
where the time goes in v22:
time: 28.4 us; the launch traced here: 28.3 us
  starting transfers between devices  7.95 us (28%)
  local copies, waits for them, and re-layouts  6.48 us (23%)
  waiting for transfers between devices  4.93 us (17%)
  matrix products  4.18 us (15%)
  other arithmetic  3.47 us (12%)
  between operations  1.25 us (4%)
    ppermute x1, starting transfers between devices, padded(): lax.ppermute(lax.slice_in_dim(block, block.shape[dim] - width, None, axis...  4.96 us
    dot_general x6, matrix products, apply_filter(): jnp.einsum('oi,bsirw->bsorw', weight, window_slice, preferred_element_typ...  3.11 us
    unnamed x35, local copies, waits for them, and re-layouts  2.95 us
    ppermute x1, waiting for transfers between devices, padded(): lax.ppermute(lax.slice_in_dim(block, 0, width, axis=dim), axis, backward)  2.75 us
    ppermute x1, waiting for transfers between devices, exchange_sum(): chunk = lax.ppermute(chunk, 'band', perm)  2.05 us
    concatenate x2, other arithmetic, apply_filter(): jnp.concatenate([padded_input[:, :, :, first_row_index + row_offset * dil...  1.93 us
    ppermute x1, starting transfers between devices, exchange_sum(): chunk = lax.ppermute(chunk, 'band', perm)  1.55 us
    ppermute x1, starting transfers between devices, padded(): lax.ppermute(lax.slice_in_dim(block, 0, width, axis=dim), axis, backward)  1.29 us
  transfers between devices with their start and end apart: 5, of which 3 were waited for; matrix products, arithmetic and copies ran while one was open for 12% of the time, Pallas kernels for 0%

profile of v22, /device:TPU:0, one launch (start us, length us, event | category | flops | bytes accessed | tf_op | source)
XLA Modules:
  0.0 28.3 jit_solution(11408487373892352934)
XLA Ops:
  0.6 0.0 copy-start
  0.7 1.1 %copy-done = f32[2,4,16,16,128]{4,3,2,1,0:T(8,128)S(1)} copy-done((f32[2,4,16,16,128]{4,3,2,1,0:T(8,128)S(1)}, f32[2,4,16,16,128]{4,3,2,1,0:T(8,128)}, u32[]{:S(2)}) %copy-start) | copy-done | bytes 1048600
  1.9 0.2 copy.45
  2.2 0.1 select_reduce_fusion.1
  2.3 5.0 %collective-permute-start = (bf16[1,18,3,128]{3,1,2,0:T(8,128)(2,1)S(1)}, bf16[1,18,3,128]{3,1,2,0:T(8,128)(2,1)S(1)}, u32[]{:S(2)}, u32[]{:S(2)}) collective-permute-start(bf16[1,18,3,128]{3,1,2,0:T(8,128)(2,1)S(1)} %bitcast.195), channel_id=1, source_target_pairs={{0,4},{4,8},{8,12},{1,5},{5,9},{9,13},{2,6},{6,10},{10,14},{3,7},{... | collective-permute-start | bytes 41480 | tf_op jit(solution)/shard_map/ppermute | solution.py:12
  7.3 1.3 %collective-permute-start.1 = (bf16[1,18,3,128]{3,1,2,0:T(8,128)(2,1)S(1)}, bf16[1,18,3,128]{3,1,2,0:T(8,128)(2,1)S(1)}, u32[]{:S(2)}, u32[]{:S(2)}) collective-permute-start(bf16[1,18,3,128]{3,1,2,0:T(8,128)(2,1)S(1)} %bitcast.194), channel_id=1, source_target_pairs={{4,0},{8,4},{12,8},{5,1},{9,5},{13,9},{6,2},{10,6},{14,10},{7,3},{... | collective-permute-start | bytes 41480 | tf_op jit(solution)/shard_map/ppermute | solution.py:15
  8.8 0.1 compare_and_fusion
  8.9 0.1 pad_maximum_fusion.6
  9.0 0.6 %gather_fusion = bf16[4,18,3,128]{3,1,2,0:T(8,128)(2,1)S(1)} fusion(bf16[4,18,3,128]{3,1,2,0:T(8,128)(2,1)S(1)} %bitcast.191, s32[1024]{0:T(1024)S(1)} %pad_clamp_fusion.3), kind=kCustom, calls=%fused_computation.clone | custom fusion | bytes 110608 | tf_op jit(solution)/shard_map/jit(_take)/gather | solution.py:140
  9.5 0.6 %gather_fusion.1 = bf16[4,18,3,128]{3,1,2,0:T(8,128)(2,1)S(1)} fusion(bf16[4,18,3,128]{3,1,2,0:T(8,128)(2,1)S(1)} %bitcast.190, s32[1024]{0:T(1024)S(1)} %pad_clamp_fusion.2), kind=kCustom, calls=%fused_computation.2.clone | custom fusion | bytes 110608 | tf_op jit(solution)/shard_map/jit(_take)/gather | solution.py:143
  10.1 0.0 collective-permute-done
  10.1 0.1 fusion.21
  10.2 2.7 %collective-permute-done.1 = bf16[1,18,3,128]{3,1,2,0:T(8,128)(2,1)S(1)} collective-permute-done((bf16[1,18,3,128]{3,1,2,0:T(8,128)(2,1)S(1)}, bf16[1,18,3,128]{3,1,2,0:T(8,128)(2,1)S(1)}, u32[]{:S(2)}, u32[]{:S(2)}) %collective-permute-start.1) | collective-permute-done | bytes 13856 | tf_op jit(solution)/shard_map/ppermute | solution.py:15
  13.0 0.1 fusion.20
  13.0 0.2 pad_maximum_fusion.2
  13.2 0.9 %pad_slice_fusion.3 = (bf16[1,4,18,20,132]{4,2,3,1,0:T(8,128)(2,1)S(1)}, bf16[1,4,18,20,132]{4,2,3,1,0:T(8,128)(2,1)S(1)}, bf16[1,4,18,20,132]{4,2,3,1,0:T(8,128)(2,1)S(1)}) fusion(bf16[1,4,18,22,128]{4,2,3,1,0:T(8,128)(2,1)S(1)} %pad_maximum_fusion.2), kind=kLoop, calls=%fused_computation.11 | loop fusion | bytes 1545984 | tf_op jit(solution)/shard_map/slice | solution.py:26
  14.1 0.2 pad_slice_fusion
  14.3 1.1 %pad_maximum_fusion = bf16[1,4,54,20,132]{4,2,3,1,0:T(8,128)(2,1)S(1)} fusion(bf16[1,4,18,20,132]{4,2,3,1,0:T(8,128)(2,1)S(1)} %get-tuple-element.35, bf16[1,4,18,20,132]{4,2,3,1,0:T(8,128)(2,1)S(1)} %get-tuple-element.34, bf16[1,4,18,20,132]{4,2,3,1,0:T(8,128)(2,1)S(1)} %get-tuple-element.33), kind=kLoop, calls=%fused_computation.4 | loop fusion | flops 3421440 | bytes 2280960 | tf_op jit(solution)/shard_map/concatenate | solution.py:24
  15.4 0.5 %fusion.15 = f32[4,20,128,32]{2,3,1,0:T(8,128)S(1)} fusion(bf16[1,4,54,20,132]{4,2,3,1,0:T(8,128)(2,1)S(1)} %pad_maximum_fusion, bf16[32,18]{1,0:T(8,128)(2,1)S(1)} %get-tuple-element.44, bf16[32,18]{1,0:T(8,128)(2,1)S(1)} %get-tuple-element.45, bf16[32,18]{1,0:T(8,128)(2,1)S(1)} %get-tuple-element.46), kind=kOutput, calls=%fused_computation.34 | convolution fusion | flops 35399808 | bytes 2482176 | tf_op jit(solution)/shard_map/oi,bsirw->bsorw/dot_general | solution.py:50
  15.9 0.6 %convolution_add_fusion.1 = f32[4,20,128,32]{2,3,1,0:T(8,128)S(1)} fusion(f32[4,20,128,32]{2,3,1,0:T(8,128)S(1)} %fusion.15, bf16[1,4,54,20,132]{4,2,3,1,0:T(8,128)(2,1)S(1)} %pad_maximum_fusion, bf16[32,18]{1,0:T(8,128)(2,1)S(1)} %get-tuple-element.41, bf16[32,18]{1,0:T(8,128)(2,1)S(1)} %get-tuple-element.42, bf16[32,18]{1,0:T(8,128)(2,1)S(1)} %get-tuple-element.43), kind=kOutput, calls=%fused_computation.14 | convolution fusion | flops 35727488 | bytes 3792896 | tf_op jit(solution)/shard_map/oi,bsirw->bsorw/dot_general | solution.py:50
  16.5 0.7 %fusion.7 = f32[1,4,32,20,128]{4,2,3,1,0:T(8,128)S(1)} fusion(f32[4,20,128,32]{2,3,1,0:T(8,128)S(1)} %convolution_add_fusion.1, bf16[1,4,54,20,132]{4,2,3,1,0:T(8,128)(2,1)S(1)} %pad_maximum_fusion, f32[32]{0:T(128)S(1)} %pad_maximum_fusion.6, bf16[32,18]{1,0:T(8,128)(2,1)S(1)} %get-tuple-element.39, bf16[32,18]{1,0:T(8,128)(2,1)S(1)} %get-tuple-element.40, ...), kind=kOutput, calls=%fused_computation.20 | convolution fusion | flops 37038208 | bytes 3793408 | tf_op jit(solution)/shard_map/oi,bsirw->bsorw/dot_general | solution.py:50
  17.2 0.1 fusion.19
  17.3 0.6 %fusion.17 = bf16[1,4,18,20,132]{4,2,3,1,0:T(8,128)(2,1)S(1)} fusion(bf16[1,4,16,20,128]{4,2,3,1,0:T(8,128)(2,1)S(1)} %fusion.19, bf16[1,4,2,20,132]{4,2,3,1,0:T(2,128)(2,1)S(1)} %pad_slice_fusion), kind=kLoop, calls=%fused_computation.39 | loop fusion | flops 1140480 | bytes 750080 | tf_op jit(solution)/shard_map/concatenate | solution.py:173
  17.9 0.2 fusion.70
  18.1 0.8 %pad_maximum_fusion.1 = bf16[1,4,54,16,132]{4,2,3,1,0:T(8,128)(2,1)S(1)} fusion(bf16[1,4,18,16,132]{4,2,3,1,0:T(8,128)(2,1)S(1)} %get-tuple-element.29, bf16[1,4,18,16,132]{4,2,3,1,0:T(8,128)(2,1)S(1)} %get-tuple-element.30, bf16[1,4,18,16,132]{4,2,3,1,0:T(8,128)(2,1)S(1)} %get-tuple-element.28), kind=kLoop, calls=%fused_computation.7 | loop fusion | flops 2737152 | bytes 1824768 | tf_op jit(solution)/shard_map/concatenate | solution.py:24
  18.9 0.0 copy-start.12
  18.9 0.3 %fusion.18 = f32[4,16,128,16]{2,3,1,0:T(8,128)S(1)} fusion(bf16[1,4,54,16,132]{4,2,3,1,0:T(8,128)(2,1)S(1)} %pad_maximum_fusion.1, bf16[16,18]{1,0:T(8,128)(2,1)S(1)} %get-tuple-element.51, bf16[16,18]{1,0:T(8,128)(2,1)S(1)} %get-tuple-element.52, bf16[16,18]{1,0:T(8,128)(2,1)S(1)} %get-tuple-element.53), kind=kOutput, calls=%fused_computation.43 | convolution fusion | flops 14160960 | bytes 1454080 | tf_op jit(solution)/shard_map/oi,bsirw->bsorw/dot_general | solution.py:50
  19.2 0.5 %convolution_add_fusion.3 = f32[4,16,128,16]{2,3,1,0:T(8,128)S(1)} fusion(f32[4,16,128,16]{2,3,1,0:T(8,128)S(1)} %fusion.18, bf16[1,4,54,16,132]{4,2,3,1,0:T(8,128)(2,1)S(1)} %pad_maximum_fusion.1, bf16[16,18]{1,0:T(8,128)(2,1)S(1)} %get-tuple-element.48, bf16[16,18]{1,0:T(8,128)(2,1)S(1)} %get-tuple-element.49, bf16[16,18]{1,0:T(8,128)(2,1)S(1)} %get-tuple-element.50), kind=kOutput, calls=%fused_computation.23 | convolution fusion | flops 14292032 | bytes 1978368 | tf_op jit(solution)/shard_map/oi,bsirw->bsorw/dot_general | solution.py:50
  19.7 0.5 %fusion.14 = f32[1,4,16,16,128]{4,2,3,1,0:T(8,128)S(1)} fusion(f32[4,16,128,16]{2,3,1,0:T(8,128)S(1)} %convolution_add_fusion.3, bf16[1,4,54,16,132]{4,2,3,1,0:T(8,128)(2,1)S(1)} %pad_maximum_fusion.1, f32[1,4,32,20,128]{4,2,3,1,0:T(8,128)S(1)} %fusion.7, f32[1,4,16,16,128]{4,3,2,1,0:T(8,128)S(1)} %constant_dynamic-slice_fusion.3, ...), kind=kOutput, calls=%fused_computation.29 | convolution fusion | flops 15078464 | bytes 3027968 | tf_op jit(solution)/shard_map/oi,bsirw->bsorw/dot_general | solution.py:50
  20.2 0.4 %convolution_reduce_fusion = f32[4,16,4,32]{3,1,2,0:T(8,128)S(1)} fusion(f32[4,16,4,4,128]{4,1,3,2,0:T(8,128)S(1)} %bitcast.189, s32[128]{0:T(128)S(1)} %and_select_fusion), kind=kOutput, calls=%fused_computation.30 | convolution fusion | flops 50360320 | bytes 557568 | tf_op jit(solution)/shard_map/schw,wj->schj/dot_general | solution.py:199
  20.6 0.0 copy-start.1
  20.6 0.0 copy-start.7
  20.6 0.6 %gather_fusion.2 = f32[2,16,4,32]{3,1,2,0:T(8,128)S(1)} fusion(f32[4,16,4,32]{3,1,2,0:T(8,128)S(1)} %broadcast_multiply_fusion, s32[1024]{0:T(1024)S(1)} %pad_clamp_fusion.1), kind=kCustom, calls=%fused_computation.1.clone | custom fusion | bytes 32776 | tf_op jit(solution)/shard_map/jit(_take)/gather | solution.py:209
  21.2 0.3 convolution_bitcast_fusion.2
  21.5 1.6 %collective-permute-start.3 = (f32[2,16,4,32]{3,1,2,0:T(8,128)S(1)}, f32[2,16,4,32]{3,1,2,0:T(8,128)S(1)}, u32[]{:S(2)}, u32[]{:S(2)}) collective-permute-start(f32[2,16,4,32]{3,1,2,0:T(8,128)S(1)} %convolution_bitcast_fusion.2), channel_id=1, source_target_pairs={{0,2},{2,0},{1,3},{3,1},{4,6},{6,4},{5,7},{7,5},{8,10},{10,8},{9,1... | collective-permute-start | bytes 49160 | tf_op jit(solution)/shard_map/ppermute | solution.py:82
  23.1 0.1 collective-permute-start.2
  23.2 0.0 copy-start.11
  23.2 0.6 %gather_fusion.3 = f32[2,16,4,32]{3,1,2,0:T(8,128)S(1)} fusion(f32[4,16,4,32]{3,1,2,0:T(8,128)S(1)} %broadcast_multiply_fusion, s32[1024]{0:T(1024)S(1)} %pad_clamp_fusion), kind=kCustom, calls=%fused_computation.3.clone | custom fusion | bytes 32776 | tf_op jit(solution)/shard_map/jit(_take)/gather | solution.py:209
  23.8 2.1 %collective-permute-done.3 = f32[2,16,4,32]{3,1,2,0:T(8,128)S(1)} collective-permute-done((f32[2,16,4,32]{3,1,2,0:T(8,128)S(1)}, f32[2,16,4,32]{3,1,2,0:T(8,128)S(1)}, u32[]{:S(2)}, u32[]{:S(2)}) %collective-permute-start.3) | collective-permute-done | bytes 16416 | tf_op jit(solution)/shard_map/ppermute | solution.py:82
  25.8 0.3 fusion.16
  26.1 0.0 collective-permute-done.2
  26.1 0.1 select_add_fusion.1
  26.2 0.1 collective-permute-start.4
  26.3 0.2 convolution_bitcast_fusion
  26.5 0.9 %copy.27 = f32[2,4,8,16,128]{4,3,2,1,0:T(8,128)} copy(f32[2,4,8,16,128]{4,2,3,1,0:T(8,128)S(1)} %pad_maximum_fusion.3) | data formatting | bytes 1048576
  27.4 0.1 collective-permute-done.4
  27.5 0.1 tanh_add_fusion
  27.6 0.7 %copy.28 = f32[2,16,4,32]{3,2,1,0:T(4,128)} copy(f32[2,16,4,32]{3,1,2,0:T(8,128)S(1)} %tanh_add_fusion) | data formatting | bytes 32768
  (42 shorter events, 0.3 us)
Async XLA Ops:
  0.6 1.2 %copy-start = (f32[2,4,16,16,128]{4,3,2,1,0:T(8,128)S(1)}, f32[2,4,16,16,128]{4,3,2,1,0:T(8,128)}, u32[]{:S(2)}) copy-start(f32[2,4,16,16,128]{4,3,2,1,0:T(8,128)} %param.20) | copy-start | bytes 3145732
  0.6 1.4 %copy-start.6 = (bf16[2,4,2,16,128]{4,3,2,1,0:T(8,128)(2,1)S(1)}, bf16[2,4,2,16,128]{4,3,2,1,0:T(8,128)(2,1)}, u32[]{:S(2)}) copy-start(bf16[2,4,2,16,128]{4,3,2,1,0:T(8,128)(2,1)} %param.19) | copy-start | bytes 196612
  0.7 1.5 %copy-start.9 = (s32[4]{0:T(128)S(1)}, s32[4]{0:T(128)}, u32[]{:S(2)}) copy-start(s32[4]{0:T(128)} %param.21) | copy-start | bytes 52
  0.7 1.5 %copy-start.8 = (s32[4,2]{0,1:T(2,128)S(1)}, s32[4,2]{0,1:T(2,128)}, u32[]{:S(2)}) copy-start(s32[4,2]{0,1:T(2,128)} %param.22) | copy-start | bytes 100
  0.7 8.0 %copy-start.2 = (bf16[9,16,18]{2,1,0:T(8,128)(2,1)S(1)}, bf16[9,16,18]{2,1,0:T(8,128)(2,1)}, u32[]{:S(2)}) copy-start(bf16[9,16,18]{2,1,0:T(8,128)(2,1)} %param.25) | copy-start | bytes 15556
  0.7 8.0 %copy-start.3 = (bf16[9,16,18]{2,1,0:T(8,128)(2,1)S(1)}, bf16[9,16,18]{2,1,0:T(8,128)(2,1)}, u32[]{:S(2)}) copy-start(bf16[9,16,18]{2,1,0:T(8,128)(2,1)} %param.27) | copy-start | bytes 15556
  0.7 8.0 %copy-start.4 = (bf16[9,16,18]{2,1,0:T(8,128)(2,1)S(1)}, bf16[9,16,18]{2,1,0:T(8,128)(2,1)}, u32[]{:S(2)}) copy-start(bf16[9,16,18]{2,1,0:T(8,128)(2,1)} %param.29) | copy-start | bytes 15556
  0.7 8.1 %copy-start.10 = (s32[1,4]{1,0:T(1,128)S(1)}, s32[1,4]{1,0:T(1,128)}, u32[]{:S(2)}) copy-start(s32[1,4]{1,0:T(1,128)} %param.23) | copy-start | bytes 52
  0.7 8.1 %copy-start.14 = (f32[16]{0:T(128)S(1)}, f32[16]{0:T(128)}, u32[]{:S(2)}) copy-start(f32[16]{0:T(128)} %param.26) | copy-start | bytes 196
  0.7 8.1 %copy-start.13 = (f32[16]{0:T(128)S(1)}, f32[16]{0:T(128)}, u32[]{:S(2)}) copy-start(f32[16]{0:T(128)} %param.28) | copy-start | bytes 196
  2.3 7.8 %collective-permute-start = (bf16[1,18,3,128]{3,1,2,0:T(8,128)(2,1)S(1)}, bf16[1,18,3,128]{3,1,2,0:T(8,128)(2,1)S(1)}, u32[]{:S(2)}, u32[]{:S(2)}) collective-permute-start(bf16[1,18,3,128]{3,1,2,0:T(8,128)(2,1)S(1)} %bitcast.195), channel_id=1, source_target_pairs={{0,4},{4,8},{8,12},{1,5},{5,9},{9,13},{2,6},{6,10},{10,14},{3,7},{... | collective-permute-start | bytes 41480 | tf_op jit(solution)/shard_map/ppermute | solution.py:12
  7.3 5.7 %collective-permute-start.1 = (bf16[1,18,3,128]{3,1,2,0:T(8,128)(2,1)S(1)}, bf16[1,18,3,128]{3,1,2,0:T(8,128)(2,1)S(1)}, u32[]{:S(2)}, u32[]{:S(2)}) collective-permute-start(bf16[1,18,3,128]{3,1,2,0:T(8,128)(2,1)S(1)} %bitcast.194), channel_id=1, source_target_pairs={{4,0},{8,4},{12,8},{5,1},{9,5},{13,9},{6,2},{10,6},{14,10},{7,3},{... | collective-permute-start | bytes 41480 | tf_op jit(solution)/shard_map/ppermute | solution.py:15
  18.9 0.8 %copy-start.12 = (f32[16]{0:T(128)S(1)}, f32[16]{0:T(128)}, u32[]{:S(2)}) copy-start(f32[16]{0:T(128)} %param.30) | copy-start | bytes 196
  19.7 1.5 %copy-start.5 = (f32[16,16]{1,0:T(8,128)S(1)}, f32[16,16]{1,0:T(8,128)}, u32[]{:S(2)}) copy-start(f32[16,16]{1,0:T(8,128)} %param.31) | copy-start | bytes 3076
  20.6 5.7 %copy-start.1 = (f32[2,16,4,32]{3,2,1,0:T(4,128)S(1)}, f32[2,16,4,32]{3,2,1,0:T(4,128)}, u32[]{:S(2)}) copy-start(f32[2,16,4,32]{3,2,1,0:T(4,128)} %param.24) | copy-start | bytes 49156
  20.6 5.7 %copy-start.7 = (f32[16,16]{1,0:T(8,128)S(1)}, f32[16,16]{1,0:T(8,128)}, u32[]{:S(2)}) copy-start(f32[16,16]{1,0:T(8,128)} %param.32) | copy-start | bytes 3076
  21.5 4.3 %collective-permute-start.3 = (f32[2,16,4,32]{3,1,2,0:T(8,128)S(1)}, f32[2,16,4,32]{3,1,2,0:T(8,128)S(1)}, u32[]{:S(2)}, u32[]{:S(2)}) collective-permute-start(f32[2,16,4,32]{3,1,2,0:T(8,128)S(1)} %convolution_bitcast_fusion.2), channel_id=1, source_target_pairs={{0,2},{2,0},{1,3},{3,1},{4,6},{6,4},{5,7},{7,5},{8,10},{10,8},{9,1... | collective-permute-start | bytes 49160 | tf_op jit(solution)/shard_map/ppermute | solution.py:82
  23.1 3.0 %collective-permute-start.2 = (f32[1,4,8,16,128]{4,2,3,1,0:T(8,128)S(1)}, f32[1,4,8,16,128]{4,2,3,1,0:T(8,128)S(1)}, u32[]{:S(2)}, u32[]{:S(2)}) collective-permute-start(f32[1,4,8,16,128]{4,2,3,1,0:T(8,128)S(1)} %constant_dynamic-slice_fusion.2), channel_id=1, source_target_pairs={{0,1},{1,0},{2,3},{3,2},{4,5},{5,4},{6,7},{7,6},{8,9},{9,8},{10,11... | collective-permute-start | bytes 786440 | tf_op jit(solution)/shard_map/ppermute | solution.py:183
  23.2 4.4 %copy-start.11 = (f32[16]{0:T(128)S(1)}, f32[16]{0:T(128)}, u32[]{:S(2)}) copy-start(f32[16]{0:T(128)} %param.33) | copy-start | bytes 196
  26.2 1.3 %collective-permute-start.4 = (f32[2,16,4,32]{3,1,2,0:T(8,128)S(1)}, f32[2,16,4,32]{3,1,2,0:T(8,128)S(1)}, u32[]{:S(2)}, u32[]{:S(2)}) collective-permute-start(f32[2,16,4,32]{3,1,2,0:T(8,128)S(1)} %fusion.16), channel_id=1, source_target_pairs={{0,1},{1,0},{2,3},{3,2},{4,5},{5,4},{6,7},{7,6},{8,9},{9,8},{10,11... | collective-permute-start | bytes 49160 | tf_op jit(solution)/shard_map/ppermute | solution.py:70
